TPU v7x, 32 devices: a whole 2x2x4 slice. The times are simulated.
32 devices in a mesh: segment: 4 (over y, core), seq: 8 (over z, x).
Axes of the slice: x: 2, y: 2, z: 4, core: 2. Of those that a mesh axis runs over, the one named last changes fastest.
Arguments:
- patches: float32 [2, 1024, 128], P(None, 'seq'), may hold values from -6 to 6
- tile_list: int32 [8, 4], replicated, may hold values from 0 to 7, as said below
- input_weight: bfloat16 [4, 128, 1024], P('segment'), may hold values from -0.5 to 0.5
- attention_weight: bfloat16 [4, 1024, 3072], P('segment'), may hold values from -1 to 1
- mixing_weight: bfloat16 [4, 1024, 1024], P('segment'), may hold values from -0.1875 to 0.1875
- output_weight: bfloat16 [4, 1024, 256], P('segment'), may hold values from -0.09375 to 0.09375
- norm_gain: float32 [4, 1024], P('segment'), may hold values from 0.25 to 1.75
- final_gain: float32 [4, 1024], P('segment'), may hold values from 0.25 to 1.75
Outputs:
- flow_out: float32 [4, 2, 1024, 128], P('segment', None, 'seq')
Inputs may be any that keep to these rules, and one draw needn't show every extreme that they name: `tile_list`: row t lists 4 key tiles; its first entry is t, every entry lies between max(t - 2, 0) and t, entries may repeat, and the last row has an entry exactly 2 tiles back.
All inputs are finite; a program needn't handle non-finite values.
Results may differ from a plain program's by a relative error of at most 0.0085.
Values may be sent and summed in bfloat16 or wider, within the bound.
No kernel may reach another device: no remote copies, remote signals or barrier semaphores. Data moves between devices by JAX's collectives and lax.ppermute only.
A program may use at most 64 MiB of HBM per device.

v0:
```python
import jax
import jax.numpy as jnp
from jax import lax
from jax.sharding import PartitionSpec as P

HEAD_DIM = 128
TILE = 128


def from_behind(block, axis, distance):
    devices = range(lax.axis_size(axis))
    route = [(i - distance, i) for i in devices if i - distance in devices]
    return lax.ppermute(block, axis, route)


def from_partner(array, axis, bit):
    return lax.ppermute(array, axis, [(i, i ^ 1 << bit) for i in range(lax.axis_size(axis))])


def rms_scaled(values, gain):
    return values * lax.rsqrt(jnp.mean(values * values, axis=-1, keepdims=True) + 1e-06) * gain


def body(
    patches,
    tile_list,
    input_weight,
    attention_weight,
    mixing_weight,
    output_weight,
    norm_gain,
    final_gain,
):
    micro, rows, width_in = patches.shape
    heads_all = mixing_weight.shape[1]
    head_count = heads_all // HEAD_DIM
    segment = lax.axis_index("segment")
    place = lax.axis_index("seq")
    seq_count = lax.axis_size("seq")
    segment_count = lax.axis_size("segment")
    turns = micro + segment_count - 1
    per_device = rows // TILE
    tiles_all = tile_list.shape[0]
    named = jnp.any(
        tile_list[:, :, None] == jnp.arange(tiles_all, dtype=jnp.int32)[None, None, :], axis=1
    )
    padded = jnp.concatenate([jnp.zeros((tiles_all, 2 * per_device), jnp.bool_), named], axis=1)
    mine = lax.dynamic_slice(
        padded, (place * per_device, place * per_device), (per_device, 3 * per_device)
    )
    allowed = jnp.repeat(jnp.repeat(mine, TILE, axis=0), TILE, axis=1)
    query_pos = place * rows + jnp.arange(rows, dtype=jnp.int32)
    key_pos = (place - 2) * rows + jnp.arange(3 * rows, dtype=jnp.int32)
    allowed = allowed & (key_pos[None, :] <= query_pos[:, None])
    embed = input_weight[0]
    project = attention_weight[0]
    mixing = mixing_weight[0]
    readout = output_weight[0]
    gain_first = norm_gain[0]
    gain_second = final_gain[0]

    def run_block(flow_in):
        edge_row = flow_in[rows - 1 :]
        last_row = from_behind(edge_row, "seq", 1)
        shifted = jnp.concatenate([last_row, flow_in[:-1]], axis=0).astype(jnp.bfloat16)
        hidden = jnp.dot(shifted, embed, preferred_element_type=jnp.float32)
        normed = rms_scaled(hidden, gain_first).astype(jnp.bfloat16)
        projected = jnp.dot(normed, project, preferred_element_type=jnp.float32).astype(
            jnp.bfloat16
        )
        queries = projected[:, :heads_all].reshape(rows, head_count, HEAD_DIM)
        current = projected[:, heads_all:]
        window = [current]
        received = current
        for step in range(2):
            received = from_behind(received, "seq", 1)
            window = [received] + window
        gathered = jnp.concatenate(window, axis=0)
        keys = gathered[:, :heads_all].reshape(3 * rows, head_count, HEAD_DIM)
        values = gathered[:, heads_all:].reshape(3 * rows, head_count, HEAD_DIM)
        scores = jnp.einsum(
            "qhd,khd->hqk", queries, keys, preferred_element_type=jnp.float32
        ) * HEAD_DIM ** (-0.5)
        scores = jnp.where(allowed[None], scores, -jnp.inf)
        top = jnp.max(scores, axis=-1, keepdims=True)
        expo = jnp.exp(scores - top)
        total = jnp.sum(expo, axis=-1, keepdims=True)
        mixed = (
            jnp.einsum(
                "hqk,khd->hqd",
                expo.astype(jnp.bfloat16),
                values,
                preferred_element_type=jnp.float32,
            )
            / total
        )
        mixed = jnp.transpose(mixed, (1, 0, 2)).reshape(rows, heads_all).astype(jnp.bfloat16)
        residual = hidden + jnp.dot(mixed, mixing, preferred_element_type=jnp.float32)
        final_normed = rms_scaled(residual, gain_second).astype(jnp.bfloat16)
        raw = jnp.dot(final_normed, readout, preferred_element_type=jnp.float32)
        shift_mean = raw[:, :width_in]
        log_scale = 0.5 * jnp.tanh(raw[:, width_in:])
        return (flow_in - shift_mean) * jnp.exp(-log_scale)

    def turn(index, carry):
        incoming, stored = carry
        slot = index - segment
        clipped = jnp.clip(slot, 0, micro - 1)
        first = lax.dynamic_index_in_dim(patches, clipped, 0, keepdims=False)
        flow_in = jnp.where(segment == 0, first, incoming)
        flow_out = run_block(flow_in)
        live = (slot >= 0) & (slot < micro)
        updated = lax.dynamic_update_index_in_dim(stored, flow_out, clipped, 0)
        stored = jnp.where(live, updated, stored)
        moving = flow_out
        for bit in range(seq_count.bit_length() - 1):
            moving = from_partner(moving.astype(jnp.bfloat16), "seq", bit).astype(moving.dtype)
        mirrored = moving[::-1]
        incoming = from_behind(mirrored.astype(jnp.bfloat16), "segment", 1).astype(mirrored.dtype)
        return (incoming, stored)

    start = (
        jnp.zeros((rows, width_in), jnp.float32),
        jnp.zeros((micro, rows, width_in), jnp.float32),
    )
    result = lax.fori_loop(0, turns, turn, start)
    stored = result[1]
    return stored[None]


def solution(mesh):
    in_specs = (
        P(None, "seq", None),
        P(),
        P("segment", None, None),
        P("segment", None, None),
        P("segment", None, None),
        P("segment", None, None),
        P("segment", None),
        P("segment", None),
    )
    out_specs = P("segment", None, "seq", None)
    return jax.shard_map(body, mesh=mesh, in_specs=in_specs, out_specs=out_specs, check_vma=False)
```

profile of v0, /device:TPU:0, one launch (start us, length us, event | category | flops | bytes accessed | tf_op | source)
XLA Modules:
  0.0 329.2 jit_solution(7998493575811049722)
XLA Ops:
  0.9 327.6 %while.17 = (s32[]{:T(128)}, f32[128,128]{1,0:T(8,128)S(1)}, f32[2,128,128]{2,1,0:T(8,128)S(1)}, pred[]{:T(512)}, s32[]{:T(128)}, /*index=5*/f32[2,128,128]{2,1,...) while((s32[]{:T(128)}, f32[128,128]{1,0:T(8,128)S(1)}, ...), condition=%wide.region_6.7_spmd.clone, body=%wide.region_1.6_spmd.clone.sunk | while | flops 1385675008 | bytes 45076444 | solution.py:126
  1.8 4.9 %collective-permute-start = (bf16[1,128]{1,0:T(2,128)(2,1)S(1)}, bf16[1,128]{1,0:T(2,128)(2,1)S(1)}, u32[]{:S(2)}, u32[]{:S(2)}) collective-permute-start(bf16[1,128]{1,0:T(2,128)(2,1)S(1)} %slice.126), channel_id=1, source_target_pairs={{0,1},{1,2},{2,3},{3,4},{4,5},{5,6},{6,7},{8,9},{9,10},{10,11},{11... | collective-permute-start | bytes 776 | tf_op jit(solution)/shard_map/while/body/eval_jaxpr/ppermute | solution.py:13
  9.3 3.8 %convolution_convert_fusion.2 = bf16[128,3072]{1,0:T(8,128)(2,1)S(1)} fusion(bf16[1024,3072]{1,0:T(8,128)(2,1)} %get-tuple-element.500, f32[128,1024]{1,0:T(8,128)S(1)} %get-tuple-element.448, f32[1024]{0:T(1024)} %bitcast.90, f32[128]{0:T(128)S(1)} %add_rsqrt_fusion.4), kind=kOutput, calls=%fused_computation.1.clone.1 | convolution fusion | flops 806092800 | bytes 7606784 | tf_op jit(solution)/shard_map/while/body/eval_jaxpr/dot_general | solution.py:68
  13.1 4.2 %collective-permute-start.1 = (bf16[128,2048]{1,0:T(8,128)(2,1)S(1)}, bf16[128,2048]{1,0:T(8,128)(2,1)S(1)}, u32[]{:S(2)}, u32[]{:S(2)}) collective-permute-start(bf16[128,2048]{1,0:T(8,128)(2,1)S(1)} %slice.127), channel_id=1, source_target_pairs={{0,1},{1,2},{2,3},{3,4},{4,5},{5,6},{6,7},{8,9},{9,10},{10,11},{11... | collective-permute-start | bytes 1572872 | tf_op jit(solution)/shard_map/while/body/eval_jaxpr/ppermute | solution.py:13
  17.4 10.0 %collective-permute-done.1 = bf16[128,2048]{1,0:T(8,128)(2,1)S(1)} collective-permute-done((bf16[128,2048]{1,0:T(8,128)(2,1)S(1)}, bf16[128,2048]{1,0:T(8,128)(2,1)S(1)}, u32[]{:S(2)}, u32[]{:S(2)}) %collective-permute-start.1) | collective-permute-done | bytes 524320 | tf_op jit(solution)/shard_map/while/body/eval_jaxpr/ppermute | solution.py:13
  27.3 4.4 %collective-permute-start.2 = (bf16[128,2048]{1,0:T(8,128)(2,1)S(1)}, bf16[128,2048]{1,0:T(8,128)(2,1)S(1)}, u32[]{:S(2)}, u32[]{:S(2)}) collective-permute-start(bf16[128,2048]{1,0:T(8,128)(2,1)S(1)} %collective-permute-done.1), channel_id=1, source_target_pairs={{0,1},{1,2},{2,3},{3,4},{4,5},{5,6},{6,7},{8,9},{9,10},{10,11},{11... | collective-permute-start | bytes 1572872 | tf_op jit(solution)/shard_map/while/body/eval_jaxpr/ppermute | solution.py:13
  31.9 9.0 %collective-permute-done.2 = bf16[128,2048]{1,0:T(8,128)(2,1)S(1)} collective-permute-done((bf16[128,2048]{1,0:T(8,128)(2,1)S(1)}, bf16[128,2048]{1,0:T(8,128)(2,1)S(1)}, u32[]{:S(2)}, u32[]{:S(2)}) %collective-permute-start.2) | collective-permute-done | bytes 524320 | tf_op jit(solution)/shard_map/while/body/eval_jaxpr/ppermute | solution.py:13
  52.9 3.9 %collective-permute-start.4 = (bf16[128,128]{1,0:T(8,128)(2,1)S(1)}, bf16[128,128]{1,0:T(8,128)(2,1)S(1)}, u32[]{:S(2)}, u32[]{:S(2)}) collective-permute-start(bf16[128,128]{1,0:T(8,128)(2,1)S(1)} %collective-permute-done.3), channel_id=1, source_target_pairs={{0,2},{1,3},{2,0},{3,1},{4,6},{5,7},{6,4},{7,5},{8,10},{9,11},{10,... | collective-permute-start | bytes 98312 | tf_op jit(solution)/shard_map/while/body/eval_jaxpr/ppermute | solution.py:17
  71.2 3.8 %convolution_convert_fusion.2 = bf16[128,3072]{1,0:T(8,128)(2,1)S(1)} fusion(bf16[1024,3072]{1,0:T(8,128)(2,1)} %get-tuple-element.500, f32[128,1024]{1,0:T(8,128)S(1)} %get-tuple-element.448, f32[1024]{0:T(1024)} %bitcast.90, f32[128]{0:T(128)S(1)} %add_rsqrt_fusion.4), kind=kOutput, calls=%fused_computation.1.clone.1 | convolution fusion | flops 806092800 | bytes 7606784 | tf_op jit(solution)/shard_map/while/body/eval_jaxpr/dot_general | solution.py:68
  75.1 5.3 %collective-permute-start.1 = (bf16[128,2048]{1,0:T(8,128)(2,1)S(1)}, bf16[128,2048]{1,0:T(8,128)(2,1)S(1)}, u32[]{:S(2)}, u32[]{:S(2)}) collective-permute-start(bf16[128,2048]{1,0:T(8,128)(2,1)S(1)} %slice.127), channel_id=1, source_target_pairs={{0,1},{1,2},{2,3},{3,4},{4,5},{5,6},{6,7},{8,9},{9,10},{10,11},{11... | collective-permute-start | bytes 1572872 | tf_op jit(solution)/shard_map/while/body/eval_jaxpr/ppermute | solution.py:13
  80.4 11.7 %collective-permute-done.1 = bf16[128,2048]{1,0:T(8,128)(2,1)S(1)} collective-permute-done((bf16[128,2048]{1,0:T(8,128)(2,1)S(1)}, bf16[128,2048]{1,0:T(8,128)(2,1)S(1)}, u32[]{:S(2)}, u32[]{:S(2)}) %collective-permute-start.1) | collective-permute-done | bytes 524320 | tf_op jit(solution)/shard_map/while/body/eval_jaxpr/ppermute | solution.py:13
  92.1 5.4 %collective-permute-start.2 = (bf16[128,2048]{1,0:T(8,128)(2,1)S(1)}, bf16[128,2048]{1,0:T(8,128)(2,1)S(1)}, u32[]{:S(2)}, u32[]{:S(2)}) collective-permute-start(bf16[128,2048]{1,0:T(8,128)(2,1)S(1)} %collective-permute-done.1), channel_id=1, source_target_pairs={{0,1},{1,2},{2,3},{3,4},{4,5},{5,6},{6,7},{8,9},{9,10},{10,11},{11... | collective-permute-start | bytes 1572872 | tf_op jit(solution)/shard_map/while/body/eval_jaxpr/ppermute | solution.py:13
  97.6 11.6 %collective-permute-done.2 = bf16[128,2048]{1,0:T(8,128)(2,1)S(1)} collective-permute-done((bf16[128,2048]{1,0:T(8,128)(2,1)S(1)}, bf16[128,2048]{1,0:T(8,128)(2,1)S(1)}, u32[]{:S(2)}, u32[]{:S(2)}) %collective-permute-start.2) | collective-permute-done | bytes 524320 | tf_op jit(solution)/shard_map/while/body/eval_jaxpr/ppermute | solution.py:13
  121.0 3.9 %collective-permute-start.4 = (bf16[128,128]{1,0:T(8,128)(2,1)S(1)}, bf16[128,128]{1,0:T(8,128)(2,1)S(1)}, u32[]{:S(2)}, u32[]{:S(2)}) collective-permute-start(bf16[128,128]{1,0:T(8,128)(2,1)S(1)} %collective-permute-done.3), channel_id=1, source_target_pairs={{0,2},{1,3},{2,0},{3,1},{4,6},{5,7},{6,4},{7,5},{8,10},{9,11},{10,... | collective-permute-start | bytes 98312 | tf_op jit(solution)/shard_map/while/body/eval_jaxpr/ppermute | solution.py:17
  139.3 3.8 %convolution_convert_fusion.2 = bf16[128,3072]{1,0:T(8,128)(2,1)S(1)} fusion(bf16[1024,3072]{1,0:T(8,128)(2,1)} %get-tuple-element.500, f32[128,1024]{1,0:T(8,128)S(1)} %get-tuple-element.448, f32[1024]{0:T(1024)} %bitcast.90, f32[128]{0:T(128)S(1)} %add_rsqrt_fusion.4), kind=kOutput, calls=%fused_computation.1.clone.1 | convolution fusion | flops 806092800 | bytes 7606784 | tf_op jit(solution)/shard_map/while/body/eval_jaxpr/dot_general | solution.py:68
  143.2 5.2 %collective-permute-start.1 = (bf16[128,2048]{1,0:T(8,128)(2,1)S(1)}, bf16[128,2048]{1,0:T(8,128)(2,1)S(1)}, u32[]{:S(2)}, u32[]{:S(2)}) collective-permute-start(bf16[128,2048]{1,0:T(8,128)(2,1)S(1)} %slice.127), channel_id=1, source_target_pairs={{0,1},{1,2},{2,3},{3,4},{4,5},{5,6},{6,7},{8,9},{9,10},{10,11},{11... | collective-permute-start | bytes 1572872 | tf_op jit(solution)/shard_map/while/body/eval_jaxpr/ppermute | solution.py:13
  148.4 10.8 %collective-permute-done.1 = bf16[128,2048]{1,0:T(8,128)(2,1)S(1)} collective-permute-done((bf16[128,2048]{1,0:T(8,128)(2,1)S(1)}, bf16[128,2048]{1,0:T(8,128)(2,1)S(1)}, u32[]{:S(2)}, u32[]{:S(2)}) %collective-permute-start.1) | collective-permute-done | bytes 524320 | tf_op jit(solution)/shard_map/while/body/eval_jaxpr/ppermute | solution.py:13
  159.2 4.8 %collective-permute-start.2 = (bf16[128,2048]{1,0:T(8,128)(2,1)S(1)}, bf16[128,2048]{1,0:T(8,128)(2,1)S(1)}, u32[]{:S(2)}, u32[]{:S(2)}) collective-permute-start(bf16[128,2048]{1,0:T(8,128)(2,1)S(1)} %collective-permute-done.1), channel_id=1, source_target_pairs={{0,1},{1,2},{2,3},{3,4},{4,5},{5,6},{6,7},{8,9},{9,10},{10,11},{11... | collective-permute-start | bytes 1572872 | tf_op jit(solution)/shard_map/while/body/eval_jaxpr/ppermute | solution.py:13
  164.1 9.5 %collective-permute-done.2 = bf16[128,2048]{1,0:T(8,128)(2,1)S(1)} collective-permute-done((bf16[128,2048]{1,0:T(8,128)(2,1)S(1)}, bf16[128,2048]{1,0:T(8,128)(2,1)S(1)}, u32[]{:S(2)}, u32[]{:S(2)}) %collective-permute-start.2) | collective-permute-done | bytes 524320 | tf_op jit(solution)/shard_map/while/body/eval_jaxpr/ppermute | solution.py:13
  185.7 3.9 %collective-permute-start.4 = (bf16[128,128]{1,0:T(8,128)(2,1)S(1)}, bf16[128,128]{1,0:T(8,128)(2,1)S(1)}, u32[]{:S(2)}, u32[]{:S(2)}) collective-permute-start(bf16[128,128]{1,0:T(8,128)(2,1)S(1)} %collective-permute-done.3), channel_id=1, source_target_pairs={{0,2},{1,3},{2,0},{3,1},{4,6},{5,7},{6,4},{7,5},{8,10},{9,11},{10,... | collective-permute-start | bytes 98312 | tf_op jit(solution)/shard_map/while/body/eval_jaxpr/ppermute | solution.py:17
  204.3 3.8 %convolution_convert_fusion.2 = bf16[128,3072]{1,0:T(8,128)(2,1)S(1)} fusion(bf16[1024,3072]{1,0:T(8,128)(2,1)} %get-tuple-element.500, f32[128,1024]{1,0:T(8,128)S(1)} %get-tuple-element.448, f32[1024]{0:T(1024)} %bitcast.90, f32[128]{0:T(128)S(1)} %add_rsqrt_fusion.4), kind=kOutput, calls=%fused_computation.1.clone.1 | convolution fusion | flops 806092800 | bytes 7606784 | tf_op jit(solution)/shard_map/while/body/eval_jaxpr/dot_general | solution.py:68
  208.2 5.2 %collective-permute-start.1 = (bf16[128,2048]{1,0:T(8,128)(2,1)S(1)}, bf16[128,2048]{1,0:T(8,128)(2,1)S(1)}, u32[]{:S(2)}, u32[]{:S(2)}) collective-permute-start(bf16[128,2048]{1,0:T(8,128)(2,1)S(1)} %slice.127), channel_id=1, source_target_pairs={{0,1},{1,2},{2,3},{3,4},{4,5},{5,6},{6,7},{8,9},{9,10},{10,11},{11... | collective-permute-start | bytes 1572872 | tf_op jit(solution)/shard_map/while/body/eval_jaxpr/ppermute | solution.py:13
  213.4 10.8 %collective-permute-done.1 = bf16[128,2048]{1,0:T(8,128)(2,1)S(1)} collective-permute-done((bf16[128,2048]{1,0:T(8,128)(2,1)S(1)}, bf16[128,2048]{1,0:T(8,128)(2,1)S(1)}, u32[]{:S(2)}, u32[]{:S(2)}) %collective-permute-start.1) | collective-permute-done | bytes 524320 | tf_op jit(solution)/shard_map/while/body/eval_jaxpr/ppermute | solution.py:13
  224.2 4.8 %collective-permute-start.2 = (bf16[128,2048]{1,0:T(8,128)(2,1)S(1)}, bf16[128,2048]{1,0:T(8,128)(2,1)S(1)}, u32[]{:S(2)}, u32[]{:S(2)}) collective-permute-start(bf16[128,2048]{1,0:T(8,128)(2,1)S(1)} %collective-permute-done.1), channel_id=1, source_target_pairs={{0,1},{1,2},{2,3},{3,4},{4,5},{5,6},{6,7},{8,9},{9,10},{10,11},{11... | collective-permute-start | bytes 1572872 | tf_op jit(solution)/shard_map/while/body/eval_jaxpr/ppermute | solution.py:13
  229.1 9.5 %collective-permute-done.2 = bf16[128,2048]{1,0:T(8,128)(2,1)S(1)} collective-permute-done((bf16[128,2048]{1,0:T(8,128)(2,1)S(1)}, bf16[128,2048]{1,0:T(8,128)(2,1)S(1)}, u32[]{:S(2)}, u32[]{:S(2)}) %collective-permute-start.2) | collective-permute-done | bytes 524320 | tf_op jit(solution)/shard_map/while/body/eval_jaxpr/ppermute | solution.py:13
  250.7 3.9 %collective-permute-start.4 = (bf16[128,128]{1,0:T(8,128)(2,1)S(1)}, bf16[128,128]{1,0:T(8,128)(2,1)S(1)}, u32[]{:S(2)}, u32[]{:S(2)}) collective-permute-start(bf16[128,128]{1,0:T(8,128)(2,1)S(1)} %collective-permute-done.3), channel_id=1, source_target_pairs={{0,2},{1,3},{2,0},{3,1},{4,6},{5,7},{6,4},{7,5},{8,10},{9,11},{10,... | collective-permute-start | bytes 98312 | tf_op jit(solution)/shard_map/while/body/eval_jaxpr/ppermute | solution.py:17
  269.1 3.8 %convolution_convert_fusion.2 = bf16[128,3072]{1,0:T(8,128)(2,1)S(1)} fusion(bf16[1024,3072]{1,0:T(8,128)(2,1)} %get-tuple-element.500, f32[128,1024]{1,0:T(8,128)S(1)} %get-tuple-element.448, f32[1024]{0:T(1024)} %bitcast.90, f32[128]{0:T(128)S(1)} %add_rsqrt_fusion.4), kind=kOutput, calls=%fused_computation.1.clone.1 | convolution fusion | flops 806092800 | bytes 7606784 | tf_op jit(solution)/shard_map/while/body/eval_jaxpr/dot_general | solution.py:68
  273.0 5.2 %collective-permute-start.1 = (bf16[128,2048]{1,0:T(8,128)(2,1)S(1)}, bf16[128,2048]{1,0:T(8,128)(2,1)S(1)}, u32[]{:S(2)}, u32[]{:S(2)}) collective-permute-start(bf16[128,2048]{1,0:T(8,128)(2,1)S(1)} %slice.127), channel_id=1, source_target_pairs={{0,1},{1,2},{2,3},{3,4},{4,5},{5,6},{6,7},{8,9},{9,10},{10,11},{11... | collective-permute-start | bytes 1572872 | tf_op jit(solution)/shard_map/while/body/eval_jaxpr/ppermute | solution.py:13
  278.2 10.8 %collective-permute-done.1 = bf16[128,2048]{1,0:T(8,128)(2,1)S(1)} collective-permute-done((bf16[128,2048]{1,0:T(8,128)(2,1)S(1)}, bf16[128,2048]{1,0:T(8,128)(2,1)S(1)}, u32[]{:S(2)}, u32[]{:S(2)}) %collective-permute-start.1) | collective-permute-done | bytes 524320 | tf_op jit(solution)/shard_map/while/body/eval_jaxpr/ppermute | solution.py:13
  289.0 4.8 %collective-permute-start.2 = (bf16[128,2048]{1,0:T(8,128)(2,1)S(1)}, bf16[128,2048]{1,0:T(8,128)(2,1)S(1)}, u32[]{:S(2)}, u32[]{:S(2)}) collective-permute-start(bf16[128,2048]{1,0:T(8,128)(2,1)S(1)} %collective-permute-done.1), channel_id=1, source_target_pairs={{0,1},{1,2},{2,3},{3,4},{4,5},{5,6},{6,7},{8,9},{9,10},{10,11},{11... | collective-permute-start | bytes 1572872 | tf_op jit(solution)/shard_map/while/body/eval_jaxpr/ppermute | solution.py:13
  293.9 9.5 %collective-permute-done.2 = bf16[128,2048]{1,0:T(8,128)(2,1)S(1)} collective-permute-done((bf16[128,2048]{1,0:T(8,128)(2,1)S(1)}, bf16[128,2048]{1,0:T(8,128)(2,1)S(1)}, u32[]{:S(2)}, u32[]{:S(2)}) %collective-permute-start.2) | collective-permute-done | bytes 524320 | tf_op jit(solution)/shard_map/while/body/eval_jaxpr/ppermute | solution.py:13
  315.5 3.9 %collective-permute-start.4 = (bf16[128,128]{1,0:T(8,128)(2,1)S(1)}, bf16[128,128]{1,0:T(8,128)(2,1)S(1)}, u32[]{:S(2)}, u32[]{:S(2)}) collective-permute-start(bf16[128,128]{1,0:T(8,128)(2,1)S(1)} %collective-permute-done.3), channel_id=1, source_target_pairs={{0,2},{1,3},{2,0},{3,1},{4,6},{5,7},{6,4},{7,5},{8,10},{9,11},{10,... | collective-permute-start | bytes 98312 | tf_op jit(solution)/shard_map/while/body/eval_jaxpr/ppermute | solution.py:17
  (183 shorter events, 132.2 us)
Async XLA Ops:
  1.8 6.2 %collective-permute-start = (bf16[1,128]{1,0:T(2,128)(2,1)S(1)}, bf16[1,128]{1,0:T(2,128)(2,1)S(1)}, u32[]{:S(2)}, u32[]{:S(2)}) collective-permute-start(bf16[1,128]{1,0:T(2,128)(2,1)S(1)} %slice.126), channel_id=1, source_target_pairs={{0,1},{1,2},{2,3},{3,4},{4,5},{5,6},{6,7},{8,9},{9,10},{10,11},{11... | collective-permute-start | bytes 776 | tf_op jit(solution)/shard_map/while/body/eval_jaxpr/ppermute | solution.py:13
  13.1 14.2 %collective-permute-start.1 = (bf16[128,2048]{1,0:T(8,128)(2,1)S(1)}, bf16[128,2048]{1,0:T(8,128)(2,1)S(1)}, u32[]{:S(2)}, u32[]{:S(2)}) collective-permute-start(bf16[128,2048]{1,0:T(8,128)(2,1)S(1)} %slice.127), channel_id=1, source_target_pairs={{0,1},{1,2},{2,3},{3,4},{4,5},{5,6},{6,7},{8,9},{9,10},{10,11},{11... | collective-permute-start | bytes 1572872 | tf_op jit(solution)/shard_map/while/body/eval_jaxpr/ppermute | solution.py:13
  27.3 13.5 %collective-permute-start.2 = (bf16[128,2048]{1,0:T(8,128)(2,1)S(1)}, bf16[128,2048]{1,0:T(8,128)(2,1)S(1)}, u32[]{:S(2)}, u32[]{:S(2)}) collective-permute-start(bf16[128,2048]{1,0:T(8,128)(2,1)S(1)} %collective-permute-done.1), channel_id=1, source_target_pairs={{0,1},{1,2},{2,3},{3,4},{4,5},{5,6},{6,7},{8,9},{9,10},{10,11},{11... | collective-permute-start | bytes 1572872 | tf_op jit(solution)/shard_map/while/body/eval_jaxpr/ppermute | solution.py:13
  47.6 5.3 %collective-permute-start.3 = (bf16[128,128]{1,0:T(8,128)(2,1)S(1)}, bf16[128,128]{1,0:T(8,128)(2,1)S(1)}, u32[]{:S(2)}, u32[]{:S(2)}) collective-permute-start(bf16[128,128]{1,0:T(8,128)(2,1)S(1)} %fusion.61), channel_id=1, source_target_pairs={{0,1},{1,0},{2,3},{3,2},{4,5},{5,4},{6,7},{7,6},{8,9},{9,8},{10,11... | collective-permute-start | bytes 98312 | tf_op jit(solution)/shard_map/while/body/eval_jaxpr/ppermute | solution.py:17
  52.9 5.8 %collective-permute-start.4 = (bf16[128,128]{1,0:T(8,128)(2,1)S(1)}, bf16[128,128]{1,0:T(8,128)(2,1)S(1)}, u32[]{:S(2)}, u32[]{:S(2)}) collective-permute-start(bf16[128,128]{1,0:T(8,128)(2,1)S(1)} %collective-permute-done.3), channel_id=1, source_target_pairs={{0,2},{1,3},{2,0},{3,1},{4,6},{5,7},{6,4},{7,5},{8,10},{9,11},{10,... | collective-permute-start | bytes 98312 | tf_op jit(solution)/shard_map/while/body/eval_jaxpr/ppermute | solution.py:17
  58.8 4.9 %collective-permute-start.5 = (bf16[128,128]{1,0:T(8,128)(2,1)S(1)}, bf16[128,128]{1,0:T(8,128)(2,1)S(1)}, u32[]{:S(2)}, u32[]{:S(2)}) collective-permute-start(bf16[128,128]{1,0:T(8,128)(2,1)S(1)} %collective-permute-done.4), channel_id=1, source_target_pairs={{0,4},{1,5},{2,6},{3,7},{4,0},{5,1},{6,2},{7,3},{8,12},{9,13},{10,... | collective-permute-start | bytes 98312 | tf_op jit(solution)/shard_map/while/body/eval_jaxpr/ppermute | solution.py:17
  63.7 2.1 collective-permute-start.6
  66.7 3.2 collective-permute-start
  75.1 17.0 %collective-permute-start.1 = (bf16[128,2048]{1,0:T(8,128)(2,1)S(1)}, bf16[128,2048]{1,0:T(8,128)(2,1)S(1)}, u32[]{:S(2)}, u32[]{:S(2)}) collective-permute-start(bf16[128,2048]{1,0:T(8,128)(2,1)S(1)} %slice.127), channel_id=1, source_target_pairs={{0,1},{1,2},{2,3},{3,4},{4,5},{5,6},{6,7},{8,9},{9,10},{10,11},{11... | collective-permute-start | bytes 1572872 | tf_op jit(solution)/shard_map/while/body/eval_jaxpr/ppermute | solution.py:13
  92.1 17.1 %collective-permute-start.2 = (bf16[128,2048]{1,0:T(8,128)(2,1)S(1)}, bf16[128,2048]{1,0:T(8,128)(2,1)S(1)}, u32[]{:S(2)}, u32[]{:S(2)}) collective-permute-start(bf16[128,2048]{1,0:T(8,128)(2,1)S(1)} %collective-permute-done.1), channel_id=1, source_target_pairs={{0,1},{1,2},{2,3},{3,4},{4,5},{5,6},{6,7},{8,9},{9,10},{10,11},{11... | collective-permute-start | bytes 1572872 | tf_op jit(solution)/shard_map/while/body/eval_jaxpr/ppermute | solution.py:13
  115.9 5.0 %collective-permute-start.3 = (bf16[128,128]{1,0:T(8,128)(2,1)S(1)}, bf16[128,128]{1,0:T(8,128)(2,1)S(1)}, u32[]{:S(2)}, u32[]{:S(2)}) collective-permute-start(bf16[128,128]{1,0:T(8,128)(2,1)S(1)} %fusion.61), channel_id=1, source_target_pairs={{0,1},{1,0},{2,3},{3,2},{4,5},{5,4},{6,7},{7,6},{8,9},{9,8},{10,11... | collective-permute-start | bytes 98312 | tf_op jit(solution)/shard_map/while/body/eval_jaxpr/ppermute | solution.py:17
  121.0 5.8 %collective-permute-start.4 = (bf16[128,128]{1,0:T(8,128)(2,1)S(1)}, bf16[128,128]{1,0:T(8,128)(2,1)S(1)}, u32[]{:S(2)}, u32[]{:S(2)}) collective-permute-start(bf16[128,128]{1,0:T(8,128)(2,1)S(1)} %collective-permute-done.3), channel_id=1, source_target_pairs={{0,2},{1,3},{2,0},{3,1},{4,6},{5,7},{6,4},{7,5},{8,10},{9,11},{10,... | collective-permute-start | bytes 98312 | tf_op jit(solution)/shard_map/while/body/eval_jaxpr/ppermute | solution.py:17
  126.8 5.3 %collective-permute-start.5 = (bf16[128,128]{1,0:T(8,128)(2,1)S(1)}, bf16[128,128]{1,0:T(8,128)(2,1)S(1)}, u32[]{:S(2)}, u32[]{:S(2)}) collective-permute-start(bf16[128,128]{1,0:T(8,128)(2,1)S(1)} %collective-permute-done.4), channel_id=1, source_target_pairs={{0,4},{1,5},{2,6},{3,7},{4,0},{5,1},{6,2},{7,3},{8,12},{9,13},{10,... | collective-permute-start | bytes 98312 | tf_op jit(solution)/shard_map/while/body/eval_jaxpr/ppermute | solution.py:17
  132.1 2.1 collective-permute-start.6
  135.1 3.0 collective-permute-start
  143.2 16.0 %collective-permute-start.1 = (bf16[128,2048]{1,0:T(8,128)(2,1)S(1)}, bf16[128,2048]{1,0:T(8,128)(2,1)S(1)}, u32[]{:S(2)}, u32[]{:S(2)}) collective-permute-start(bf16[128,2048]{1,0:T(8,128)(2,1)S(1)} %slice.127), channel_id=1, source_target_pairs={{0,1},{1,2},{2,3},{3,4},{4,5},{5,6},{6,7},{8,9},{9,10},{10,11},{11... | collective-permute-start | bytes 1572872 | tf_op jit(solution)/shard_map/while/body/eval_jaxpr/ppermute | solution.py:13
  159.2 14.4 %collective-permute-start.2 = (bf16[128,2048]{1,0:T(8,128)(2,1)S(1)}, bf16[128,2048]{1,0:T(8,128)(2,1)S(1)}, u32[]{:S(2)}, u32[]{:S(2)}) collective-permute-start(bf16[128,2048]{1,0:T(8,128)(2,1)S(1)} %collective-permute-done.1), channel_id=1, source_target_pairs={{0,1},{1,2},{2,3},{3,4},{4,5},{5,6},{6,7},{8,9},{9,10},{10,11},{11... | collective-permute-start | bytes 1572872 | tf_op jit(solution)/shard_map/while/body/eval_jaxpr/ppermute | solution.py:13
  180.4 5.3 %collective-permute-start.3 = (bf16[128,128]{1,0:T(8,128)(2,1)S(1)}, bf16[128,128]{1,0:T(8,128)(2,1)S(1)}, u32[]{:S(2)}, u32[]{:S(2)}) collective-permute-start(bf16[128,128]{1,0:T(8,128)(2,1)S(1)} %fusion.61), channel_id=1, source_target_pairs={{0,1},{1,0},{2,3},{3,2},{4,5},{5,4},{6,7},{7,6},{8,9},{9,8},{10,11... | collective-permute-start | bytes 98312 | tf_op jit(solution)/shard_map/while/body/eval_jaxpr/ppermute | solution.py:17
  185.7 6.0 %collective-permute-start.4 = (bf16[128,128]{1,0:T(8,128)(2,1)S(1)}, bf16[128,128]{1,0:T(8,128)(2,1)S(1)}, u32[]{:S(2)}, u32[]{:S(2)}) collective-permute-start(bf16[128,128]{1,0:T(8,128)(2,1)S(1)} %collective-permute-done.3), channel_id=1, source_target_pairs={{0,2},{1,3},{2,0},{3,1},{4,6},{5,7},{6,4},{7,5},{8,10},{9,11},{10,... | collective-permute-start | bytes 98312 | tf_op jit(solution)/shard_map/while/body/eval_jaxpr/ppermute | solution.py:17
  191.7 5.1 %collective-permute-start.5 = (bf16[128,128]{1,0:T(8,128)(2,1)S(1)}, bf16[128,128]{1,0:T(8,128)(2,1)S(1)}, u32[]{:S(2)}, u32[]{:S(2)}) collective-permute-start(bf16[128,128]{1,0:T(8,128)(2,1)S(1)} %collective-permute-done.4), channel_id=1, source_target_pairs={{0,4},{1,5},{2,6},{3,7},{4,0},{5,1},{6,2},{7,3},{8,12},{9,13},{10,... | collective-permute-start | bytes 98312 | tf_op jit(solution)/shard_map/while/body/eval_jaxpr/ppermute | solution.py:17
  199.9 3.2 collective-permute-start
  208.2 16.0 %collective-permute-start.1 = (bf16[128,2048]{1,0:T(8,128)(2,1)S(1)}, bf16[128,2048]{1,0:T(8,128)(2,1)S(1)}, u32[]{:S(2)}, u32[]{:S(2)}) collective-permute-start(bf16[128,2048]{1,0:T(8,128)(2,1)S(1)} %slice.127), channel_id=1, source_target_pairs={{0,1},{1,2},{2,3},{3,4},{4,5},{5,6},{6,7},{8,9},{9,10},{10,11},{11... | collective-permute-start | bytes 1572872 | tf_op jit(solution)/shard_map/while/body/eval_jaxpr/ppermute | solution.py:13
  224.2 14.5 %collective-permute-start.2 = (bf16[128,2048]{1,0:T(8,128)(2,1)S(1)}, bf16[128,2048]{1,0:T(8,128)(2,1)S(1)}, u32[]{:S(2)}, u32[]{:S(2)}) collective-permute-start(bf16[128,2048]{1,0:T(8,128)(2,1)S(1)} %collective-permute-done.1), channel_id=1, source_target_pairs={{0,1},{1,2},{2,3},{3,4},{4,5},{5,6},{6,7},{8,9},{9,10},{10,11},{11... | collective-permute-start | bytes 1572872 | tf_op jit(solution)/shard_map/while/body/eval_jaxpr/ppermute | solution.py:13
  245.4 5.3 %collective-permute-start.3 = (bf16[128,128]{1,0:T(8,128)(2,1)S(1)}, bf16[128,128]{1,0:T(8,128)(2,1)S(1)}, u32[]{:S(2)}, u32[]{:S(2)}) collective-permute-start(bf16[128,128]{1,0:T(8,128)(2,1)S(1)} %fusion.61), channel_id=1, source_target_pairs={{0,1},{1,0},{2,3},{3,2},{4,5},{5,4},{6,7},{7,6},{8,9},{9,8},{10,11... | collective-permute-start | bytes 98312 | tf_op jit(solution)/shard_map/while/body/eval_jaxpr/ppermute | solution.py:17
  250.7 5.8 %collective-permute-start.4 = (bf16[128,128]{1,0:T(8,128)(2,1)S(1)}, bf16[128,128]{1,0:T(8,128)(2,1)S(1)}, u32[]{:S(2)}, u32[]{:S(2)}) collective-permute-start(bf16[128,128]{1,0:T(8,128)(2,1)S(1)} %collective-permute-done.3), channel_id=1, source_target_pairs={{0,2},{1,3},{2,0},{3,1},{4,6},{5,7},{6,4},{7,5},{8,10},{9,11},{10,... | collective-permute-start | bytes 98312 | tf_op jit(solution)/shard_map/while/body/eval_jaxpr/ppermute | solution.py:17
  256.6 5.0 %collective-permute-start.5 = (bf16[128,128]{1,0:T(8,128)(2,1)S(1)}, bf16[128,128]{1,0:T(8,128)(2,1)S(1)}, u32[]{:S(2)}, u32[]{:S(2)}) collective-permute-start(bf16[128,128]{1,0:T(8,128)(2,1)S(1)} %collective-permute-done.4), channel_id=1, source_target_pairs={{0,4},{1,5},{2,6},{3,7},{4,0},{5,1},{6,2},{7,3},{8,12},{9,13},{10,... | collective-permute-start | bytes 98312 | tf_op jit(solution)/shard_map/while/body/eval_jaxpr/ppermute | solution.py:17
  264.6 3.2 collective-permute-start
  273.0 16.0 %collective-permute-start.1 = (bf16[128,2048]{1,0:T(8,128)(2,1)S(1)}, bf16[128,2048]{1,0:T(8,128)(2,1)S(1)}, u32[]{:S(2)}, u32[]{:S(2)}) collective-permute-start(bf16[128,2048]{1,0:T(8,128)(2,1)S(1)} %slice.127), channel_id=1, source_target_pairs={{0,1},{1,2},{2,3},{3,4},{4,5},{5,6},{6,7},{8,9},{9,10},{10,11},{11... | collective-permute-start | bytes 1572872 | tf_op jit(solution)/shard_map/while/body/eval_jaxpr/ppermute | solution.py:13
  289.0 14.5 %collective-permute-start.2 = (bf16[128,2048]{1,0:T(8,128)(2,1)S(1)}, bf16[128,2048]{1,0:T(8,128)(2,1)S(1)}, u32[]{:S(2)}, u32[]{:S(2)}) collective-permute-start(bf16[128,2048]{1,0:T(8,128)(2,1)S(1)} %collective-permute-done.1), channel_id=1, source_target_pairs={{0,1},{1,2},{2,3},{3,4},{4,5},{5,6},{6,7},{8,9},{9,10},{10,11},{11... | collective-permute-start | bytes 1572872 | tf_op jit(solution)/shard_map/while/body/eval_jaxpr/ppermute | solution.py:13
  310.2 5.3 %collective-permute-start.3 = (bf16[128,128]{1,0:T(8,128)(2,1)S(1)}, bf16[128,128]{1,0:T(8,128)(2,1)S(1)}, u32[]{:S(2)}, u32[]{:S(2)}) collective-permute-start(bf16[128,128]{1,0:T(8,128)(2,1)S(1)} %fusion.61), channel_id=1, source_target_pairs={{0,1},{1,0},{2,3},{3,2},{4,5},{5,4},{6,7},{7,6},{8,9},{9,8},{10,11... | collective-permute-start | bytes 98312 | tf_op jit(solution)/shard_map/while/body/eval_jaxpr/ppermute | solution.py:17
  315.5 5.8 %collective-permute-start.4 = (bf16[128,128]{1,0:T(8,128)(2,1)S(1)}, bf16[128,128]{1,0:T(8,128)(2,1)S(1)}, u32[]{:S(2)}, u32[]{:S(2)}) collective-permute-start(bf16[128,128]{1,0:T(8,128)(2,1)S(1)} %collective-permute-done.3), channel_id=1, source_target_pairs={{0,2},{1,3},{2,0},{3,1},{4,6},{5,7},{6,4},{7,5},{8,10},{9,11},{10,... | collective-permute-start | bytes 98312 | tf_op jit(solution)/shard_map/while/body/eval_jaxpr/ppermute | solution.py:17
  321.4 5.0 %collective-permute-start.5 = (bf16[128,128]{1,0:T(8,128)(2,1)S(1)}, bf16[128,128]{1,0:T(8,128)(2,1)S(1)}, u32[]{:S(2)}, u32[]{:S(2)}) collective-permute-start(bf16[128,128]{1,0:T(8,128)(2,1)S(1)} %collective-permute-done.4), channel_id=1, source_target_pairs={{0,4},{1,5},{2,6},{3,7},{4,0},{5,1},{6,2},{7,3},{8,12},{9,13},{10,... | collective-permute-start | bytes 98312 | tf_op jit(solution)/shard_map/while/body/eval_jaxpr/ppermute | solution.py:17
  (19 other events, 25.5 us)
where the time goes:
time: 331 us; the launch traced here: 329 us
  waiting for transfers between devices  142 us (43%)
  starting transfers between devices  121 us (37%)
  matrix products  40.7 us (12%)
  local copies, waits for them, and re-layouts  15.5 us (5%)
  other arithmetic  9.55 us (3%)
    ppermute x20, waiting for transfers between devices, from_behind(): return lax.ppermute(block, axis, route)  114 us
    ppermute x20, starting transfers between devices, from_behind(): return lax.ppermute(block, axis, route)  68.1 us
    ppermute x15, starting transfers between devices, from_partner(): lax.ppermute(array, axis, [(i, i ^ 1 << bit) for i in range(lax.axis_size...  52.5 us
    ppermute x15, waiting for transfers between devices, from_partner(): lax.ppermute(array, axis, [(i, i ^ 1 << bit) for i in range(lax.axis_size...  28.6 us
    dot_general x5, matrix products, run_block(): jnp.dot(normed, project, preferred_element_type=jnp.float32)  19.2 us
    while x35, local copies, waits for them, and re-layouts  12.6 us
    dot_general x5, matrix products, run_block(): jnp.einsum('qhd,khd->hqk', queries, keys, preferred_element_type=jnp.floa...  8.41 us
  transfers between devices with their start and end apart: 35, of which 35 were waited for; matrix products, arithmetic and copies ran while one was open for 0% of the time, Pallas kernels for 0%

commit v1 on v0

v1 whole, which is shorter than its diff:
```python
import jax
import jax.numpy as jnp
from jax import lax
from jax.sharding import PartitionSpec as P

HEAD_DIM = 128
TILE = 128
BACK = 2


def rms_scaled(values, gain):
    return values * lax.rsqrt(jnp.mean(values * values, axis=-1, keepdims=True) + 1e-06) * gain


def body(
    patches,
    tile_list,
    input_weight,
    attention_weight,
    mixing_weight,
    output_weight,
    norm_gain,
    final_gain,
):
    micro, rows, width_in = patches.shape
    assert rows == TILE
    heads_all = mixing_weight.shape[1]
    head_count = heads_all // HEAD_DIM
    segment = lax.axis_index("segment")
    place = lax.axis_index("seq")
    n_seq = lax.axis_size("seq")
    n_seg = lax.axis_size("segment")
    tiles_all = tile_list.shape[0]
    span = (BACK + 1) * rows

    window_tiles = place - BACK + jnp.arange(BACK + 1, dtype=jnp.int32)
    my_list = lax.dynamic_index_in_dim(tile_list, place, 0, keepdims=False)
    listed = jnp.any(my_list[:, None] == window_tiles[None, :], axis=0) & (window_tiles >= 0)
    listed = jnp.repeat(listed, rows)
    query_pos = jnp.arange(rows, dtype=jnp.int32) + BACK * rows
    key_pos = jnp.arange(span, dtype=jnp.int32)
    allowed = listed[None, :] & (key_pos[None, :] <= query_pos[:, None])

    embed = input_weight[0]
    w_query = attention_weight[0][:, :heads_all]
    w_keyval = attention_weight[0][:, heads_all:]
    mixing = mixing_weight[0]
    readout = output_weight[0]
    gain_first = norm_gain[0]
    gain_second = final_gain[0]

    def run_block(own, back1, back2, row3):
        window = jnp.concatenate([row3, back2, back1, own], axis=1)
        shifted = window[:, :-1].astype(jnp.bfloat16)
        hidden = jnp.einsum("mrc,cd->mrd", shifted, embed, preferred_element_type=jnp.float32)
        normed = rms_scaled(hidden, gain_first).astype(jnp.bfloat16)
        queries = jnp.einsum(
            "mrc,cd->mrd", normed[:, BACK * rows :], w_query, preferred_element_type=jnp.float32
        ).astype(jnp.bfloat16)
        keyval = jnp.einsum(
            "mrc,cd->mrd", normed, w_keyval, preferred_element_type=jnp.float32
        ).astype(jnp.bfloat16)
        queries = queries.reshape(micro, rows, head_count, HEAD_DIM)
        keys = keyval[:, :, :heads_all].reshape(micro, span, head_count, HEAD_DIM)
        values = keyval[:, :, heads_all:].reshape(micro, span, head_count, HEAD_DIM)
        scores = jnp.einsum(
            "mqhd,mkhd->mhqk", queries, keys, preferred_element_type=jnp.float32
        ) * HEAD_DIM ** (-0.5)
        scores = jnp.where(allowed[None, None], scores, -jnp.inf)
        top = jnp.max(scores, axis=-1, keepdims=True)
        expo = jnp.exp(scores - top)
        total = jnp.sum(expo, axis=-1, keepdims=True)
        mixed = (
            jnp.einsum(
                "mhqk,mkhd->mhqd",
                expo.astype(jnp.bfloat16),
                values,
                preferred_element_type=jnp.float32,
            )
            / total
        )
        mixed = jnp.transpose(mixed, (0, 2, 1, 3)).reshape(micro, rows, heads_all)
        mixed = mixed.astype(jnp.bfloat16)
        residual = hidden[:, BACK * rows :] + jnp.einsum(
            "mrc,cd->mrd", mixed, mixing, preferred_element_type=jnp.float32
        )
        final_normed = rms_scaled(residual, gain_second).astype(jnp.bfloat16)
        raw = jnp.einsum("mrc,cd->mrd", final_normed, readout, preferred_element_type=jnp.float32)
        shift_mean = raw[..., :width_in]
        log_scale = 0.5 * jnp.tanh(raw[..., width_in:])
        return (own - shift_mean) * jnp.exp(-log_scale)

    axes = ("segment", "seq")

    def first_inputs():
        def behind(block, distance):
            pairs = [(q, q + distance) for q in range(n_seq) if q + distance < n_seq]
            pairs = [(s, t) for s, t in pairs]
            return lax.ppermute(
                block, axes, [(0 * n_seq + s, 0 * n_seq + t) for s, t in pairs]
            )

        back1 = behind(patches, 1)
        back2 = behind(patches, 2)
        row3 = behind(patches[:, rows - 1 :], BACK + 1)
        return patches, back1, back2, row3

    def next_inputs(result, turn):
        mirrored = result[:, ::-1]
        src = turn * n_seq
        dst = (turn + 1) * n_seq

        def send(block, offset):
            pairs = []
            for q in range(n_seq):
                target = n_seq - 1 - q + offset
                if 0 <= target < n_seq:
                    pairs.append((src + q, dst + target))
            return lax.ppermute(block, axes, pairs)

        own = send(mirrored, 0)
        back1 = send(mirrored, 1)
        back2 = send(mirrored, 2)
        row3 = send(mirrored[:, rows - 1 :], BACK + 1)
        return own, back1, back2, row3

    inputs = first_inputs()
    out = jnp.zeros((micro, rows, width_in), jnp.float32)
    for turn in range(n_seg):
        result = run_block(*inputs)
        out = jnp.where(segment == turn, result, out)
        if turn + 1 < n_seg:
            inputs = next_inputs(result, turn)
    return out[None]


def solution(mesh):
    in_specs = (
        P(None, "seq", None),
        P(),
        P("segment", None, None),
        P("segment", None, None),
        P("segment", None, None),
        P("segment", None, None),
        P("segment", None),
        P("segment", None),
    )
    out_specs = P("segment", None, "seq", None)
    return jax.shard_map(body, mesh=mesh, in_specs=in_specs, out_specs=out_specs, check_vma=False)
```

time: 331 us -> 128 us (0.39)
  the two profiles are of different devices: /device:TPU:0 before, /device:TPU:15 now
where the time goes in v1:
time: 128 us; the launch traced here: 127 us
  matrix products  50 us (39%)
  local copies, waits for them, and re-layouts  30.7 us (24%)
  waiting for transfers between devices  23 us (18%)
  starting transfers between devices  13.1 us (10%)
  other arithmetic  9.44 us (7%)
    ppermute x12, waiting for transfers between devices, send(): return lax.ppermute(block, axes, pairs)  23 us
    unnamed x52, local copies, waits for them, and re-layouts  17.9 us
    dot_general x4, matrix products, run_block(): jnp.einsum('mrc,cd->mrd', normed, w_keyval, preferred_element_type=jnp.fl...  14.5 us
    ppermute x12, starting transfers between devices, send(): return lax.ppermute(block, axes, pairs)  11.1 us
    dot_general x4, matrix products, run_block(): jnp.einsum('mrc,cd->mrd', normed[:, BACK * rows:], w_query, preferred_ele...  10.9 us
    reshape x4, local copies, waits for them, and re-layouts, run_block(): values = keyval[:, :, heads_all:].reshape(micro, span, head_count, HEAD_DIM)  10.3 us
    dot_general x4, matrix products, run_block(): jnp.einsum('mqhd,mkhd->mhqk', queries, keys, preferred_element_type=jnp.f...  10 us
    dot_general x4, matrix products, run_block(): jnp.einsum('mrc,cd->mrd', shifted, embed, preferred_element_type=jnp.floa...  4.67 us
  transfers between devices with their start and end apart: 15, of which 2 were waited for; matrix products, arithmetic and copies ran while one was open for 3% of the time, Pallas kernels for 0%

profile of v1, /device:TPU:15, one launch (start us, length us, event | category | flops | bytes accessed | tf_op | source)
XLA Modules:
  0.0 127.1 jit_solution(11387243749798828186)
XLA Ops:
  5.0 1.7 %multiply_reduce_fusion.3 = (f32[2,384]{1,0:T(2,128)S(1)}, f32[2,384,1024]{2,1,0:T(8,128)S(1)}) fusion(bf16[1,128,1024]{2,1,0:T(8,128)(2,1)} %param.10, bf16[2,128,128]{2,1,0:T(8,128)(2,1)S(1)} %convert.88, bf16[2,128,128]{2,1,0:T(8,128)(2,1)S(1)} %collective-permute-done.2, bf16[2,128,128]{2,1,0:T(8,128)(2,1)S(1)} %collective-permute-done.1, ...), kind=kOutput, calls=%fused_computation.20 | convolution fusion | flops 203685120 | bytes 3608064 | tf_op jit(solution)/shard_map/mrc,cd->mrd/dot_general | solution.py:55
  6.8 1.6 %copy-done.7 = f32[2,384,1024]{2,1,0:T(8,128)} copy-done((f32[2,384,1024]{2,1,0:T(8,128)}, f32[2,384,1024]{2,1,0:T(8,128)S(1)}, u32[]{:S(2)}) %copy-start.7) | copy-done | bytes 3145752
  9.5 3.6 %convolution_convert_fusion.3 = bf16[2,384,2048]{2,1,0:T(8,128)(2,1)S(1)} fusion(bf16[2,384,1024]{2,1,0:T(8,128)(2,1)S(1)} %multiply_convert_fusion.3, bf16[1024,3072]{1,0:T(8,128)(2,1)S(1)} %bitcast.187), kind=kOutput, calls=%fused_computation.4 | convolution fusion | flops 3222798336 | bytes 8912896 | tf_op jit(solution)/shard_map/mrc,cd->mrd/dot_general | solution.py:60
  13.1 2.2 %slice_bitcast_fusion.5 = (bf16[2,48,8,8,128]{4,3,2,1,0:T(8,128)(2,1)}, bf16[2,384,1024]{2,1,0:T(8,128)(2,1)}) fusion(bf16[2,384,2048]{2,1,0:T(8,128)(2,1)S(1)} %convolution_convert_fusion.3), kind=kLoop, calls=%fused_computation.61 | loop fusion | bytes 6291456
  15.3 2.6 %copy.45 = bf16[2,384,1024]{1,2,0:T(8,128)(2,1)} copy(bf16[2,384,1024]{2,1,0:T(8,128)(2,1)} %get-tuple-element.12) | data formatting | bytes 3145728 | tf_op jit(solution)/shard_map/reshape | solution.py:65
  17.9 2.4 %fusion = (f32[2,8,128]{2,1,0:T(8,128)S(1)}, f32[2,8,128,384]{3,2,1,0:T(8,128)S(1)}) fusion(pred[128,384]{1,0:T(8,128)(4,1)S(1)} %fusion.123, bf16[2,48,8,8,128]{4,3,2,1,0:T(8,128)(2,1)} %get-tuple-element.11, bf16[2,16,8,8,128]{4,3,2,1,0:T(8,128)(2,1)S(1)} %fusion.71), kind=kOutput, calls=%fused_computation.21 | convolution fusion | flops 203683840 | bytes 5300224 | tf_op jit(solution)/shard_map/mqhd,mkhd->mhqk/dot_general | solution.py:66
  22.4 2.1 %multiply_reduce_fusion.7 = (f32[2,128]{1,0:T(2,128)S(1)}, f32[2,128,1024]{2,1,0:T(8,128)S(1)}) fusion(bf16[2,128,1024]{1,2,0:T(8,128)(2,1)S(1)} %bitcast.167, bf16[1,1024,1024]{2,1,0:T(8,128)(2,1)S(1)} %copy-done, f32[2,384,1024]{2,1,0:T(8,128)} %copy-done.7), kind=kOutput, calls=%fused_computation.104 | convolution fusion | flops 537657088 | bytes 4719616 | tf_op jit(solution)/shard_map/mrc,cd->mrd/dot_general | solution.py:84
  28.7 1.6 %copy-done.3 = f32[2,384,1024]{2,1,0:T(8,128)} copy-done((f32[2,384,1024]{2,1,0:T(8,128)}, f32[2,384,1024]{2,1,0:T(8,128)S(1)}, u32[]{:S(2)}) %copy-start.3) | copy-done | bytes 3145752
  30.7 3.4 %fusion.72 = bf16[2,16,8,8,128]{4,3,2,1,0:T(8,128)(2,1)} fusion(bf16[1024,3072]{1,0:T(8,128)(2,1)} %bitcast.183, bf16[2,384,1024]{2,1,0:T(8,128)(2,1)S(1)} %multiply_convert_fusion.2), kind=kOutput, calls=%fused_computation.88 | convolution fusion | flops 537133056 | bytes 3145728 | tf_op jit(solution)/shard_map/mrc,cd->mrd/dot_general | solution.py:57
  34.1 3.6 %convolution_convert_fusion.2 = bf16[2,384,2048]{2,1,0:T(8,128)(2,1)S(1)} fusion(bf16[2,384,1024]{2,1,0:T(8,128)(2,1)S(1)} %multiply_convert_fusion.2, bf16[1024,3072]{1,0:T(8,128)(2,1)S(1)} %bitcast.190), kind=kOutput, calls=%fused_computation.3 | convolution fusion | flops 3222798336 | bytes 8912896 | tf_op jit(solution)/shard_map/mrc,cd->mrd/dot_general | solution.py:60
  37.7 2.1 %slice_bitcast_fusion.4 = (bf16[2,48,8,8,128]{4,3,2,1,0:T(8,128)(2,1)}, bf16[2,384,1024]{2,1,0:T(8,128)(2,1)}) fusion(bf16[2,384,2048]{2,1,0:T(8,128)(2,1)S(1)} %convolution_convert_fusion.2), kind=kLoop, calls=%fused_computation.60 | loop fusion | bytes 6291456
  39.8 2.6 %copy.46 = bf16[2,384,1024]{1,2,0:T(8,128)(2,1)} copy(bf16[2,384,1024]{2,1,0:T(8,128)(2,1)} %get-tuple-element.10) | data formatting | bytes 3145728 | tf_op jit(solution)/shard_map/reshape | solution.py:65
  42.4 2.5 %fusion.1 = (f32[2,8,128]{2,1,0:T(8,128)S(1)}, f32[2,8,128,384]{3,2,1,0:T(8,128)S(1)}) fusion(pred[128,384]{1,0:T(8,128)(4,1)S(1)} %fusion.123, bf16[2,48,8,8,128]{4,3,2,1,0:T(8,128)(2,1)} %get-tuple-element.9, bf16[2,16,8,8,128]{4,3,2,1,0:T(8,128)(2,1)} %fusion.72), kind=kOutput, calls=%fused_computation.22 | convolution fusion | flops 203683840 | bytes 5300224 | tf_op jit(solution)/shard_map/mqhd,mkhd->mhqk/dot_general | solution.py:66
  53.0 1.6 %copy-done.5 = f32[2,384,1024]{2,1,0:T(8,128)} copy-done((f32[2,384,1024]{2,1,0:T(8,128)}, f32[2,384,1024]{2,1,0:T(8,128)S(1)}, u32[]{:S(2)}) %copy-start.5) | copy-done | bytes 3145752
  55.0 3.4 %fusion.73 = bf16[2,16,8,8,128]{4,3,2,1,0:T(8,128)(2,1)} fusion(bf16[1024,3072]{1,0:T(8,128)(2,1)} %bitcast.184, bf16[2,384,1024]{2,1,0:T(8,128)(2,1)S(1)} %multiply_convert_fusion.1), kind=kOutput, calls=%fused_computation.89 | convolution fusion | flops 537133056 | bytes 3145728 | tf_op jit(solution)/shard_map/mrc,cd->mrd/dot_general | solution.py:57
  58.4 3.6 %convolution_convert_fusion.1 = bf16[2,384,2048]{2,1,0:T(8,128)(2,1)S(1)} fusion(bf16[2,384,1024]{2,1,0:T(8,128)(2,1)S(1)} %multiply_convert_fusion.1, bf16[1024,3072]{1,0:T(8,128)(2,1)S(1)} %bitcast.193), kind=kOutput, calls=%fused_computation.2 | convolution fusion | flops 3222798336 | bytes 8912896 | tf_op jit(solution)/shard_map/mrc,cd->mrd/dot_general | solution.py:60
  62.0 2.1 %slice_bitcast_fusion.3 = (bf16[2,48,8,8,128]{4,3,2,1,0:T(8,128)(2,1)}, bf16[2,384,1024]{2,1,0:T(8,128)(2,1)}) fusion(bf16[2,384,2048]{2,1,0:T(8,128)(2,1)S(1)} %convolution_convert_fusion.1), kind=kLoop, calls=%fused_computation.59 | loop fusion | bytes 6291456
  64.1 2.6 %copy.47 = bf16[2,384,1024]{1,2,0:T(8,128)(2,1)} copy(bf16[2,384,1024]{2,1,0:T(8,128)(2,1)} %get-tuple-element.8) | data formatting | bytes 3145728 | tf_op jit(solution)/shard_map/reshape | solution.py:65
  66.7 2.5 %fusion.2 = (f32[2,8,128]{2,1,0:T(8,128)S(1)}, f32[2,8,128,384]{3,2,1,0:T(8,128)S(1)}) fusion(pred[128,384]{1,0:T(8,128)(4,1)S(1)} %fusion.123, bf16[2,48,8,8,128]{4,3,2,1,0:T(8,128)(2,1)} %get-tuple-element.7, bf16[2,16,8,8,128]{4,3,2,1,0:T(8,128)(2,1)} %fusion.73), kind=kOutput, calls=%fused_computation.23 | convolution fusion | flops 203683840 | bytes 5300224 | tf_op jit(solution)/shard_map/mqhd,mkhd->mhqk/dot_general | solution.py:66
  74.2 1.3 %collective-permute-start.11 = (f32[2,128,128]{2,1,0:T(8,128)}, f32[2,128,128]{2,1,0:T(8,128)S(1)}, u32[]{:S(2)}, u32[]{:S(2)}) collective-permute-start(f32[2,128,128]{2,1,0:T(8,128)} %rev.11), channel_id=1, source_target_pairs={{16,31},{17,30},{18,29},{19,28},{20,27},{21,26},{22,25},{23,24}} | collective-permute-start | bytes 393224 | tf_op jit(solution)/shard_map/ppermute | solution.py:119
  75.5 1.5 %convert.85 = bf16[2,128,128]{2,1,0:T(8,128)(2,1)} convert(f32[2,128,128]{2,1,0:T(8,128)} %rev.11) | non-fusion elementwise | flops 32768 | bytes 196608
  78.3 1.3 %collective-permute-start.13 = (bf16[2,128,128]{2,1,0:T(8,128)(2,1)}, bf16[2,128,128]{2,1,0:T(8,128)(2,1)}, u32[]{:S(2)}, u32[]{:S(2)}) collective-permute-start(bf16[2,128,128]{2,1,0:T(8,128)(2,1)} %convert.85), channel_id=1, source_target_pairs={{18,31},{19,30},{20,29},{21,28},{22,27},{23,26}} | collective-permute-start | bytes 196616 | tf_op jit(solution)/shard_map/ppermute | solution.py:119
  79.7 1.6 %collective-permute-start.12 = (bf16[2,1,128]{2,1,0:T(2,128)(2,1)S(1)}, bf16[2,1,128]{2,1,0:T(2,128)(2,1)S(1)}, u32[]{:S(2)}, u32[]{:S(2)}) collective-permute-start(bf16[2,1,128]{2,1,0:T(2,128)(2,1)S(1)} %slice.165), channel_id=1, source_target_pairs={{19,31},{20,30},{21,29},{22,28},{23,27}} | collective-permute-start | bytes 1544 | tf_op jit(solution)/shard_map/ppermute | solution.py:119
  81.2 20.1 %collective-permute-done.11 = f32[2,128,128]{2,1,0:T(8,128)S(1)} collective-permute-done((f32[2,128,128]{2,1,0:T(8,128)}, f32[2,128,128]{2,1,0:T(8,128)S(1)}, u32[]{:S(2)}, u32[]{:S(2)}) %collective-permute-start.11) | collective-permute-done | bytes 131104 | tf_op jit(solution)/shard_map/ppermute | solution.py:119
  101.4 2.9 %collective-permute-done.12 = bf16[2,1,128]{2,1,0:T(2,128)(2,1)S(1)} collective-permute-done((bf16[2,1,128]{2,1,0:T(2,128)(2,1)S(1)}, bf16[2,1,128]{2,1,0:T(2,128)(2,1)S(1)}, u32[]{:S(2)}, u32[]{:S(2)}) %collective-permute-start.12) | collective-permute-done | bytes 544 | tf_op jit(solution)/shard_map/ppermute | solution.py:119
  104.3 1.6 %multiply_reduce_fusion = (f32[2,384]{1,0:T(2,128)S(1)}, f32[2,384,1024]{2,1,0:T(8,128)S(1)}) fusion(bf16[1,128,1024]{2,1,0:T(8,128)(2,1)S(1)} %copy-done.9, bf16[2,128,128]{2,1,0:T(8,128)(2,1)S(1)} %convert.67, bf16[2,128,128]{2,1,0:T(8,128)(2,1)S(1)} %collective-permute-done.14, bf16[2,128,128]{2,1,0:T(8,128)(2,1)} %collective-permute-done.13, ...), kind=kOutput, calls=%fused_computation.8 | convolution fusion | flops 203685120 | bytes 3608064 | tf_op jit(solution)/shard_map/mrc,cd->mrd/dot_general | solution.py:55
  105.9 1.6 %copy-done.1 = f32[2,384,1024]{2,1,0:T(8,128)} copy-done((f32[2,384,1024]{2,1,0:T(8,128)}, f32[2,384,1024]{2,1,0:T(8,128)S(1)}, u32[]{:S(2)}) %copy-start.1) | copy-done | bytes 3145752
  107.9 3.3 %fusion.74 = bf16[2,16,8,8,128]{4,3,2,1,0:T(8,128)(2,1)} fusion(bf16[1024,3072]{1,0:T(8,128)(2,1)} %bitcast.185, bf16[2,384,1024]{2,1,0:T(8,128)(2,1)S(1)} %multiply_convert_fusion), kind=kOutput, calls=%fused_computation.90 | convolution fusion | flops 537133056 | bytes 3145728 | tf_op jit(solution)/shard_map/mrc,cd->mrd/dot_general | solution.py:57
  111.2 3.6 %convolution_convert_fusion = bf16[2,384,2048]{2,1,0:T(8,128)(2,1)S(1)} fusion(bf16[2,384,1024]{2,1,0:T(8,128)(2,1)S(1)} %multiply_convert_fusion, bf16[1024,3072]{1,0:T(8,128)(2,1)S(1)} %bitcast.196), kind=kOutput, calls=%fused_computation.1 | convolution fusion | flops 3222798336 | bytes 8912896 | tf_op jit(solution)/shard_map/mrc,cd->mrd/dot_general | solution.py:60
  114.9 2.1 %slice_bitcast_fusion.2 = (bf16[2,48,8,8,128]{4,3,2,1,0:T(8,128)(2,1)}, bf16[2,384,1024]{2,1,0:T(8,128)(2,1)}) fusion(bf16[2,384,2048]{2,1,0:T(8,128)(2,1)S(1)} %convolution_convert_fusion), kind=kLoop, calls=%fused_computation.58 | loop fusion | bytes 6291456
  117.0 2.6 %copy.48 = bf16[2,384,1024]{1,2,0:T(8,128)(2,1)} copy(bf16[2,384,1024]{2,1,0:T(8,128)(2,1)} %get-tuple-element.6) | data formatting | bytes 3145728 | tf_op jit(solution)/shard_map/reshape | solution.py:65
  119.6 2.5 %fusion.3 = (f32[2,8,128]{2,1,0:T(8,128)S(1)}, f32[2,8,128,384]{3,2,1,0:T(8,128)S(1)}) fusion(pred[128,384]{1,0:T(8,128)(4,1)S(1)} %fusion.123, bf16[2,48,8,8,128]{4,3,2,1,0:T(8,128)(2,1)} %get-tuple-element.5, bf16[2,16,8,8,128]{4,3,2,1,0:T(8,128)(2,1)} %fusion.74), kind=kOutput, calls=%fused_computation.24 | convolution fusion | flops 203683840 | bytes 5300224 | tf_op jit(solution)/shard_map/mqhd,mkhd->mhqk/dot_general | solution.py:66
  (126 shorter events, 32.2 us)
Async XLA Ops:
  0.0 22.4 %copy-start = (bf16[1,1024,1024]{2,1,0:T(8,128)(2,1)S(1)}, bf16[1,1024,1024]{2,1,0:T(8,128)(2,1)}, u32[]{:S(2)}) copy-start(bf16[1,1024,1024]{2,1,0:T(8,128)(2,1)} %param.12) | copy-start | bytes 6291460
  0.0 8.4 %copy-start.16 = (f32[1,1024]{1,0:T(1,128)S(1)}, f32[1,1024]{1,0:T(1,128)}, u32[]{:S(2)}) copy-start(f32[1,1024]{1,0:T(1,128)} %param.14) | copy-start | bytes 12292
  1.1 3.9 %collective-permute-start.2 = (bf16[2,128,128]{2,1,0:T(8,128)(2,1)S(1)}, bf16[2,128,128]{2,1,0:T(8,128)(2,1)S(1)}, u32[]{:S(2)}, u32[]{:S(2)}) collective-permute-start(bf16[2,128,128]{2,1,0:T(8,128)(2,1)S(1)} %convert.88), channel_id=1, source_target_pairs={{0,1},{1,2},{2,3},{3,4},{4,5},{5,6},{6,7}} | collective-permute-start | bytes 196616 | tf_op jit(solution)/shard_map/ppermute | solution.py:99
  1.8 3.2 %collective-permute-start.1 = (bf16[2,128,128]{2,1,0:T(8,128)(2,1)S(1)}, bf16[2,128,128]{2,1,0:T(8,128)(2,1)S(1)}, u32[]{:S(2)}, u32[]{:S(2)}) collective-permute-start(bf16[2,128,128]{2,1,0:T(8,128)(2,1)S(1)} %convert.88), channel_id=1, source_target_pairs={{0,2},{1,3},{2,4},{3,5},{4,6},{5,7}} | collective-permute-start | bytes 196616 | tf_op jit(solution)/shard_map/ppermute | solution.py:99
  3.1 1.9 %collective-permute-start = (bf16[2,1,128]{2,1,0:T(2,128)(2,1)S(1)}, bf16[2,1,128]{2,1,0:T(2,128)(2,1)S(1)}, u32[]{:S(2)}, u32[]{:S(2)}) collective-permute-start(bf16[2,1,128]{2,1,0:T(2,128)(2,1)S(1)} %slice.109), channel_id=1, source_target_pairs={{0,3},{1,4},{2,5},{3,6},{4,7}} | collective-permute-start | bytes 1544 | tf_op jit(solution)/shard_map/ppermute | solution.py:99
  5.0 3.7 %copy-start.17 = (bf16[1,1024,3072]{2,1,0:T(8,128)(2,1)S(1)}, bf16[1,1024,3072]{2,1,0:T(8,128)(2,1)}, u32[]{:S(2)}) copy-start(bf16[1,1024,3072]{2,1,0:T(8,128)(2,1)} %param.11) | copy-start | bytes 18874372
  17.9 3.5 %copy-start.11 = (bf16[2,384,1024]{1,2,0:T(8,128)(2,1)S(1)}, bf16[2,384,1024]{1,2,0:T(8,128)(2,1)}, u32[]{:S(2)}) copy-start(bf16[2,384,1024]{1,2,0:T(8,128)(2,1)} %copy.45) | copy-start | bytes 4718596
  22.3 2.2 %copy-start.8 = (bf16[1,1024,256]{2,1,0:T(8,128)(2,1)S(1)}, bf16[1,1024,256]{2,1,0:T(8,128)(2,1)}, u32[]{:S(2)}) copy-start(bf16[1,1024,256]{2,1,0:T(8,128)(2,1)} %param.13) | copy-start | bytes 1572868
  22.4 2.2 %copy-start.15 = (f32[1,1024]{1,0:T(1,128)S(1)}, f32[1,1024]{1,0:T(1,128)}, u32[]{:S(2)}) copy-start(f32[1,1024]{1,0:T(1,128)} %param.15) | copy-start | bytes 12292
  22.4 2.5 %copy-start.14 = (f32[2,128,128]{2,1,0:T(8,128)S(1)}, f32[2,128,128]{2,1,0:T(8,128)}, u32[]{:S(2)}) copy-start(f32[2,128,128]{2,1,0:T(8,128)} %param.8) | copy-start | bytes 393220
  22.4 5.6 %copy-start.9 = (bf16[1,128,1024]{2,1,0:T(8,128)(2,1)S(1)}, bf16[1,128,1024]{2,1,0:T(8,128)(2,1)}, u32[]{:S(2)}) copy-start(bf16[1,128,1024]{2,1,0:T(8,128)(2,1)} %param.10) | copy-start | bytes 786436
  25.1 2.9 %collective-permute-start.3 = (f32[2,128,128]{2,1,0:T(8,128)S(1)}, f32[2,128,128]{2,1,0:T(8,128)S(1)}, u32[]{:S(2)}, u32[]{:S(2)}) collective-permute-start(f32[2,128,128]{2,1,0:T(8,128)S(1)} %rev.9), channel_id=1, source_target_pairs={{0,15},{1,14},{2,13},{3,12},{4,11},{5,10},{6,9},{7,8}} | collective-permute-start | bytes 393224 | tf_op jit(solution)/shard_map/ppermute | solution.py:119
  25.8 2.3 %collective-permute-start.6 = (bf16[2,128,128]{2,1,0:T(8,128)(2,1)S(1)}, bf16[2,128,128]{2,1,0:T(8,128)(2,1)S(1)}, u32[]{:S(2)}, u32[]{:S(2)}) collective-permute-start(bf16[2,128,128]{2,1,0:T(8,128)(2,1)S(1)} %convert.87), channel_id=1, source_target_pairs={{1,15},{2,14},{3,13},{4,12},{5,11},{6,10},{7,9}} | collective-permute-start | bytes 196616 | tf_op jit(solution)/shard_map/ppermute | solution.py:119
  26.4 1.6 %collective-permute-start.5 = (bf16[2,128,128]{2,1,0:T(8,128)(2,1)S(1)}, bf16[2,128,128]{2,1,0:T(8,128)(2,1)S(1)}, u32[]{:S(2)}, u32[]{:S(2)}) collective-permute-start(bf16[2,128,128]{2,1,0:T(8,128)(2,1)S(1)} %convert.87), channel_id=1, source_target_pairs={{2,15},{3,14},{4,13},{5,12},{6,11},{7,10}} | collective-permute-start | bytes 196616 | tf_op jit(solution)/shard_map/ppermute | solution.py:119
  27.1 0.9 collective-permute-start.4
  28.0 6.0 %slice-start = ((s8[6291456]{0:T(1024)(128)(4,1)}), s8[4194304]{0:T(1024)(128)(4,1)S(1)}, s32[]{:S(2)}) async-start(s8[6291456]{0:T(1024)(128)(4,1)} %bitcast.188), calls=%async_computation | async-start | bytes 8388608
  30.3 3.7 %slice-start.1 = ((s8[6291456]{0:T(1024)(128)(4,1)}), s8[2097152]{0:T(1024)(128)(4,1)S(1)}, s32[]{:S(2)}) async-start(s8[6291456]{0:T(1024)(128)(4,1)} %bitcast.188), calls=%async_computation.1 | async-start | bytes 4194304
  42.4 3.6 %copy-start.12 = (bf16[2,384,1024]{1,2,0:T(8,128)(2,1)S(1)}, bf16[2,384,1024]{1,2,0:T(8,128)(2,1)}, u32[]{:S(2)}) copy-start(bf16[2,384,1024]{1,2,0:T(8,128)(2,1)} %copy.46) | copy-start | bytes 4718596
  49.3 2.9 %collective-permute-start.7 = (f32[2,128,128]{2,1,0:T(8,128)S(1)}, f32[2,128,128]{2,1,0:T(8,128)S(1)}, u32[]{:S(2)}, u32[]{:S(2)}) collective-permute-start(f32[2,128,128]{2,1,0:T(8,128)S(1)} %rev.10), channel_id=1, source_target_pairs={{8,23},{9,22},{10,21},{11,20},{12,19},{13,18},{14,17},{15,16}} | collective-permute-start | bytes 393224 | tf_op jit(solution)/shard_map/ppermute | solution.py:119
  50.0 2.3 %collective-permute-start.10 = (bf16[2,128,128]{2,1,0:T(8,128)(2,1)S(1)}, bf16[2,128,128]{2,1,0:T(8,128)(2,1)S(1)}, u32[]{:S(2)}, u32[]{:S(2)}) collective-permute-start(bf16[2,128,128]{2,1,0:T(8,128)(2,1)S(1)} %convert.86), channel_id=1, source_target_pairs={{9,23},{10,22},{11,21},{12,20},{13,19},{14,18},{15,17}} | collective-permute-start | bytes 196616 | tf_op jit(solution)/shard_map/ppermute | solution.py:119
  50.7 1.6 %collective-permute-start.9 = (bf16[2,128,128]{2,1,0:T(8,128)(2,1)S(1)}, bf16[2,128,128]{2,1,0:T(8,128)(2,1)S(1)}, u32[]{:S(2)}, u32[]{:S(2)}) collective-permute-start(bf16[2,128,128]{2,1,0:T(8,128)(2,1)S(1)} %convert.86), channel_id=1, source_target_pairs={{10,23},{11,22},{12,21},{13,20},{14,19},{15,18}} | collective-permute-start | bytes 196616 | tf_op jit(solution)/shard_map/ppermute | solution.py:119
  51.4 0.9 collective-permute-start.8
  52.3 6.0 %slice-start.2 = ((s8[6291456]{0:T(1024)(128)(4,1)}), s8[4194304]{0:T(1024)(128)(4,1)S(1)}, s32[]{:S(2)}) async-start(s8[6291456]{0:T(1024)(128)(4,1)} %bitcast.191), calls=%async_computation.2 | async-start | bytes 8388608
  54.6 3.7 %slice-start.3 = ((s8[6291456]{0:T(1024)(128)(4,1)}), s8[2097152]{0:T(1024)(128)(4,1)S(1)}, s32[]{:S(2)}) async-start(s8[6291456]{0:T(1024)(128)(4,1)} %bitcast.191), calls=%async_computation.3 | async-start | bytes 4194304
  66.7 3.6 %copy-start.13 = (bf16[2,384,1024]{1,2,0:T(8,128)(2,1)S(1)}, bf16[2,384,1024]{1,2,0:T(8,128)(2,1)}, u32[]{:S(2)}) copy-start(bf16[2,384,1024]{1,2,0:T(8,128)(2,1)} %copy.47) | copy-start | bytes 4718596
  74.2 27.1 %collective-permute-start.11 = (f32[2,128,128]{2,1,0:T(8,128)}, f32[2,128,128]{2,1,0:T(8,128)S(1)}, u32[]{:S(2)}, u32[]{:S(2)}) collective-permute-start(f32[2,128,128]{2,1,0:T(8,128)} %rev.11), channel_id=1, source_target_pairs={{16,31},{17,30},{18,29},{19,28},{20,27},{21,26},{22,25},{23,24}} | collective-permute-start | bytes 393224 | tf_op jit(solution)/shard_map/ppermute | solution.py:119
  77.1 27.2 %collective-permute-start.14 = (bf16[2,128,128]{2,1,0:T(8,128)(2,1)}, bf16[2,128,128]{2,1,0:T(8,128)(2,1)S(1)}, u32[]{:S(2)}, u32[]{:S(2)}) collective-permute-start(bf16[2,128,128]{2,1,0:T(8,128)(2,1)} %convert.85), channel_id=1, source_target_pairs={{17,31},{18,30},{19,29},{20,28},{21,27},{22,26},{23,25}} | collective-permute-start | bytes 196616 | tf_op jit(solution)/shard_map/ppermute | solution.py:119
  78.3 25.9 %collective-permute-start.13 = (bf16[2,128,128]{2,1,0:T(8,128)(2,1)}, bf16[2,128,128]{2,1,0:T(8,128)(2,1)}, u32[]{:S(2)}, u32[]{:S(2)}) collective-permute-start(bf16[2,128,128]{2,1,0:T(8,128)(2,1)} %convert.85), channel_id=1, source_target_pairs={{18,31},{19,30},{20,29},{21,28},{22,27},{23,26}} | collective-permute-start | bytes 196616 | tf_op jit(solution)/shard_map/ppermute | solution.py:119
  79.7 24.6 %collective-permute-start.12 = (bf16[2,1,128]{2,1,0:T(2,128)(2,1)S(1)}, bf16[2,1,128]{2,1,0:T(2,128)(2,1)S(1)}, u32[]{:S(2)}, u32[]{:S(2)}) collective-permute-start(bf16[2,1,128]{2,1,0:T(2,128)(2,1)S(1)} %slice.165), channel_id=1, source_target_pairs={{19,31},{20,30},{21,29},{22,28},{23,27}} | collective-permute-start | bytes 1544 | tf_op jit(solution)/shard_map/ppermute | solution.py:119
  104.3 7.0 %slice-start.4 = ((s8[6291456]{0:T(1024)(128)(4,1)}), s8[4194304]{0:T(1024)(128)(4,1)S(1)}, s32[]{:S(2)}) async-start(s8[6291456]{0:T(1024)(128)(4,1)} %bitcast.194), calls=%async_computation.4 | async-start | bytes 8388608
  107.6 3.7 %slice-start.5 = ((s8[6291456]{0:T(1024)(128)(4,1)}), s8[2097152]{0:T(1024)(128)(4,1)S(1)}, s32[]{:S(2)}) async-start(s8[6291456]{0:T(1024)(128)(4,1)} %bitcast.194), calls=%async_computation.5 | async-start | bytes 4194304
  119.6 3.6 %copy-start.10 = (bf16[2,384,1024]{1,2,0:T(8,128)(2,1)S(1)}, bf16[2,384,1024]{1,2,0:T(8,128)(2,1)}, u32[]{:S(2)}) copy-start(bf16[2,384,1024]{1,2,0:T(8,128)(2,1)} %copy.48) | copy-start | bytes 4718596
  (7 other events, 12.3 us)

commit v2 on v1

--- a/solution.py
+++ b/solution.py
@@ -1,11 +1,132 @@
 import jax
 import jax.numpy as jnp
 from jax import lax
+from jax.experimental import pallas as pl
+from jax.experimental.pallas import tpu as pltpu
 from jax.sharding import PartitionSpec as P
 
 HEAD_DIM = 128
 TILE = 128
 BACK = 2
+
+CHUNK = 256
+
+
+def make_block_call(micro, rows, width_in, heads_all):
+    span = (BACK + 1) * rows
+    own_at = BACK * rows
+    n_rows = micro * span
+    scale = HEAD_DIM ** (-0.5)
+    heads = heads_all // HEAD_DIM
+
+    def kernel(shifted_ref, own_ref, mask_ref, ga_ref, gb_ref,
+               embed_hbm, attn_hbm, mix_hbm, read_hbm,
+               out_ref,
+               embed_v, attn_v, mix_v, read_v, sems,
+               hidden_s, normed_s, q_s, kv_s, mixed_s, res_s):
+        copies = [
+            pltpu.make_async_copy(embed_hbm, embed_v, sems.at[0]),
+            pltpu.make_async_copy(attn_hbm, attn_v, sems.at[1]),
+            pltpu.make_async_copy(mix_hbm, mix_v, sems.at[2]),
+            pltpu.make_async_copy(read_hbm, read_v, sems.at[3]),
+        ]
+        for copy in copies:
+            copy.start()
+        copies[0].wait()
+        hidden = jnp.dot(shifted_ref[...], embed_v[...], preferred_element_type=jnp.float32)
+        hidden_s[...] = hidden
+        square = jnp.mean(hidden * hidden, axis=-1, keepdims=True)
+        normed_s[...] = (hidden * lax.rsqrt(square + 1e-06) * ga_ref[...]).astype(jnp.bfloat16)
+        copies[1].wait()
+
+        def kv_step(j, carry):
+            cols = pl.ds(pl.multiple_of(j * CHUNK, CHUNK), CHUNK)
+            wcols = pl.ds(pl.multiple_of(heads_all + j * CHUNK, CHUNK), CHUNK)
+            kv_s[:, cols] = jnp.dot(
+                normed_s[...], attn_v[:, wcols], preferred_element_type=jnp.float32
+            ).astype(jnp.bfloat16)
+            return carry
+
+        lax.fori_loop(0, 2 * heads_all // CHUNK, kv_step, 0)
+
+        def q_step(j, carry):
+            cols = pl.ds(pl.multiple_of(j * CHUNK, CHUNK), CHUNK)
+            for m in range(micro):
+                q_s[m * rows:(m + 1) * rows, cols] = jnp.dot(
+                    normed_s[m * span + own_at:(m + 1) * span, :], attn_v[:, cols],
+                    preferred_element_type=jnp.float32,
+                ).astype(jnp.bfloat16)
+            return carry
+
+        lax.fori_loop(0, heads_all // CHUNK, q_step, 0)
+
+        for m in range(micro):
+            def head_step(h, carry):
+                qcols = pl.ds(pl.multiple_of(h * HEAD_DIM, HEAD_DIM), HEAD_DIM)
+                vcols = pl.ds(pl.multiple_of(heads_all + h * HEAD_DIM, HEAD_DIM), HEAD_DIM)
+                qh = q_s[m * rows:(m + 1) * rows, qcols]
+                kh = kv_s[m * span:(m + 1) * span, qcols]
+                vh = kv_s[m * span:(m + 1) * span, vcols]
+                scores = lax.dot_general(
+                    qh, kh, (((1,), (1,)), ((), ())), preferred_element_type=jnp.float32
+                ) * scale
+                scores = jnp.where(mask_ref[...] > 0.5, scores, -jnp.inf)
+                top = jnp.max(scores, axis=-1, keepdims=True)
+                expo = jnp.exp(scores - top)
+                total = jnp.sum(expo, axis=-1, keepdims=True)
+                mixed = jnp.dot(
+                    expo.astype(jnp.bfloat16), vh, preferred_element_type=jnp.float32
+                ) / total
+                mixed_s[m * rows:(m + 1) * rows, qcols] = mixed.astype(jnp.bfloat16)
+                return carry
+
+            lax.fori_loop(0, heads, head_step, 0)
+
+        copies[2].wait()
+        for m in range(micro):
+            res_s[m * rows:(m + 1) * rows, :] = hidden_s[m * span + own_at:(m + 1) * span, :] + jnp.dot(
+                mixed_s[m * rows:(m + 1) * rows, :], mix_v[...], preferred_element_type=jnp.float32
+            )
+        residual = res_s[...]
+        square = jnp.mean(residual * residual, axis=-1, keepdims=True)
+        final_normed = (residual * lax.rsqrt(square + 1e-06) * gb_ref[...]).astype(jnp.bfloat16)
+        copies[3].wait()
+        raw = jnp.dot(final_normed, read_v[...], preferred_element_type=jnp.float32)
+        shift_mean = raw[:, :width_in]
+        log_scale = 0.5 * jnp.tanh(raw[:, width_in:])
+        out_ref[...] = (own_ref[...] - shift_mean) * jnp.exp(-log_scale)
+
+    width = heads_all
+    flops = 2 * n_rows * (width_in * width + width * 2 * heads_all)
+    flops += 2 * micro * rows * (width * heads_all + 2 * heads * span * HEAD_DIM + heads_all * width + width * 2 * width_in)
+    weight_bytes = 2 * (width_in * width + width * 3 * heads_all + heads_all * width + width * 2 * width_in)
+    vmem = pltpu.VMEM
+    call = pl.pallas_call(
+        kernel,
+        out_shape=jax.ShapeDtypeStruct((micro * rows, width_in), jnp.float32),
+        in_specs=[pl.BlockSpec(memory_space=vmem)] * 5 + [pl.BlockSpec(memory_space=pl.ANY)] * 4,
+        out_specs=pl.BlockSpec(memory_space=vmem),
+        scratch_shapes=[
+            vmem((width_in, width), jnp.bfloat16),
+            vmem((width, 3 * heads_all), jnp.bfloat16),
+            vmem((heads_all, width), jnp.bfloat16),
+            vmem((width, 2 * width_in), jnp.bfloat16),
+            pltpu.SemaphoreType.DMA((4,)),
+            vmem((n_rows, width), jnp.float32),
+            vmem((n_rows, width), jnp.bfloat16),
+            vmem((micro * rows, heads_all), jnp.bfloat16),
+            vmem((n_rows, 2 * heads_all), jnp.bfloat16),
+            vmem((micro * rows, heads_all), jnp.bfloat16),
+            vmem((micro * rows, width), jnp.float32),
+        ],
+        compiler_params=pltpu.CompilerParams(vmem_limit_bytes=56 * 1024 * 1024),
+        cost_estimate=pl.CostEstimate(
+            flops=flops,
+            bytes_accessed=weight_bytes + n_rows * width_in * 2 + 2 * micro * rows * width_in * 4,
+            transcendentals=micro * heads * rows * span + micro * rows * 2 * width_in,
+        ),
+    )
+    return call
 
 
 def rms_scaled(values, gain):
@@ -41,54 +162,23 @@
     key_pos = jnp.arange(span, dtype=jnp.int32)
     allowed = listed[None, :] & (key_pos[None, :] <= query_pos[:, None])
 
-    embed = input_weight[0]
-    w_query = attention_weight[0][:, :heads_all]
-    w_keyval = attention_weight[0][:, heads_all:]
-    mixing = mixing_weight[0]
-    readout = output_weight[0]
-    gain_first = norm_gain[0]
-    gain_second = final_gain[0]
+    block_call = make_block_call(micro, rows, width_in, heads_all)
+    mask = allowed.astype(jnp.float32)
+    embed_w = input_weight[0]
+    attn_w = attention_weight[0]
+    mix_w = mixing_weight[0]
+    read_w = output_weight[0]
+    gain_a = norm_gain[0].reshape(1, -1)
+    gain_b = final_gain[0].reshape(1, -1)
 
     def run_block(own, back1, back2, row3):
         window = jnp.concatenate([row3, back2, back1, own], axis=1)
-        shifted = window[:, :-1].astype(jnp.bfloat16)
-        hidden = jnp.einsum("mrc,cd->mrd", shifted, embed, preferred_element_type=jnp.float32)
-        normed = rms_scaled(hidden, gain_first).astype(jnp.bfloat16)
-        queries = jnp.einsum(
-            "mrc,cd->mrd", normed[:, BACK * rows :], w_query, preferred_element_type=jnp.float32
-        ).astype(jnp.bfloat16)
-        keyval = jnp.einsum(
-            "mrc,cd->mrd", normed, w_keyval, preferred_element_type=jnp.float32
-        ).astype(jnp.bfloat16)
-        queries = queries.reshape(micro, rows, head_count, HEAD_DIM)
-        keys = keyval[:, :, :heads_all].reshape(micro, span, head_count, HEAD_DIM)
-        values = keyval[:, :, heads_all:].reshape(micro, span, head_count, HEAD_DIM)
-        scores = jnp.einsum(
-            "mqhd,mkhd->mhqk", queries, keys, preferred_element_type=jnp.float32
-        ) * HEAD_DIM ** (-0.5)
-        scores = jnp.where(allowed[None, None], scores, -jnp.inf)
-        top = jnp.max(scores, axis=-1, keepdims=True)
-        expo = jnp.exp(scores - top)
-        total = jnp.sum(expo, axis=-1, keepdims=True)
-        mixed = (
-            jnp.einsum(
-                "mhqk,mkhd->mhqd",
-                expo.astype(jnp.bfloat16),
-                values,
-                preferred_element_type=jnp.float32,
-            )
-            / total
+        shifted = window[:, :-1].astype(jnp.bfloat16).reshape(micro * span, width_in)
+        result = block_call(
+            shifted, own.reshape(micro * rows, width_in), mask, gain_a, gain_b,
+            embed_w, attn_w, mix_w, read_w,
         )
-        mixed = jnp.transpose(mixed, (0, 2, 1, 3)).reshape(micro, rows, heads_all)
-        mixed = mixed.astype(jnp.bfloat16)
-        residual = hidden[:, BACK * rows :] + jnp.einsum(
-            "mrc,cd->mrd", mixed, mixing, preferred_element_type=jnp.float32
-        )
-        final_normed = rms_scaled(residual, gain_second).astype(jnp.bfloat16)
-        raw = jnp.einsum("mrc,cd->mrd", final_normed, readout, preferred_element_type=jnp.float32)
-        shift_mean = raw[..., :width_in]
-        log_scale = 0.5 * jnp.tanh(raw[..., width_in:])
-        return (own - shift_mean) * jnp.exp(-log_scale)
+        return result.reshape(micro, rows, width_in)
 
     axes = ("segment", "seq")
 

time: 128 us -> 122 us (0.953)
  Pallas kernels: 0 us -> 74 us
  matrix products: 50 us -> 0 us
  local copies, waits for them, and re-layouts: 30.7 us -> 5.75 us
  other arithmetic: 9.44 us -> 6.5 us
    pallas_call x0 -> x4, Pallas kernels: none -> 74 us  [run_block(): block_call(shifted, own.reshape(micro * rows, width_in), mask, gain_a, ga...]
    dot_general x28 -> x0, matrix products: 50 us -> none  [the longest x4 14.5 us: run_block(): jnp.einsum('mrc,cd->mrd', normed, w_keyval, preferred_element_type=jnp.fl...]
    unnamed x52 -> x14, local copies, waits for them, and re-layouts: 17.9 us -> 0.03 us
    reshape x4 -> x0, local copies, waits for them, and re-layouts: 10.3 us -> none  [run_block(): values = keyval[:, :, heads_all:].reshape(micro, span, head_count, HEAD_DIM)]
    reduce_sum x4 -> x0, other arithmetic: 4.35 us -> none  [run_block(): total = jnp.sum(expo, axis=-1, keepdims=True)]
    concatenate x0 -> x4, other arithmetic: none -> 3.01 us  [run_block(): window = jnp.concatenate([row3, back2, back1, own], axis=1)]
    slice x3, local copies, waits for them, and re-layouts: 0.01 us -> 2.1 us  [next_inputs(): row3 = send(mirrored[:, rows - 1:], BACK + 1)]
    rev x3, local copies, waits for them, and re-layouts: 0.85 us -> 2.66 us  [next_inputs(): mirrored = result[:, ::-1]]
where the time goes in v2:
time: 122 us; the launch traced here: 121 us
  Pallas kernels  74 us (61%)
  waiting for transfers between devices  22.3 us (18%)
  starting transfers between devices  12.6 us (10%)
  other arithmetic  6.5 us (5%)
  local copies, waits for them, and re-layouts  5.75 us (5%)
    pallas_call x4, Pallas kernels, run_block(): block_call(shifted, own.reshape(micro * rows, width_in), mask, gain_a, ga...  74 us
    ppermute x12, waiting for transfers between devices, send(): return lax.ppermute(block, axes, pairs)  22.3 us
    ppermute x12, starting transfers between devices, send(): return lax.ppermute(block, axes, pairs)  10.6 us
    concatenate x4, other arithmetic, run_block(): window = jnp.concatenate([row3, back2, back1, own], axis=1)  3.01 us
    rev x3, local copies, waits for them, and re-layouts, next_inputs(): mirrored = result[:, ::-1]  2.66 us
  transfers between devices with their start and end apart: 15, of which 2 were waited for; matrix products, arithmetic and copies ran while one was open for 3% of the time, Pallas kernels for 0%

profile of v2, /device:TPU:15, one launch (start us, length us, event | category | flops | bytes accessed | tf_op | source)
XLA Modules:
  0.0 121.5 jit_solution(17082718112128012441)
XLA Ops:
  0.0 0.9 convert.88
  0.9 0.7 collective-permute-start.1
  1.6 0.7 collective-permute-start.2
  2.3 0.7 slice.31
  4.0 0.8 fusion.1.mask_ref
  4.8 0.8 pad_maximum_fusion.9
  5.6 18.5 %shard_map.82 = f32[256,128]{1,0:T(8,128)} custom-call(bf16[768,128]{1,0:T(8,128)(2,1)} %bitcast.27, f32[256,128]{1,0:T(8,128)} %bitcast.28, f32[128,384]{1,0:T(8,128)} %fusion.1.mask_ref, f32[1,1024]{1,0:T(1,128)} %ga_ref.7, f32[1,1024]{1,0:T(1,128)} %gb_ref.7, bf16[128,1024]{1,0:T(8,128)(2,1)} %bitcast.44, bf16[1024,3072]{1,0:T(8,128)(2,1)} %bitcast.32, ...), custom_call_target="tpu_custom_call" | custom-call | flops 5033164800 | bytes 9633792 | tf_op jit(solution)/shard_map/pallas_call | solution.py:177
  24.1 0.9 rev.9
  24.9 0.7 collective-permute-start.6
  25.6 0.7 collective-permute-start.4
  26.3 0.7 collective-permute-start.5
  27.0 0.7 slice.39
  28.4 0.8 pad_maximum_fusion.6
  29.2 18.5 %shard_map.83 = f32[256,128]{1,0:T(8,128)} custom-call(bf16[768,128]{1,0:T(8,128)(2,1)} %bitcast.25, f32[256,128]{1,0:T(8,128)} %bitcast.30, f32[128,384]{1,0:T(8,128)} %fusion.1.mask_ref, f32[1,1024]{1,0:T(1,128)} %ga_ref.7, f32[1,1024]{1,0:T(1,128)} %gb_ref.7, bf16[128,1024]{1,0:T(8,128)(2,1)} %bitcast.45, bf16[1024,3072]{1,0:T(8,128)(2,1)} %bitcast.33, ...), custom_call_target="tpu_custom_call" | custom-call | flops 5033164800 | bytes 9633792 | tf_op jit(solution)/shard_map/pallas_call | solution.py:177
  47.7 0.9 rev.10
  48.6 0.7 collective-permute-start.10
  49.2 0.7 collective-permute-start.8
  49.9 0.7 collective-permute-start.9
  50.6 0.7 slice.40
  52.0 0.8 pad_maximum_fusion.3
  52.8 18.5 %shard_map.84 = f32[256,128]{1,0:T(8,128)} custom-call(bf16[768,128]{1,0:T(8,128)(2,1)} %bitcast.26, f32[256,128]{1,0:T(8,128)} %bitcast.31, f32[128,384]{1,0:T(8,128)} %fusion.1.mask_ref, f32[1,1024]{1,0:T(1,128)} %ga_ref.7, f32[1,1024]{1,0:T(1,128)} %gb_ref.7, bf16[128,1024]{1,0:T(8,128)(2,1)} %bitcast.46, bf16[1024,3072]{1,0:T(8,128)(2,1)} %bitcast.34, ...), custom_call_target="tpu_custom_call" | custom-call | flops 5033164800 | bytes 9633792 | tf_op jit(solution)/shard_map/pallas_call | solution.py:177
  71.3 0.9 rev.11
  72.2 1.3 %collective-permute-start.14 = (f32[2,128,128]{2,1,0:T(8,128)S(1)}, f32[2,128,128]{2,1,0:T(8,128)S(1)}, u32[]{:S(2)}, u32[]{:S(2)}) collective-permute-start(f32[2,128,128]{2,1,0:T(8,128)S(1)} %rev.11), channel_id=1, source_target_pairs={{16,31},{17,30},{18,29},{19,28},{20,27},{21,26},{22,25},{23,24}} | collective-permute-start | bytes 393224 | tf_op jit(solution)/shard_map/ppermute | solution.py:209
  73.5 1.3 %collective-permute-start.12 = (bf16[2,128,128]{2,1,0:T(8,128)(2,1)S(1)}, bf16[2,128,128]{2,1,0:T(8,128)(2,1)S(1)}, u32[]{:S(2)}, u32[]{:S(2)}) collective-permute-start(bf16[2,128,128]{2,1,0:T(8,128)(2,1)S(1)} %convert.85), channel_id=1, source_target_pairs={{18,31},{19,30},{20,29},{21,28},{22,27},{23,26}} | collective-permute-start | bytes 196616 | tf_op jit(solution)/shard_map/ppermute | solution.py:209
  74.8 1.3 %collective-permute-start.13 = (bf16[2,128,128]{2,1,0:T(8,128)(2,1)S(1)}, bf16[2,128,128]{2,1,0:T(8,128)(2,1)S(1)}, u32[]{:S(2)}, u32[]{:S(2)}) collective-permute-start(bf16[2,128,128]{2,1,0:T(8,128)(2,1)S(1)} %convert.85), channel_id=1, source_target_pairs={{17,31},{18,30},{19,29},{20,28},{21,27},{22,26},{23,25}} | collective-permute-start | bytes 196616 | tf_op jit(solution)/shard_map/ppermute | solution.py:209
  76.1 0.7 slice.41
  76.8 1.5 %collective-permute-start.11 = (bf16[2,1,128]{2,1,0:T(2,128)(2,1)S(1)}, bf16[2,1,128]{2,1,0:T(2,128)(2,1)S(1)}, u32[]{:S(2)}, u32[]{:S(2)}) collective-permute-start(bf16[2,1,128]{2,1,0:T(2,128)(2,1)S(1)} %slice.41), channel_id=1, source_target_pairs={{19,31},{20,30},{21,29},{22,28},{23,27}} | collective-permute-start | bytes 1544 | tf_op jit(solution)/shard_map/ppermute | solution.py:209
  78.3 21.3 %collective-permute-done.14 = f32[2,128,128]{2,1,0:T(8,128)S(1)} collective-permute-done((f32[2,128,128]{2,1,0:T(8,128)S(1)}, f32[2,128,128]{2,1,0:T(8,128)S(1)}, u32[]{:S(2)}, u32[]{:S(2)}) %collective-permute-start.14) | collective-permute-done | bytes 131104 | tf_op jit(solution)/shard_map/ppermute | solution.py:209
  99.6 0.9 collective-permute-done.11
  100.5 0.8 pad_maximum_fusion
  101.3 18.5 %shard_map.85 = f32[256,128]{1,0:T(8,128)} custom-call(bf16[768,128]{1,0:T(8,128)(2,1)} %bitcast.24, f32[256,128]{1,0:T(8,128)} %bitcast.29, f32[128,384]{1,0:T(8,128)} %fusion.1.mask_ref, f32[1,1024]{1,0:T(1,128)} %ga_ref.7, f32[1,1024]{1,0:T(1,128)} %gb_ref.7, bf16[128,1024]{1,0:T(8,128)(2,1)} %bitcast.47, bf16[1024,3072]{1,0:T(8,128)(2,1)} %bitcast.35, ...), custom_call_target="tpu_custom_call" | custom-call | flops 5033164800 | bytes 9633792 | tf_op jit(solution)/shard_map/pallas_call | solution.py:177
  119.9 1.6 %select_select_fusion = f32[256,128]{1,0:T(8,128)} fusion(f32[256,128]{1,0:T(8,128)} %shard_map.85, f32[256,128]{1,0:T(8,128)S(1)} %copy-done.3, f32[256,128]{1,0:T(8,128)S(1)} %copy-done.2, f32[256,128]{1,0:T(8,128)S(1)} %copy-done.1, pred[]{:T(512)S(6)} %eq.34, pred[]{:T(512)S(6)} %eq.33, pred[]{:T(512)S(6)} %eq.32, pred[]{:T(512)S(6)} %eq.27), kind=kLoop, calls=%fused_computation.15 | loop fusion | flops 131072 | bytes 655364 | tf_op jit(solution)/shard_map/jit(_where)/select_n | solution.py:221
  (42 shorter events, 2.5 us)
Async XLA Ops:
  0.0 3.7 %copy-start = (s32[8,4]{0,1:T(4,128)S(1)}, s32[8,4]{0,1:T(4,128)}, u32[]{:S(2)}) copy-start(s32[8,4]{0,1:T(4,128)} %param.9) | copy-start | bytes 388
  0.9 3.9 %collective-permute-start.1 = (bf16[2,128,128]{2,1,0:T(8,128)(2,1)S(1)}, bf16[2,128,128]{2,1,0:T(8,128)(2,1)S(1)}, u32[]{:S(2)}, u32[]{:S(2)}) collective-permute-start(bf16[2,128,128]{2,1,0:T(8,128)(2,1)S(1)} %convert.88), channel_id=1, source_target_pairs={{0,2},{1,3},{2,4},{3,5},{4,6},{5,7}} | collective-permute-start | bytes 196616 | tf_op jit(solution)/shard_map/ppermute | solution.py:189
  1.6 3.2 %collective-permute-start.2 = (bf16[2,128,128]{2,1,0:T(8,128)(2,1)S(1)}, bf16[2,128,128]{2,1,0:T(8,128)(2,1)S(1)}, u32[]{:S(2)}, u32[]{:S(2)}) collective-permute-start(bf16[2,128,128]{2,1,0:T(8,128)(2,1)S(1)} %convert.88), channel_id=1, source_target_pairs={{0,1},{1,2},{2,3},{3,4},{4,5},{5,6},{6,7}} | collective-permute-start | bytes 196616 | tf_op jit(solution)/shard_map/ppermute | solution.py:189
  3.0 1.8 %collective-permute-start = (bf16[2,1,128]{2,1,0:T(2,128)(2,1)S(1)}, bf16[2,1,128]{2,1,0:T(2,128)(2,1)S(1)}, u32[]{:S(2)}, u32[]{:S(2)}) collective-permute-start(bf16[2,1,128]{2,1,0:T(2,128)(2,1)S(1)} %slice.31), channel_id=1, source_target_pairs={{0,3},{1,4},{2,5},{3,6},{4,7}} | collective-permute-start | bytes 1544 | tf_op jit(solution)/shard_map/ppermute | solution.py:189
  24.9 3.4 %collective-permute-start.6 = (f32[2,128,128]{2,1,0:T(8,128)S(1)}, f32[2,128,128]{2,1,0:T(8,128)S(1)}, u32[]{:S(2)}, u32[]{:S(2)}) collective-permute-start(f32[2,128,128]{2,1,0:T(8,128)S(1)} %rev.9), channel_id=1, source_target_pairs={{0,15},{1,14},{2,13},{3,12},{4,11},{5,10},{6,9},{7,8}} | collective-permute-start | bytes 393224 | tf_op jit(solution)/shard_map/ppermute | solution.py:209
  25.6 2.8 %collective-permute-start.4 = (bf16[2,128,128]{2,1,0:T(8,128)(2,1)S(1)}, bf16[2,128,128]{2,1,0:T(8,128)(2,1)S(1)}, u32[]{:S(2)}, u32[]{:S(2)}) collective-permute-start(bf16[2,128,128]{2,1,0:T(8,128)(2,1)S(1)} %convert.87), channel_id=1, source_target_pairs={{2,15},{3,14},{4,13},{5,12},{6,11},{7,10}} | collective-permute-start | bytes 196616 | tf_op jit(solution)/shard_map/ppermute | solution.py:209
  26.3 2.1 %collective-permute-start.5 = (bf16[2,128,128]{2,1,0:T(8,128)(2,1)S(1)}, bf16[2,128,128]{2,1,0:T(8,128)(2,1)S(1)}, u32[]{:S(2)}, u32[]{:S(2)}) collective-permute-start(bf16[2,128,128]{2,1,0:T(8,128)(2,1)S(1)} %convert.87), channel_id=1, source_target_pairs={{1,15},{2,14},{3,13},{4,12},{5,11},{6,10},{7,9}} | collective-permute-start | bytes 196616 | tf_op jit(solution)/shard_map/ppermute | solution.py:209
  27.7 0.7 collective-permute-start.3
  28.4 0.8 copy-start.5
  48.6 3.4 %collective-permute-start.10 = (f32[2,128,128]{2,1,0:T(8,128)S(1)}, f32[2,128,128]{2,1,0:T(8,128)S(1)}, u32[]{:S(2)}, u32[]{:S(2)}) collective-permute-start(f32[2,128,128]{2,1,0:T(8,128)S(1)} %rev.10), channel_id=1, source_target_pairs={{8,23},{9,22},{10,21},{11,20},{12,19},{13,18},{14,17},{15,16}} | collective-permute-start | bytes 393224 | tf_op jit(solution)/shard_map/ppermute | solution.py:209
  49.2 2.8 %collective-permute-start.8 = (bf16[2,128,128]{2,1,0:T(8,128)(2,1)S(1)}, bf16[2,128,128]{2,1,0:T(8,128)(2,1)S(1)}, u32[]{:S(2)}, u32[]{:S(2)}) collective-permute-start(bf16[2,128,128]{2,1,0:T(8,128)(2,1)S(1)} %convert.86), channel_id=1, source_target_pairs={{10,23},{11,22},{12,21},{13,20},{14,19},{15,18}} | collective-permute-start | bytes 196616 | tf_op jit(solution)/shard_map/ppermute | solution.py:209
  49.9 2.1 %collective-permute-start.9 = (bf16[2,128,128]{2,1,0:T(8,128)(2,1)S(1)}, bf16[2,128,128]{2,1,0:T(8,128)(2,1)S(1)}, u32[]{:S(2)}, u32[]{:S(2)}) collective-permute-start(bf16[2,128,128]{2,1,0:T(8,128)(2,1)S(1)} %convert.86), channel_id=1, source_target_pairs={{9,23},{10,22},{11,21},{12,20},{13,19},{14,18},{15,17}} | collective-permute-start | bytes 196616 | tf_op jit(solution)/shard_map/ppermute | solution.py:209
  51.3 0.7 collective-permute-start.7
  52.0 0.8 copy-start.6
  72.2 27.4 %collective-permute-start.14 = (f32[2,128,128]{2,1,0:T(8,128)S(1)}, f32[2,128,128]{2,1,0:T(8,128)S(1)}, u32[]{:S(2)}, u32[]{:S(2)}) collective-permute-start(f32[2,128,128]{2,1,0:T(8,128)S(1)} %rev.11), channel_id=1, source_target_pairs={{16,31},{17,30},{18,29},{19,28},{20,27},{21,26},{22,25},{23,24}} | collective-permute-start | bytes 393224 | tf_op jit(solution)/shard_map/ppermute | solution.py:209
  73.5 27.0 %collective-permute-start.12 = (bf16[2,128,128]{2,1,0:T(8,128)(2,1)S(1)}, bf16[2,128,128]{2,1,0:T(8,128)(2,1)S(1)}, u32[]{:S(2)}, u32[]{:S(2)}) collective-permute-start(bf16[2,128,128]{2,1,0:T(8,128)(2,1)S(1)} %convert.85), channel_id=1, source_target_pairs={{18,31},{19,30},{20,29},{21,28},{22,27},{23,26}} | collective-permute-start | bytes 196616 | tf_op jit(solution)/shard_map/ppermute | solution.py:209
  74.8 25.7 %collective-permute-start.13 = (bf16[2,128,128]{2,1,0:T(8,128)(2,1)S(1)}, bf16[2,128,128]{2,1,0:T(8,128)(2,1)S(1)}, u32[]{:S(2)}, u32[]{:S(2)}) collective-permute-start(bf16[2,128,128]{2,1,0:T(8,128)(2,1)S(1)} %convert.85), channel_id=1, source_target_pairs={{17,31},{18,30},{19,29},{20,28},{21,27},{22,26},{23,25}} | collective-permute-start | bytes 196616 | tf_op jit(solution)/shard_map/ppermute | solution.py:209
  76.8 23.7 %collective-permute-start.11 = (bf16[2,1,128]{2,1,0:T(2,128)(2,1)S(1)}, bf16[2,1,128]{2,1,0:T(2,128)(2,1)S(1)}, u32[]{:S(2)}, u32[]{:S(2)}) collective-permute-start(bf16[2,1,128]{2,1,0:T(2,128)(2,1)S(1)} %slice.41), channel_id=1, source_target_pairs={{19,31},{20,30},{21,29},{22,28},{23,27}} | collective-permute-start | bytes 1544 | tf_op jit(solution)/shard_map/ppermute | solution.py:209
  99.6 1.7 %copy-start.4 = (f32[2,128,128]{2,1,0:T(8,128)}, f32[2,128,128]{2,1,0:T(8,128)S(1)}, u32[]{:S(2)}) copy-start(f32[2,128,128]{2,1,0:T(8,128)S(1)} %collective-permute-done.14) | copy-start | bytes 393220
  101.3 18.6 %copy-start.1 = (f32[256,128]{1,0:T(8,128)S(1)}, f32[256,128]{1,0:T(8,128)}, u32[]{:S(2)}) copy-start(f32[256,128]{1,0:T(8,128)} %shard_map.82) | copy-start | bytes 393220
  101.3 18.6 %copy-start.2 = (f32[256,128]{1,0:T(8,128)S(1)}, f32[256,128]{1,0:T(8,128)}, u32[]{:S(2)}) copy-start(f32[256,128]{1,0:T(8,128)} %shard_map.83) | copy-start | bytes 393220
  101.3 18.6 %copy-start.3 = (f32[256,128]{1,0:T(8,128)S(1)}, f32[256,128]{1,0:T(8,128)}, u32[]{:S(2)}) copy-start(f32[256,128]{1,0:T(8,128)} %shard_map.84) | copy-start | bytes 393220

commit v3 on v2

--- a/solution.py
+++ b/solution.py
@@ -9,7 +9,7 @@
 TILE = 128
 BACK = 2
 
-CHUNK = 256
+CHUNK = 512
 
 
 def make_block_call(micro, rows, width_in, heads_all):
@@ -24,30 +24,38 @@
                out_ref,
                embed_v, attn_v, mix_v, read_v, sems,
                hidden_s, normed_s, q_s, kv_s, mixed_s, res_s):
+        n_kv = 2 * heads_all // CHUNK
+        kv_copies = [
+            pltpu.make_async_copy(
+                attn_hbm.at[:, heads_all + j * CHUNK:heads_all + (j + 1) * CHUNK],
+                attn_v.at[:, heads_all + j * CHUNK:heads_all + (j + 1) * CHUNK],
+                sems.at[4 + j],
+            )
+            for j in range(n_kv)
+        ]
         copies = [
             pltpu.make_async_copy(embed_hbm, embed_v, sems.at[0]),
-            pltpu.make_async_copy(attn_hbm, attn_v, sems.at[1]),
+            pltpu.make_async_copy(attn_hbm.at[:, :heads_all], attn_v.at[:, :heads_all], sems.at[1]),
             pltpu.make_async_copy(mix_hbm, mix_v, sems.at[2]),
             pltpu.make_async_copy(read_hbm, read_v, sems.at[3]),
         ]
-        for copy in copies:
+        copies[0].start()
+        for copy in kv_copies:
+            copy.start()
+        for copy in copies[1:]:
             copy.start()
         copies[0].wait()
         hidden = jnp.dot(shifted_ref[...], embed_v[...], preferred_element_type=jnp.float32)
         hidden_s[...] = hidden
         square = jnp.mean(hidden * hidden, axis=-1, keepdims=True)
         normed_s[...] = (hidden * lax.rsqrt(square + 1e-06) * ga_ref[...]).astype(jnp.bfloat16)
+        for j in range(n_kv):
+            kv_copies[j].wait()
+            kv_s[:, j * CHUNK:(j + 1) * CHUNK] = jnp.dot(
+                normed_s[...], attn_v[:, heads_all + j * CHUNK:heads_all + (j + 1) * CHUNK],
+                preferred_element_type=jnp.float32,
+            ).astype(jnp.bfloat16)
         copies[1].wait()
-
-        def kv_step(j, carry):
-            cols = pl.ds(pl.multiple_of(j * CHUNK, CHUNK), CHUNK)
-            wcols = pl.ds(pl.multiple_of(heads_all + j * CHUNK, CHUNK), CHUNK)
-            kv_s[:, cols] = jnp.dot(
-                normed_s[...], attn_v[:, wcols], preferred_element_type=jnp.float32
-            ).astype(jnp.bfloat16)
-            return carry
-
-        lax.fori_loop(0, 2 * heads_all // CHUNK, kv_step, 0)
 
         def q_step(j, carry):
             cols = pl.ds(pl.multiple_of(j * CHUNK, CHUNK), CHUNK)
@@ -61,26 +69,22 @@
         lax.fori_loop(0, heads_all // CHUNK, q_step, 0)
 
         for m in range(micro):
-            def head_step(h, carry):
-                qcols = pl.ds(pl.multiple_of(h * HEAD_DIM, HEAD_DIM), HEAD_DIM)
-                vcols = pl.ds(pl.multiple_of(heads_all + h * HEAD_DIM, HEAD_DIM), HEAD_DIM)
-                qh = q_s[m * rows:(m + 1) * rows, qcols]
-                kh = kv_s[m * span:(m + 1) * span, qcols]
-                vh = kv_s[m * span:(m + 1) * span, vcols]
-                scores = lax.dot_general(
-                    qh, kh, (((1,), (1,)), ((), ())), preferred_element_type=jnp.float32
-                ) * scale
-                scores = jnp.where(mask_ref[...] > 0.5, scores, -jnp.inf)
-                top = jnp.max(scores, axis=-1, keepdims=True)
-                expo = jnp.exp(scores - top)
-                total = jnp.sum(expo, axis=-1, keepdims=True)
-                mixed = jnp.dot(
-                    expo.astype(jnp.bfloat16), vh, preferred_element_type=jnp.float32
-                ) / total
-                mixed_s[m * rows:(m + 1) * rows, qcols] = mixed.astype(jnp.bfloat16)
-                return carry
-
-            lax.fori_loop(0, heads, head_step, 0)
+            q3 = jnp.stack([q_s[m * rows:(m + 1) * rows, h * HEAD_DIM:(h + 1) * HEAD_DIM] for h in range(heads)])
+            k3 = jnp.stack([kv_s[m * span:(m + 1) * span, h * HEAD_DIM:(h + 1) * HEAD_DIM] for h in range(heads)])
+            v3 = jnp.stack([
+                kv_s[m * span:(m + 1) * span, heads_all + h * HEAD_DIM:heads_all + (h + 1) * HEAD_DIM]
+                for h in range(heads)
+            ])
+            scores = jnp.einsum("hqd,hkd->hqk", q3, k3, preferred_element_type=jnp.float32) * scale
+            scores = jnp.where(mask_ref[...][None] > 0.5, scores, -jnp.inf)
+            top = jnp.max(scores, axis=-1, keepdims=True)
+            expo = jnp.exp(scores - top)
+            total = jnp.sum(expo, axis=-1, keepdims=True)
+            mixed = jnp.einsum(
+                "hqk,hkd->hqd", expo.astype(jnp.bfloat16), v3, preferred_element_type=jnp.float32
+            ) / total
+            for h in range(heads):
+                mixed_s[m * rows:(m + 1) * rows, h * HEAD_DIM:(h + 1) * HEAD_DIM] = mixed[h].astype(jnp.bfloat16)
 
         copies[2].wait()
         for m in range(micro):
@@ -111,7 +115,7 @@
             vmem((width, 3 * heads_all), jnp.bfloat16),
             vmem((heads_all, width), jnp.bfloat16),
             vmem((width, 2 * width_in), jnp.bfloat16),
-            pltpu.SemaphoreType.DMA((4,)),
+            pltpu.SemaphoreType.DMA((4 + 2 * heads_all // CHUNK,)),
             vmem((n_rows, width), jnp.float32),
             vmem((n_rows, width), jnp.bfloat16),
             vmem((micro * rows, heads_all), jnp.bfloat16),

time: 122 us -> 93.7 us (0.77)
  Pallas kernels: 74 us -> 45.5 us
    pallas_call x4, Pallas kernels: 74 us -> 45.5 us  [run_block(): block_call(shifted, own.reshape(micro * rows, width_in), mask, gain_a, ga...]
  transfers between devices with their start and end apart: 15 -> 15, of which waited for: 2 -> 2; matrix products, arithmetic and copies ran while one was open for 3% -> 4% of each run, Pallas kernels for 0% -> 0%
where the time goes in v3:
time: 93.7 us; the launch traced here: 93 us
  Pallas kernels  45.5 us (49%)
  waiting for transfers between devices  21.8 us (23%)
  starting transfers between devices  13.1 us (14%)
  other arithmetic  6.5 us (7%)
  local copies, waits for them, and re-layouts  5.75 us (6%)
    pallas_call x4, Pallas kernels, run_block(): block_call(shifted, own.reshape(micro * rows, width_in), mask, gain_a, ga...  45.5 us
    ppermute x12, waiting for transfers between devices, send(): return lax.ppermute(block, axes, pairs)  21.8 us
    ppermute x12, starting transfers between devices, send(): return lax.ppermute(block, axes, pairs)  11.1 us
    concatenate x4, other arithmetic, run_block(): window = jnp.concatenate([row3, back2, back1, own], axis=1)  3.01 us
    rev x3, local copies, waits for them, and re-layouts, next_inputs(): mirrored = result[:, ::-1]  2.66 us
    slice x3, local copies, waits for them, and re-layouts, next_inputs(): row3 = send(mirrored[:, rows - 1:], BACK + 1)  2.1 us
    ppermute x3, starting transfers between devices, behind(): lax.ppermute(block, axes, [(0 * n_seq + s, 0 * n_seq + t) for s, t in pai...  1.98 us
  transfers between devices with their start and end apart: 15, of which 2 were waited for; matrix products, arithmetic and copies ran while one was open for 4% of the time, Pallas kernels for 0%

profile of v3, /device:TPU:15, one launch (start us, length us, event | category | flops | bytes accessed | tf_op | source)
XLA Modules:
  0.0 93.0 jit_solution(3240794069403857870)
XLA Ops:
  0.0 0.9 convert.88
  0.9 0.7 collective-permute-start.1
  1.6 0.7 collective-permute-start.2
  2.3 0.7 slice.31
  4.0 0.8 fusion.1.mask_ref
  4.8 0.8 pad_maximum_fusion.9
  5.6 11.4 %shard_map.82 = f32[256,128]{1,0:T(8,128)} custom-call(bf16[768,128]{1,0:T(8,128)(2,1)} %bitcast.27, f32[256,128]{1,0:T(8,128)} %bitcast.28, f32[128,384]{1,0:T(8,128)} %fusion.1.mask_ref, f32[1,1024]{1,0:T(1,128)} %ga_ref.7, f32[1,1024]{1,0:T(1,128)} %gb_ref.7, bf16[128,1024]{1,0:T(8,128)(2,1)} %bitcast.44, bf16[1024,3072]{1,0:T(8,128)(2,1)} %bitcast.32, ...), custom_call_target="tpu_custom_call" | custom-call | flops 5033164800 | bytes 9633792 | tf_op jit(solution)/shard_map/pallas_call | solution.py:181
  16.9 0.9 rev.9
  18.5 0.7 collective-permute-start.4
  19.2 0.7 collective-permute-start.5
  19.9 0.7 slice.39
  20.6 0.8 collective-permute-start.3
  21.5 0.8 pad_maximum_fusion.6
  22.2 11.4 %shard_map.83 = f32[256,128]{1,0:T(8,128)} custom-call(bf16[768,128]{1,0:T(8,128)(2,1)} %bitcast.25, f32[256,128]{1,0:T(8,128)} %bitcast.30, f32[128,384]{1,0:T(8,128)} %fusion.1.mask_ref, f32[1,1024]{1,0:T(1,128)} %ga_ref.7, f32[1,1024]{1,0:T(1,128)} %gb_ref.7, bf16[128,1024]{1,0:T(8,128)(2,1)} %bitcast.45, bf16[1024,3072]{1,0:T(8,128)(2,1)} %bitcast.33, ...), custom_call_target="tpu_custom_call" | custom-call | flops 5033164800 | bytes 9633792 | tf_op jit(solution)/shard_map/pallas_call | solution.py:181
  33.6 0.9 rev.10
  35.2 0.7 collective-permute-start.8
  35.9 0.7 collective-permute-start.9
  36.5 0.7 slice.40
  37.2 0.9 collective-permute-start.7
  38.2 0.8 pad_maximum_fusion.3
  38.9 11.4 %shard_map.84 = f32[256,128]{1,0:T(8,128)} custom-call(bf16[768,128]{1,0:T(8,128)(2,1)} %bitcast.26, f32[256,128]{1,0:T(8,128)} %bitcast.31, f32[128,384]{1,0:T(8,128)} %fusion.1.mask_ref, f32[1,1024]{1,0:T(1,128)} %ga_ref.7, f32[1,1024]{1,0:T(1,128)} %gb_ref.7, bf16[128,1024]{1,0:T(8,128)(2,1)} %bitcast.46, bf16[1024,3072]{1,0:T(8,128)(2,1)} %bitcast.34, ...), custom_call_target="tpu_custom_call" | custom-call | flops 5033164800 | bytes 9633792 | tf_op jit(solution)/shard_map/pallas_call | solution.py:181
  50.3 0.9 rev.11
  51.2 1.3 %collective-permute-start.14 = (f32[2,128,128]{2,1,0:T(8,128)S(1)}, f32[2,128,128]{2,1,0:T(8,128)S(1)}, u32[]{:S(2)}, u32[]{:S(2)}) collective-permute-start(f32[2,128,128]{2,1,0:T(8,128)S(1)} %rev.11), channel_id=1, source_target_pairs={{16,31},{17,30},{18,29},{19,28},{20,27},{21,26},{22,25},{23,24}} | collective-permute-start | bytes 393224 | tf_op jit(solution)/shard_map/ppermute | solution.py:213
  52.5 1.3 %collective-permute-start.12 = (bf16[2,128,128]{2,1,0:T(8,128)(2,1)S(1)}, bf16[2,128,128]{2,1,0:T(8,128)(2,1)S(1)}, u32[]{:S(2)}, u32[]{:S(2)}) collective-permute-start(bf16[2,128,128]{2,1,0:T(8,128)(2,1)S(1)} %convert.85), channel_id=1, source_target_pairs={{18,31},{19,30},{20,29},{21,28},{22,27},{23,26}} | collective-permute-start | bytes 196616 | tf_op jit(solution)/shard_map/ppermute | solution.py:213
  53.8 1.3 %collective-permute-start.13 = (bf16[2,128,128]{2,1,0:T(8,128)(2,1)S(1)}, bf16[2,128,128]{2,1,0:T(8,128)(2,1)S(1)}, u32[]{:S(2)}, u32[]{:S(2)}) collective-permute-start(bf16[2,128,128]{2,1,0:T(8,128)(2,1)S(1)} %convert.85), channel_id=1, source_target_pairs={{17,31},{18,30},{19,29},{20,28},{21,27},{22,26},{23,25}} | collective-permute-start | bytes 196616 | tf_op jit(solution)/shard_map/ppermute | solution.py:213
  55.1 0.7 slice.41
  55.8 1.5 %collective-permute-start.11 = (bf16[2,1,128]{2,1,0:T(2,128)(2,1)S(1)}, bf16[2,1,128]{2,1,0:T(2,128)(2,1)S(1)}, u32[]{:S(2)}, u32[]{:S(2)}) collective-permute-start(bf16[2,1,128]{2,1,0:T(2,128)(2,1)S(1)} %slice.41), channel_id=1, source_target_pairs={{19,31},{20,30},{21,29},{22,28},{23,27}} | collective-permute-start | bytes 1544 | tf_op jit(solution)/shard_map/ppermute | solution.py:213
  57.4 20.8 %collective-permute-done.14 = f32[2,128,128]{2,1,0:T(8,128)S(1)} collective-permute-done((f32[2,128,128]{2,1,0:T(8,128)S(1)}, f32[2,128,128]{2,1,0:T(8,128)S(1)}, u32[]{:S(2)}, u32[]{:S(2)}) %collective-permute-start.14) | collective-permute-done | bytes 131104 | tf_op jit(solution)/shard_map/ppermute | solution.py:213
  78.2 0.9 %collective-permute-done.11 = bf16[2,1,128]{2,1,0:T(2,128)(2,1)S(1)} collective-permute-done((bf16[2,1,128]{2,1,0:T(2,128)(2,1)S(1)}, bf16[2,1,128]{2,1,0:T(2,128)(2,1)S(1)}, u32[]{:S(2)}, u32[]{:S(2)}) %collective-permute-start.11) | collective-permute-done | bytes 544 | tf_op jit(solution)/shard_map/ppermute | solution.py:213
  79.1 0.8 pad_maximum_fusion
  79.9 11.4 %shard_map.85 = f32[256,128]{1,0:T(8,128)} custom-call(bf16[768,128]{1,0:T(8,128)(2,1)} %bitcast.24, f32[256,128]{1,0:T(8,128)} %bitcast.29, f32[128,384]{1,0:T(8,128)} %fusion.1.mask_ref, f32[1,1024]{1,0:T(1,128)} %ga_ref.7, f32[1,1024]{1,0:T(1,128)} %gb_ref.7, bf16[128,1024]{1,0:T(8,128)(2,1)} %bitcast.47, bf16[1024,3072]{1,0:T(8,128)(2,1)} %bitcast.35, ...), custom_call_target="tpu_custom_call" | custom-call | flops 5033164800 | bytes 9633792 | tf_op jit(solution)/shard_map/pallas_call | solution.py:181
  91.4 1.6 %select_select_fusion = f32[256,128]{1,0:T(8,128)} fusion(f32[256,128]{1,0:T(8,128)} %shard_map.85, f32[256,128]{1,0:T(8,128)S(1)} %copy-done.3, f32[256,128]{1,0:T(8,128)S(1)} %copy-done.2, f32[256,128]{1,0:T(8,128)S(1)} %copy-done.1, pred[]{:T(512)S(6)} %eq.34, pred[]{:T(512)S(6)} %eq.33, pred[]{:T(512)S(6)} %eq.32, pred[]{:T(512)S(6)} %eq.27), kind=kLoop, calls=%fused_computation.15 | loop fusion | flops 131072 | bytes 655364 | tf_op jit(solution)/shard_map/jit(_where)/select_n | solution.py:225
  (42 shorter events, 2.5 us)
Async XLA Ops:
  0.0 3.7 %copy-start = (s32[8,4]{0,1:T(4,128)S(1)}, s32[8,4]{0,1:T(4,128)}, u32[]{:S(2)}) copy-start(s32[8,4]{0,1:T(4,128)} %param.9) | copy-start | bytes 388
  0.9 3.9 %collective-permute-start.1 = (bf16[2,128,128]{2,1,0:T(8,128)(2,1)S(1)}, bf16[2,128,128]{2,1,0:T(8,128)(2,1)S(1)}, u32[]{:S(2)}, u32[]{:S(2)}) collective-permute-start(bf16[2,128,128]{2,1,0:T(8,128)(2,1)S(1)} %convert.88), channel_id=1, source_target_pairs={{0,2},{1,3},{2,4},{3,5},{4,6},{5,7}} | collective-permute-start | bytes 196616 | tf_op jit(solution)/shard_map/ppermute | solution.py:193
  1.6 3.2 %collective-permute-start.2 = (bf16[2,128,128]{2,1,0:T(8,128)(2,1)S(1)}, bf16[2,128,128]{2,1,0:T(8,128)(2,1)S(1)}, u32[]{:S(2)}, u32[]{:S(2)}) collective-permute-start(bf16[2,128,128]{2,1,0:T(8,128)(2,1)S(1)} %convert.88), channel_id=1, source_target_pairs={{0,1},{1,2},{2,3},{3,4},{4,5},{5,6},{6,7}} | collective-permute-start | bytes 196616 | tf_op jit(solution)/shard_map/ppermute | solution.py:193
  3.0 1.8 %collective-permute-start = (bf16[2,1,128]{2,1,0:T(2,128)(2,1)S(1)}, bf16[2,1,128]{2,1,0:T(2,128)(2,1)S(1)}, u32[]{:S(2)}, u32[]{:S(2)}) collective-permute-start(bf16[2,1,128]{2,1,0:T(2,128)(2,1)S(1)} %slice.31), channel_id=1, source_target_pairs={{0,3},{1,4},{2,5},{3,6},{4,7}} | collective-permute-start | bytes 1544 | tf_op jit(solution)/shard_map/ppermute | solution.py:193
  17.8 3.6 %collective-permute-start.6 = (f32[2,128,128]{2,1,0:T(8,128)S(1)}, f32[2,128,128]{2,1,0:T(8,128)S(1)}, u32[]{:S(2)}, u32[]{:S(2)}) collective-permute-start(f32[2,128,128]{2,1,0:T(8,128)S(1)} %rev.9), channel_id=1, source_target_pairs={{0,15},{1,14},{2,13},{3,12},{4,11},{5,10},{6,9},{7,8}} | collective-permute-start | bytes 393224 | tf_op jit(solution)/shard_map/ppermute | solution.py:213
  18.5 2.9 %collective-permute-start.4 = (bf16[2,128,128]{2,1,0:T(8,128)(2,1)S(1)}, bf16[2,128,128]{2,1,0:T(8,128)(2,1)S(1)}, u32[]{:S(2)}, u32[]{:S(2)}) collective-permute-start(bf16[2,128,128]{2,1,0:T(8,128)(2,1)S(1)} %convert.87), channel_id=1, source_target_pairs={{2,15},{3,14},{4,13},{5,12},{6,11},{7,10}} | collective-permute-start | bytes 196616 | tf_op jit(solution)/shard_map/ppermute | solution.py:213
  19.2 2.3 %collective-permute-start.5 = (bf16[2,128,128]{2,1,0:T(8,128)(2,1)S(1)}, bf16[2,128,128]{2,1,0:T(8,128)(2,1)S(1)}, u32[]{:S(2)}, u32[]{:S(2)}) collective-permute-start(bf16[2,128,128]{2,1,0:T(8,128)(2,1)S(1)} %convert.87), channel_id=1, source_target_pairs={{1,15},{2,14},{3,13},{4,12},{5,11},{6,10},{7,9}} | collective-permute-start | bytes 196616 | tf_op jit(solution)/shard_map/ppermute | solution.py:213
  20.6 0.9 collective-permute-start.3
  21.4 0.8 copy-start.5
  34.5 3.6 %collective-permute-start.10 = (f32[2,128,128]{2,1,0:T(8,128)S(1)}, f32[2,128,128]{2,1,0:T(8,128)S(1)}, u32[]{:S(2)}, u32[]{:S(2)}) collective-permute-start(f32[2,128,128]{2,1,0:T(8,128)S(1)} %rev.10), channel_id=1, source_target_pairs={{8,23},{9,22},{10,21},{11,20},{12,19},{13,18},{14,17},{15,16}} | collective-permute-start | bytes 393224 | tf_op jit(solution)/shard_map/ppermute | solution.py:213
  35.2 3.0 %collective-permute-start.8 = (bf16[2,128,128]{2,1,0:T(8,128)(2,1)S(1)}, bf16[2,128,128]{2,1,0:T(8,128)(2,1)S(1)}, u32[]{:S(2)}, u32[]{:S(2)}) collective-permute-start(bf16[2,128,128]{2,1,0:T(8,128)(2,1)S(1)} %convert.86), channel_id=1, source_target_pairs={{10,23},{11,22},{12,21},{13,20},{14,19},{15,18}} | collective-permute-start | bytes 196616 | tf_op jit(solution)/shard_map/ppermute | solution.py:213
  35.9 2.3 %collective-permute-start.9 = (bf16[2,128,128]{2,1,0:T(8,128)(2,1)S(1)}, bf16[2,128,128]{2,1,0:T(8,128)(2,1)S(1)}, u32[]{:S(2)}, u32[]{:S(2)}) collective-permute-start(bf16[2,128,128]{2,1,0:T(8,128)(2,1)S(1)} %convert.86), channel_id=1, source_target_pairs={{9,23},{10,22},{11,21},{12,20},{13,19},{14,18},{15,17}} | collective-permute-start | bytes 196616 | tf_op jit(solution)/shard_map/ppermute | solution.py:213
  37.2 0.9 collective-permute-start.7
  38.1 0.8 copy-start.6
  51.2 27.0 %collective-permute-start.14 = (f32[2,128,128]{2,1,0:T(8,128)S(1)}, f32[2,128,128]{2,1,0:T(8,128)S(1)}, u32[]{:S(2)}, u32[]{:S(2)}) collective-permute-start(f32[2,128,128]{2,1,0:T(8,128)S(1)} %rev.11), channel_id=1, source_target_pairs={{16,31},{17,30},{18,29},{19,28},{20,27},{21,26},{22,25},{23,24}} | collective-permute-start | bytes 393224 | tf_op jit(solution)/shard_map/ppermute | solution.py:213
  52.5 26.6 %collective-permute-start.12 = (bf16[2,128,128]{2,1,0:T(8,128)(2,1)S(1)}, bf16[2,128,128]{2,1,0:T(8,128)(2,1)S(1)}, u32[]{:S(2)}, u32[]{:S(2)}) collective-permute-start(bf16[2,128,128]{2,1,0:T(8,128)(2,1)S(1)} %convert.85), channel_id=1, source_target_pairs={{18,31},{19,30},{20,29},{21,28},{22,27},{23,26}} | collective-permute-start | bytes 196616 | tf_op jit(solution)/shard_map/ppermute | solution.py:213
  53.8 25.3 %collective-permute-start.13 = (bf16[2,128,128]{2,1,0:T(8,128)(2,1)S(1)}, bf16[2,128,128]{2,1,0:T(8,128)(2,1)S(1)}, u32[]{:S(2)}, u32[]{:S(2)}) collective-permute-start(bf16[2,128,128]{2,1,0:T(8,128)(2,1)S(1)} %convert.85), channel_id=1, source_target_pairs={{17,31},{18,30},{19,29},{20,28},{21,27},{22,26},{23,25}} | collective-permute-start | bytes 196616 | tf_op jit(solution)/shard_map/ppermute | solution.py:213
  55.8 23.3 %collective-permute-start.11 = (bf16[2,1,128]{2,1,0:T(2,128)(2,1)S(1)}, bf16[2,1,128]{2,1,0:T(2,128)(2,1)S(1)}, u32[]{:S(2)}, u32[]{:S(2)}) collective-permute-start(bf16[2,1,128]{2,1,0:T(2,128)(2,1)S(1)} %slice.41), channel_id=1, source_target_pairs={{19,31},{20,30},{21,29},{22,28},{23,27}} | collective-permute-start | bytes 1544 | tf_op jit(solution)/shard_map/ppermute | solution.py:213
  78.2 1.7 %copy-start.4 = (f32[2,128,128]{2,1,0:T(8,128)}, f32[2,128,128]{2,1,0:T(8,128)S(1)}, u32[]{:S(2)}) copy-start(f32[2,128,128]{2,1,0:T(8,128)S(1)} %collective-permute-done.14) | copy-start | bytes 393220
  79.9 11.4 %copy-start.1 = (f32[256,128]{1,0:T(8,128)S(1)}, f32[256,128]{1,0:T(8,128)}, u32[]{:S(2)}) copy-start(f32[256,128]{1,0:T(8,128)} %shard_map.82) | copy-start | bytes 393220
  79.9 11.5 %copy-start.2 = (f32[256,128]{1,0:T(8,128)S(1)}, f32[256,128]{1,0:T(8,128)}, u32[]{:S(2)}) copy-start(f32[256,128]{1,0:T(8,128)} %shard_map.83) | copy-start | bytes 393220
  79.9 11.5 %copy-start.3 = (f32[256,128]{1,0:T(8,128)S(1)}, f32[256,128]{1,0:T(8,128)}, u32[]{:S(2)}) copy-start(f32[256,128]{1,0:T(8,128)} %shard_map.84) | copy-start | bytes 393220

commit v4 on v3

--- a/solution.py
+++ b/solution.py
@@ -12,18 +12,19 @@
 CHUNK = 512
 
 
-def make_block_call(micro, rows, width_in, heads_all):
+def make_block_call(micro, rows, width_in, heads_all, mirrored, piece_dtype):
     span = (BACK + 1) * rows
     own_at = BACK * rows
     n_rows = micro * span
+    n_in = (BACK + 2) * rows
     scale = HEAD_DIM ** (-0.5)
     heads = heads_all // HEAD_DIM
 
-    def kernel(shifted_ref, own_ref, mask_ref, ga_ref, gb_ref,
+    def kernel(own_ref, back1_ref, back2_ref, edge_ref, mask_ref, ga_ref, gb_ref,
                embed_hbm, attn_hbm, mix_hbm, read_hbm,
-               out_ref,
+               out_ref, outb_ref,
                embed_v, attn_v, mix_v, read_v, sems,
-               hidden_s, normed_s, q_s, kv_s, mixed_s, res_s):
+               pieces_s, shifted_s, hidden_s, normed_s, q_s, kv_s, mixed_s, res_s):
         n_kv = 2 * heads_all // CHUNK
         kv_copies = [
             pltpu.make_async_copy(
@@ -44,8 +45,23 @@
             copy.start()
         for copy in copies[1:]:
             copy.start()
+        before = lax.broadcasted_iota(jnp.int32, (span, n_in), 0) + (rows - 1)
+        column = lax.broadcasted_iota(jnp.int32, (span, n_in), 1)
+        if mirrored:
+            source = ((before >> 7) << 7) + (rows - 1) - (before & (rows - 1))
+        else:
+            source = before
+        select = (column == source).astype(jnp.bfloat16)
+        for m in range(micro):
+            pieces_s[0:rows, :] = edge_ref[m].astype(jnp.bfloat16)
+            pieces_s[rows:2 * rows, :] = back2_ref[m].astype(jnp.bfloat16)
+            pieces_s[2 * rows:3 * rows, :] = back1_ref[m].astype(jnp.bfloat16)
+            pieces_s[3 * rows:4 * rows, :] = own_ref[m].astype(jnp.bfloat16)
+            shifted_s[m * span:(m + 1) * span, :] = jnp.dot(
+                select, pieces_s[...], preferred_element_type=jnp.float32
+            ).astype(jnp.bfloat16)
         copies[0].wait()
-        hidden = jnp.dot(shifted_ref[...], embed_v[...], preferred_element_type=jnp.float32)
+        hidden = jnp.dot(shifted_s[...], embed_v[...], preferred_element_type=jnp.float32)
         hidden_s[...] = hidden
         square = jnp.mean(hidden * hidden, axis=-1, keepdims=True)
         normed_s[...] = (hidden * lax.rsqrt(square + 1e-06) * ga_ref[...]).astype(jnp.bfloat16)
@@ -98,7 +114,23 @@
         raw = jnp.dot(final_normed, read_v[...], preferred_element_type=jnp.float32)
         shift_mean = raw[:, :width_in]
         log_scale = 0.5 * jnp.tanh(raw[:, width_in:])
-        out_ref[...] = (own_ref[...] - shift_mean) * jnp.exp(-log_scale)
+        if mirrored:
+            i = lax.broadcasted_iota(jnp.int32, (rows, rows), 0)
+            c = lax.broadcasted_iota(jnp.int32, (rows, rows), 1)
+            flip = (c == (rows - 1) - i).astype(jnp.bfloat16)
+        for m in range(micro):
+            own = own_ref[m]
+            if mirrored:
+                high = own.astype(jnp.bfloat16)
+                rest = own - high.astype(jnp.float32)
+                middle = rest.astype(jnp.bfloat16)
+                low = (rest - middle.astype(jnp.float32)).astype(jnp.bfloat16)
+                parts = [jnp.dot(flip, part, preferred_element_type=jnp.float32) for part in (high, middle, low)]
+                own = (parts[0] + parts[1]) + parts[2]
+            rows_m = slice(m * rows, (m + 1) * rows)
+            result = (own - shift_mean[rows_m]) * jnp.exp(-log_scale[rows_m])
+            out_ref[m] = result
+            outb_ref[m] = result.astype(jnp.bfloat16)
 
     width = heads_all
     flops = 2 * n_rows * (width_in * width + width * 2 * heads_all)
@@ -107,15 +139,20 @@
     vmem = pltpu.VMEM
     call = pl.pallas_call(
         kernel,
-        out_shape=jax.ShapeDtypeStruct((micro * rows, width_in), jnp.float32),
-        in_specs=[pl.BlockSpec(memory_space=vmem)] * 5 + [pl.BlockSpec(memory_space=pl.ANY)] * 4,
-        out_specs=pl.BlockSpec(memory_space=vmem),
+        out_shape=(
+            jax.ShapeDtypeStruct((micro, rows, width_in), jnp.float32),
+            jax.ShapeDtypeStruct((micro, rows, width_in), jnp.bfloat16),
+        ),
+        in_specs=[pl.BlockSpec(memory_space=vmem)] * 7 + [pl.BlockSpec(memory_space=pl.ANY)] * 4,
+        out_specs=(pl.BlockSpec(memory_space=vmem), pl.BlockSpec(memory_space=vmem)),
         scratch_shapes=[
             vmem((width_in, width), jnp.bfloat16),
             vmem((width, 3 * heads_all), jnp.bfloat16),
             vmem((heads_all, width), jnp.bfloat16),
             vmem((width, 2 * width_in), jnp.bfloat16),
             pltpu.SemaphoreType.DMA((4 + 2 * heads_all // CHUNK,)),
+            vmem((n_in, width_in), jnp.bfloat16),
+            vmem((n_rows, width_in), jnp.bfloat16),
             vmem((n_rows, width), jnp.float32),
             vmem((n_rows, width), jnp.bfloat16),
             vmem((micro * rows, heads_all), jnp.bfloat16),
@@ -166,41 +203,28 @@
     key_pos = jnp.arange(span, dtype=jnp.int32)
     allowed = listed[None, :] & (key_pos[None, :] <= query_pos[:, None])
 
-    block_call = make_block_call(micro, rows, width_in, heads_all)
+    first_call = make_block_call(micro, rows, width_in, heads_all, False, jnp.float32)
+    later_call = make_block_call(micro, rows, width_in, heads_all, True, jnp.bfloat16)
     mask = allowed.astype(jnp.float32)
-    embed_w = input_weight[0]
-    attn_w = attention_weight[0]
-    mix_w = mixing_weight[0]
-    read_w = output_weight[0]
-    gain_a = norm_gain[0].reshape(1, -1)
-    gain_b = final_gain[0].reshape(1, -1)
-
-    def run_block(own, back1, back2, row3):
-        window = jnp.concatenate([row3, back2, back1, own], axis=1)
-        shifted = window[:, :-1].astype(jnp.bfloat16).reshape(micro * span, width_in)
-        result = block_call(
-            shifted, own.reshape(micro * rows, width_in), mask, gain_a, gain_b,
-            embed_w, attn_w, mix_w, read_w,
-        )
-        return result.reshape(micro, rows, width_in)
+    weights = (
+        norm_gain[0].reshape(1, -1),
+        final_gain[0].reshape(1, -1),
+        input_weight[0],
+        attention_weight[0],
+        mixing_weight[0],
+        output_weight[0],
+    )
 
     axes = ("segment", "seq")
 
     def first_inputs():
-        def behind(block, distance):
+        def behind(distance):
             pairs = [(q, q + distance) for q in range(n_seq) if q + distance < n_seq]
-            pairs = [(s, t) for s, t in pairs]
-            return lax.ppermute(
-                block, axes, [(0 * n_seq + s, 0 * n_seq + t) for s, t in pairs]
-            )
-
-        back1 = behind(patches, 1)
-        back2 = behind(patches, 2)
-        row3 = behind(patches[:, rows - 1 :], BACK + 1)
-        return patches, back1, back2, row3
-
-    def next_inputs(result, turn):
-        mirrored = result[:, ::-1]
+            return lax.ppermute(patches, axes, pairs)
+
+        return patches, behind(1), behind(2), behind(BACK + 1)
+
+    def next_inputs(result, result_low, turn):
         src = turn * n_seq
         dst = (turn + 1) * n_seq
 
@@ -212,19 +236,21 @@
                     pairs.append((src + q, dst + target))
             return lax.ppermute(block, axes, pairs)
 
-        own = send(mirrored, 0)
-        back1 = send(mirrored, 1)
-        back2 = send(mirrored, 2)
-        row3 = send(mirrored[:, rows - 1 :], BACK + 1)
-        return own, back1, back2, row3
+        return (
+            send(result, 0),
+            send(result_low, 1),
+            send(result_low, 2),
+            send(result_low, BACK + 1),
+        )
 
     inputs = first_inputs()
     out = jnp.zeros((micro, rows, width_in), jnp.float32)
     for turn in range(n_seg):
-        result = run_block(*inputs)
+        call = first_call if turn == 0 else later_call
+        result, result_low = call(*inputs, mask, *weights)
         out = jnp.where(segment == turn, result, out)
         if turn + 1 < n_seg:
-            inputs = next_inputs(result, turn)
+            inputs = next_inputs(result, result_low, turn)
     return out[None]
 
 

time: 93.7 us -> 93.7 us (level)
  other arithmetic: 6.5 us -> 2.48 us
  waiting for transfers between devices: 21.8 us -> 25.8 us
    unnamed x14 -> x38, local copies, waits for them, and re-layouts: 0.03 us -> 4.58 us
    ppermute x12, waiting for transfers between devices: 21.8 us -> 25.8 us  [send(): return lax.ppermute(block, axes, pairs)]
    concatenate x4 -> x0, other arithmetic: 3.01 us -> none  [run_block(): window = jnp.concatenate([row3, back2, back1, own], axis=1)]
    slice x4 -> x0, local copies, waits for them, and re-layouts: 2.81 us -> none  [the longest x3 2.1 us: next_inputs(): row3 = send(mirrored[:, rows - 1:], BACK + 1)]
    rev x3 -> x0, local copies, waits for them, and re-layouts: 2.66 us -> none  [next_inputs(): mirrored = result[:, ::-1]]
    select_n x1 -> x0, other arithmetic: 1.61 us -> none  [body(): out = jnp.where(segment == turn, result, out)]
    broadcast_in_dim x0 -> x1, other arithmetic: none -> 1.6 us  [body(): return out[None]]
    unnamed x4 -> x0, other arithmetic: 0.96 us -> none
  transfers between devices with their start and end apart: 15 -> 15, of which waited for: 2 -> 2; matrix products, arithmetic and copies ran while one was open for 4% -> 1% of each run, Pallas kernels for 0% -> 0%
where the time goes in v4:
time: 93.7 us; the launch traced here: 92.6 us
  Pallas kernels  45.8 us (49%)
  waiting for transfers between devices  25.8 us (28%)
  starting transfers between devices  13.3 us (14%)
  local copies, waits for them, and re-layouts  4.85 us (5%)
  other arithmetic  2.48 us (3%)
    pallas_call x4, Pallas kernels, body(): result, result_low = call(*inputs, mask, *weights)  45.8 us
    ppermute x12, waiting for transfers between devices, send(): return lax.ppermute(block, axes, pairs)  25.8 us
    ppermute x12, starting transfers between devices, send(): return lax.ppermute(block, axes, pairs)  11.2 us
    unnamed x38, local copies, waits for them, and re-layouts  4.58 us
    ppermute x3, starting transfers between devices, behind(): return lax.ppermute(patches, axes, pairs)  2.13 us
  transfers between devices with their start and end apart: 15, of which 2 were waited for; matrix products, arithmetic and copies ran while one was open for 1% of the time, Pallas kernels for 0%

profile of v4, /device:TPU:15, one launch (start us, length us, event | category | flops | bytes accessed | tf_op | source)
XLA Modules:
  0.0 92.6 jit_solution(660418697795674757)
XLA Ops:
  0.0 0.8 collective-permute-start
  0.8 0.7 collective-permute-start.1
  1.5 0.7 collective-permute-start.2
  2.2 0.2 dynamic-slice_reduce_fusion
  2.6 0.8 fusion.1.mask_ref
  3.4 0.6 copy-done.4
  4.1 11.5 %shard_map.82 = (f32[2,128,128]{2,1,0:T(8,128)}, bf16[2,128,128]{2,1,0:T(8,128)(2,1)}) custom-call(f32[2,128,128]{2,1,0:T(8,128)} %own_ref.1, f32[2,128,128]{2,1,0:T(8,128)} %copy-done.4, f32[2,128,128]{2,1,0:T(8,128)} %copy-done.5, f32[2,128,128]{2,1,0:T(8,128)} %copy-done.7, f32[128,384]{1,0:T(8,128)} %fusion.1.mask_ref, f32[1,1024]{1,0:T(1,128)} %ga_ref.7, ...), custom_call_target="tpu_custom_call" | custom-call | flops 5033164800 | bytes 9633792 | tf_op jit(solution)/shard_map/pallas_call | solution.py:250
  15.6 0.7 collective-permute-start.3
  16.3 0.7 collective-permute-start.4
  16.9 0.7 collective-permute-start.5
  17.6 0.8 collective-permute-start.6
  18.5 0.6 copy-done.13
  19.2 0.7 copy-done.8
  19.8 11.4 %shard_map.83 = (f32[2,128,128]{2,1,0:T(8,128)}, bf16[2,128,128]{2,1,0:T(8,128)(2,1)}) custom-call(f32[2,128,128]{2,1,0:T(8,128)} %copy-done.8, bf16[2,128,128]{2,1,0:T(8,128)(2,1)} %copy-done.13, bf16[2,128,128]{2,1,0:T(8,128)(2,1)} %copy-done.15, bf16[2,128,128]{2,1,0:T(8,128)(2,1)} %copy-done.17, f32[128,384]{1,0:T(8,128)} %fusion.1.mask_ref, ...), custom_call_target="tpu_custom_call" | custom-call | flops 5033164800 | bytes 9633792 | tf_op jit(solution)/shard_map/pallas_call | solution.py:250
  31.3 0.7 collective-permute-start.7
  31.9 0.7 collective-permute-start.10
  32.6 0.7 collective-permute-start.8
  33.3 0.9 collective-permute-start.9
  34.2 0.6 copy-done.14
  34.9 0.7 copy-done.9
  35.5 11.4 %shard_map.84 = (f32[2,128,128]{2,1,0:T(8,128)}, bf16[2,128,128]{2,1,0:T(8,128)(2,1)}) custom-call(f32[2,128,128]{2,1,0:T(8,128)} %copy-done.9, bf16[2,128,128]{2,1,0:T(8,128)(2,1)} %copy-done.16, bf16[2,128,128]{2,1,0:T(8,128)(2,1)} %copy-done.18, bf16[2,128,128]{2,1,0:T(8,128)(2,1)} %copy-done.14, f32[128,384]{1,0:T(8,128)} %fusion.1.mask_ref, ...), custom_call_target="tpu_custom_call" | custom-call | flops 5033164800 | bytes 9633792 | tf_op jit(solution)/shard_map/pallas_call | solution.py:250
  47.0 1.3 %collective-permute-start.11 = (f32[2,128,128]{2,1,0:T(8,128)}, f32[2,128,128]{2,1,0:T(8,128)S(1)}, u32[]{:S(2)}, u32[]{:S(2)}) collective-permute-start(f32[2,128,128]{2,1,0:T(8,128)} %get-tuple-element.16), channel_id=1, source_target_pairs={{16,31},{17,30},{18,29},{19,28},{20,27},{21,26},{22,25},{23,24}} | collective-permute-start | bytes 393224 | tf_op jit(solution)/shard_map/ppermute | solution.py:237
  48.3 1.3 %collective-permute-start.12 = (bf16[2,128,128]{2,1,0:T(8,128)(2,1)}, bf16[2,128,128]{2,1,0:T(8,128)(2,1)S(1)}, u32[]{:S(2)}, u32[]{:S(2)}) collective-permute-start(bf16[2,128,128]{2,1,0:T(8,128)(2,1)} %get-tuple-element.17), channel_id=1, source_target_pairs={{17,31},{18,30},{19,29},{20,28},{21,27},{22,26},{23,25}} | collective-permute-start | bytes 196616 | tf_op jit(solution)/shard_map/ppermute | solution.py:237
  49.6 1.3 %collective-permute-start.13 = (bf16[2,128,128]{2,1,0:T(8,128)(2,1)}, bf16[2,128,128]{2,1,0:T(8,128)(2,1)S(1)}, u32[]{:S(2)}, u32[]{:S(2)}) collective-permute-start(bf16[2,128,128]{2,1,0:T(8,128)(2,1)} %get-tuple-element.17), channel_id=1, source_target_pairs={{18,31},{19,30},{20,29},{21,28},{22,27},{23,26}} | collective-permute-start | bytes 196616 | tf_op jit(solution)/shard_map/ppermute | solution.py:237
  50.9 1.6 %collective-permute-start.14 = (bf16[2,128,128]{2,1,0:T(8,128)(2,1)}, bf16[2,128,128]{2,1,0:T(8,128)(2,1)S(1)}, u32[]{:S(2)}, u32[]{:S(2)}) collective-permute-start(bf16[2,128,128]{2,1,0:T(8,128)(2,1)} %get-tuple-element.17), channel_id=1, source_target_pairs={{19,31},{20,30},{21,29},{22,28},{23,27}} | collective-permute-start | bytes 196616 | tf_op jit(solution)/shard_map/ppermute | solution.py:237
  52.5 25.7 %collective-permute-done.12.back1_ref = bf16[2,128,128]{2,1,0:T(8,128)(2,1)S(1)} collective-permute-done((bf16[2,128,128]{2,1,0:T(8,128)(2,1)}, bf16[2,128,128]{2,1,0:T(8,128)(2,1)S(1)}, u32[]{:S(2)}, u32[]{:S(2)}) %collective-permute-start.12) | collective-permute-done | bytes 65568 | tf_op jit(solution)/shard_map/ppermute | solution.py:237
  78.1 0.1 collective-permute-done.13.back2_ref
  78.2 0.5 copy-done.10
  78.8 0.1 copy-done.11
  78.9 0.7 copy-done.6
  79.5 11.5 %shard_map.85 = (f32[2,128,128]{2,1,0:T(8,128)}, bf16[2,128,128]{2,1,0:T(8,128)(2,1)}) custom-call(f32[2,128,128]{2,1,0:T(8,128)} %copy-done.6, bf16[2,128,128]{2,1,0:T(8,128)(2,1)} %copy-done.10, bf16[2,128,128]{2,1,0:T(8,128)(2,1)} %copy-done.11, bf16[2,128,128]{2,1,0:T(8,128)(2,1)} %copy-done.12, f32[128,384]{1,0:T(8,128)} %fusion.1.mask_ref, ...), custom_call_target="tpu_custom_call" | custom-call | flops 5033164800 | bytes 9633792 | tf_op jit(solution)/shard_map/pallas_call | solution.py:250
  91.0 1.6 %select_bitcast_fusion = f32[1,2,128,128]{3,2,1,0:T(8,128)} fusion(f32[2,128,128]{2,1,0:T(8,128)} %get-tuple-element.18, f32[2,128,128]{2,1,0:T(8,128)S(1)} %copy-done.3, f32[2,128,128]{2,1,0:T(8,128)S(1)} %copy-done.2, f32[2,128,128]{2,1,0:T(8,128)S(1)} %copy-done.1, pred[]{:T(512)S(6)} %eq.34, pred[]{:T(512)S(6)} %eq.33, pred[]{:T(512)S(6)} %eq.32, pred[]{:T(512)S(6)} %eq.27), kind=kLoop, calls=%fused_computation.3 | loop fusion | flops 131072 | bytes 655364 | tf_op jit(solution)/shard_map/broadcast_in_dim | solution.py:254
  (48 shorter events, 0.5 us)
Async XLA Ops:
  0.0 2.2 %copy-start = (s32[8,4]{0,1:T(4,128)S(1)}, s32[8,4]{0,1:T(4,128)}, u32[]{:S(2)}) copy-start(s32[8,4]{0,1:T(4,128)} %param.9) | copy-start | bytes 388
  0.0 3.3 %collective-permute-start = (f32[2,128,128]{2,1,0:T(8,128)}, f32[2,128,128]{2,1,0:T(8,128)S(1)}, u32[]{:S(2)}, u32[]{:S(2)}) collective-permute-start(f32[2,128,128]{2,1,0:T(8,128)} %own_ref.1), channel_id=1, source_target_pairs={{0,1},{1,2},{2,3},{3,4},{4,5},{5,6},{6,7}} | collective-permute-start | bytes 393224 | tf_op jit(solution)/shard_map/ppermute | solution.py:223
  0.8 2.5 %collective-permute-start.1 = (f32[2,128,128]{2,1,0:T(8,128)}, f32[2,128,128]{2,1,0:T(8,128)S(1)}, u32[]{:S(2)}, u32[]{:S(2)}) collective-permute-start(f32[2,128,128]{2,1,0:T(8,128)} %own_ref.1), channel_id=1, source_target_pairs={{0,2},{1,3},{2,4},{3,5},{4,6},{5,7}} | collective-permute-start | bytes 393224 | tf_op jit(solution)/shard_map/ppermute | solution.py:223
  1.5 1.9 %collective-permute-start.2 = (f32[2,128,128]{2,1,0:T(8,128)}, f32[2,128,128]{2,1,0:T(8,128)S(1)}, u32[]{:S(2)}, u32[]{:S(2)}) collective-permute-start(f32[2,128,128]{2,1,0:T(8,128)} %own_ref.1), channel_id=1, source_target_pairs={{0,3},{1,4},{2,5},{3,6},{4,7}} | collective-permute-start | bytes 393224 | tf_op jit(solution)/shard_map/ppermute | solution.py:223
  3.3 0.7 copy-start.4
  3.3 0.7 copy-start.5
  3.4 0.7 copy-start.7
  15.6 2.9 %collective-permute-start.3 = (f32[2,128,128]{2,1,0:T(8,128)}, f32[2,128,128]{2,1,0:T(8,128)S(1)}, u32[]{:S(2)}, u32[]{:S(2)}) collective-permute-start(f32[2,128,128]{2,1,0:T(8,128)} %get-tuple-element.12), channel_id=1, source_target_pairs={{0,15},{1,14},{2,13},{3,12},{4,11},{5,10},{6,9},{7,8}} | collective-permute-start | bytes 393224 | tf_op jit(solution)/shard_map/ppermute | solution.py:237
  16.3 2.2 %collective-permute-start.4 = (bf16[2,128,128]{2,1,0:T(8,128)(2,1)}, bf16[2,128,128]{2,1,0:T(8,128)(2,1)S(1)}, u32[]{:S(2)}, u32[]{:S(2)}) collective-permute-start(bf16[2,128,128]{2,1,0:T(8,128)(2,1)} %get-tuple-element.13), channel_id=1, source_target_pairs={{1,15},{2,14},{3,13},{4,12},{5,11},{6,10},{7,9}} | collective-permute-start | bytes 196616 | tf_op jit(solution)/shard_map/ppermute | solution.py:237
  16.9 1.5 %collective-permute-start.5 = (bf16[2,128,128]{2,1,0:T(8,128)(2,1)}, bf16[2,128,128]{2,1,0:T(8,128)(2,1)S(1)}, u32[]{:S(2)}, u32[]{:S(2)}) collective-permute-start(bf16[2,128,128]{2,1,0:T(8,128)(2,1)} %get-tuple-element.13), channel_id=1, source_target_pairs={{2,15},{3,14},{4,13},{5,12},{6,11},{7,10}} | collective-permute-start | bytes 196616 | tf_op jit(solution)/shard_map/ppermute | solution.py:237
  17.6 0.9 collective-permute-start.6
  18.5 0.6 copy-start.13
  18.5 0.6 copy-start.15
  18.5 0.6 copy-start.17
  19.1 0.7 copy-start.8
  31.3 3.0 %collective-permute-start.7 = (f32[2,128,128]{2,1,0:T(8,128)}, f32[2,128,128]{2,1,0:T(8,128)S(1)}, u32[]{:S(2)}, u32[]{:S(2)}) collective-permute-start(f32[2,128,128]{2,1,0:T(8,128)} %get-tuple-element.14), channel_id=1, source_target_pairs={{8,23},{9,22},{10,21},{11,20},{12,19},{13,18},{14,17},{15,16}} | collective-permute-start | bytes 393224 | tf_op jit(solution)/shard_map/ppermute | solution.py:237
  31.9 2.2 %collective-permute-start.10 = (bf16[2,128,128]{2,1,0:T(8,128)(2,1)}, bf16[2,128,128]{2,1,0:T(8,128)(2,1)S(1)}, u32[]{:S(2)}, u32[]{:S(2)}) collective-permute-start(bf16[2,128,128]{2,1,0:T(8,128)(2,1)} %get-tuple-element.15), channel_id=1, source_target_pairs={{11,23},{12,22},{13,21},{14,20},{15,19}} | collective-permute-start | bytes 196616 | tf_op jit(solution)/shard_map/ppermute | solution.py:237
  32.6 1.6 %collective-permute-start.8 = (bf16[2,128,128]{2,1,0:T(8,128)(2,1)}, bf16[2,128,128]{2,1,0:T(8,128)(2,1)S(1)}, u32[]{:S(2)}, u32[]{:S(2)}) collective-permute-start(bf16[2,128,128]{2,1,0:T(8,128)(2,1)} %get-tuple-element.15), channel_id=1, source_target_pairs={{9,23},{10,22},{11,21},{12,20},{13,19},{14,18},{15,17}} | collective-permute-start | bytes 196616 | tf_op jit(solution)/shard_map/ppermute | solution.py:237
  33.3 0.9 %collective-permute-start.9 = (bf16[2,128,128]{2,1,0:T(8,128)(2,1)}, bf16[2,128,128]{2,1,0:T(8,128)(2,1)S(1)}, u32[]{:S(2)}, u32[]{:S(2)}) collective-permute-start(bf16[2,128,128]{2,1,0:T(8,128)(2,1)} %get-tuple-element.15), channel_id=1, source_target_pairs={{10,23},{11,22},{12,21},{13,20},{14,19},{15,18}} | collective-permute-start | bytes 196616 | tf_op jit(solution)/shard_map/ppermute | solution.py:237
  34.2 0.6 copy-start.14
  34.2 0.6 copy-start.16
  34.2 0.6 copy-start.18
  34.9 0.7 copy-start.9
  47.0 31.3 %collective-permute-start.11 = (f32[2,128,128]{2,1,0:T(8,128)}, f32[2,128,128]{2,1,0:T(8,128)S(1)}, u32[]{:S(2)}, u32[]{:S(2)}) collective-permute-start(f32[2,128,128]{2,1,0:T(8,128)} %get-tuple-element.16), channel_id=1, source_target_pairs={{16,31},{17,30},{18,29},{19,28},{20,27},{21,26},{22,25},{23,24}} | collective-permute-start | bytes 393224 | tf_op jit(solution)/shard_map/ppermute | solution.py:237
  48.3 29.9 %collective-permute-start.12 = (bf16[2,128,128]{2,1,0:T(8,128)(2,1)}, bf16[2,128,128]{2,1,0:T(8,128)(2,1)S(1)}, u32[]{:S(2)}, u32[]{:S(2)}) collective-permute-start(bf16[2,128,128]{2,1,0:T(8,128)(2,1)} %get-tuple-element.17), channel_id=1, source_target_pairs={{17,31},{18,30},{19,29},{20,28},{21,27},{22,26},{23,25}} | collective-permute-start | bytes 196616 | tf_op jit(solution)/shard_map/ppermute | solution.py:237
  49.6 28.7 %collective-permute-start.13 = (bf16[2,128,128]{2,1,0:T(8,128)(2,1)}, bf16[2,128,128]{2,1,0:T(8,128)(2,1)S(1)}, u32[]{:S(2)}, u32[]{:S(2)}) collective-permute-start(bf16[2,128,128]{2,1,0:T(8,128)(2,1)} %get-tuple-element.17), channel_id=1, source_target_pairs={{18,31},{19,30},{20,29},{21,28},{22,27},{23,26}} | collective-permute-start | bytes 196616 | tf_op jit(solution)/shard_map/ppermute | solution.py:237
  50.9 27.4 %collective-permute-start.14 = (bf16[2,128,128]{2,1,0:T(8,128)(2,1)}, bf16[2,128,128]{2,1,0:T(8,128)(2,1)S(1)}, u32[]{:S(2)}, u32[]{:S(2)}) collective-permute-start(bf16[2,128,128]{2,1,0:T(8,128)(2,1)} %get-tuple-element.17), channel_id=1, source_target_pairs={{19,31},{20,30},{21,29},{22,28},{23,27}} | collective-permute-start | bytes 196616 | tf_op jit(solution)/shard_map/ppermute | solution.py:237
  52.4 38.6 %copy-start.1 = (f32[2,128,128]{2,1,0:T(8,128)S(1)}, f32[2,128,128]{2,1,0:T(8,128)}, u32[]{:S(2)}) copy-start(f32[2,128,128]{2,1,0:T(8,128)} %get-tuple-element.12) | copy-start | bytes 393220
  52.4 38.6 %copy-start.2 = (f32[2,128,128]{2,1,0:T(8,128)S(1)}, f32[2,128,128]{2,1,0:T(8,128)}, u32[]{:S(2)}) copy-start(f32[2,128,128]{2,1,0:T(8,128)} %get-tuple-element.14) | copy-start | bytes 393220
  52.5 38.6 %copy-start.3 = (f32[2,128,128]{2,1,0:T(8,128)S(1)}, f32[2,128,128]{2,1,0:T(8,128)}, u32[]{:S(2)}) copy-start(f32[2,128,128]{2,1,0:T(8,128)} %get-tuple-element.16) | copy-start | bytes 393220
  78.2 0.7 copy-start.12
  78.9 0.7 copy-start.6
  (2 other events, 1.2 us)

commit v5 on v4

--- a/solution.py
+++ b/solution.py
@@ -20,11 +20,22 @@
     scale = HEAD_DIM ** (-0.5)
     heads = heads_all // HEAD_DIM
 
-    def kernel(own_ref, back1_ref, back2_ref, edge_ref, mask_ref, ga_ref, gb_ref,
+    def kernel(keep_ref, mask_ref, ga_ref, gb_ref,
+               own_hbm, back1_hbm, back2_hbm, edge_hbm, prev_hbm,
                embed_hbm, attn_hbm, mix_hbm, read_hbm,
-               out_ref, outb_ref,
-               embed_v, attn_v, mix_v, read_v, sems,
+               stored_hbm, low_hbm,
+               embed_v, attn_v, mix_v, read_v, sems, io_sems,
+               own_ref, back1_ref, back2_ref, edge_ref, prev_v, stored_v, low_v,
                pieces_s, shifted_s, hidden_s, normed_s, q_s, kv_s, mixed_s, res_s):
+        inputs = [
+            pltpu.make_async_copy(src, dst, io_sems.at[k])
+            for k, (src, dst) in enumerate(
+                [(own_hbm, own_ref), (back1_hbm, back1_ref), (back2_hbm, back2_ref), (edge_hbm, edge_ref)]
+            )
+        ]
+        for copy in inputs:
+            copy.start()
+        prev_copy = pltpu.make_async_copy(prev_hbm, prev_v, io_sems.at[4])
         n_kv = 2 * heads_all // CHUNK
         kv_copies = [
             pltpu.make_async_copy(
@@ -45,6 +56,9 @@
             copy.start()
         for copy in copies[1:]:
             copy.start()
+        prev_copy.start()
+        for copy in inputs:
+            copy.wait()
         before = lax.broadcasted_iota(jnp.int32, (span, n_in), 0) + (rows - 1)
         column = lax.broadcasted_iota(jnp.int32, (span, n_in), 1)
         if mirrored:
@@ -129,8 +143,18 @@
                 own = (parts[0] + parts[1]) + parts[2]
             rows_m = slice(m * rows, (m + 1) * rows)
             result = (own - shift_mean[rows_m]) * jnp.exp(-log_scale[rows_m])
-            out_ref[m] = result
-            outb_ref[m] = result.astype(jnp.bfloat16)
+            low_v[m] = result.astype(jnp.bfloat16)
+            if m == 0:
+                prev_copy.wait()
+            stored_v[m] = jnp.where(keep_ref[0] > 0, result, prev_v[m])
+        outputs = [
+            pltpu.make_async_copy(stored_v, stored_hbm, io_sems.at[5]),
+            pltpu.make_async_copy(low_v, low_hbm, io_sems.at[6]),
+        ]
+        for copy in outputs:
+            copy.start()
+        for copy in outputs:
+            copy.wait()
 
     width = heads_all
     flops = 2 * n_rows * (width_in * width + width * 2 * heads_all)
@@ -143,14 +167,23 @@
             jax.ShapeDtypeStruct((micro, rows, width_in), jnp.float32),
             jax.ShapeDtypeStruct((micro, rows, width_in), jnp.bfloat16),
         ),
-        in_specs=[pl.BlockSpec(memory_space=vmem)] * 7 + [pl.BlockSpec(memory_space=pl.ANY)] * 4,
-        out_specs=(pl.BlockSpec(memory_space=vmem), pl.BlockSpec(memory_space=vmem)),
+        in_specs=[pl.BlockSpec(memory_space=pltpu.SMEM)] + [pl.BlockSpec(memory_space=vmem)] * 3
+        + [pl.BlockSpec(memory_space=pltpu.HBM)] * 9,
+        out_specs=(pl.BlockSpec(memory_space=pltpu.HBM), pl.BlockSpec(memory_space=pltpu.HBM)),
         scratch_shapes=[
             vmem((width_in, width), jnp.bfloat16),
             vmem((width, 3 * heads_all), jnp.bfloat16),
             vmem((heads_all, width), jnp.bfloat16),
             vmem((width, 2 * width_in), jnp.bfloat16),
             pltpu.SemaphoreType.DMA((4 + 2 * heads_all // CHUNK,)),
+            pltpu.SemaphoreType.DMA((7,)),
+            vmem((micro, rows, width_in), jnp.float32),
+            vmem((micro, rows, width_in), piece_dtype),
+            vmem((micro, rows, width_in), piece_dtype),
+            vmem((micro, rows, width_in), piece_dtype),
+            vmem((micro, rows, width_in), jnp.float32),
+            vmem((micro, rows, width_in), jnp.float32),
+            vmem((micro, rows, width_in), jnp.bfloat16),
             vmem((n_in, width_in), jnp.bfloat16),
             vmem((n_rows, width_in), jnp.bfloat16),
             vmem((n_rows, width), jnp.float32),
@@ -245,12 +278,13 @@
 
     inputs = first_inputs()
     out = jnp.zeros((micro, rows, width_in), jnp.float32)
+    gains, matrices = weights[:2], weights[2:]
     for turn in range(n_seg):
         call = first_call if turn == 0 else later_call
-        result, result_low = call(*inputs, mask, *weights)
-        out = jnp.where(segment == turn, result, out)
+        keep = (segment == turn).astype(jnp.int32).reshape(1)
+        out, result_low = call(keep, mask, *gains, *inputs, out, *matrices)
         if turn + 1 < n_seg:
-            inputs = next_inputs(result, result_low, turn)
+            inputs = next_inputs(out, result_low, turn)
     return out[None]
 
 

time: 93.7 us -> 100 us (1.067)
  Pallas kernels: 45.8 us -> 55.3 us
  local copies, waits for them, and re-layouts: 4.85 us -> 3 us
  other arithmetic: 2.48 us -> 0.89 us
    pallas_call x4, Pallas kernels: 45.8 us -> 55.3 us  [body(): out, result_low = call(keep, mask, *gains, *inputs, out, *matrices)]
    unnamed x38 -> x32, local copies, waits for them, and re-layouts: 4.58 us -> 2.02 us
    broadcast_in_dim x1 -> x0, other arithmetic: 1.6 us -> none  [body(): return out[None]]
where the time goes in v5:
time: 100 us; the launch traced here: 98.9 us
  Pallas kernels  55.3 us (55%)
  waiting for transfers between devices  25.8 us (26%)
  starting transfers between devices  13.3 us (13%)
  local copies, waits for them, and re-layouts  3 us (3%)
    pallas_call x4, Pallas kernels, body(): out, result_low = call(keep, mask, *gains, *inputs, out, *matrices)  55.3 us
    ppermute x12, waiting for transfers between devices, send(): return lax.ppermute(block, axes, pairs)  25.8 us
    ppermute x12, starting transfers between devices, send(): return lax.ppermute(block, axes, pairs)  11.2 us
    ppermute x3, starting transfers between devices, behind(): return lax.ppermute(patches, axes, pairs)  2.13 us
    unnamed x32, local copies, waits for them, and re-layouts  2.02 us
  transfers between devices with their start and end apart: 15, of which 2 were waited for; matrix products, arithmetic and copies ran while one was open for 1% of the time, Pallas kernels for 0%

profile of v5, /device:TPU:15, one launch (start us, length us, event | category | flops | bytes accessed | tf_op | source)
XLA Modules:
  0.0 98.9 jit_solution(6536995191657511850)
XLA Ops:
  0.0 0.8 collective-permute-start
  0.8 0.7 collective-permute-start.1
  1.5 0.7 collective-permute-start.2
  2.2 0.2 dynamic-slice_reduce_fusion
  2.4 0.1 compare_reduce_fusion
  2.5 0.1 broadcast_bitcast_fusion
  2.6 0.8 fusion.1.mask_ref
  3.4 0.7 broadcast_in_dim.14.prev_hbm
  4.1 13.7 %shard_map.82 = (f32[2,128,128]{2,1,0:T(8,128)}, bf16[2,128,128]{2,1,0:T(8,128)(2,1)}) custom-call(s32[1]{0:T(128)} %bitcast.4.keep_ref, f32[128,384]{1,0:T(8,128)} %fusion.1.mask_ref, f32[1,1024]{1,0:T(1,128)} %ga_ref.7, f32[1,1024]{1,0:T(1,128)} %gb_ref.7, f32[2,128,128]{2,1,0:T(8,128)} %own_hbm.1, f32[2,128,128]{2,1,0:T(8,128)} %copy-done.1, ...), custom_call_target="tpu_custom_call" | custom-call | flops 5033164800 | bytes 9633792 | tf_op jit(solution)/shard_map/pallas_call | solution.py:285
  17.9 0.7 collective-permute-start.3
  18.5 0.7 collective-permute-start.4
  19.2 0.7 collective-permute-start.5
  19.9 0.8 collective-permute-start.6
  20.8 0.5 copy-done.8
  21.4 0.0 copy-done.11
  21.5 13.8 %shard_map.83 = (f32[2,128,128]{2,1,0:T(8,128)}, bf16[2,128,128]{2,1,0:T(8,128)(2,1)}) custom-call(s32[1]{0:T(128)} %bitcast.3.keep_ref, f32[128,384]{1,0:T(8,128)} %fusion.1.mask_ref, f32[1,1024]{1,0:T(1,128)} %ga_ref.7, f32[1,1024]{1,0:T(1,128)} %gb_ref.7, f32[2,128,128]{2,1,0:T(8,128)} %copy-done.5, bf16[2,128,128]{2,1,0:T(8,128)(2,1)} %copy-done.8, ...), custom_call_target="tpu_custom_call" | custom-call | flops 5033164800 | bytes 9633792 | tf_op jit(solution)/shard_map/pallas_call | solution.py:285
  35.3 0.7 collective-permute-start.7
  36.0 0.7 collective-permute-start.10
  36.7 0.7 collective-permute-start.8
  37.3 0.9 collective-permute-start.9
  38.3 0.6 copy-done.9
  38.9 0.0 copy-done.6
  39.0 13.9 %shard_map.84 = (f32[2,128,128]{2,1,0:T(8,128)}, bf16[2,128,128]{2,1,0:T(8,128)(2,1)}) custom-call(s32[1]{0:T(128)} %bitcast.2.keep_ref, f32[128,384]{1,0:T(8,128)} %fusion.1.mask_ref, f32[1,1024]{1,0:T(1,128)} %ga_ref.7, f32[1,1024]{1,0:T(1,128)} %gb_ref.7, f32[2,128,128]{2,1,0:T(8,128)} %copy-done.6, bf16[2,128,128]{2,1,0:T(8,128)(2,1)} %copy-done.12, ...), custom_call_target="tpu_custom_call" | custom-call | flops 5033164800 | bytes 9633792 | tf_op jit(solution)/shard_map/pallas_call | solution.py:285
  52.8 1.3 %collective-permute-start.11 = (f32[2,128,128]{2,1,0:T(8,128)}, f32[2,128,128]{2,1,0:T(8,128)S(1)}, u32[]{:S(2)}, u32[]{:S(2)}) collective-permute-start(f32[2,128,128]{2,1,0:T(8,128)} %get-tuple-element.16.prev_hbm), channel_id=1, source_target_pairs={{16,31},{17,30},{18,29},{19,28},{20,27},{21,26},{22,25},{23,24}} | collective-permute-start | bytes 393224 | tf_op jit(solution)/shard_map/ppermute | solution.py:270
  54.1 1.3 %collective-permute-start.12 = (bf16[2,128,128]{2,1,0:T(8,128)(2,1)}, bf16[2,128,128]{2,1,0:T(8,128)(2,1)S(1)}, u32[]{:S(2)}, u32[]{:S(2)}) collective-permute-start(bf16[2,128,128]{2,1,0:T(8,128)(2,1)} %get-tuple-element.17), channel_id=1, source_target_pairs={{17,31},{18,30},{19,29},{20,28},{21,27},{22,26},{23,25}} | collective-permute-start | bytes 196616 | tf_op jit(solution)/shard_map/ppermute | solution.py:270
  55.4 1.3 %collective-permute-start.13 = (bf16[2,128,128]{2,1,0:T(8,128)(2,1)}, bf16[2,128,128]{2,1,0:T(8,128)(2,1)S(1)}, u32[]{:S(2)}, u32[]{:S(2)}) collective-permute-start(bf16[2,128,128]{2,1,0:T(8,128)(2,1)} %get-tuple-element.17), channel_id=1, source_target_pairs={{18,31},{19,30},{20,29},{21,28},{22,27},{23,26}} | collective-permute-start | bytes 196616 | tf_op jit(solution)/shard_map/ppermute | solution.py:270
  56.7 1.6 %collective-permute-start.14 = (bf16[2,128,128]{2,1,0:T(8,128)(2,1)}, bf16[2,128,128]{2,1,0:T(8,128)(2,1)S(1)}, u32[]{:S(2)}, u32[]{:S(2)}) collective-permute-start(bf16[2,128,128]{2,1,0:T(8,128)(2,1)} %get-tuple-element.17), channel_id=1, source_target_pairs={{19,31},{20,30},{21,29},{22,28},{23,27}} | collective-permute-start | bytes 196616 | tf_op jit(solution)/shard_map/ppermute | solution.py:270
  58.3 25.1 %collective-permute-done.12.back1_hbm = bf16[2,128,128]{2,1,0:T(8,128)(2,1)S(1)} collective-permute-done((bf16[2,128,128]{2,1,0:T(8,128)(2,1)}, bf16[2,128,128]{2,1,0:T(8,128)(2,1)S(1)}, u32[]{:S(2)}, u32[]{:S(2)}) %collective-permute-start.12) | collective-permute-done | bytes 65568 | tf_op jit(solution)/shard_map/ppermute | solution.py:270
  83.4 0.8 collective-permute-done.13.back2_hbm
  84.2 0.6 copy-done.10
  84.8 0.0 copy-done.4
  84.8 13.9 %shard_map.85 = (f32[2,128,128]{2,1,0:T(8,128)}, bf16[2,128,128]{2,1,0:T(8,128)(2,1)}) custom-call(s32[1]{0:T(128)} %bitcast.keep_ref, f32[128,384]{1,0:T(8,128)} %fusion.1.mask_ref, f32[1,1024]{1,0:T(1,128)} %ga_ref.7, f32[1,1024]{1,0:T(1,128)} %gb_ref.7, f32[2,128,128]{2,1,0:T(8,128)} %copy-done.4, bf16[2,128,128]{2,1,0:T(8,128)(2,1)} %copy-done.7, ...), custom_call_target="tpu_custom_call" | custom-call | flops 5033164800 | bytes 9633792 | tf_op jit(solution)/shard_map/pallas_call | solution.py:285
  (42 shorter events, 0.2 us)
Async XLA Ops:
  0.0 2.2 %copy-start = (s32[8,4]{0,1:T(4,128)S(1)}, s32[8,4]{0,1:T(4,128)}, u32[]{:S(2)}) copy-start(s32[8,4]{0,1:T(4,128)} %param.9) | copy-start | bytes 388
  0.0 3.3 %collective-permute-start = (f32[2,128,128]{2,1,0:T(8,128)}, f32[2,128,128]{2,1,0:T(8,128)S(1)}, u32[]{:S(2)}, u32[]{:S(2)}) collective-permute-start(f32[2,128,128]{2,1,0:T(8,128)} %own_hbm.1), channel_id=1, source_target_pairs={{0,1},{1,2},{2,3},{3,4},{4,5},{5,6},{6,7}} | collective-permute-start | bytes 393224 | tf_op jit(solution)/shard_map/ppermute | solution.py:256
  0.8 2.6 %collective-permute-start.1 = (f32[2,128,128]{2,1,0:T(8,128)}, f32[2,128,128]{2,1,0:T(8,128)S(1)}, u32[]{:S(2)}, u32[]{:S(2)}) collective-permute-start(f32[2,128,128]{2,1,0:T(8,128)} %own_hbm.1), channel_id=1, source_target_pairs={{0,2},{1,3},{2,4},{3,5},{4,6},{5,7}} | collective-permute-start | bytes 393224 | tf_op jit(solution)/shard_map/ppermute | solution.py:256
  1.5 1.9 %collective-permute-start.2 = (f32[2,128,128]{2,1,0:T(8,128)}, f32[2,128,128]{2,1,0:T(8,128)S(1)}, u32[]{:S(2)}, u32[]{:S(2)}) collective-permute-start(f32[2,128,128]{2,1,0:T(8,128)} %own_hbm.1), channel_id=1, source_target_pairs={{0,3},{1,4},{2,5},{3,6},{4,7}} | collective-permute-start | bytes 393224 | tf_op jit(solution)/shard_map/ppermute | solution.py:256
  3.3 0.8 copy-start.1
  3.4 0.8 copy-start.2
  3.4 0.8 copy-start.3
  17.9 2.9 %collective-permute-start.3 = (f32[2,128,128]{2,1,0:T(8,128)}, f32[2,128,128]{2,1,0:T(8,128)S(1)}, u32[]{:S(2)}, u32[]{:S(2)}) collective-permute-start(f32[2,128,128]{2,1,0:T(8,128)} %get-tuple-element.12.prev_hbm), channel_id=1, source_target_pairs={{0,15},{1,14},{2,13},{3,12},{4,11},{5,10},{6,9},{7,8}} | collective-permute-start | bytes 393224 | tf_op jit(solution)/shard_map/ppermute | solution.py:270
  18.5 2.2 %collective-permute-start.4 = (bf16[2,128,128]{2,1,0:T(8,128)(2,1)}, bf16[2,128,128]{2,1,0:T(8,128)(2,1)S(1)}, u32[]{:S(2)}, u32[]{:S(2)}) collective-permute-start(bf16[2,128,128]{2,1,0:T(8,128)(2,1)} %get-tuple-element.13), channel_id=1, source_target_pairs={{1,15},{2,14},{3,13},{4,12},{5,11},{6,10},{7,9}} | collective-permute-start | bytes 196616 | tf_op jit(solution)/shard_map/ppermute | solution.py:270
  19.2 1.6 %collective-permute-start.5 = (bf16[2,128,128]{2,1,0:T(8,128)(2,1)}, bf16[2,128,128]{2,1,0:T(8,128)(2,1)S(1)}, u32[]{:S(2)}, u32[]{:S(2)}) collective-permute-start(bf16[2,128,128]{2,1,0:T(8,128)(2,1)} %get-tuple-element.13), channel_id=1, source_target_pairs={{2,15},{3,14},{4,13},{5,12},{6,11},{7,10}} | collective-permute-start | bytes 196616 | tf_op jit(solution)/shard_map/ppermute | solution.py:270
  19.9 0.9 collective-permute-start.6
  20.7 0.6 copy-start.8
  20.8 0.6 copy-start.11
  20.8 0.6 copy-start.14
  20.8 0.7 copy-start.5
  35.3 3.0 %collective-permute-start.7 = (f32[2,128,128]{2,1,0:T(8,128)}, f32[2,128,128]{2,1,0:T(8,128)S(1)}, u32[]{:S(2)}, u32[]{:S(2)}) collective-permute-start(f32[2,128,128]{2,1,0:T(8,128)} %get-tuple-element.14.prev_hbm), channel_id=1, source_target_pairs={{8,23},{9,22},{10,21},{11,20},{12,19},{13,18},{14,17},{15,16}} | collective-permute-start | bytes 393224 | tf_op jit(solution)/shard_map/ppermute | solution.py:270
  36.0 2.2 %collective-permute-start.10 = (bf16[2,128,128]{2,1,0:T(8,128)(2,1)}, bf16[2,128,128]{2,1,0:T(8,128)(2,1)S(1)}, u32[]{:S(2)}, u32[]{:S(2)}) collective-permute-start(bf16[2,128,128]{2,1,0:T(8,128)(2,1)} %get-tuple-element.15), channel_id=1, source_target_pairs={{11,23},{12,22},{13,21},{14,20},{15,19}} | collective-permute-start | bytes 196616 | tf_op jit(solution)/shard_map/ppermute | solution.py:270
  36.7 1.6 %collective-permute-start.8 = (bf16[2,128,128]{2,1,0:T(8,128)(2,1)}, bf16[2,128,128]{2,1,0:T(8,128)(2,1)S(1)}, u32[]{:S(2)}, u32[]{:S(2)}) collective-permute-start(bf16[2,128,128]{2,1,0:T(8,128)(2,1)} %get-tuple-element.15), channel_id=1, source_target_pairs={{9,23},{10,22},{11,21},{12,20},{13,19},{14,18},{15,17}} | collective-permute-start | bytes 196616 | tf_op jit(solution)/shard_map/ppermute | solution.py:270
  37.3 0.9 collective-permute-start.9
  38.2 0.6 copy-start.9
  38.3 0.6 copy-start.12
  38.3 0.6 copy-start.15
  38.3 0.7 copy-start.6
  52.8 31.3 %collective-permute-start.11 = (f32[2,128,128]{2,1,0:T(8,128)}, f32[2,128,128]{2,1,0:T(8,128)S(1)}, u32[]{:S(2)}, u32[]{:S(2)}) collective-permute-start(f32[2,128,128]{2,1,0:T(8,128)} %get-tuple-element.16.prev_hbm), channel_id=1, source_target_pairs={{16,31},{17,30},{18,29},{19,28},{20,27},{21,26},{22,25},{23,24}} | collective-permute-start | bytes 393224 | tf_op jit(solution)/shard_map/ppermute | solution.py:270
  54.1 29.2 %collective-permute-start.12 = (bf16[2,128,128]{2,1,0:T(8,128)(2,1)}, bf16[2,128,128]{2,1,0:T(8,128)(2,1)S(1)}, u32[]{:S(2)}, u32[]{:S(2)}) collective-permute-start(bf16[2,128,128]{2,1,0:T(8,128)(2,1)} %get-tuple-element.17), channel_id=1, source_target_pairs={{17,31},{18,30},{19,29},{20,28},{21,27},{22,26},{23,25}} | collective-permute-start | bytes 196616 | tf_op jit(solution)/shard_map/ppermute | solution.py:270
  55.4 28.7 %collective-permute-start.13 = (bf16[2,128,128]{2,1,0:T(8,128)(2,1)}, bf16[2,128,128]{2,1,0:T(8,128)(2,1)S(1)}, u32[]{:S(2)}, u32[]{:S(2)}) collective-permute-start(bf16[2,128,128]{2,1,0:T(8,128)(2,1)} %get-tuple-element.17), channel_id=1, source_target_pairs={{18,31},{19,30},{20,29},{21,28},{22,27},{23,26}} | collective-permute-start | bytes 196616 | tf_op jit(solution)/shard_map/ppermute | solution.py:270
  56.7 27.4 %collective-permute-start.14 = (bf16[2,128,128]{2,1,0:T(8,128)(2,1)}, bf16[2,128,128]{2,1,0:T(8,128)(2,1)S(1)}, u32[]{:S(2)}, u32[]{:S(2)}) collective-permute-start(bf16[2,128,128]{2,1,0:T(8,128)(2,1)} %get-tuple-element.17), channel_id=1, source_target_pairs={{19,31},{20,30},{21,29},{22,28},{23,27}} | collective-permute-start | bytes 196616 | tf_op jit(solution)/shard_map/ppermute | solution.py:270
  83.4 0.8 copy-start.7
  84.1 0.6 copy-start.10
  84.1 0.6 copy-start.13
  84.1 0.7 copy-start.4

commit v6 on v4

--- a/solution.py
+++ b/solution.py
@@ -20,7 +20,7 @@
     scale = HEAD_DIM ** (-0.5)
     heads = heads_all // HEAD_DIM
 
-    def kernel(own_ref, back1_ref, back2_ref, edge_ref, mask_ref, ga_ref, gb_ref,
+    def kernel(keep_ref, prev_ref, own_ref, back1_ref, back2_ref, edge_ref, mask_ref, ga_ref, gb_ref,
                embed_hbm, attn_hbm, mix_hbm, read_hbm,
                out_ref, outb_ref,
                embed_v, attn_v, mix_v, read_v, sems,
@@ -129,7 +129,7 @@
                 own = (parts[0] + parts[1]) + parts[2]
             rows_m = slice(m * rows, (m + 1) * rows)
             result = (own - shift_mean[rows_m]) * jnp.exp(-log_scale[rows_m])
-            out_ref[m] = result
+            out_ref[m] = jnp.where(keep_ref[0] > 0, result, prev_ref[m])
             outb_ref[m] = result.astype(jnp.bfloat16)
 
     width = heads_all
@@ -143,7 +143,8 @@
             jax.ShapeDtypeStruct((micro, rows, width_in), jnp.float32),
             jax.ShapeDtypeStruct((micro, rows, width_in), jnp.bfloat16),
         ),
-        in_specs=[pl.BlockSpec(memory_space=vmem)] * 7 + [pl.BlockSpec(memory_space=pl.ANY)] * 4,
+        in_specs=[pl.BlockSpec(memory_space=pltpu.SMEM)] + [pl.BlockSpec(memory_space=vmem)] * 8
+        + [pl.BlockSpec(memory_space=pl.ANY)] * 4,
         out_specs=(pl.BlockSpec(memory_space=vmem), pl.BlockSpec(memory_space=vmem)),
         scratch_shapes=[
             vmem((width_in, width), jnp.bfloat16),
@@ -247,10 +248,10 @@
     out = jnp.zeros((micro, rows, width_in), jnp.float32)
     for turn in range(n_seg):
         call = first_call if turn == 0 else later_call
-        result, result_low = call(*inputs, mask, *weights)
-        out = jnp.where(segment == turn, result, out)
+        keep = (segment == turn).astype(jnp.int32).reshape(1)
+        out, result_low = call(keep, out, *inputs, mask, *weights)
         if turn + 1 < n_seg:
-            inputs = next_inputs(result, result_low, turn)
+            inputs = next_inputs(out, result_low, turn)
     return out[None]
 
 

time: 93.7 us -> 90.6 us (0.967)
  local copies, waits for them, and re-layouts: 4.85 us -> 3.02 us
  other arithmetic: 2.48 us -> 0.89 us
    unnamed x38 -> x32, local copies, waits for them, and re-layouts: 4.58 us -> 2.01 us
    broadcast_in_dim x1 -> x0, other arithmetic: 1.6 us -> none  [body(): return out[None]]
where the time goes in v6:
time: 90.6 us; the launch traced here: 89.5 us
  Pallas kernels  45.9 us (51%)
  waiting for transfers between devices  25.8 us (28%)
  starting transfers between devices  13.3 us (15%)
  local copies, waits for them, and re-layouts  3.02 us (3%)
    pallas_call x4, Pallas kernels, body(): out, result_low = call(keep, out, *inputs, mask, *weights)  45.9 us
    ppermute x12, waiting for transfers between devices, send(): return lax.ppermute(block, axes, pairs)  25.8 us
    ppermute x12, starting transfers between devices, send(): return lax.ppermute(block, axes, pairs)  11.2 us
    ppermute x3, starting transfers between devices, behind(): return lax.ppermute(patches, axes, pairs)  2.13 us
    unnamed x32, local copies, waits for them, and re-layouts  2.01 us
  transfers between devices with their start and end apart: 15, of which 2 were waited for; matrix products, arithmetic and copies ran while one was open for 1% of the time, Pallas kernels for 0%

profile of v6, /device:TPU:15, one launch (start us, length us, event | category | flops | bytes accessed | tf_op | source)
XLA Modules:
  0.0 89.5 jit_solution(15171611529307017187)
XLA Ops:
  0.0 0.8 collective-permute-start
  0.8 0.7 collective-permute-start.1
  1.5 0.7 collective-permute-start.2
  2.2 0.2 dynamic-slice_reduce_fusion
  2.4 0.1 compare_reduce_fusion
  2.5 0.1 broadcast_bitcast_fusion
  2.6 0.8 fusion.1.mask_ref
  3.4 0.7 broadcast_in_dim.6.prev_ref
  4.1 11.5 %shard_map.82 = (f32[2,128,128]{2,1,0:T(8,128)}, bf16[2,128,128]{2,1,0:T(8,128)(2,1)}) custom-call(s32[1]{0:T(128)} %bitcast.3.keep_ref, f32[2,128,128]{2,1,0:T(8,128)} %broadcast_in_dim.6.prev_ref, f32[2,128,128]{2,1,0:T(8,128)} %own_ref.1, f32[2,128,128]{2,1,0:T(8,128)} %copy-done.1, f32[2,128,128]{2,1,0:T(8,128)} %copy-done.2, f32[2,128,128]{2,1,0:T(8,128)} %copy-done.3, ...), custom_call_target="tpu_custom_call" | custom-call | flops 5033164800 | bytes 9633792 | tf_op jit(solution)/shard_map/pallas_call | solution.py:252
  15.6 0.7 collective-permute-start.3
  16.3 0.7 collective-permute-start.4
  17.0 0.7 collective-permute-start.5
  17.7 0.8 collective-permute-start.6
  18.6 0.5 copy-done.8
  19.1 0.0 copy-done.11
  19.3 11.5 %shard_map.83 = (f32[2,128,128]{2,1,0:T(8,128)}, bf16[2,128,128]{2,1,0:T(8,128)(2,1)}) custom-call(s32[1]{0:T(128)} %bitcast.2.keep_ref, f32[2,128,128]{2,1,0:T(8,128)} %get-tuple-element.12.prev_ref, f32[2,128,128]{2,1,0:T(8,128)} %copy-done.5, bf16[2,128,128]{2,1,0:T(8,128)(2,1)} %copy-done.8, bf16[2,128,128]{2,1,0:T(8,128)(2,1)} %copy-done.11, ...), custom_call_target="tpu_custom_call" | custom-call | flops 5033164800 | bytes 9633792 | tf_op jit(solution)/shard_map/pallas_call | solution.py:252
  30.7 0.7 collective-permute-start.7
  31.4 0.7 collective-permute-start.10
  32.1 0.7 collective-permute-start.8
  32.8 0.9 collective-permute-start.9
  33.7 0.6 copy-done.9
  34.3 0.0 copy-done.6
  34.4 11.4 %shard_map.84 = (f32[2,128,128]{2,1,0:T(8,128)}, bf16[2,128,128]{2,1,0:T(8,128)(2,1)}) custom-call(s32[1]{0:T(128)} %bitcast.1.keep_ref, f32[2,128,128]{2,1,0:T(8,128)} %get-tuple-element.14.prev_ref, f32[2,128,128]{2,1,0:T(8,128)} %copy-done.6, bf16[2,128,128]{2,1,0:T(8,128)(2,1)} %copy-done.12, bf16[2,128,128]{2,1,0:T(8,128)(2,1)} %copy-done.15, ...), custom_call_target="tpu_custom_call" | custom-call | flops 5033164800 | bytes 9633792 | tf_op jit(solution)/shard_map/pallas_call | solution.py:252
  45.8 1.3 %collective-permute-start.11 = (f32[2,128,128]{2,1,0:T(8,128)}, f32[2,128,128]{2,1,0:T(8,128)S(1)}, u32[]{:S(2)}, u32[]{:S(2)}) collective-permute-start(f32[2,128,128]{2,1,0:T(8,128)} %get-tuple-element.16.prev_ref), channel_id=1, source_target_pairs={{16,31},{17,30},{18,29},{19,28},{20,27},{21,26},{22,25},{23,24}} | collective-permute-start | bytes 393224 | tf_op jit(solution)/shard_map/ppermute | solution.py:238
  47.1 1.3 %collective-permute-start.12 = (bf16[2,128,128]{2,1,0:T(8,128)(2,1)}, bf16[2,128,128]{2,1,0:T(8,128)(2,1)S(1)}, u32[]{:S(2)}, u32[]{:S(2)}) collective-permute-start(bf16[2,128,128]{2,1,0:T(8,128)(2,1)} %get-tuple-element.17), channel_id=1, source_target_pairs={{17,31},{18,30},{19,29},{20,28},{21,27},{22,26},{23,25}} | collective-permute-start | bytes 196616 | tf_op jit(solution)/shard_map/ppermute | solution.py:238
  48.4 1.3 %collective-permute-start.13 = (bf16[2,128,128]{2,1,0:T(8,128)(2,1)}, bf16[2,128,128]{2,1,0:T(8,128)(2,1)S(1)}, u32[]{:S(2)}, u32[]{:S(2)}) collective-permute-start(bf16[2,128,128]{2,1,0:T(8,128)(2,1)} %get-tuple-element.17), channel_id=1, source_target_pairs={{18,31},{19,30},{20,29},{21,28},{22,27},{23,26}} | collective-permute-start | bytes 196616 | tf_op jit(solution)/shard_map/ppermute | solution.py:238
  49.7 1.6 %collective-permute-start.14 = (bf16[2,128,128]{2,1,0:T(8,128)(2,1)}, bf16[2,128,128]{2,1,0:T(8,128)(2,1)S(1)}, u32[]{:S(2)}, u32[]{:S(2)}) collective-permute-start(bf16[2,128,128]{2,1,0:T(8,128)(2,1)} %get-tuple-element.17), channel_id=1, source_target_pairs={{19,31},{20,30},{21,29},{22,28},{23,27}} | collective-permute-start | bytes 196616 | tf_op jit(solution)/shard_map/ppermute | solution.py:238
  51.3 25.0 %collective-permute-done.12.back1_ref = bf16[2,128,128]{2,1,0:T(8,128)(2,1)S(1)} collective-permute-done((bf16[2,128,128]{2,1,0:T(8,128)(2,1)}, bf16[2,128,128]{2,1,0:T(8,128)(2,1)S(1)}, u32[]{:S(2)}, u32[]{:S(2)}) %collective-permute-start.12) | collective-permute-done | bytes 65568 | tf_op jit(solution)/shard_map/ppermute | solution.py:238
  76.3 0.8 collective-permute-done.13.back2_ref
  77.1 0.6 copy-done.10
  77.8 0.0 copy-done.4
  77.8 11.4 %shard_map.85 = (f32[2,128,128]{2,1,0:T(8,128)}, bf16[2,128,128]{2,1,0:T(8,128)(2,1)}) custom-call(s32[1]{0:T(128)} %bitcast.keep_ref, f32[2,128,128]{2,1,0:T(8,128)} %get-tuple-element.16.prev_ref, f32[2,128,128]{2,1,0:T(8,128)} %copy-done.4, bf16[2,128,128]{2,1,0:T(8,128)(2,1)} %copy-done.7, bf16[2,128,128]{2,1,0:T(8,128)(2,1)} %copy-done.10, ...), custom_call_target="tpu_custom_call" | custom-call | flops 5033164800 | bytes 9633792 | tf_op jit(solution)/shard_map/pallas_call | solution.py:252
  (42 shorter events, 0.2 us)
Async XLA Ops:
  0.0 2.2 %copy-start = (s32[8,4]{0,1:T(4,128)S(1)}, s32[8,4]{0,1:T(4,128)}, u32[]{:S(2)}) copy-start(s32[8,4]{0,1:T(4,128)} %param.9) | copy-start | bytes 388
  0.0 3.3 %collective-permute-start = (f32[2,128,128]{2,1,0:T(8,128)}, f32[2,128,128]{2,1,0:T(8,128)S(1)}, u32[]{:S(2)}, u32[]{:S(2)}) collective-permute-start(f32[2,128,128]{2,1,0:T(8,128)} %own_ref.1), channel_id=1, source_target_pairs={{0,1},{1,2},{2,3},{3,4},{4,5},{5,6},{6,7}} | collective-permute-start | bytes 393224 | tf_op jit(solution)/shard_map/ppermute | solution.py:224
  0.8 2.6 %collective-permute-start.1 = (f32[2,128,128]{2,1,0:T(8,128)}, f32[2,128,128]{2,1,0:T(8,128)S(1)}, u32[]{:S(2)}, u32[]{:S(2)}) collective-permute-start(f32[2,128,128]{2,1,0:T(8,128)} %own_ref.1), channel_id=1, source_target_pairs={{0,2},{1,3},{2,4},{3,5},{4,6},{5,7}} | collective-permute-start | bytes 393224 | tf_op jit(solution)/shard_map/ppermute | solution.py:224
  1.5 1.9 %collective-permute-start.2 = (f32[2,128,128]{2,1,0:T(8,128)}, f32[2,128,128]{2,1,0:T(8,128)S(1)}, u32[]{:S(2)}, u32[]{:S(2)}) collective-permute-start(f32[2,128,128]{2,1,0:T(8,128)} %own_ref.1), channel_id=1, source_target_pairs={{0,3},{1,4},{2,5},{3,6},{4,7}} | collective-permute-start | bytes 393224 | tf_op jit(solution)/shard_map/ppermute | solution.py:224
  3.3 0.8 copy-start.1
  3.4 0.8 copy-start.2
  3.4 0.8 copy-start.3
  15.6 2.9 %collective-permute-start.3 = (f32[2,128,128]{2,1,0:T(8,128)}, f32[2,128,128]{2,1,0:T(8,128)S(1)}, u32[]{:S(2)}, u32[]{:S(2)}) collective-permute-start(f32[2,128,128]{2,1,0:T(8,128)} %get-tuple-element.12.prev_ref), channel_id=1, source_target_pairs={{0,15},{1,14},{2,13},{3,12},{4,11},{5,10},{6,9},{7,8}} | collective-permute-start | bytes 393224 | tf_op jit(solution)/shard_map/ppermute | solution.py:238
  16.3 2.2 %collective-permute-start.4 = (bf16[2,128,128]{2,1,0:T(8,128)(2,1)}, bf16[2,128,128]{2,1,0:T(8,128)(2,1)S(1)}, u32[]{:S(2)}, u32[]{:S(2)}) collective-permute-start(bf16[2,128,128]{2,1,0:T(8,128)(2,1)} %get-tuple-element.13), channel_id=1, source_target_pairs={{1,15},{2,14},{3,13},{4,12},{5,11},{6,10},{7,9}} | collective-permute-start | bytes 196616 | tf_op jit(solution)/shard_map/ppermute | solution.py:238
  17.0 1.6 %collective-permute-start.5 = (bf16[2,128,128]{2,1,0:T(8,128)(2,1)}, bf16[2,128,128]{2,1,0:T(8,128)(2,1)S(1)}, u32[]{:S(2)}, u32[]{:S(2)}) collective-permute-start(bf16[2,128,128]{2,1,0:T(8,128)(2,1)} %get-tuple-element.13), channel_id=1, source_target_pairs={{2,15},{3,14},{4,13},{5,12},{6,11},{7,10}} | collective-permute-start | bytes 196616 | tf_op jit(solution)/shard_map/ppermute | solution.py:238
  17.7 0.9 %collective-permute-start.6 = (bf16[2,128,128]{2,1,0:T(8,128)(2,1)}, bf16[2,128,128]{2,1,0:T(8,128)(2,1)S(1)}, u32[]{:S(2)}, u32[]{:S(2)}) collective-permute-start(bf16[2,128,128]{2,1,0:T(8,128)(2,1)} %get-tuple-element.13), channel_id=1, source_target_pairs={{3,15},{4,14},{5,13},{6,12},{7,11}} | collective-permute-start | bytes 196616 | tf_op jit(solution)/shard_map/ppermute | solution.py:238
  18.5 0.6 copy-start.8
  18.6 0.6 copy-start.11
  18.6 0.6 copy-start.14
  18.6 0.7 copy-start.5
  30.7 3.0 %collective-permute-start.7 = (f32[2,128,128]{2,1,0:T(8,128)}, f32[2,128,128]{2,1,0:T(8,128)S(1)}, u32[]{:S(2)}, u32[]{:S(2)}) collective-permute-start(f32[2,128,128]{2,1,0:T(8,128)} %get-tuple-element.14.prev_ref), channel_id=1, source_target_pairs={{8,23},{9,22},{10,21},{11,20},{12,19},{13,18},{14,17},{15,16}} | collective-permute-start | bytes 393224 | tf_op jit(solution)/shard_map/ppermute | solution.py:238
  31.4 2.2 %collective-permute-start.10 = (bf16[2,128,128]{2,1,0:T(8,128)(2,1)}, bf16[2,128,128]{2,1,0:T(8,128)(2,1)S(1)}, u32[]{:S(2)}, u32[]{:S(2)}) collective-permute-start(bf16[2,128,128]{2,1,0:T(8,128)(2,1)} %get-tuple-element.15), channel_id=1, source_target_pairs={{11,23},{12,22},{13,21},{14,20},{15,19}} | collective-permute-start | bytes 196616 | tf_op jit(solution)/shard_map/ppermute | solution.py:238
  32.1 1.6 %collective-permute-start.8 = (bf16[2,128,128]{2,1,0:T(8,128)(2,1)}, bf16[2,128,128]{2,1,0:T(8,128)(2,1)S(1)}, u32[]{:S(2)}, u32[]{:S(2)}) collective-permute-start(bf16[2,128,128]{2,1,0:T(8,128)(2,1)} %get-tuple-element.15), channel_id=1, source_target_pairs={{9,23},{10,22},{11,21},{12,20},{13,19},{14,18},{15,17}} | collective-permute-start | bytes 196616 | tf_op jit(solution)/shard_map/ppermute | solution.py:238
  32.8 0.9 %collective-permute-start.9 = (bf16[2,128,128]{2,1,0:T(8,128)(2,1)}, bf16[2,128,128]{2,1,0:T(8,128)(2,1)S(1)}, u32[]{:S(2)}, u32[]{:S(2)}) collective-permute-start(bf16[2,128,128]{2,1,0:T(8,128)(2,1)} %get-tuple-element.15), channel_id=1, source_target_pairs={{10,23},{11,22},{12,21},{13,20},{14,19},{15,18}} | collective-permute-start | bytes 196616 | tf_op jit(solution)/shard_map/ppermute | solution.py:238
  33.7 0.6 copy-start.9
  33.7 0.6 copy-start.12
  33.7 0.6 copy-start.15
  33.7 0.7 copy-start.6
  45.8 31.3 %collective-permute-start.11 = (f32[2,128,128]{2,1,0:T(8,128)}, f32[2,128,128]{2,1,0:T(8,128)S(1)}, u32[]{:S(2)}, u32[]{:S(2)}) collective-permute-start(f32[2,128,128]{2,1,0:T(8,128)} %get-tuple-element.16.prev_ref), channel_id=1, source_target_pairs={{16,31},{17,30},{18,29},{19,28},{20,27},{21,26},{22,25},{23,24}} | collective-permute-start | bytes 393224 | tf_op jit(solution)/shard_map/ppermute | solution.py:238
  47.1 29.2 %collective-permute-start.12 = (bf16[2,128,128]{2,1,0:T(8,128)(2,1)}, bf16[2,128,128]{2,1,0:T(8,128)(2,1)S(1)}, u32[]{:S(2)}, u32[]{:S(2)}) collective-permute-start(bf16[2,128,128]{2,1,0:T(8,128)(2,1)} %get-tuple-element.17), channel_id=1, source_target_pairs={{17,31},{18,30},{19,29},{20,28},{21,27},{22,26},{23,25}} | collective-permute-start | bytes 196616 | tf_op jit(solution)/shard_map/ppermute | solution.py:238
  48.4 28.7 %collective-permute-start.13 = (bf16[2,128,128]{2,1,0:T(8,128)(2,1)}, bf16[2,128,128]{2,1,0:T(8,128)(2,1)S(1)}, u32[]{:S(2)}, u32[]{:S(2)}) collective-permute-start(bf16[2,128,128]{2,1,0:T(8,128)(2,1)} %get-tuple-element.17), channel_id=1, source_target_pairs={{18,31},{19,30},{20,29},{21,28},{22,27},{23,26}} | collective-permute-start | bytes 196616 | tf_op jit(solution)/shard_map/ppermute | solution.py:238
  49.7 27.4 %collective-permute-start.14 = (bf16[2,128,128]{2,1,0:T(8,128)(2,1)}, bf16[2,128,128]{2,1,0:T(8,128)(2,1)S(1)}, u32[]{:S(2)}, u32[]{:S(2)}) collective-permute-start(bf16[2,128,128]{2,1,0:T(8,128)(2,1)} %get-tuple-element.17), channel_id=1, source_target_pairs={{19,31},{20,30},{21,29},{22,28},{23,27}} | collective-permute-start | bytes 196616 | tf_op jit(solution)/shard_map/ppermute | solution.py:238
  76.3 0.8 copy-start.7
  77.1 0.6 copy-start.10
  77.1 0.6 copy-start.13
  77.1 0.7 copy-start.4

commit v7 on v6

--- a/solution.py
+++ b/solution.py
@@ -9,7 +9,8 @@
 TILE = 128
 BACK = 2
 
-CHUNK = 512
+CHUNK = 1024
+VMEM_LIMIT = 24 * 1024 * 1024
 
 
 def make_block_call(micro, rows, width_in, heads_all, mirrored, piece_dtype):
@@ -21,30 +22,9 @@
     heads = heads_all // HEAD_DIM
 
     def kernel(keep_ref, prev_ref, own_ref, back1_ref, back2_ref, edge_ref, mask_ref, ga_ref, gb_ref,
-               embed_hbm, attn_hbm, mix_hbm, read_hbm,
+               embed_v, attn_v, mix_v, read_v,
                out_ref, outb_ref,
-               embed_v, attn_v, mix_v, read_v, sems,
                pieces_s, shifted_s, hidden_s, normed_s, q_s, kv_s, mixed_s, res_s):
-        n_kv = 2 * heads_all // CHUNK
-        kv_copies = [
-            pltpu.make_async_copy(
-                attn_hbm.at[:, heads_all + j * CHUNK:heads_all + (j + 1) * CHUNK],
-                attn_v.at[:, heads_all + j * CHUNK:heads_all + (j + 1) * CHUNK],
-                sems.at[4 + j],
-            )
-            for j in range(n_kv)
-        ]
-        copies = [
-            pltpu.make_async_copy(embed_hbm, embed_v, sems.at[0]),
-            pltpu.make_async_copy(attn_hbm.at[:, :heads_all], attn_v.at[:, :heads_all], sems.at[1]),
-            pltpu.make_async_copy(mix_hbm, mix_v, sems.at[2]),
-            pltpu.make_async_copy(read_hbm, read_v, sems.at[3]),
-        ]
-        copies[0].start()
-        for copy in kv_copies:
-            copy.start()
-        for copy in copies[1:]:
-            copy.start()
         before = lax.broadcasted_iota(jnp.int32, (span, n_in), 0) + (rows - 1)
         column = lax.broadcasted_iota(jnp.int32, (span, n_in), 1)
         if mirrored:
@@ -60,18 +40,16 @@
             shifted_s[m * span:(m + 1) * span, :] = jnp.dot(
                 select, pieces_s[...], preferred_element_type=jnp.float32
             ).astype(jnp.bfloat16)
-        copies[0].wait()
         hidden = jnp.dot(shifted_s[...], embed_v[...], preferred_element_type=jnp.float32)
         hidden_s[...] = hidden
         square = jnp.mean(hidden * hidden, axis=-1, keepdims=True)
         normed_s[...] = (hidden * lax.rsqrt(square + 1e-06) * ga_ref[...]).astype(jnp.bfloat16)
+        n_kv = 2 * heads_all // CHUNK
         for j in range(n_kv):
-            kv_copies[j].wait()
             kv_s[:, j * CHUNK:(j + 1) * CHUNK] = jnp.dot(
                 normed_s[...], attn_v[:, heads_all + j * CHUNK:heads_all + (j + 1) * CHUNK],
                 preferred_element_type=jnp.float32,
             ).astype(jnp.bfloat16)
-        copies[1].wait()
 
         def q_step(j, carry):
             cols = pl.ds(pl.multiple_of(j * CHUNK, CHUNK), CHUNK)
@@ -102,7 +80,6 @@
             for h in range(heads):
                 mixed_s[m * rows:(m + 1) * rows, h * HEAD_DIM:(h + 1) * HEAD_DIM] = mixed[h].astype(jnp.bfloat16)
 
-        copies[2].wait()
         for m in range(micro):
             res_s[m * rows:(m + 1) * rows, :] = hidden_s[m * span + own_at:(m + 1) * span, :] + jnp.dot(
                 mixed_s[m * rows:(m + 1) * rows, :], mix_v[...], preferred_element_type=jnp.float32
@@ -110,7 +87,6 @@
         residual = res_s[...]
         square = jnp.mean(residual * residual, axis=-1, keepdims=True)
         final_normed = (residual * lax.rsqrt(square + 1e-06) * gb_ref[...]).astype(jnp.bfloat16)
-        copies[3].wait()
         raw = jnp.dot(final_normed, read_v[...], preferred_element_type=jnp.float32)
         shift_mean = raw[:, :width_in]
         log_scale = 0.5 * jnp.tanh(raw[:, width_in:])
@@ -143,15 +119,9 @@
             jax.ShapeDtypeStruct((micro, rows, width_in), jnp.float32),
             jax.ShapeDtypeStruct((micro, rows, width_in), jnp.bfloat16),
         ),
-        in_specs=[pl.BlockSpec(memory_space=pltpu.SMEM)] + [pl.BlockSpec(memory_space=vmem)] * 8
-        + [pl.BlockSpec(memory_space=pl.ANY)] * 4,
+        in_specs=[pl.BlockSpec(memory_space=pltpu.SMEM)] + [pl.BlockSpec(memory_space=vmem)] * 12,
         out_specs=(pl.BlockSpec(memory_space=vmem), pl.BlockSpec(memory_space=vmem)),
         scratch_shapes=[
-            vmem((width_in, width), jnp.bfloat16),
-            vmem((width, 3 * heads_all), jnp.bfloat16),
-            vmem((heads_all, width), jnp.bfloat16),
-            vmem((width, 2 * width_in), jnp.bfloat16),
-            pltpu.SemaphoreType.DMA((4 + 2 * heads_all // CHUNK,)),
             vmem((n_in, width_in), jnp.bfloat16),
             vmem((n_rows, width_in), jnp.bfloat16),
             vmem((n_rows, width), jnp.float32),
@@ -161,7 +131,7 @@
             vmem((micro * rows, heads_all), jnp.bfloat16),
             vmem((micro * rows, width), jnp.float32),
         ],
-        compiler_params=pltpu.CompilerParams(vmem_limit_bytes=56 * 1024 * 1024),
+        compiler_params=pltpu.CompilerParams(vmem_limit_bytes=VMEM_LIMIT),
         cost_estimate=pl.CostEstimate(
             flops=flops,
             bytes_accessed=weight_bytes + n_rows * width_in * 2 + 2 * micro * rows * width_in * 4,

time: 90.6 us -> 96.7 us (1.067)
  the two profiles are of different devices: /device:TPU:15 before, /device:TPU:29 now
where the time goes in v7:
time: 96.7 us; the launch traced here: 95.8 us
  Pallas kernels  34 us (35%)
  waiting for transfers between devices  25.9 us (27%)
  local copies, waits for them, and re-layouts  21.7 us (22%)
  starting transfers between devices  13.7 us (14%)
    pallas_call x4, Pallas kernels, body(): out, result_low = call(keep, out, *inputs, mask, *weights)  34 us
    ppermute x12, waiting for transfers between devices, send(): return lax.ppermute(block, axes, pairs)  25.9 us
    unnamed x44, local copies, waits for them, and re-layouts  21.4 us
    ppermute x12, starting transfers between devices, send(): return lax.ppermute(block, axes, pairs)  11.5 us
    ppermute x3, starting transfers between devices, behind(): return lax.ppermute(patches, axes, pairs)  2.13 us
  transfers between devices with their start and end apart: 15, of which 2 were waited for; matrix products, arithmetic and copies ran while one was open for 0% of the time, Pallas kernels for 0%

profile of v7, /device:TPU:29, one launch (start us, length us, event | category | flops | bytes accessed | tf_op | source)
XLA Modules:
  0.0 95.8 jit_solution(9909665798030299343)
XLA Ops:
  0.0 0.8 collective-permute-start
  0.8 0.7 collective-permute-start.1
  1.5 0.7 collective-permute-start.2
  2.7 2.8 %copy-done.1 = bf16[1,1024,3072]{2,1,0:T(8,128)(2,1)S(1)} copy-done((bf16[1,1024,3072]{2,1,0:T(8,128)(2,1)S(1)}, bf16[1,1024,3072]{2,1,0:T(8,128)(2,1)}, u32[]{:S(2)}) %copy-start.1) | copy-done | bytes 6291480
  5.5 1.6 %copy-done.5 = bf16[1,1024,1024]{2,1,0:T(8,128)(2,1)S(1)} copy-done((bf16[1,1024,1024]{2,1,0:T(8,128)(2,1)S(1)}, bf16[1,1024,1024]{2,1,0:T(8,128)(2,1)}, u32[]{:S(2)}) %copy-start.5) | copy-done | bytes 2097176
  7.1 1.0 %copy-done.7 = bf16[1,1024,256]{2,1,0:T(8,128)(2,1)S(1)} copy-done((bf16[1,1024,256]{2,1,0:T(8,128)(2,1)S(1)}, bf16[1,1024,256]{2,1,0:T(8,128)(2,1)}, u32[]{:S(2)}) %copy-start.7) | copy-done | bytes 524312
  8.1 0.9 copy-done.9
  9.1 0.9 copy-done.11
  10.0 0.7 copy-done.18
  10.7 0.7 copy-done.20
  11.4 8.3 %shard_map.82 = (f32[2,128,128]{2,1,0:T(8,128)}, bf16[2,128,128]{2,1,0:T(8,128)(2,1)S(1)}) custom-call(s32[1]{0:T(128)} %bitcast.3.keep_ref, f32[2,128,128]{2,1,0:T(8,128)S(1)} %broadcast_in_dim.6.prev_ref, f32[2,128,128]{2,1,0:T(8,128)S(1)} %copy-done.11, f32[2,128,128]{2,1,0:T(8,128)S(1)} %collective-permute-done.back1_ref, ...), custom_call_target="tpu_custom_call" | custom-call | flops 5033164800 | bytes 9633792 | tf_op jit(solution)/shard_map/pallas_call | solution.py:222
  20.4 0.7 collective-permute-start.4
  21.0 0.7 collective-permute-start.5
  21.7 0.8 collective-permute-start.6
  23.3 2.8 %copy-done.2 = bf16[1,1024,3072]{2,1,0:T(8,128)(2,1)S(1)} copy-done((bf16[1,1024,3072]{2,1,0:T(8,128)(2,1)S(1)}, bf16[1,1024,3072]{2,1,0:T(8,128)(2,1)}, u32[]{:S(2)}) %copy-start.2) | copy-done | bytes 6291480
  26.0 0.8 copy-done.17
  26.9 8.4 %shard_map.83 = (f32[2,128,128]{2,1,0:T(8,128)S(1)}, bf16[2,128,128]{2,1,0:T(8,128)(2,1)S(1)}) custom-call(s32[1]{0:T(128)} %bitcast.2.keep_ref, f32[2,128,128]{2,1,0:T(8,128)} %get-tuple-element.12.prev_ref, f32[2,128,128]{2,1,0:T(8,128)S(1)} %collective-permute-done.3.own_ref, bf16[2,128,128]{2,1,0:T(8,128)(2,1)S(1)} %collective-permute-done.4.back1_ref, ...), custom_call_target="tpu_custom_call" | custom-call | flops 5033164800 | bytes 9633792 | tf_op jit(solution)/shard_map/pallas_call | solution.py:222
  35.3 0.7 collective-permute-start.7
  36.0 0.7 collective-permute-start.10
  37.3 1.3 %collective-permute-start.9 = (bf16[2,128,128]{2,1,0:T(8,128)(2,1)S(1)}, bf16[2,128,128]{2,1,0:T(8,128)(2,1)}, u32[]{:S(2)}, u32[]{:S(2)}) collective-permute-start(bf16[2,128,128]{2,1,0:T(8,128)(2,1)S(1)} %get-tuple-element.15), channel_id=1, source_target_pairs={{10,23},{11,22},{12,21},{13,20},{14,19},{15,18}} | collective-permute-start | bytes 196616 | tf_op jit(solution)/shard_map/ppermute | solution.py:208
  39.9 2.8 %copy-done.3 = bf16[1,1024,3072]{2,1,0:T(8,128)(2,1)S(1)} copy-done((bf16[1,1024,3072]{2,1,0:T(8,128)(2,1)S(1)}, bf16[1,1024,3072]{2,1,0:T(8,128)(2,1)}, u32[]{:S(2)}) %copy-start.3) | copy-done | bytes 6291480
  42.6 0.8 copy-done.13
  43.5 0.8 copy-done.15
  44.3 8.3 %shard_map.84 = (f32[2,128,128]{2,1,0:T(8,128)S(1)}, bf16[2,128,128]{2,1,0:T(8,128)(2,1)S(1)}) custom-call(s32[1]{0:T(128)} %bitcast.1.keep_ref, f32[2,128,128]{2,1,0:T(8,128)S(1)} %get-tuple-element.14.prev_ref, f32[2,128,128]{2,1,0:T(8,128)S(1)} %collective-permute-done.7.own_ref, bf16[2,128,128]{2,1,0:T(8,128)(2,1)S(1)} %copy-done.15, ...), custom_call_target="tpu_custom_call" | custom-call | flops 5033164800 | bytes 9633792 | tf_op jit(solution)/shard_map/pallas_call | solution.py:222
  52.7 1.3 %collective-permute-start.11 = (f32[2,128,128]{2,1,0:T(8,128)S(1)}, f32[2,128,128]{2,1,0:T(8,128)S(1)}, u32[]{:S(2)}, u32[]{:S(2)}) collective-permute-start(f32[2,128,128]{2,1,0:T(8,128)S(1)} %get-tuple-element.16.prev_ref), channel_id=1, source_target_pairs={{16,31},{17,30},{18,29},{19,28},{20,27},{21,26},{22,25},{23,24}} | collective-permute-start | bytes 393224 | tf_op jit(solution)/shard_map/ppermute | solution.py:208
  54.0 1.3 %collective-permute-start.12 = (bf16[2,128,128]{2,1,0:T(8,128)(2,1)S(1)}, bf16[2,128,128]{2,1,0:T(8,128)(2,1)S(1)}, u32[]{:S(2)}, u32[]{:S(2)}) collective-permute-start(bf16[2,128,128]{2,1,0:T(8,128)(2,1)S(1)} %get-tuple-element.17), channel_id=1, source_target_pairs={{17,31},{18,30},{19,29},{20,28},{21,27},{22,26},{23,25}} | collective-permute-start | bytes 196616 | tf_op jit(solution)/shard_map/ppermute | solution.py:208
  55.3 1.3 %collective-permute-start.13 = (bf16[2,128,128]{2,1,0:T(8,128)(2,1)S(1)}, bf16[2,128,128]{2,1,0:T(8,128)(2,1)S(1)}, u32[]{:S(2)}, u32[]{:S(2)}) collective-permute-start(bf16[2,128,128]{2,1,0:T(8,128)(2,1)S(1)} %get-tuple-element.17), channel_id=1, source_target_pairs={{18,31},{19,30},{20,29},{21,28},{22,27},{23,26}} | collective-permute-start | bytes 196616 | tf_op jit(solution)/shard_map/ppermute | solution.py:208
  56.6 1.6 %collective-permute-start.14 = (bf16[2,128,128]{2,1,0:T(8,128)(2,1)S(1)}, bf16[2,128,128]{2,1,0:T(8,128)(2,1)}, u32[]{:S(2)}, u32[]{:S(2)}) collective-permute-start(bf16[2,128,128]{2,1,0:T(8,128)(2,1)S(1)} %get-tuple-element.17), channel_id=1, source_target_pairs={{19,31},{20,30},{21,29},{22,28},{23,27}} | collective-permute-start | bytes 196616 | tf_op jit(solution)/shard_map/ppermute | solution.py:208
  58.1 23.0 %collective-permute-done.12.back1_ref = bf16[2,128,128]{2,1,0:T(8,128)(2,1)S(1)} collective-permute-done((bf16[2,128,128]{2,1,0:T(8,128)(2,1)S(1)}, bf16[2,128,128]{2,1,0:T(8,128)(2,1)S(1)}, u32[]{:S(2)}, u32[]{:S(2)}) %collective-permute-start.12) | collective-permute-done | bytes 65568 | tf_op jit(solution)/shard_map/ppermute | solution.py:208
  81.1 2.9 %collective-permute-done.13.back2_ref = bf16[2,128,128]{2,1,0:T(8,128)(2,1)S(1)} collective-permute-done((bf16[2,128,128]{2,1,0:T(8,128)(2,1)S(1)}, bf16[2,128,128]{2,1,0:T(8,128)(2,1)S(1)}, u32[]{:S(2)}, u32[]{:S(2)}) %collective-permute-start.13) | collective-permute-done | bytes 65568 | tf_op jit(solution)/shard_map/ppermute | solution.py:208
  84.0 2.8 %copy-done.4 = bf16[1,1024,3072]{2,1,0:T(8,128)(2,1)S(1)} copy-done((bf16[1,1024,3072]{2,1,0:T(8,128)(2,1)S(1)}, bf16[1,1024,3072]{2,1,0:T(8,128)(2,1)}, u32[]{:S(2)}) %copy-start.4) | copy-done | bytes 6291480
  86.8 9.0 %shard_map.85 = (f32[2,128,128]{2,1,0:T(8,128)}, bf16[2,128,128]{2,1,0:T(8,128)(2,1)}) custom-call(s32[1]{0:T(128)} %bitcast.keep_ref, f32[2,128,128]{2,1,0:T(8,128)S(1)} %get-tuple-element.16.prev_ref, f32[2,128,128]{2,1,0:T(8,128)S(1)} %collective-permute-done.11.own_ref, bf16[2,128,128]{2,1,0:T(8,128)(2,1)S(1)} %collective-permute-done.12.back1_ref, ...), custom_call_target="tpu_custom_call" | custom-call | flops 5033164800 | bytes 9633792 | tf_op jit(solution)/shard_map/pallas_call | solution.py:222
  (54 shorter events, 3.7 us)
Async XLA Ops:
  0.0 2.2 %copy-start = (s32[8,4]{0,1:T(4,128)S(1)}, s32[8,4]{0,1:T(4,128)}, u32[]{:S(2)}) copy-start(s32[8,4]{0,1:T(4,128)} %param.9) | copy-start | bytes 388
  0.0 2.7 %collective-permute-start = (f32[2,128,128]{2,1,0:T(8,128)}, f32[2,128,128]{2,1,0:T(8,128)S(1)}, u32[]{:S(2)}, u32[]{:S(2)}) collective-permute-start(f32[2,128,128]{2,1,0:T(8,128)} %own_ref.1), channel_id=1, source_target_pairs={{0,1},{1,2},{2,3},{3,4},{4,5},{5,6},{6,7}} | collective-permute-start | bytes 393224 | tf_op jit(solution)/shard_map/ppermute | solution.py:194
  0.8 1.9 %collective-permute-start.1 = (f32[2,128,128]{2,1,0:T(8,128)}, f32[2,128,128]{2,1,0:T(8,128)S(1)}, u32[]{:S(2)}, u32[]{:S(2)}) collective-permute-start(f32[2,128,128]{2,1,0:T(8,128)} %own_ref.1), channel_id=1, source_target_pairs={{0,2},{1,3},{2,4},{3,5},{4,6},{5,7}} | collective-permute-start | bytes 393224 | tf_op jit(solution)/shard_map/ppermute | solution.py:194
  1.5 1.2 %collective-permute-start.2 = (f32[2,128,128]{2,1,0:T(8,128)}, f32[2,128,128]{2,1,0:T(8,128)S(1)}, u32[]{:S(2)}, u32[]{:S(2)}) collective-permute-start(f32[2,128,128]{2,1,0:T(8,128)} %own_ref.1), channel_id=1, source_target_pairs={{0,3},{1,4},{2,5},{3,6},{4,7}} | collective-permute-start | bytes 393224 | tf_op jit(solution)/shard_map/ppermute | solution.py:194
  2.7 2.8 %copy-start.1 = (bf16[1,1024,3072]{2,1,0:T(8,128)(2,1)S(1)}, bf16[1,1024,3072]{2,1,0:T(8,128)(2,1)}, u32[]{:S(2)}) copy-start(bf16[1,1024,3072]{2,1,0:T(8,128)(2,1)} %param.11) | copy-start | bytes 18874372
  5.5 1.6 %copy-start.5 = (bf16[1,1024,1024]{2,1,0:T(8,128)(2,1)S(1)}, bf16[1,1024,1024]{2,1,0:T(8,128)(2,1)}, u32[]{:S(2)}) copy-start(bf16[1,1024,1024]{2,1,0:T(8,128)(2,1)} %param.12) | copy-start | bytes 6291460
  7.1 1.0 %copy-start.7 = (bf16[1,1024,256]{2,1,0:T(8,128)(2,1)S(1)}, bf16[1,1024,256]{2,1,0:T(8,128)(2,1)}, u32[]{:S(2)}) copy-start(bf16[1,1024,256]{2,1,0:T(8,128)(2,1)} %param.13) | copy-start | bytes 1572868
  8.1 0.9 copy-start.9
  9.1 0.9 copy-start.11
  11.4 11.8 %copy-start.6 = (bf16[1,1024,1024]{2,1,0:T(8,128)(2,1)S(1)}, bf16[1,1024,1024]{2,1,0:T(8,128)(2,1)}, u32[]{:S(2)}) copy-start(bf16[1,1024,1024]{2,1,0:T(8,128)(2,1)} %param.12) | copy-start | bytes 6291460
  11.4 11.8 %copy-start.8 = (bf16[1,1024,256]{2,1,0:T(8,128)(2,1)S(1)}, bf16[1,1024,256]{2,1,0:T(8,128)(2,1)}, u32[]{:S(2)}) copy-start(bf16[1,1024,256]{2,1,0:T(8,128)(2,1)} %param.13) | copy-start | bytes 1572868
  11.4 11.9 %copy-start.10 = (bf16[1,128,1024]{2,1,0:T(8,128)(2,1)S(1)}, bf16[1,128,1024]{2,1,0:T(8,128)(2,1)}, u32[]{:S(2)}) copy-start(bf16[1,128,1024]{2,1,0:T(8,128)(2,1)} %param.10) | copy-start | bytes 786436
  11.4 11.9 %copy-start.19 = (f32[1,1024]{1,0:T(1,128)S(1)}, f32[1,1024]{1,0:T(1,128)}, u32[]{:S(2)}) copy-start(f32[1,1024]{1,0:T(1,128)} %ga_ref.7) | copy-start | bytes 12292
  11.4 11.9 %copy-start.21 = (f32[1,1024]{1,0:T(1,128)S(1)}, f32[1,1024]{1,0:T(1,128)}, u32[]{:S(2)}) copy-start(f32[1,1024]{1,0:T(1,128)} %gb_ref.7) | copy-start | bytes 12292
  19.7 3.5 %collective-permute-start.3 = (f32[2,128,128]{2,1,0:T(8,128)}, f32[2,128,128]{2,1,0:T(8,128)S(1)}, u32[]{:S(2)}, u32[]{:S(2)}) collective-permute-start(f32[2,128,128]{2,1,0:T(8,128)} %get-tuple-element.12.prev_ref), channel_id=1, source_target_pairs={{0,15},{1,14},{2,13},{3,12},{4,11},{5,10},{6,9},{7,8}} | collective-permute-start | bytes 393224 | tf_op jit(solution)/shard_map/ppermute | solution.py:208
  20.4 2.2 %collective-permute-start.4 = (bf16[2,128,128]{2,1,0:T(8,128)(2,1)S(1)}, bf16[2,128,128]{2,1,0:T(8,128)(2,1)S(1)}, u32[]{:S(2)}, u32[]{:S(2)}) collective-permute-start(bf16[2,128,128]{2,1,0:T(8,128)(2,1)S(1)} %get-tuple-element.13), channel_id=1, source_target_pairs={{1,15},{2,14},{3,13},{4,12},{5,11},{6,10},{7,9}} | collective-permute-start | bytes 196616 | tf_op jit(solution)/shard_map/ppermute | solution.py:208
  21.0 1.5 %collective-permute-start.5 = (bf16[2,128,128]{2,1,0:T(8,128)(2,1)S(1)}, bf16[2,128,128]{2,1,0:T(8,128)(2,1)S(1)}, u32[]{:S(2)}, u32[]{:S(2)}) collective-permute-start(bf16[2,128,128]{2,1,0:T(8,128)(2,1)S(1)} %get-tuple-element.13), channel_id=1, source_target_pairs={{2,15},{3,14},{4,13},{5,12},{6,11},{7,10}} | collective-permute-start | bytes 196616 | tf_op jit(solution)/shard_map/ppermute | solution.py:208
  21.7 0.9 collective-permute-start.6
  23.2 2.8 %copy-start.2 = (bf16[1,1024,3072]{2,1,0:T(8,128)(2,1)S(1)}, bf16[1,1024,3072]{2,1,0:T(8,128)(2,1)}, u32[]{:S(2)}) copy-start(bf16[1,1024,3072]{2,1,0:T(8,128)(2,1)} %param.11) | copy-start | bytes 18874372
  26.0 0.8 copy-start.17
  35.3 4.6 %collective-permute-start.7 = (f32[2,128,128]{2,1,0:T(8,128)S(1)}, f32[2,128,128]{2,1,0:T(8,128)S(1)}, u32[]{:S(2)}, u32[]{:S(2)}) collective-permute-start(f32[2,128,128]{2,1,0:T(8,128)S(1)} %get-tuple-element.14.prev_ref), channel_id=1, source_target_pairs={{8,23},{9,22},{10,21},{11,20},{12,19},{13,18},{14,17},{15,16}} | collective-permute-start | bytes 393224 | tf_op jit(solution)/shard_map/ppermute | solution.py:208
  36.0 2.6 %collective-permute-start.10 = (bf16[2,128,128]{2,1,0:T(8,128)(2,1)S(1)}, bf16[2,128,128]{2,1,0:T(8,128)(2,1)S(1)}, u32[]{:S(2)}, u32[]{:S(2)}) collective-permute-start(bf16[2,128,128]{2,1,0:T(8,128)(2,1)S(1)} %get-tuple-element.15), channel_id=1, source_target_pairs={{11,23},{12,22},{13,21},{14,20},{15,19}} | collective-permute-start | bytes 196616 | tf_op jit(solution)/shard_map/ppermute | solution.py:208
  36.6 2.6 %collective-permute-start.8 = (bf16[2,128,128]{2,1,0:T(8,128)(2,1)S(1)}, bf16[2,128,128]{2,1,0:T(8,128)(2,1)S(1)}, u32[]{:S(2)}, u32[]{:S(2)}) collective-permute-start(bf16[2,128,128]{2,1,0:T(8,128)(2,1)S(1)} %get-tuple-element.15), channel_id=1, source_target_pairs={{9,23},{10,22},{11,21},{12,20},{13,19},{14,18},{15,17}} | collective-permute-start | bytes 196616 | tf_op jit(solution)/shard_map/ppermute | solution.py:208
  37.3 2.5 %collective-permute-start.9 = (bf16[2,128,128]{2,1,0:T(8,128)(2,1)S(1)}, bf16[2,128,128]{2,1,0:T(8,128)(2,1)}, u32[]{:S(2)}, u32[]{:S(2)}) collective-permute-start(bf16[2,128,128]{2,1,0:T(8,128)(2,1)S(1)} %get-tuple-element.15), channel_id=1, source_target_pairs={{10,23},{11,22},{12,21},{13,20},{14,19},{15,18}} | collective-permute-start | bytes 196616 | tf_op jit(solution)/shard_map/ppermute | solution.py:208
  39.9 2.8 %copy-start.3 = (bf16[1,1024,3072]{2,1,0:T(8,128)(2,1)S(1)}, bf16[1,1024,3072]{2,1,0:T(8,128)(2,1)}, u32[]{:S(2)}) copy-start(bf16[1,1024,3072]{2,1,0:T(8,128)(2,1)} %param.11) | copy-start | bytes 18874372
  42.6 0.8 copy-start.13
  43.5 0.8 copy-start.15
  52.7 31.4 %collective-permute-start.11 = (f32[2,128,128]{2,1,0:T(8,128)S(1)}, f32[2,128,128]{2,1,0:T(8,128)S(1)}, u32[]{:S(2)}, u32[]{:S(2)}) collective-permute-start(f32[2,128,128]{2,1,0:T(8,128)S(1)} %get-tuple-element.16.prev_ref), channel_id=1, source_target_pairs={{16,31},{17,30},{18,29},{19,28},{20,27},{21,26},{22,25},{23,24}} | collective-permute-start | bytes 393224 | tf_op jit(solution)/shard_map/ppermute | solution.py:208
  54.0 27.1 %collective-permute-start.12 = (bf16[2,128,128]{2,1,0:T(8,128)(2,1)S(1)}, bf16[2,128,128]{2,1,0:T(8,128)(2,1)S(1)}, u32[]{:S(2)}, u32[]{:S(2)}) collective-permute-start(bf16[2,128,128]{2,1,0:T(8,128)(2,1)S(1)} %get-tuple-element.17), channel_id=1, source_target_pairs={{17,31},{18,30},{19,29},{20,28},{21,27},{22,26},{23,25}} | collective-permute-start | bytes 196616 | tf_op jit(solution)/shard_map/ppermute | solution.py:208
  55.3 28.8 %collective-permute-start.13 = (bf16[2,128,128]{2,1,0:T(8,128)(2,1)S(1)}, bf16[2,128,128]{2,1,0:T(8,128)(2,1)S(1)}, u32[]{:S(2)}, u32[]{:S(2)}) collective-permute-start(bf16[2,128,128]{2,1,0:T(8,128)(2,1)S(1)} %get-tuple-element.17), channel_id=1, source_target_pairs={{18,31},{19,30},{20,29},{21,28},{22,27},{23,26}} | collective-permute-start | bytes 196616 | tf_op jit(solution)/shard_map/ppermute | solution.py:208
  56.6 27.5 %collective-permute-start.14 = (bf16[2,128,128]{2,1,0:T(8,128)(2,1)S(1)}, bf16[2,128,128]{2,1,0:T(8,128)(2,1)}, u32[]{:S(2)}, u32[]{:S(2)}) collective-permute-start(bf16[2,128,128]{2,1,0:T(8,128)(2,1)S(1)} %get-tuple-element.17), channel_id=1, source_target_pairs={{19,31},{20,30},{21,29},{22,28},{23,27}} | collective-permute-start | bytes 196616 | tf_op jit(solution)/shard_map/ppermute | solution.py:208
  84.0 2.8 %copy-start.4 = (bf16[1,1024,3072]{2,1,0:T(8,128)(2,1)S(1)}, bf16[1,1024,3072]{2,1,0:T(8,128)(2,1)}, u32[]{:S(2)}) copy-start(bf16[1,1024,3072]{2,1,0:T(8,128)(2,1)} %param.11) | copy-start | bytes 18874372
  (5 other events, 3.2 us)

commit v8 on v6

--- a/solution.py
+++ b/solution.py
@@ -9,7 +9,7 @@
 TILE = 128
 BACK = 2
 
-CHUNK = 512
+CHUNK = 1024
 
 
 def make_block_call(micro, rows, width_in, heads_all, mirrored, piece_dtype):

time: 90.6 us -> 88.1 us (0.972)
  Pallas kernels: 45.9 us -> 43.4 us
    pallas_call x4, Pallas kernels: 45.9 us -> 43.4 us  [body(): out, result_low = call(keep, out, *inputs, mask, *weights)]
where the time goes in v8:
time: 88.1 us; the launch traced here: 87 us
  Pallas kernels  43.4 us (49%)
  waiting for transfers between devices  25.8 us (29%)
  starting transfers between devices  13.3 us (15%)
  local copies, waits for them, and re-layouts  3.02 us (3%)
  other arithmetic  0.89 us (1%)
    pallas_call x4, Pallas kernels, body(): out, result_low = call(keep, out, *inputs, mask, *weights)  43.4 us
    ppermute x12, waiting for transfers between devices, send(): return lax.ppermute(block, axes, pairs)  25.8 us
    ppermute x12, starting transfers between devices, send(): return lax.ppermute(block, axes, pairs)  11.2 us
    ppermute x3, starting transfers between devices, behind(): return lax.ppermute(patches, axes, pairs)  2.13 us
    unnamed x32, local copies, waits for them, and re-layouts  2.01 us
  transfers between devices with their start and end apart: 15, of which 2 were waited for; matrix products, arithmetic and copies ran while one was open for 1% of the time, Pallas kernels for 0%

profile of v8, /device:TPU:15, one launch (start us, length us, event | category | flops | bytes accessed | tf_op | source)
XLA Modules:
  0.0 87.0 jit_solution(8817491612332453260)
XLA Ops:
  0.0 0.8 collective-permute-start
  0.8 0.7 collective-permute-start.1
  1.5 0.7 collective-permute-start.2
  2.2 0.2 dynamic-slice_reduce_fusion
  2.4 0.1 compare_reduce_fusion
  2.5 0.1 broadcast_bitcast_fusion
  2.6 0.8 fusion.1.mask_ref
  3.4 0.7 broadcast_in_dim.6.prev_ref
  4.1 11.0 %shard_map.82 = (f32[2,128,128]{2,1,0:T(8,128)}, bf16[2,128,128]{2,1,0:T(8,128)(2,1)}) custom-call(s32[1]{0:T(128)} %bitcast.3.keep_ref, f32[2,128,128]{2,1,0:T(8,128)} %broadcast_in_dim.6.prev_ref, f32[2,128,128]{2,1,0:T(8,128)} %own_ref.1, f32[2,128,128]{2,1,0:T(8,128)} %copy-done.1, f32[2,128,128]{2,1,0:T(8,128)} %copy-done.2, f32[2,128,128]{2,1,0:T(8,128)} %copy-done.3, ...), custom_call_target="tpu_custom_call" | custom-call | flops 5033164800 | bytes 9633792 | tf_op jit(solution)/shard_map/pallas_call | solution.py:252
  15.2 0.7 collective-permute-start.3
  15.8 0.7 collective-permute-start.4
  16.5 0.7 collective-permute-start.5
  17.2 0.8 collective-permute-start.6
  18.1 0.5 copy-done.8
  18.7 0.0 copy-done.11
  18.8 10.8 %shard_map.83 = (f32[2,128,128]{2,1,0:T(8,128)}, bf16[2,128,128]{2,1,0:T(8,128)(2,1)}) custom-call(s32[1]{0:T(128)} %bitcast.2.keep_ref, f32[2,128,128]{2,1,0:T(8,128)} %get-tuple-element.12.prev_ref, f32[2,128,128]{2,1,0:T(8,128)} %copy-done.5, bf16[2,128,128]{2,1,0:T(8,128)(2,1)} %copy-done.8, bf16[2,128,128]{2,1,0:T(8,128)(2,1)} %copy-done.11, ...), custom_call_target="tpu_custom_call" | custom-call | flops 5033164800 | bytes 9633792 | tf_op jit(solution)/shard_map/pallas_call | solution.py:252
  29.6 0.7 collective-permute-start.7
  30.3 0.7 collective-permute-start.10
  30.9 0.7 collective-permute-start.8
  31.6 0.9 %collective-permute-start.9 = (bf16[2,128,128]{2,1,0:T(8,128)(2,1)}, bf16[2,128,128]{2,1,0:T(8,128)(2,1)S(1)}, u32[]{:S(2)}, u32[]{:S(2)}) collective-permute-start(bf16[2,128,128]{2,1,0:T(8,128)(2,1)} %get-tuple-element.15), channel_id=1, source_target_pairs={{10,23},{11,22},{12,21},{13,20},{14,19},{15,18}} | collective-permute-start | bytes 196616 | tf_op jit(solution)/shard_map/ppermute | solution.py:238
  32.6 0.6 copy-done.9
  33.2 0.0 copy-done.6
  33.2 10.8 %shard_map.84 = (f32[2,128,128]{2,1,0:T(8,128)}, bf16[2,128,128]{2,1,0:T(8,128)(2,1)}) custom-call(s32[1]{0:T(128)} %bitcast.1.keep_ref, f32[2,128,128]{2,1,0:T(8,128)} %get-tuple-element.14.prev_ref, f32[2,128,128]{2,1,0:T(8,128)} %copy-done.6, bf16[2,128,128]{2,1,0:T(8,128)(2,1)} %copy-done.12, bf16[2,128,128]{2,1,0:T(8,128)(2,1)} %copy-done.15, ...), custom_call_target="tpu_custom_call" | custom-call | flops 5033164800 | bytes 9633792 | tf_op jit(solution)/shard_map/pallas_call | solution.py:252
  44.1 1.3 %collective-permute-start.11 = (f32[2,128,128]{2,1,0:T(8,128)}, f32[2,128,128]{2,1,0:T(8,128)S(1)}, u32[]{:S(2)}, u32[]{:S(2)}) collective-permute-start(f32[2,128,128]{2,1,0:T(8,128)} %get-tuple-element.16.prev_ref), channel_id=1, source_target_pairs={{16,31},{17,30},{18,29},{19,28},{20,27},{21,26},{22,25},{23,24}} | collective-permute-start | bytes 393224 | tf_op jit(solution)/shard_map/ppermute | solution.py:238
  45.4 1.3 %collective-permute-start.12 = (bf16[2,128,128]{2,1,0:T(8,128)(2,1)}, bf16[2,128,128]{2,1,0:T(8,128)(2,1)S(1)}, u32[]{:S(2)}, u32[]{:S(2)}) collective-permute-start(bf16[2,128,128]{2,1,0:T(8,128)(2,1)} %get-tuple-element.17), channel_id=1, source_target_pairs={{17,31},{18,30},{19,29},{20,28},{21,27},{22,26},{23,25}} | collective-permute-start | bytes 196616 | tf_op jit(solution)/shard_map/ppermute | solution.py:238
  46.7 1.3 %collective-permute-start.13 = (bf16[2,128,128]{2,1,0:T(8,128)(2,1)}, bf16[2,128,128]{2,1,0:T(8,128)(2,1)S(1)}, u32[]{:S(2)}, u32[]{:S(2)}) collective-permute-start(bf16[2,128,128]{2,1,0:T(8,128)(2,1)} %get-tuple-element.17), channel_id=1, source_target_pairs={{18,31},{19,30},{20,29},{21,28},{22,27},{23,26}} | collective-permute-start | bytes 196616 | tf_op jit(solution)/shard_map/ppermute | solution.py:238
  48.0 1.6 %collective-permute-start.14 = (bf16[2,128,128]{2,1,0:T(8,128)(2,1)}, bf16[2,128,128]{2,1,0:T(8,128)(2,1)S(1)}, u32[]{:S(2)}, u32[]{:S(2)}) collective-permute-start(bf16[2,128,128]{2,1,0:T(8,128)(2,1)} %get-tuple-element.17), channel_id=1, source_target_pairs={{19,31},{20,30},{21,29},{22,28},{23,27}} | collective-permute-start | bytes 196616 | tf_op jit(solution)/shard_map/ppermute | solution.py:238
  49.5 25.0 %collective-permute-done.12.back1_ref = bf16[2,128,128]{2,1,0:T(8,128)(2,1)S(1)} collective-permute-done((bf16[2,128,128]{2,1,0:T(8,128)(2,1)}, bf16[2,128,128]{2,1,0:T(8,128)(2,1)S(1)}, u32[]{:S(2)}, u32[]{:S(2)}) %collective-permute-start.12) | collective-permute-done | bytes 65568 | tf_op jit(solution)/shard_map/ppermute | solution.py:238
  74.6 0.8 collective-permute-done.13.back2_ref
  75.4 0.6 copy-done.10
  76.0 0.0 copy-done.4
  76.0 10.8 %shard_map.85 = (f32[2,128,128]{2,1,0:T(8,128)}, bf16[2,128,128]{2,1,0:T(8,128)(2,1)}) custom-call(s32[1]{0:T(128)} %bitcast.keep_ref, f32[2,128,128]{2,1,0:T(8,128)} %get-tuple-element.16.prev_ref, f32[2,128,128]{2,1,0:T(8,128)} %copy-done.4, bf16[2,128,128]{2,1,0:T(8,128)(2,1)} %copy-done.7, bf16[2,128,128]{2,1,0:T(8,128)(2,1)} %copy-done.10, ...), custom_call_target="tpu_custom_call" | custom-call | flops 5033164800 | bytes 9633792 | tf_op jit(solution)/shard_map/pallas_call | solution.py:252
  (42 shorter events, 0.2 us)
Async XLA Ops:
  0.0 2.2 %copy-start = (s32[8,4]{0,1:T(4,128)S(1)}, s32[8,4]{0,1:T(4,128)}, u32[]{:S(2)}) copy-start(s32[8,4]{0,1:T(4,128)} %param.9) | copy-start | bytes 388
  0.0 3.3 %collective-permute-start = (f32[2,128,128]{2,1,0:T(8,128)}, f32[2,128,128]{2,1,0:T(8,128)S(1)}, u32[]{:S(2)}, u32[]{:S(2)}) collective-permute-start(f32[2,128,128]{2,1,0:T(8,128)} %own_ref.1), channel_id=1, source_target_pairs={{0,1},{1,2},{2,3},{3,4},{4,5},{5,6},{6,7}} | collective-permute-start | bytes 393224 | tf_op jit(solution)/shard_map/ppermute | solution.py:224
  0.8 2.6 %collective-permute-start.1 = (f32[2,128,128]{2,1,0:T(8,128)}, f32[2,128,128]{2,1,0:T(8,128)S(1)}, u32[]{:S(2)}, u32[]{:S(2)}) collective-permute-start(f32[2,128,128]{2,1,0:T(8,128)} %own_ref.1), channel_id=1, source_target_pairs={{0,2},{1,3},{2,4},{3,5},{4,6},{5,7}} | collective-permute-start | bytes 393224 | tf_op jit(solution)/shard_map/ppermute | solution.py:224
  1.5 1.9 %collective-permute-start.2 = (f32[2,128,128]{2,1,0:T(8,128)}, f32[2,128,128]{2,1,0:T(8,128)S(1)}, u32[]{:S(2)}, u32[]{:S(2)}) collective-permute-start(f32[2,128,128]{2,1,0:T(8,128)} %own_ref.1), channel_id=1, source_target_pairs={{0,3},{1,4},{2,5},{3,6},{4,7}} | collective-permute-start | bytes 393224 | tf_op jit(solution)/shard_map/ppermute | solution.py:224
  3.3 0.8 copy-start.1
  3.4 0.8 copy-start.2
  3.4 0.8 copy-start.3
  15.2 2.9 %collective-permute-start.3 = (f32[2,128,128]{2,1,0:T(8,128)}, f32[2,128,128]{2,1,0:T(8,128)S(1)}, u32[]{:S(2)}, u32[]{:S(2)}) collective-permute-start(f32[2,128,128]{2,1,0:T(8,128)} %get-tuple-element.12.prev_ref), channel_id=1, source_target_pairs={{0,15},{1,14},{2,13},{3,12},{4,11},{5,10},{6,9},{7,8}} | collective-permute-start | bytes 393224 | tf_op jit(solution)/shard_map/ppermute | solution.py:238
  15.8 2.2 %collective-permute-start.4 = (bf16[2,128,128]{2,1,0:T(8,128)(2,1)}, bf16[2,128,128]{2,1,0:T(8,128)(2,1)S(1)}, u32[]{:S(2)}, u32[]{:S(2)}) collective-permute-start(bf16[2,128,128]{2,1,0:T(8,128)(2,1)} %get-tuple-element.13), channel_id=1, source_target_pairs={{1,15},{2,14},{3,13},{4,12},{5,11},{6,10},{7,9}} | collective-permute-start | bytes 196616 | tf_op jit(solution)/shard_map/ppermute | solution.py:238
  16.5 1.6 %collective-permute-start.5 = (bf16[2,128,128]{2,1,0:T(8,128)(2,1)}, bf16[2,128,128]{2,1,0:T(8,128)(2,1)S(1)}, u32[]{:S(2)}, u32[]{:S(2)}) collective-permute-start(bf16[2,128,128]{2,1,0:T(8,128)(2,1)} %get-tuple-element.13), channel_id=1, source_target_pairs={{2,15},{3,14},{4,13},{5,12},{6,11},{7,10}} | collective-permute-start | bytes 196616 | tf_op jit(solution)/shard_map/ppermute | solution.py:238
  17.2 0.9 %collective-permute-start.6 = (bf16[2,128,128]{2,1,0:T(8,128)(2,1)}, bf16[2,128,128]{2,1,0:T(8,128)(2,1)S(1)}, u32[]{:S(2)}, u32[]{:S(2)}) collective-permute-start(bf16[2,128,128]{2,1,0:T(8,128)(2,1)} %get-tuple-element.13), channel_id=1, source_target_pairs={{3,15},{4,14},{5,13},{6,12},{7,11}} | collective-permute-start | bytes 196616 | tf_op jit(solution)/shard_map/ppermute | solution.py:238
  18.1 0.6 copy-start.8
  18.1 0.6 copy-start.11
  18.1 0.6 copy-start.14
  18.1 0.7 copy-start.5
  29.6 3.0 %collective-permute-start.7 = (f32[2,128,128]{2,1,0:T(8,128)}, f32[2,128,128]{2,1,0:T(8,128)S(1)}, u32[]{:S(2)}, u32[]{:S(2)}) collective-permute-start(f32[2,128,128]{2,1,0:T(8,128)} %get-tuple-element.14.prev_ref), channel_id=1, source_target_pairs={{8,23},{9,22},{10,21},{11,20},{12,19},{13,18},{14,17},{15,16}} | collective-permute-start | bytes 393224 | tf_op jit(solution)/shard_map/ppermute | solution.py:238
  30.3 2.2 %collective-permute-start.10 = (bf16[2,128,128]{2,1,0:T(8,128)(2,1)}, bf16[2,128,128]{2,1,0:T(8,128)(2,1)S(1)}, u32[]{:S(2)}, u32[]{:S(2)}) collective-permute-start(bf16[2,128,128]{2,1,0:T(8,128)(2,1)} %get-tuple-element.15), channel_id=1, source_target_pairs={{11,23},{12,22},{13,21},{14,20},{15,19}} | collective-permute-start | bytes 196616 | tf_op jit(solution)/shard_map/ppermute | solution.py:238
  30.9 1.6 %collective-permute-start.8 = (bf16[2,128,128]{2,1,0:T(8,128)(2,1)}, bf16[2,128,128]{2,1,0:T(8,128)(2,1)S(1)}, u32[]{:S(2)}, u32[]{:S(2)}) collective-permute-start(bf16[2,128,128]{2,1,0:T(8,128)(2,1)} %get-tuple-element.15), channel_id=1, source_target_pairs={{9,23},{10,22},{11,21},{12,20},{13,19},{14,18},{15,17}} | collective-permute-start | bytes 196616 | tf_op jit(solution)/shard_map/ppermute | solution.py:238
  31.6 0.9 %collective-permute-start.9 = (bf16[2,128,128]{2,1,0:T(8,128)(2,1)}, bf16[2,128,128]{2,1,0:T(8,128)(2,1)S(1)}, u32[]{:S(2)}, u32[]{:S(2)}) collective-permute-start(bf16[2,128,128]{2,1,0:T(8,128)(2,1)} %get-tuple-element.15), channel_id=1, source_target_pairs={{10,23},{11,22},{12,21},{13,20},{14,19},{15,18}} | collective-permute-start | bytes 196616 | tf_op jit(solution)/shard_map/ppermute | solution.py:238
  32.5 0.6 copy-start.9
  32.5 0.6 copy-start.12
  32.6 0.6 copy-start.15
  32.6 0.7 copy-start.6
  44.1 31.3 %collective-permute-start.11 = (f32[2,128,128]{2,1,0:T(8,128)}, f32[2,128,128]{2,1,0:T(8,128)S(1)}, u32[]{:S(2)}, u32[]{:S(2)}) collective-permute-start(f32[2,128,128]{2,1,0:T(8,128)} %get-tuple-element.16.prev_ref), channel_id=1, source_target_pairs={{16,31},{17,30},{18,29},{19,28},{20,27},{21,26},{22,25},{23,24}} | collective-permute-start | bytes 393224 | tf_op jit(solution)/shard_map/ppermute | solution.py:238
  45.4 29.2 %collective-permute-start.12 = (bf16[2,128,128]{2,1,0:T(8,128)(2,1)}, bf16[2,128,128]{2,1,0:T(8,128)(2,1)S(1)}, u32[]{:S(2)}, u32[]{:S(2)}) collective-permute-start(bf16[2,128,128]{2,1,0:T(8,128)(2,1)} %get-tuple-element.17), channel_id=1, source_target_pairs={{17,31},{18,30},{19,29},{20,28},{21,27},{22,26},{23,25}} | collective-permute-start | bytes 196616 | tf_op jit(solution)/shard_map/ppermute | solution.py:238
  46.7 28.7 %collective-permute-start.13 = (bf16[2,128,128]{2,1,0:T(8,128)(2,1)}, bf16[2,128,128]{2,1,0:T(8,128)(2,1)S(1)}, u32[]{:S(2)}, u32[]{:S(2)}) collective-permute-start(bf16[2,128,128]{2,1,0:T(8,128)(2,1)} %get-tuple-element.17), channel_id=1, source_target_pairs={{18,31},{19,30},{20,29},{21,28},{22,27},{23,26}} | collective-permute-start | bytes 196616 | tf_op jit(solution)/shard_map/ppermute | solution.py:238
  48.0 27.4 %collective-permute-start.14 = (bf16[2,128,128]{2,1,0:T(8,128)(2,1)}, bf16[2,128,128]{2,1,0:T(8,128)(2,1)S(1)}, u32[]{:S(2)}, u32[]{:S(2)}) collective-permute-start(bf16[2,128,128]{2,1,0:T(8,128)(2,1)} %get-tuple-element.17), channel_id=1, source_target_pairs={{19,31},{20,30},{21,29},{22,28},{23,27}} | collective-permute-start | bytes 196616 | tf_op jit(solution)/shard_map/ppermute | solution.py:238
  74.6 0.8 copy-start.7
  75.3 0.6 copy-start.10
  75.3 0.6 copy-start.13
  75.3 0.7 copy-start.4

commit v9 on v8

--- a/solution.py
+++ b/solution.py
@@ -21,29 +21,26 @@
     heads = heads_all // HEAD_DIM
 
     def kernel(keep_ref, prev_ref, own_ref, back1_ref, back2_ref, edge_ref, mask_ref, ga_ref, gb_ref,
-               embed_hbm, attn_hbm, mix_hbm, read_hbm,
+               embed_v, read_v, attn_hbm, mix_hbm,
                out_ref, outb_ref,
-               embed_v, attn_v, mix_v, read_v, sems,
+               attn_v, mix_v, sems,
                pieces_s, shifted_s, hidden_s, normed_s, q_s, kv_s, mixed_s, res_s):
         n_kv = 2 * heads_all // CHUNK
         kv_copies = [
             pltpu.make_async_copy(
                 attn_hbm.at[:, heads_all + j * CHUNK:heads_all + (j + 1) * CHUNK],
                 attn_v.at[:, heads_all + j * CHUNK:heads_all + (j + 1) * CHUNK],
-                sems.at[4 + j],
+                sems.at[2 + j],
             )
             for j in range(n_kv)
         ]
         copies = [
-            pltpu.make_async_copy(embed_hbm, embed_v, sems.at[0]),
-            pltpu.make_async_copy(attn_hbm.at[:, :heads_all], attn_v.at[:, :heads_all], sems.at[1]),
-            pltpu.make_async_copy(mix_hbm, mix_v, sems.at[2]),
-            pltpu.make_async_copy(read_hbm, read_v, sems.at[3]),
+            pltpu.make_async_copy(attn_hbm.at[:, :heads_all], attn_v.at[:, :heads_all], sems.at[0]),
+            pltpu.make_async_copy(mix_hbm, mix_v, sems.at[1]),
         ]
-        copies[0].start()
         for copy in kv_copies:
             copy.start()
-        for copy in copies[1:]:
+        for copy in copies:
             copy.start()
         before = lax.broadcasted_iota(jnp.int32, (span, n_in), 0) + (rows - 1)
         column = lax.broadcasted_iota(jnp.int32, (span, n_in), 1)
@@ -60,7 +57,6 @@
             shifted_s[m * span:(m + 1) * span, :] = jnp.dot(
                 select, pieces_s[...], preferred_element_type=jnp.float32
             ).astype(jnp.bfloat16)
-        copies[0].wait()
         hidden = jnp.dot(shifted_s[...], embed_v[...], preferred_element_type=jnp.float32)
         hidden_s[...] = hidden
         square = jnp.mean(hidden * hidden, axis=-1, keepdims=True)
@@ -71,7 +67,7 @@
                 normed_s[...], attn_v[:, heads_all + j * CHUNK:heads_all + (j + 1) * CHUNK],
                 preferred_element_type=jnp.float32,
             ).astype(jnp.bfloat16)
-        copies[1].wait()
+        copies[0].wait()
 
         def q_step(j, carry):
             cols = pl.ds(pl.multiple_of(j * CHUNK, CHUNK), CHUNK)
@@ -102,7 +98,7 @@
             for h in range(heads):
                 mixed_s[m * rows:(m + 1) * rows, h * HEAD_DIM:(h + 1) * HEAD_DIM] = mixed[h].astype(jnp.bfloat16)
 
-        copies[2].wait()
+        copies[1].wait()
         for m in range(micro):
             res_s[m * rows:(m + 1) * rows, :] = hidden_s[m * span + own_at:(m + 1) * span, :] + jnp.dot(
                 mixed_s[m * rows:(m + 1) * rows, :], mix_v[...], preferred_element_type=jnp.float32
@@ -110,7 +106,6 @@
         residual = res_s[...]
         square = jnp.mean(residual * residual, axis=-1, keepdims=True)
         final_normed = (residual * lax.rsqrt(square + 1e-06) * gb_ref[...]).astype(jnp.bfloat16)
-        copies[3].wait()
         raw = jnp.dot(final_normed, read_v[...], preferred_element_type=jnp.float32)
         shift_mean = raw[:, :width_in]
         log_scale = 0.5 * jnp.tanh(raw[:, width_in:])
@@ -143,15 +138,13 @@
             jax.ShapeDtypeStruct((micro, rows, width_in), jnp.float32),
             jax.ShapeDtypeStruct((micro, rows, width_in), jnp.bfloat16),
         ),
-        in_specs=[pl.BlockSpec(memory_space=pltpu.SMEM)] + [pl.BlockSpec(memory_space=vmem)] * 8
-        + [pl.BlockSpec(memory_space=pl.ANY)] * 4,
+        in_specs=[pl.BlockSpec(memory_space=pltpu.SMEM)] + [pl.BlockSpec(memory_space=vmem)] * 10
+        + [pl.BlockSpec(memory_space=pl.ANY)] * 2,
         out_specs=(pl.BlockSpec(memory_space=vmem), pl.BlockSpec(memory_space=vmem)),
         scratch_shapes=[
-            vmem((width_in, width), jnp.bfloat16),
             vmem((width, 3 * heads_all), jnp.bfloat16),
             vmem((heads_all, width), jnp.bfloat16),
-            vmem((width, 2 * width_in), jnp.bfloat16),
-            pltpu.SemaphoreType.DMA((4 + 2 * heads_all // CHUNK,)),
+            pltpu.SemaphoreType.DMA((2 + 2 * heads_all // CHUNK,)),
             vmem((n_in, width_in), jnp.bfloat16),
             vmem((n_rows, width_in), jnp.bfloat16),
             vmem((n_rows, width), jnp.float32),
@@ -211,9 +204,9 @@
         norm_gain[0].reshape(1, -1),
         final_gain[0].reshape(1, -1),
         input_weight[0],
+        output_weight[0],
         attention_weight[0],
         mixing_weight[0],
-        output_weight[0],
     )
 
     axes = ("segment", "seq")

time: 88.1 us -> 88.1 us (level)
  no operation moved by 1% of the time
where the time goes in v9:
time: 88.1 us; the launch traced here: 87 us
  Pallas kernels  43.4 us (49%)
  waiting for transfers between devices  25.8 us (29%)
  starting transfers between devices  13.3 us (15%)
  local copies, waits for them, and re-layouts  3.02 us (3%)
  other arithmetic  0.89 us (1%)
    pallas_call x4, Pallas kernels, body(): out, result_low = call(keep, out, *inputs, mask, *weights)  43.4 us
    ppermute x12, waiting for transfers between devices, send(): return lax.ppermute(block, axes, pairs)  25.8 us
    ppermute x12, starting transfers between devices, send(): return lax.ppermute(block, axes, pairs)  11.2 us
    ppermute x3, starting transfers between devices, behind(): return lax.ppermute(patches, axes, pairs)  2.13 us
    unnamed x32, local copies, waits for them, and re-layouts  2.01 us
  transfers between devices with their start and end apart: 15, of which 2 were waited for; matrix products, arithmetic and copies ran while one was open for 1% of the time, Pallas kernels for 0%

profile of v9, /device:TPU:15, one launch (start us, length us, event | category | flops | bytes accessed | tf_op | source)
XLA Modules:
  0.0 87.0 jit_solution(1934281723957375446)
XLA Ops:
  0.0 0.8 collective-permute-start
  0.8 0.7 collective-permute-start.1
  1.5 0.7 collective-permute-start.2
  2.2 0.2 dynamic-slice_reduce_fusion
  2.4 0.1 compare_reduce_fusion
  2.5 0.1 broadcast_bitcast_fusion
  2.6 0.8 fusion.1.mask_ref
  3.4 0.7 broadcast_in_dim.6.prev_ref
  4.1 10.9 %shard_map.82 = (f32[2,128,128]{2,1,0:T(8,128)}, bf16[2,128,128]{2,1,0:T(8,128)(2,1)}) custom-call(s32[1]{0:T(128)} %bitcast.3.keep_ref, f32[2,128,128]{2,1,0:T(8,128)} %broadcast_in_dim.6.prev_ref, f32[2,128,128]{2,1,0:T(8,128)} %own_ref.1, f32[2,128,128]{2,1,0:T(8,128)} %copy-done.1, f32[2,128,128]{2,1,0:T(8,128)} %copy-done.2, f32[2,128,128]{2,1,0:T(8,128)} %copy-done.3, ...), custom_call_target="tpu_custom_call" | custom-call | flops 5033164800 | bytes 9633792 | tf_op jit(solution)/shard_map/pallas_call | solution.py:245
  15.0 0.7 collective-permute-start.3
  15.7 0.7 collective-permute-start.4
  16.4 0.7 collective-permute-start.5
  17.1 0.8 collective-permute-start.6
  18.0 0.5 copy-done.8
  18.5 0.0 copy-done.11
  18.7 10.8 %shard_map.83 = (f32[2,128,128]{2,1,0:T(8,128)}, bf16[2,128,128]{2,1,0:T(8,128)(2,1)}) custom-call(s32[1]{0:T(128)} %bitcast.2.keep_ref, f32[2,128,128]{2,1,0:T(8,128)} %get-tuple-element.12.prev_ref, f32[2,128,128]{2,1,0:T(8,128)} %copy-done.5, bf16[2,128,128]{2,1,0:T(8,128)(2,1)} %copy-done.8, bf16[2,128,128]{2,1,0:T(8,128)(2,1)} %copy-done.11, ...), custom_call_target="tpu_custom_call" | custom-call | flops 5033164800 | bytes 9633792 | tf_op jit(solution)/shard_map/pallas_call | solution.py:245
  29.5 0.7 collective-permute-start.7
  30.2 0.7 collective-permute-start.10
  30.8 0.7 collective-permute-start.8
  31.5 0.9 %collective-permute-start.9 = (bf16[2,128,128]{2,1,0:T(8,128)(2,1)}, bf16[2,128,128]{2,1,0:T(8,128)(2,1)S(1)}, u32[]{:S(2)}, u32[]{:S(2)}) collective-permute-start(bf16[2,128,128]{2,1,0:T(8,128)(2,1)} %get-tuple-element.15), channel_id=1, source_target_pairs={{10,23},{11,22},{12,21},{13,20},{14,19},{15,18}} | collective-permute-start | bytes 196616 | tf_op jit(solution)/shard_map/ppermute | solution.py:231
  32.5 0.6 copy-done.9
  33.1 0.0 copy-done.6
  33.1 10.8 %shard_map.84 = (f32[2,128,128]{2,1,0:T(8,128)}, bf16[2,128,128]{2,1,0:T(8,128)(2,1)}) custom-call(s32[1]{0:T(128)} %bitcast.1.keep_ref, f32[2,128,128]{2,1,0:T(8,128)} %get-tuple-element.14.prev_ref, f32[2,128,128]{2,1,0:T(8,128)} %copy-done.6, bf16[2,128,128]{2,1,0:T(8,128)(2,1)} %copy-done.12, bf16[2,128,128]{2,1,0:T(8,128)(2,1)} %copy-done.15, ...), custom_call_target="tpu_custom_call" | custom-call | flops 5033164800 | bytes 9633792 | tf_op jit(solution)/shard_map/pallas_call | solution.py:245
  44.0 1.3 %collective-permute-start.11 = (f32[2,128,128]{2,1,0:T(8,128)}, f32[2,128,128]{2,1,0:T(8,128)S(1)}, u32[]{:S(2)}, u32[]{:S(2)}) collective-permute-start(f32[2,128,128]{2,1,0:T(8,128)} %get-tuple-element.16.prev_ref), channel_id=1, source_target_pairs={{16,31},{17,30},{18,29},{19,28},{20,27},{21,26},{22,25},{23,24}} | collective-permute-start | bytes 393224 | tf_op jit(solution)/shard_map/ppermute | solution.py:231
  45.3 1.3 %collective-permute-start.12 = (bf16[2,128,128]{2,1,0:T(8,128)(2,1)}, bf16[2,128,128]{2,1,0:T(8,128)(2,1)S(1)}, u32[]{:S(2)}, u32[]{:S(2)}) collective-permute-start(bf16[2,128,128]{2,1,0:T(8,128)(2,1)} %get-tuple-element.17), channel_id=1, source_target_pairs={{17,31},{18,30},{19,29},{20,28},{21,27},{22,26},{23,25}} | collective-permute-start | bytes 196616 | tf_op jit(solution)/shard_map/ppermute | solution.py:231
  46.6 1.3 %collective-permute-start.13 = (bf16[2,128,128]{2,1,0:T(8,128)(2,1)}, bf16[2,128,128]{2,1,0:T(8,128)(2,1)S(1)}, u32[]{:S(2)}, u32[]{:S(2)}) collective-permute-start(bf16[2,128,128]{2,1,0:T(8,128)(2,1)} %get-tuple-element.17), channel_id=1, source_target_pairs={{18,31},{19,30},{20,29},{21,28},{22,27},{23,26}} | collective-permute-start | bytes 196616 | tf_op jit(solution)/shard_map/ppermute | solution.py:231
  47.9 1.6 %collective-permute-start.14 = (bf16[2,128,128]{2,1,0:T(8,128)(2,1)}, bf16[2,128,128]{2,1,0:T(8,128)(2,1)S(1)}, u32[]{:S(2)}, u32[]{:S(2)}) collective-permute-start(bf16[2,128,128]{2,1,0:T(8,128)(2,1)} %get-tuple-element.17), channel_id=1, source_target_pairs={{19,31},{20,30},{21,29},{22,28},{23,27}} | collective-permute-start | bytes 196616 | tf_op jit(solution)/shard_map/ppermute | solution.py:231
  49.5 25.1 %collective-permute-done.12.back1_ref = bf16[2,128,128]{2,1,0:T(8,128)(2,1)S(1)} collective-permute-done((bf16[2,128,128]{2,1,0:T(8,128)(2,1)}, bf16[2,128,128]{2,1,0:T(8,128)(2,1)S(1)}, u32[]{:S(2)}, u32[]{:S(2)}) %collective-permute-start.12) | collective-permute-done | bytes 65568 | tf_op jit(solution)/shard_map/ppermute | solution.py:231
  74.5 0.7 collective-permute-done.13.back2_ref
  75.3 0.6 copy-done.10
  75.9 0.0 copy-done.4
  76.0 10.8 %shard_map.85 = (f32[2,128,128]{2,1,0:T(8,128)}, bf16[2,128,128]{2,1,0:T(8,128)(2,1)}) custom-call(s32[1]{0:T(128)} %bitcast.keep_ref, f32[2,128,128]{2,1,0:T(8,128)} %get-tuple-element.16.prev_ref, f32[2,128,128]{2,1,0:T(8,128)} %copy-done.4, bf16[2,128,128]{2,1,0:T(8,128)(2,1)} %copy-done.7, bf16[2,128,128]{2,1,0:T(8,128)(2,1)} %copy-done.10, ...), custom_call_target="tpu_custom_call" | custom-call | flops 5033164800 | bytes 9633792 | tf_op jit(solution)/shard_map/pallas_call | solution.py:245
  (42 shorter events, 0.2 us)
Async XLA Ops:
  0.0 2.2 %copy-start = (s32[8,4]{0,1:T(4,128)S(1)}, s32[8,4]{0,1:T(4,128)}, u32[]{:S(2)}) copy-start(s32[8,4]{0,1:T(4,128)} %param.9) | copy-start | bytes 388
  0.0 3.3 %collective-permute-start = (f32[2,128,128]{2,1,0:T(8,128)}, f32[2,128,128]{2,1,0:T(8,128)S(1)}, u32[]{:S(2)}, u32[]{:S(2)}) collective-permute-start(f32[2,128,128]{2,1,0:T(8,128)} %own_ref.1), channel_id=1, source_target_pairs={{0,1},{1,2},{2,3},{3,4},{4,5},{5,6},{6,7}} | collective-permute-start | bytes 393224 | tf_op jit(solution)/shard_map/ppermute | solution.py:217
  0.8 2.6 %collective-permute-start.1 = (f32[2,128,128]{2,1,0:T(8,128)}, f32[2,128,128]{2,1,0:T(8,128)S(1)}, u32[]{:S(2)}, u32[]{:S(2)}) collective-permute-start(f32[2,128,128]{2,1,0:T(8,128)} %own_ref.1), channel_id=1, source_target_pairs={{0,2},{1,3},{2,4},{3,5},{4,6},{5,7}} | collective-permute-start | bytes 393224 | tf_op jit(solution)/shard_map/ppermute | solution.py:217
  1.5 1.9 %collective-permute-start.2 = (f32[2,128,128]{2,1,0:T(8,128)}, f32[2,128,128]{2,1,0:T(8,128)S(1)}, u32[]{:S(2)}, u32[]{:S(2)}) collective-permute-start(f32[2,128,128]{2,1,0:T(8,128)} %own_ref.1), channel_id=1, source_target_pairs={{0,3},{1,4},{2,5},{3,6},{4,7}} | collective-permute-start | bytes 393224 | tf_op jit(solution)/shard_map/ppermute | solution.py:217
  3.3 0.8 copy-start.1
  3.4 0.8 copy-start.2
  3.4 0.8 copy-start.3
  15.0 2.9 %collective-permute-start.3 = (f32[2,128,128]{2,1,0:T(8,128)}, f32[2,128,128]{2,1,0:T(8,128)S(1)}, u32[]{:S(2)}, u32[]{:S(2)}) collective-permute-start(f32[2,128,128]{2,1,0:T(8,128)} %get-tuple-element.12.prev_ref), channel_id=1, source_target_pairs={{0,15},{1,14},{2,13},{3,12},{4,11},{5,10},{6,9},{7,8}} | collective-permute-start | bytes 393224 | tf_op jit(solution)/shard_map/ppermute | solution.py:231
  15.7 2.2 %collective-permute-start.4 = (bf16[2,128,128]{2,1,0:T(8,128)(2,1)}, bf16[2,128,128]{2,1,0:T(8,128)(2,1)S(1)}, u32[]{:S(2)}, u32[]{:S(2)}) collective-permute-start(bf16[2,128,128]{2,1,0:T(8,128)(2,1)} %get-tuple-element.13), channel_id=1, source_target_pairs={{1,15},{2,14},{3,13},{4,12},{5,11},{6,10},{7,9}} | collective-permute-start | bytes 196616 | tf_op jit(solution)/shard_map/ppermute | solution.py:231
  16.4 1.6 %collective-permute-start.5 = (bf16[2,128,128]{2,1,0:T(8,128)(2,1)}, bf16[2,128,128]{2,1,0:T(8,128)(2,1)S(1)}, u32[]{:S(2)}, u32[]{:S(2)}) collective-permute-start(bf16[2,128,128]{2,1,0:T(8,128)(2,1)} %get-tuple-element.13), channel_id=1, source_target_pairs={{2,15},{3,14},{4,13},{5,12},{6,11},{7,10}} | collective-permute-start | bytes 196616 | tf_op jit(solution)/shard_map/ppermute | solution.py:231
  17.1 0.9 %collective-permute-start.6 = (bf16[2,128,128]{2,1,0:T(8,128)(2,1)}, bf16[2,128,128]{2,1,0:T(8,128)(2,1)S(1)}, u32[]{:S(2)}, u32[]{:S(2)}) collective-permute-start(bf16[2,128,128]{2,1,0:T(8,128)(2,1)} %get-tuple-element.13), channel_id=1, source_target_pairs={{3,15},{4,14},{5,13},{6,12},{7,11}} | collective-permute-start | bytes 196616 | tf_op jit(solution)/shard_map/ppermute | solution.py:231
  17.9 0.6 copy-start.8
  18.0 0.6 copy-start.11
  18.0 0.6 copy-start.14
  18.0 0.7 copy-start.5
  29.5 3.0 %collective-permute-start.7 = (f32[2,128,128]{2,1,0:T(8,128)}, f32[2,128,128]{2,1,0:T(8,128)S(1)}, u32[]{:S(2)}, u32[]{:S(2)}) collective-permute-start(f32[2,128,128]{2,1,0:T(8,128)} %get-tuple-element.14.prev_ref), channel_id=1, source_target_pairs={{8,23},{9,22},{10,21},{11,20},{12,19},{13,18},{14,17},{15,16}} | collective-permute-start | bytes 393224 | tf_op jit(solution)/shard_map/ppermute | solution.py:231
  30.2 2.2 %collective-permute-start.10 = (bf16[2,128,128]{2,1,0:T(8,128)(2,1)}, bf16[2,128,128]{2,1,0:T(8,128)(2,1)S(1)}, u32[]{:S(2)}, u32[]{:S(2)}) collective-permute-start(bf16[2,128,128]{2,1,0:T(8,128)(2,1)} %get-tuple-element.15), channel_id=1, source_target_pairs={{11,23},{12,22},{13,21},{14,20},{15,19}} | collective-permute-start | bytes 196616 | tf_op jit(solution)/shard_map/ppermute | solution.py:231
  30.8 1.6 %collective-permute-start.8 = (bf16[2,128,128]{2,1,0:T(8,128)(2,1)}, bf16[2,128,128]{2,1,0:T(8,128)(2,1)S(1)}, u32[]{:S(2)}, u32[]{:S(2)}) collective-permute-start(bf16[2,128,128]{2,1,0:T(8,128)(2,1)} %get-tuple-element.15), channel_id=1, source_target_pairs={{9,23},{10,22},{11,21},{12,20},{13,19},{14,18},{15,17}} | collective-permute-start | bytes 196616 | tf_op jit(solution)/shard_map/ppermute | solution.py:231
  31.5 0.9 %collective-permute-start.9 = (bf16[2,128,128]{2,1,0:T(8,128)(2,1)}, bf16[2,128,128]{2,1,0:T(8,128)(2,1)S(1)}, u32[]{:S(2)}, u32[]{:S(2)}) collective-permute-start(bf16[2,128,128]{2,1,0:T(8,128)(2,1)} %get-tuple-element.15), channel_id=1, source_target_pairs={{10,23},{11,22},{12,21},{13,20},{14,19},{15,18}} | collective-permute-start | bytes 196616 | tf_op jit(solution)/shard_map/ppermute | solution.py:231
  32.4 0.6 copy-start.9
  32.4 0.6 copy-start.12
  32.5 0.6 copy-start.15
  32.5 0.7 copy-start.6
  44.0 31.3 %collective-permute-start.11 = (f32[2,128,128]{2,1,0:T(8,128)}, f32[2,128,128]{2,1,0:T(8,128)S(1)}, u32[]{:S(2)}, u32[]{:S(2)}) collective-permute-start(f32[2,128,128]{2,1,0:T(8,128)} %get-tuple-element.16.prev_ref), channel_id=1, source_target_pairs={{16,31},{17,30},{18,29},{19,28},{20,27},{21,26},{22,25},{23,24}} | collective-permute-start | bytes 393224 | tf_op jit(solution)/shard_map/ppermute | solution.py:231
  45.3 29.2 %collective-permute-start.12 = (bf16[2,128,128]{2,1,0:T(8,128)(2,1)}, bf16[2,128,128]{2,1,0:T(8,128)(2,1)S(1)}, u32[]{:S(2)}, u32[]{:S(2)}) collective-permute-start(bf16[2,128,128]{2,1,0:T(8,128)(2,1)} %get-tuple-element.17), channel_id=1, source_target_pairs={{17,31},{18,30},{19,29},{20,28},{21,27},{22,26},{23,25}} | collective-permute-start | bytes 196616 | tf_op jit(solution)/shard_map/ppermute | solution.py:231
  46.6 28.7 %collective-permute-start.13 = (bf16[2,128,128]{2,1,0:T(8,128)(2,1)}, bf16[2,128,128]{2,1,0:T(8,128)(2,1)S(1)}, u32[]{:S(2)}, u32[]{:S(2)}) collective-permute-start(bf16[2,128,128]{2,1,0:T(8,128)(2,1)} %get-tuple-element.17), channel_id=1, source_target_pairs={{18,31},{19,30},{20,29},{21,28},{22,27},{23,26}} | collective-permute-start | bytes 196616 | tf_op jit(solution)/shard_map/ppermute | solution.py:231
  47.9 27.4 %collective-permute-start.14 = (bf16[2,128,128]{2,1,0:T(8,128)(2,1)}, bf16[2,128,128]{2,1,0:T(8,128)(2,1)S(1)}, u32[]{:S(2)}, u32[]{:S(2)}) collective-permute-start(bf16[2,128,128]{2,1,0:T(8,128)(2,1)} %get-tuple-element.17), channel_id=1, source_target_pairs={{19,31},{20,30},{21,29},{22,28},{23,27}} | collective-permute-start | bytes 196616 | tf_op jit(solution)/shard_map/ppermute | solution.py:231
  74.5 0.8 copy-start.7
  75.3 0.6 copy-start.10
  75.3 0.6 copy-start.13
  75.3 0.7 copy-start.4

commit v10 on v9

--- a/solution.py
+++ b/solution.py
@@ -213,7 +213,7 @@
 
     def first_inputs():
         def behind(distance):
-            pairs = [(q, q + distance) for q in range(n_seq) if q + distance < n_seq]
+            pairs = [(n_seq + q, q + distance) for q in range(n_seq) if q + distance < n_seq]
             return lax.ppermute(patches, axes, pairs)
 
         return patches, behind(1), behind(2), behind(BACK + 1)

time: 88.1 us -> 85.6 us (0.972)
  waiting for transfers between devices: 25.8 us -> 23.9 us
    ppermute x12, waiting for transfers between devices: 25.8 us -> 23.8 us  [send(): return lax.ppermute(block, axes, pairs)]
  transfers between devices with their start and end apart: 15 -> 15, of which waited for: 2 -> 1; matrix products, arithmetic and copies ran while one was open for 1% -> 1% of each run, Pallas kernels for 0% -> 0%
where the time goes in v10:
time: 85.6 us; the launch traced here: 85 us
  Pallas kernels  43.4 us (51%)
  waiting for transfers between devices  23.9 us (28%)
  starting transfers between devices  13.3 us (16%)
  local copies, waits for them, and re-layouts  3.02 us (4%)
  other arithmetic  0.89 us (1%)
    pallas_call x4, Pallas kernels, body(): out, result_low = call(keep, out, *inputs, mask, *weights)  43.4 us
    ppermute x12, waiting for transfers between devices, send(): return lax.ppermute(block, axes, pairs)  23.8 us
    ppermute x12, starting transfers between devices, send(): return lax.ppermute(block, axes, pairs)  11.2 us
    ppermute x3, starting transfers between devices, behind(): return lax.ppermute(patches, axes, pairs)  2.13 us
    unnamed x32, local copies, waits for them, and re-layouts  2.01 us
  transfers between devices with their start and end apart: 15, of which 1 were waited for; matrix products, arithmetic and copies ran while one was open for 1% of the time, Pallas kernels for 0%

profile of v10, /device:TPU:15, one launch (start us, length us, event | category | flops | bytes accessed | tf_op | source)
XLA Modules:
  0.0 85.0 jit_solution(12473919755708418128)
XLA Ops:
  0.0 0.8 collective-permute-start
  0.8 0.7 collective-permute-start.1
  1.5 0.7 collective-permute-start.2
  2.2 0.2 dynamic-slice_reduce_fusion
  2.4 0.1 compare_reduce_fusion
  2.5 0.1 broadcast_bitcast_fusion
  2.6 0.8 fusion.1.mask_ref
  3.4 0.7 broadcast_in_dim.6.prev_ref
  4.1 10.9 %shard_map.82 = (f32[2,128,128]{2,1,0:T(8,128)}, bf16[2,128,128]{2,1,0:T(8,128)(2,1)}) custom-call(s32[1]{0:T(128)} %bitcast.3.keep_ref, f32[2,128,128]{2,1,0:T(8,128)} %broadcast_in_dim.6.prev_ref, f32[2,128,128]{2,1,0:T(8,128)} %own_ref.1, f32[2,128,128]{2,1,0:T(8,128)} %copy-done.1, f32[2,128,128]{2,1,0:T(8,128)} %copy-done.2, f32[2,128,128]{2,1,0:T(8,128)} %copy-done.3, ...), custom_call_target="tpu_custom_call" | custom-call | flops 5033164800 | bytes 9633792 | tf_op jit(solution)/shard_map/pallas_call | solution.py:245
  15.0 0.7 collective-permute-start.3
  15.7 0.7 collective-permute-start.4
  16.4 0.7 collective-permute-start.5
  17.1 0.8 collective-permute-start.6
  18.0 0.5 copy-done.8
  18.5 0.0 copy-done.11
  18.7 10.8 %shard_map.83 = (f32[2,128,128]{2,1,0:T(8,128)}, bf16[2,128,128]{2,1,0:T(8,128)(2,1)}) custom-call(s32[1]{0:T(128)} %bitcast.2.keep_ref, f32[2,128,128]{2,1,0:T(8,128)} %get-tuple-element.12.prev_ref, f32[2,128,128]{2,1,0:T(8,128)} %copy-done.5, bf16[2,128,128]{2,1,0:T(8,128)(2,1)} %copy-done.8, bf16[2,128,128]{2,1,0:T(8,128)(2,1)} %copy-done.11, ...), custom_call_target="tpu_custom_call" | custom-call | flops 5033164800 | bytes 9633792 | tf_op jit(solution)/shard_map/pallas_call | solution.py:245
  29.5 0.7 collective-permute-start.7
  30.2 0.7 collective-permute-start.10
  30.8 0.7 collective-permute-start.8
  31.5 0.9 %collective-permute-start.9 = (bf16[2,128,128]{2,1,0:T(8,128)(2,1)}, bf16[2,128,128]{2,1,0:T(8,128)(2,1)S(1)}, u32[]{:S(2)}, u32[]{:S(2)}) collective-permute-start(bf16[2,128,128]{2,1,0:T(8,128)(2,1)} %get-tuple-element.15), channel_id=1, source_target_pairs={{10,23},{11,22},{12,21},{13,20},{14,19},{15,18}} | collective-permute-start | bytes 196616 | tf_op jit(solution)/shard_map/ppermute | solution.py:231
  32.5 0.6 copy-done.9
  33.1 0.0 copy-done.6
  33.1 10.8 %shard_map.84 = (f32[2,128,128]{2,1,0:T(8,128)}, bf16[2,128,128]{2,1,0:T(8,128)(2,1)}) custom-call(s32[1]{0:T(128)} %bitcast.1.keep_ref, f32[2,128,128]{2,1,0:T(8,128)} %get-tuple-element.14.prev_ref, f32[2,128,128]{2,1,0:T(8,128)} %copy-done.6, bf16[2,128,128]{2,1,0:T(8,128)(2,1)} %copy-done.12, bf16[2,128,128]{2,1,0:T(8,128)(2,1)} %copy-done.15, ...), custom_call_target="tpu_custom_call" | custom-call | flops 5033164800 | bytes 9633792 | tf_op jit(solution)/shard_map/pallas_call | solution.py:245
  44.0 1.3 %collective-permute-start.11 = (f32[2,128,128]{2,1,0:T(8,128)}, f32[2,128,128]{2,1,0:T(8,128)S(1)}, u32[]{:S(2)}, u32[]{:S(2)}) collective-permute-start(f32[2,128,128]{2,1,0:T(8,128)} %get-tuple-element.16.prev_ref), channel_id=1, source_target_pairs={{16,31},{17,30},{18,29},{19,28},{20,27},{21,26},{22,25},{23,24}} | collective-permute-start | bytes 393224 | tf_op jit(solution)/shard_map/ppermute | solution.py:231
  45.3 1.3 %collective-permute-start.12 = (bf16[2,128,128]{2,1,0:T(8,128)(2,1)}, bf16[2,128,128]{2,1,0:T(8,128)(2,1)S(1)}, u32[]{:S(2)}, u32[]{:S(2)}) collective-permute-start(bf16[2,128,128]{2,1,0:T(8,128)(2,1)} %get-tuple-element.17), channel_id=1, source_target_pairs={{17,31},{18,30},{19,29},{20,28},{21,27},{22,26},{23,25}} | collective-permute-start | bytes 196616 | tf_op jit(solution)/shard_map/ppermute | solution.py:231
  46.6 1.3 %collective-permute-start.13 = (bf16[2,128,128]{2,1,0:T(8,128)(2,1)}, bf16[2,128,128]{2,1,0:T(8,128)(2,1)S(1)}, u32[]{:S(2)}, u32[]{:S(2)}) collective-permute-start(bf16[2,128,128]{2,1,0:T(8,128)(2,1)} %get-tuple-element.17), channel_id=1, source_target_pairs={{18,31},{19,30},{20,29},{21,28},{22,27},{23,26}} | collective-permute-start | bytes 196616 | tf_op jit(solution)/shard_map/ppermute | solution.py:231
  47.9 1.6 %collective-permute-start.14 = (bf16[2,128,128]{2,1,0:T(8,128)(2,1)}, bf16[2,128,128]{2,1,0:T(8,128)(2,1)S(1)}, u32[]{:S(2)}, u32[]{:S(2)}) collective-permute-start(bf16[2,128,128]{2,1,0:T(8,128)(2,1)} %get-tuple-element.17), channel_id=1, source_target_pairs={{19,31},{20,30},{21,29},{22,28},{23,27}} | collective-permute-start | bytes 196616 | tf_op jit(solution)/shard_map/ppermute | solution.py:231
  49.5 23.8 %collective-permute-done.12.back1_ref = bf16[2,128,128]{2,1,0:T(8,128)(2,1)S(1)} collective-permute-done((bf16[2,128,128]{2,1,0:T(8,128)(2,1)}, bf16[2,128,128]{2,1,0:T(8,128)(2,1)S(1)}, u32[]{:S(2)}, u32[]{:S(2)}) %collective-permute-start.12) | collective-permute-done | bytes 65568 | tf_op jit(solution)/shard_map/ppermute | solution.py:231
  73.3 0.6 copy-done.7
  73.9 0.0 copy-done.10
  73.9 0.0 copy-done.4
  74.0 10.8 %shard_map.85 = (f32[2,128,128]{2,1,0:T(8,128)}, bf16[2,128,128]{2,1,0:T(8,128)(2,1)}) custom-call(s32[1]{0:T(128)} %bitcast.keep_ref, f32[2,128,128]{2,1,0:T(8,128)} %get-tuple-element.16.prev_ref, f32[2,128,128]{2,1,0:T(8,128)} %copy-done.4, bf16[2,128,128]{2,1,0:T(8,128)(2,1)} %copy-done.7, bf16[2,128,128]{2,1,0:T(8,128)(2,1)} %copy-done.10, ...), custom_call_target="tpu_custom_call" | custom-call | flops 5033164800 | bytes 9633792 | tf_op jit(solution)/shard_map/pallas_call | solution.py:245
  (42 shorter events, 0.2 us)
Async XLA Ops:
  0.0 2.2 %copy-start = (s32[8,4]{0,1:T(4,128)S(1)}, s32[8,4]{0,1:T(4,128)}, u32[]{:S(2)}) copy-start(s32[8,4]{0,1:T(4,128)} %param.9) | copy-start | bytes 388
  0.0 3.3 %collective-permute-start = (f32[2,128,128]{2,1,0:T(8,128)}, f32[2,128,128]{2,1,0:T(8,128)S(1)}, u32[]{:S(2)}, u32[]{:S(2)}) collective-permute-start(f32[2,128,128]{2,1,0:T(8,128)} %own_ref.1), channel_id=1, source_target_pairs={{8,1},{9,2},{10,3},{11,4},{12,5},{13,6},{14,7}} | collective-permute-start | bytes 393224 | tf_op jit(solution)/shard_map/ppermute | solution.py:217
  0.8 2.6 %collective-permute-start.1 = (f32[2,128,128]{2,1,0:T(8,128)}, f32[2,128,128]{2,1,0:T(8,128)S(1)}, u32[]{:S(2)}, u32[]{:S(2)}) collective-permute-start(f32[2,128,128]{2,1,0:T(8,128)} %own_ref.1), channel_id=1, source_target_pairs={{8,2},{9,3},{10,4},{11,5},{12,6},{13,7}} | collective-permute-start | bytes 393224 | tf_op jit(solution)/shard_map/ppermute | solution.py:217
  1.5 1.9 %collective-permute-start.2 = (f32[2,128,128]{2,1,0:T(8,128)}, f32[2,128,128]{2,1,0:T(8,128)S(1)}, u32[]{:S(2)}, u32[]{:S(2)}) collective-permute-start(f32[2,128,128]{2,1,0:T(8,128)} %own_ref.1), channel_id=1, source_target_pairs={{8,3},{9,4},{10,5},{11,6},{12,7}} | collective-permute-start | bytes 393224 | tf_op jit(solution)/shard_map/ppermute | solution.py:217
  3.3 0.8 copy-start.1
  3.4 0.8 copy-start.2
  3.4 0.8 copy-start.3
  15.0 2.9 %collective-permute-start.3 = (f32[2,128,128]{2,1,0:T(8,128)}, f32[2,128,128]{2,1,0:T(8,128)S(1)}, u32[]{:S(2)}, u32[]{:S(2)}) collective-permute-start(f32[2,128,128]{2,1,0:T(8,128)} %get-tuple-element.12.prev_ref), channel_id=1, source_target_pairs={{0,15},{1,14},{2,13},{3,12},{4,11},{5,10},{6,9},{7,8}} | collective-permute-start | bytes 393224 | tf_op jit(solution)/shard_map/ppermute | solution.py:231
  15.7 2.2 %collective-permute-start.4 = (bf16[2,128,128]{2,1,0:T(8,128)(2,1)}, bf16[2,128,128]{2,1,0:T(8,128)(2,1)S(1)}, u32[]{:S(2)}, u32[]{:S(2)}) collective-permute-start(bf16[2,128,128]{2,1,0:T(8,128)(2,1)} %get-tuple-element.13), channel_id=1, source_target_pairs={{1,15},{2,14},{3,13},{4,12},{5,11},{6,10},{7,9}} | collective-permute-start | bytes 196616 | tf_op jit(solution)/shard_map/ppermute | solution.py:231
  16.4 1.6 %collective-permute-start.5 = (bf16[2,128,128]{2,1,0:T(8,128)(2,1)}, bf16[2,128,128]{2,1,0:T(8,128)(2,1)S(1)}, u32[]{:S(2)}, u32[]{:S(2)}) collective-permute-start(bf16[2,128,128]{2,1,0:T(8,128)(2,1)} %get-tuple-element.13), channel_id=1, source_target_pairs={{2,15},{3,14},{4,13},{5,12},{6,11},{7,10}} | collective-permute-start | bytes 196616 | tf_op jit(solution)/shard_map/ppermute | solution.py:231
  17.1 0.9 %collective-permute-start.6 = (bf16[2,128,128]{2,1,0:T(8,128)(2,1)}, bf16[2,128,128]{2,1,0:T(8,128)(2,1)S(1)}, u32[]{:S(2)}, u32[]{:S(2)}) collective-permute-start(bf16[2,128,128]{2,1,0:T(8,128)(2,1)} %get-tuple-element.13), channel_id=1, source_target_pairs={{3,15},{4,14},{5,13},{6,12},{7,11}} | collective-permute-start | bytes 196616 | tf_op jit(solution)/shard_map/ppermute | solution.py:231
  17.9 0.6 copy-start.8
  18.0 0.6 copy-start.11
  18.0 0.6 copy-start.14
  18.0 0.7 copy-start.5
  29.5 3.0 %collective-permute-start.7 = (f32[2,128,128]{2,1,0:T(8,128)}, f32[2,128,128]{2,1,0:T(8,128)S(1)}, u32[]{:S(2)}, u32[]{:S(2)}) collective-permute-start(f32[2,128,128]{2,1,0:T(8,128)} %get-tuple-element.14.prev_ref), channel_id=1, source_target_pairs={{8,23},{9,22},{10,21},{11,20},{12,19},{13,18},{14,17},{15,16}} | collective-permute-start | bytes 393224 | tf_op jit(solution)/shard_map/ppermute | solution.py:231
  30.2 2.2 %collective-permute-start.10 = (bf16[2,128,128]{2,1,0:T(8,128)(2,1)}, bf16[2,128,128]{2,1,0:T(8,128)(2,1)S(1)}, u32[]{:S(2)}, u32[]{:S(2)}) collective-permute-start(bf16[2,128,128]{2,1,0:T(8,128)(2,1)} %get-tuple-element.15), channel_id=1, source_target_pairs={{11,23},{12,22},{13,21},{14,20},{15,19}} | collective-permute-start | bytes 196616 | tf_op jit(solution)/shard_map/ppermute | solution.py:231
  30.8 1.6 %collective-permute-start.8 = (bf16[2,128,128]{2,1,0:T(8,128)(2,1)}, bf16[2,128,128]{2,1,0:T(8,128)(2,1)S(1)}, u32[]{:S(2)}, u32[]{:S(2)}) collective-permute-start(bf16[2,128,128]{2,1,0:T(8,128)(2,1)} %get-tuple-element.15), channel_id=1, source_target_pairs={{9,23},{10,22},{11,21},{12,20},{13,19},{14,18},{15,17}} | collective-permute-start | bytes 196616 | tf_op jit(solution)/shard_map/ppermute | solution.py:231
  31.5 0.9 %collective-permute-start.9 = (bf16[2,128,128]{2,1,0:T(8,128)(2,1)}, bf16[2,128,128]{2,1,0:T(8,128)(2,1)S(1)}, u32[]{:S(2)}, u32[]{:S(2)}) collective-permute-start(bf16[2,128,128]{2,1,0:T(8,128)(2,1)} %get-tuple-element.15), channel_id=1, source_target_pairs={{10,23},{11,22},{12,21},{13,20},{14,19},{15,18}} | collective-permute-start | bytes 196616 | tf_op jit(solution)/shard_map/ppermute | solution.py:231
  32.4 0.6 copy-start.9
  32.4 0.6 copy-start.12
  32.5 0.6 copy-start.15
  32.5 0.7 copy-start.6
  44.0 29.3 %collective-permute-start.11 = (f32[2,128,128]{2,1,0:T(8,128)}, f32[2,128,128]{2,1,0:T(8,128)S(1)}, u32[]{:S(2)}, u32[]{:S(2)}) collective-permute-start(f32[2,128,128]{2,1,0:T(8,128)} %get-tuple-element.16.prev_ref), channel_id=1, source_target_pairs={{16,31},{17,30},{18,29},{19,28},{20,27},{21,26},{22,25},{23,24}} | collective-permute-start | bytes 393224 | tf_op jit(solution)/shard_map/ppermute | solution.py:231
  45.3 28.0 %collective-permute-start.12 = (bf16[2,128,128]{2,1,0:T(8,128)(2,1)}, bf16[2,128,128]{2,1,0:T(8,128)(2,1)S(1)}, u32[]{:S(2)}, u32[]{:S(2)}) collective-permute-start(bf16[2,128,128]{2,1,0:T(8,128)(2,1)} %get-tuple-element.17), channel_id=1, source_target_pairs={{17,31},{18,30},{19,29},{20,28},{21,27},{22,26},{23,25}} | collective-permute-start | bytes 196616 | tf_op jit(solution)/shard_map/ppermute | solution.py:231
  46.6 26.7 %collective-permute-start.13 = (bf16[2,128,128]{2,1,0:T(8,128)(2,1)}, bf16[2,128,128]{2,1,0:T(8,128)(2,1)S(1)}, u32[]{:S(2)}, u32[]{:S(2)}) collective-permute-start(bf16[2,128,128]{2,1,0:T(8,128)(2,1)} %get-tuple-element.17), channel_id=1, source_target_pairs={{18,31},{19,30},{20,29},{21,28},{22,27},{23,26}} | collective-permute-start | bytes 196616 | tf_op jit(solution)/shard_map/ppermute | solution.py:231
  47.9 25.4 %collective-permute-start.14 = (bf16[2,128,128]{2,1,0:T(8,128)(2,1)}, bf16[2,128,128]{2,1,0:T(8,128)(2,1)S(1)}, u32[]{:S(2)}, u32[]{:S(2)}) collective-permute-start(bf16[2,128,128]{2,1,0:T(8,128)(2,1)} %get-tuple-element.17), channel_id=1, source_target_pairs={{19,31},{20,30},{21,29},{22,28},{23,27}} | collective-permute-start | bytes 196616 | tf_op jit(solution)/shard_map/ppermute | solution.py:231
  73.3 0.6 copy-start.7
  73.3 0.7 copy-start.10
  73.3 0.7 copy-start.13
  73.3 0.7 copy-start.4

commit v11 on v10

--- a/solution.py
+++ b/solution.py
@@ -213,7 +213,8 @@
 
     def first_inputs():
         def behind(distance):
-            pairs = [(n_seq + q, q + distance) for q in range(n_seq) if q + distance < n_seq]
+            source = (n_seg - 1) * n_seq
+            pairs = [(source + q, q + distance) for q in range(n_seq) if q + distance < n_seq]
             return lax.ppermute(patches, axes, pairs)
 
         return patches, behind(1), behind(2), behind(BACK + 1)

time: 85.6 us -> 86.4 us (level)
  starting transfers between devices: 13.3 us -> 18.6 us
  waiting for transfers between devices: 23.9 us -> 19.4 us
    ppermute x12, waiting for transfers between devices: 23.8 us -> 17.2 us  [send(): return lax.ppermute(block, axes, pairs)]
    ppermute x3, starting transfers between devices: 2.13 us -> 7.4 us  [behind(): return lax.ppermute(patches, axes, pairs)]
    ppermute x3, waiting for transfers between devices: 0.01 us -> 2.29 us  [behind(): return lax.ppermute(patches, axes, pairs)]
  transfers between devices with their start and end apart: 15 -> 15, of which waited for: 1 -> 2; matrix products, arithmetic and copies ran while one was open for 1% -> 1% of each run, Pallas kernels for 0% -> 0%
where the time goes in v11:
time: 86.4 us; the launch traced here: 85.8 us
  Pallas kernels  43.4 us (50%)
  waiting for transfers between devices  19.4 us (22%)
  starting transfers between devices  18.6 us (22%)
  local copies, waits for them, and re-layouts  2.97 us (3%)
  other arithmetic  0.89 us (1%)
    pallas_call x4, Pallas kernels, body(): out, result_low = call(keep, out, *inputs, mask, *weights)  43.4 us
    ppermute x12, waiting for transfers between devices, send(): return lax.ppermute(block, axes, pairs)  17.2 us
    ppermute x12, starting transfers between devices, send(): return lax.ppermute(block, axes, pairs)  11.2 us
    ppermute x3, starting transfers between devices, behind(): return lax.ppermute(patches, axes, pairs)  7.4 us
    ppermute x3, waiting for transfers between devices, behind(): return lax.ppermute(patches, axes, pairs)  2.29 us
    unnamed x32, local copies, waits for them, and re-layouts  2.01 us
  transfers between devices with their start and end apart: 15, of which 2 were waited for; matrix products, arithmetic and copies ran while one was open for 1% of the time, Pallas kernels for 0%

profile of v11, /device:TPU:15, one launch (start us, length us, event | category | flops | bytes accessed | tf_op | source)
XLA Modules:
  0.0 85.8 jit_solution(13178670088938127748)
XLA Ops:
  0.0 3.8 %collective-permute-start = (f32[2,128,128]{2,1,0:T(8,128)}, f32[2,128,128]{2,1,0:T(8,128)S(1)}, u32[]{:S(2)}, u32[]{:S(2)}) collective-permute-start(f32[2,128,128]{2,1,0:T(8,128)} %own_ref.1), channel_id=1, source_target_pairs={{24,1},{25,2},{26,3},{27,4},{28,5},{29,6},{30,7}} | collective-permute-start | bytes 393224 | tf_op jit(solution)/shard_map/ppermute | solution.py:218
  3.8 1.3 %collective-permute-start.1 = (f32[2,128,128]{2,1,0:T(8,128)}, f32[2,128,128]{2,1,0:T(8,128)S(1)}, u32[]{:S(2)}, u32[]{:S(2)}) collective-permute-start(f32[2,128,128]{2,1,0:T(8,128)} %own_ref.1), channel_id=1, source_target_pairs={{24,2},{25,3},{26,4},{27,5},{28,6},{29,7}} | collective-permute-start | bytes 393224 | tf_op jit(solution)/shard_map/ppermute | solution.py:218
  5.1 2.3 %collective-permute-start.2 = (f32[2,128,128]{2,1,0:T(8,128)}, f32[2,128,128]{2,1,0:T(8,128)S(1)}, u32[]{:S(2)}, u32[]{:S(2)}) collective-permute-start(f32[2,128,128]{2,1,0:T(8,128)} %own_ref.1), channel_id=1, source_target_pairs={{24,3},{25,4},{26,5},{27,6},{28,7}} | collective-permute-start | bytes 393224 | tf_op jit(solution)/shard_map/ppermute | solution.py:218
  7.5 0.2 dynamic-slice_reduce_fusion
  7.7 0.1 compare_reduce_fusion
  7.8 0.1 broadcast_bitcast_fusion
  7.8 0.8 fusion.1.mask_ref
  8.6 2.3 %collective-permute-done.2.edge_ref = f32[2,128,128]{2,1,0:T(8,128)S(1)} collective-permute-done((f32[2,128,128]{2,1,0:T(8,128)}, f32[2,128,128]{2,1,0:T(8,128)S(1)}, u32[]{:S(2)}, u32[]{:S(2)}) %collective-permute-start.2) | collective-permute-done | bytes 131104 | tf_op jit(solution)/shard_map/ppermute | solution.py:218
  10.9 0.7 broadcast_in_dim.6.prev_ref
  11.6 10.9 %shard_map.82 = (f32[2,128,128]{2,1,0:T(8,128)}, bf16[2,128,128]{2,1,0:T(8,128)(2,1)}) custom-call(s32[1]{0:T(128)} %bitcast.3.keep_ref, f32[2,128,128]{2,1,0:T(8,128)} %broadcast_in_dim.6.prev_ref, f32[2,128,128]{2,1,0:T(8,128)} %own_ref.1, f32[2,128,128]{2,1,0:T(8,128)} %copy-done.1, f32[2,128,128]{2,1,0:T(8,128)} %copy-done.2, f32[2,128,128]{2,1,0:T(8,128)} %copy-done.3, ...), custom_call_target="tpu_custom_call" | custom-call | flops 5033164800 | bytes 9633792 | tf_op jit(solution)/shard_map/pallas_call | solution.py:246
  22.5 0.7 collective-permute-start.3
  23.2 0.7 collective-permute-start.4
  23.9 0.7 collective-permute-start.5
  24.6 0.8 collective-permute-start.6
  25.5 0.5 copy-done.8
  26.0 0.0 copy-done.11
  26.1 10.8 %shard_map.83 = (f32[2,128,128]{2,1,0:T(8,128)}, bf16[2,128,128]{2,1,0:T(8,128)(2,1)}) custom-call(s32[1]{0:T(128)} %bitcast.2.keep_ref, f32[2,128,128]{2,1,0:T(8,128)} %get-tuple-element.12.prev_ref, f32[2,128,128]{2,1,0:T(8,128)} %copy-done.5, bf16[2,128,128]{2,1,0:T(8,128)(2,1)} %copy-done.8, bf16[2,128,128]{2,1,0:T(8,128)(2,1)} %copy-done.11, ...), custom_call_target="tpu_custom_call" | custom-call | flops 5033164800 | bytes 9633792 | tf_op jit(solution)/shard_map/pallas_call | solution.py:246
  37.0 0.7 collective-permute-start.7
  37.7 0.7 collective-permute-start.10
  38.3 0.7 collective-permute-start.8
  39.0 0.9 %collective-permute-start.9 = (bf16[2,128,128]{2,1,0:T(8,128)(2,1)}, bf16[2,128,128]{2,1,0:T(8,128)(2,1)S(1)}, u32[]{:S(2)}, u32[]{:S(2)}) collective-permute-start(bf16[2,128,128]{2,1,0:T(8,128)(2,1)} %get-tuple-element.15), channel_id=1, source_target_pairs={{10,23},{11,22},{12,21},{13,20},{14,19},{15,18}} | collective-permute-start | bytes 196616 | tf_op jit(solution)/shard_map/ppermute | solution.py:232
  40.0 0.6 copy-done.9
  40.6 0.0 copy-done.6
  40.6 10.8 %shard_map.84 = (f32[2,128,128]{2,1,0:T(8,128)}, bf16[2,128,128]{2,1,0:T(8,128)(2,1)}) custom-call(s32[1]{0:T(128)} %bitcast.1.keep_ref, f32[2,128,128]{2,1,0:T(8,128)} %get-tuple-element.14.prev_ref, f32[2,128,128]{2,1,0:T(8,128)} %copy-done.6, bf16[2,128,128]{2,1,0:T(8,128)(2,1)} %copy-done.12, bf16[2,128,128]{2,1,0:T(8,128)(2,1)} %copy-done.15, ...), custom_call_target="tpu_custom_call" | custom-call | flops 5033164800 | bytes 9633792 | tf_op jit(solution)/shard_map/pallas_call | solution.py:246
  51.5 1.3 %collective-permute-start.11 = (f32[2,128,128]{2,1,0:T(8,128)}, f32[2,128,128]{2,1,0:T(8,128)S(1)}, u32[]{:S(2)}, u32[]{:S(2)}) collective-permute-start(f32[2,128,128]{2,1,0:T(8,128)} %get-tuple-element.16.prev_ref), channel_id=1, source_target_pairs={{16,31},{17,30},{18,29},{19,28},{20,27},{21,26},{22,25},{23,24}} | collective-permute-start | bytes 393224 | tf_op jit(solution)/shard_map/ppermute | solution.py:232
  52.8 1.3 %collective-permute-start.12 = (bf16[2,128,128]{2,1,0:T(8,128)(2,1)}, bf16[2,128,128]{2,1,0:T(8,128)(2,1)S(1)}, u32[]{:S(2)}, u32[]{:S(2)}) collective-permute-start(bf16[2,128,128]{2,1,0:T(8,128)(2,1)} %get-tuple-element.17), channel_id=1, source_target_pairs={{17,31},{18,30},{19,29},{20,28},{21,27},{22,26},{23,25}} | collective-permute-start | bytes 196616 | tf_op jit(solution)/shard_map/ppermute | solution.py:232
  54.1 1.3 %collective-permute-start.13 = (bf16[2,128,128]{2,1,0:T(8,128)(2,1)}, bf16[2,128,128]{2,1,0:T(8,128)(2,1)S(1)}, u32[]{:S(2)}, u32[]{:S(2)}) collective-permute-start(bf16[2,128,128]{2,1,0:T(8,128)(2,1)} %get-tuple-element.17), channel_id=1, source_target_pairs={{18,31},{19,30},{20,29},{21,28},{22,27},{23,26}} | collective-permute-start | bytes 196616 | tf_op jit(solution)/shard_map/ppermute | solution.py:232
  55.4 1.6 %collective-permute-start.14 = (bf16[2,128,128]{2,1,0:T(8,128)(2,1)}, bf16[2,128,128]{2,1,0:T(8,128)(2,1)S(1)}, u32[]{:S(2)}, u32[]{:S(2)}) collective-permute-start(bf16[2,128,128]{2,1,0:T(8,128)(2,1)} %get-tuple-element.17), channel_id=1, source_target_pairs={{19,31},{20,30},{21,29},{22,28},{23,27}} | collective-permute-start | bytes 196616 | tf_op jit(solution)/shard_map/ppermute | solution.py:232
  56.9 17.1 %collective-permute-done.12.back1_ref = bf16[2,128,128]{2,1,0:T(8,128)(2,1)S(1)} collective-permute-done((bf16[2,128,128]{2,1,0:T(8,128)(2,1)}, bf16[2,128,128]{2,1,0:T(8,128)(2,1)S(1)}, u32[]{:S(2)}, u32[]{:S(2)}) %collective-permute-start.12) | collective-permute-done | bytes 65568 | tf_op jit(solution)/shard_map/ppermute | solution.py:232
  74.1 0.6 copy-done.7
  74.8 0.0 copy-done.4
  74.8 10.8 %shard_map.85 = (f32[2,128,128]{2,1,0:T(8,128)}, bf16[2,128,128]{2,1,0:T(8,128)(2,1)}) custom-call(s32[1]{0:T(128)} %bitcast.keep_ref, f32[2,128,128]{2,1,0:T(8,128)} %get-tuple-element.16.prev_ref, f32[2,128,128]{2,1,0:T(8,128)} %copy-done.4, bf16[2,128,128]{2,1,0:T(8,128)(2,1)} %copy-done.7, bf16[2,128,128]{2,1,0:T(8,128)(2,1)} %copy-done.10, ...), custom_call_target="tpu_custom_call" | custom-call | flops 5033164800 | bytes 9633792 | tf_op jit(solution)/shard_map/pallas_call | solution.py:246
  (42 shorter events, 0.3 us)
Async XLA Ops:
  0.0 7.5 %copy-start = (s32[8,4]{0,1:T(4,128)S(1)}, s32[8,4]{0,1:T(4,128)}, u32[]{:S(2)}) copy-start(s32[8,4]{0,1:T(4,128)} %param.9) | copy-start | bytes 388
  0.0 8.6 %collective-permute-start = (f32[2,128,128]{2,1,0:T(8,128)}, f32[2,128,128]{2,1,0:T(8,128)S(1)}, u32[]{:S(2)}, u32[]{:S(2)}) collective-permute-start(f32[2,128,128]{2,1,0:T(8,128)} %own_ref.1), channel_id=1, source_target_pairs={{24,1},{25,2},{26,3},{27,4},{28,5},{29,6},{30,7}} | collective-permute-start | bytes 393224 | tf_op jit(solution)/shard_map/ppermute | solution.py:218
  3.8 4.8 %collective-permute-start.1 = (f32[2,128,128]{2,1,0:T(8,128)}, f32[2,128,128]{2,1,0:T(8,128)S(1)}, u32[]{:S(2)}, u32[]{:S(2)}) collective-permute-start(f32[2,128,128]{2,1,0:T(8,128)} %own_ref.1), channel_id=1, source_target_pairs={{24,2},{25,3},{26,4},{27,5},{28,6},{29,7}} | collective-permute-start | bytes 393224 | tf_op jit(solution)/shard_map/ppermute | solution.py:218
  5.1 5.8 %collective-permute-start.2 = (f32[2,128,128]{2,1,0:T(8,128)}, f32[2,128,128]{2,1,0:T(8,128)S(1)}, u32[]{:S(2)}, u32[]{:S(2)}) collective-permute-start(f32[2,128,128]{2,1,0:T(8,128)} %own_ref.1), channel_id=1, source_target_pairs={{24,3},{25,4},{26,5},{27,6},{28,7}} | collective-permute-start | bytes 393224 | tf_op jit(solution)/shard_map/ppermute | solution.py:218
  8.6 3.0 %copy-start.1 = (f32[2,128,128]{2,1,0:T(8,128)}, f32[2,128,128]{2,1,0:T(8,128)S(1)}, u32[]{:S(2)}) copy-start(f32[2,128,128]{2,1,0:T(8,128)S(1)} %collective-permute-done.back1_ref) | copy-start | bytes 393220
  8.6 3.0 %copy-start.2 = (f32[2,128,128]{2,1,0:T(8,128)}, f32[2,128,128]{2,1,0:T(8,128)S(1)}, u32[]{:S(2)}) copy-start(f32[2,128,128]{2,1,0:T(8,128)S(1)} %collective-permute-done.1.back2_ref) | copy-start | bytes 393220
  10.9 0.7 copy-start.3
  22.5 2.9 %collective-permute-start.3 = (f32[2,128,128]{2,1,0:T(8,128)}, f32[2,128,128]{2,1,0:T(8,128)S(1)}, u32[]{:S(2)}, u32[]{:S(2)}) collective-permute-start(f32[2,128,128]{2,1,0:T(8,128)} %get-tuple-element.12.prev_ref), channel_id=1, source_target_pairs={{0,15},{1,14},{2,13},{3,12},{4,11},{5,10},{6,9},{7,8}} | collective-permute-start | bytes 393224 | tf_op jit(solution)/shard_map/ppermute | solution.py:232
  23.2 2.2 %collective-permute-start.4 = (bf16[2,128,128]{2,1,0:T(8,128)(2,1)}, bf16[2,128,128]{2,1,0:T(8,128)(2,1)S(1)}, u32[]{:S(2)}, u32[]{:S(2)}) collective-permute-start(bf16[2,128,128]{2,1,0:T(8,128)(2,1)} %get-tuple-element.13), channel_id=1, source_target_pairs={{1,15},{2,14},{3,13},{4,12},{5,11},{6,10},{7,9}} | collective-permute-start | bytes 196616 | tf_op jit(solution)/shard_map/ppermute | solution.py:232
  23.9 1.6 %collective-permute-start.5 = (bf16[2,128,128]{2,1,0:T(8,128)(2,1)}, bf16[2,128,128]{2,1,0:T(8,128)(2,1)S(1)}, u32[]{:S(2)}, u32[]{:S(2)}) collective-permute-start(bf16[2,128,128]{2,1,0:T(8,128)(2,1)} %get-tuple-element.13), channel_id=1, source_target_pairs={{2,15},{3,14},{4,13},{5,12},{6,11},{7,10}} | collective-permute-start | bytes 196616 | tf_op jit(solution)/shard_map/ppermute | solution.py:232
  24.6 0.9 %collective-permute-start.6 = (bf16[2,128,128]{2,1,0:T(8,128)(2,1)}, bf16[2,128,128]{2,1,0:T(8,128)(2,1)S(1)}, u32[]{:S(2)}, u32[]{:S(2)}) collective-permute-start(bf16[2,128,128]{2,1,0:T(8,128)(2,1)} %get-tuple-element.13), channel_id=1, source_target_pairs={{3,15},{4,14},{5,13},{6,12},{7,11}} | collective-permute-start | bytes 196616 | tf_op jit(solution)/shard_map/ppermute | solution.py:232
  25.4 0.6 copy-start.8
  25.4 0.6 copy-start.11
  25.5 0.6 copy-start.14
  25.5 0.7 copy-start.5
  37.0 3.0 %collective-permute-start.7 = (f32[2,128,128]{2,1,0:T(8,128)}, f32[2,128,128]{2,1,0:T(8,128)S(1)}, u32[]{:S(2)}, u32[]{:S(2)}) collective-permute-start(f32[2,128,128]{2,1,0:T(8,128)} %get-tuple-element.14.prev_ref), channel_id=1, source_target_pairs={{8,23},{9,22},{10,21},{11,20},{12,19},{13,18},{14,17},{15,16}} | collective-permute-start | bytes 393224 | tf_op jit(solution)/shard_map/ppermute | solution.py:232
  37.7 2.2 %collective-permute-start.10 = (bf16[2,128,128]{2,1,0:T(8,128)(2,1)}, bf16[2,128,128]{2,1,0:T(8,128)(2,1)S(1)}, u32[]{:S(2)}, u32[]{:S(2)}) collective-permute-start(bf16[2,128,128]{2,1,0:T(8,128)(2,1)} %get-tuple-element.15), channel_id=1, source_target_pairs={{11,23},{12,22},{13,21},{14,20},{15,19}} | collective-permute-start | bytes 196616 | tf_op jit(solution)/shard_map/ppermute | solution.py:232
  38.3 1.6 %collective-permute-start.8 = (bf16[2,128,128]{2,1,0:T(8,128)(2,1)}, bf16[2,128,128]{2,1,0:T(8,128)(2,1)S(1)}, u32[]{:S(2)}, u32[]{:S(2)}) collective-permute-start(bf16[2,128,128]{2,1,0:T(8,128)(2,1)} %get-tuple-element.15), channel_id=1, source_target_pairs={{9,23},{10,22},{11,21},{12,20},{13,19},{14,18},{15,17}} | collective-permute-start | bytes 196616 | tf_op jit(solution)/shard_map/ppermute | solution.py:232
  39.0 0.9 %collective-permute-start.9 = (bf16[2,128,128]{2,1,0:T(8,128)(2,1)}, bf16[2,128,128]{2,1,0:T(8,128)(2,1)S(1)}, u32[]{:S(2)}, u32[]{:S(2)}) collective-permute-start(bf16[2,128,128]{2,1,0:T(8,128)(2,1)} %get-tuple-element.15), channel_id=1, source_target_pairs={{10,23},{11,22},{12,21},{13,20},{14,19},{15,18}} | collective-permute-start | bytes 196616 | tf_op jit(solution)/shard_map/ppermute | solution.py:232
  39.9 0.6 copy-start.9
  39.9 0.6 copy-start.12
  40.0 0.6 copy-start.15
  40.0 0.7 copy-start.6
  51.5 22.6 %collective-permute-start.11 = (f32[2,128,128]{2,1,0:T(8,128)}, f32[2,128,128]{2,1,0:T(8,128)S(1)}, u32[]{:S(2)}, u32[]{:S(2)}) collective-permute-start(f32[2,128,128]{2,1,0:T(8,128)} %get-tuple-element.16.prev_ref), channel_id=1, source_target_pairs={{16,31},{17,30},{18,29},{19,28},{20,27},{21,26},{22,25},{23,24}} | collective-permute-start | bytes 393224 | tf_op jit(solution)/shard_map/ppermute | solution.py:232
  52.8 21.3 %collective-permute-start.12 = (bf16[2,128,128]{2,1,0:T(8,128)(2,1)}, bf16[2,128,128]{2,1,0:T(8,128)(2,1)S(1)}, u32[]{:S(2)}, u32[]{:S(2)}) collective-permute-start(bf16[2,128,128]{2,1,0:T(8,128)(2,1)} %get-tuple-element.17), channel_id=1, source_target_pairs={{17,31},{18,30},{19,29},{20,28},{21,27},{22,26},{23,25}} | collective-permute-start | bytes 196616 | tf_op jit(solution)/shard_map/ppermute | solution.py:232
  54.1 20.0 %collective-permute-start.13 = (bf16[2,128,128]{2,1,0:T(8,128)(2,1)}, bf16[2,128,128]{2,1,0:T(8,128)(2,1)S(1)}, u32[]{:S(2)}, u32[]{:S(2)}) collective-permute-start(bf16[2,128,128]{2,1,0:T(8,128)(2,1)} %get-tuple-element.17), channel_id=1, source_target_pairs={{18,31},{19,30},{20,29},{21,28},{22,27},{23,26}} | collective-permute-start | bytes 196616 | tf_op jit(solution)/shard_map/ppermute | solution.py:232
  55.4 18.7 %collective-permute-start.14 = (bf16[2,128,128]{2,1,0:T(8,128)(2,1)}, bf16[2,128,128]{2,1,0:T(8,128)(2,1)S(1)}, u32[]{:S(2)}, u32[]{:S(2)}) collective-permute-start(bf16[2,128,128]{2,1,0:T(8,128)(2,1)} %get-tuple-element.17), channel_id=1, source_target_pairs={{19,31},{20,30},{21,29},{22,28},{23,27}} | collective-permute-start | bytes 196616 | tf_op jit(solution)/shard_map/ppermute | solution.py:232
  74.1 0.6 copy-start.7
  74.1 0.7 copy-start.10
  74.1 0.7 copy-start.13
  74.1 0.7 copy-start.4

commit v12 on v11

--- a/solution.py
+++ b/solution.py
@@ -197,7 +197,7 @@
     key_pos = jnp.arange(span, dtype=jnp.int32)
     allowed = listed[None, :] & (key_pos[None, :] <= query_pos[:, None])
 
-    first_call = make_block_call(micro, rows, width_in, heads_all, False, jnp.float32)
+    first_call = make_block_call(micro, rows, width_in, heads_all, False, jnp.bfloat16)
     later_call = make_block_call(micro, rows, width_in, heads_all, True, jnp.bfloat16)
     mask = allowed.astype(jnp.float32)
     weights = (
@@ -215,8 +215,9 @@
         def behind(distance):
             source = (n_seg - 1) * n_seq
             pairs = [(source + q, q + distance) for q in range(n_seq) if q + distance < n_seq]
-            return lax.ppermute(patches, axes, pairs)
-
+            return lax.ppermute(patches_low, axes, pairs)
+
+        patches_low = patches.astype(jnp.bfloat16)
         return patches, behind(1), behind(2), behind(BACK + 1)
 
     def next_inputs(result, result_low, turn):

time: 86.4 us -> 85.7 us (level)
  waiting for transfers between devices: 19.4 us -> 18.1 us
  other arithmetic: 0.89 us -> 1.82 us
    ppermute x3, waiting for transfers between devices: 2.29 us -> 0.57 us  [behind(): return lax.ppermute(patches_low, axes, pairs)]
    convert_element_type x0 -> x1, other arithmetic: none -> 0.93 us  [first_inputs(): patches_low = patches.astype(jnp.bfloat16)]
where the time goes in v12:
time: 85.7 us; the launch traced here: 85.2 us
  Pallas kernels  43.3 us (51%)
  starting transfers between devices  18.4 us (21%)
  waiting for transfers between devices  18.1 us (21%)
  local copies, waits for them, and re-layouts  2.95 us (3%)
  other arithmetic  1.82 us (2%)
    pallas_call x4, Pallas kernels, body(): out, result_low = call(keep, out, *inputs, mask, *weights)  43.3 us
    ppermute x12, waiting for transfers between devices, send(): return lax.ppermute(block, axes, pairs)  17.5 us
    ppermute x12, starting transfers between devices, send(): return lax.ppermute(block, axes, pairs)  11.2 us
    ppermute x3, starting transfers between devices, behind(): return lax.ppermute(patches_low, axes, pairs)  7.28 us
    unnamed x32, local copies, waits for them, and re-layouts  2.01 us
  transfers between devices with their start and end apart: 15, of which 2 were waited for; matrix products, arithmetic and copies ran while one was open for 1% of the time, Pallas kernels for 0%

profile of v12, /device:TPU:15, one launch (start us, length us, event | category | flops | bytes accessed | tf_op | source)
XLA Modules:
  0.0 85.2 jit_solution(11900872436902793667)
XLA Ops:
  0.0 0.9 %convert_element_type.4 = bf16[2,128,128]{2,1,0:T(8,128)(2,1)S(1)} convert(f32[2,128,128]{2,1,0:T(8,128)} %own_ref.1) | non-fusion elementwise | flops 32768 | bytes 196608 | tf_op jit(solution)/shard_map/convert_element_type | solution.py:220
  0.9 3.7 %collective-permute-start = (bf16[2,128,128]{2,1,0:T(8,128)(2,1)S(1)}, bf16[2,128,128]{2,1,0:T(8,128)(2,1)S(1)}, u32[]{:S(2)}, u32[]{:S(2)}) collective-permute-start(bf16[2,128,128]{2,1,0:T(8,128)(2,1)S(1)} %convert_element_type.4), channel_id=1, source_target_pairs={{24,1},{25,2},{26,3},{27,4},{28,5},{29,6},{30,7}} | collective-permute-start | bytes 196616 | tf_op jit(solution)/shard_map/ppermute | solution.py:218
  4.6 1.3 %collective-permute-start.1 = (bf16[2,128,128]{2,1,0:T(8,128)(2,1)S(1)}, bf16[2,128,128]{2,1,0:T(8,128)(2,1)S(1)}, u32[]{:S(2)}, u32[]{:S(2)}) collective-permute-start(bf16[2,128,128]{2,1,0:T(8,128)(2,1)S(1)} %convert_element_type.4), channel_id=1, source_target_pairs={{24,2},{25,3},{26,4},{27,5},{28,6},{29,7}} | collective-permute-start | bytes 196616 | tf_op jit(solution)/shard_map/ppermute | solution.py:218
  5.9 2.3 %collective-permute-start.2 = (bf16[2,128,128]{2,1,0:T(8,128)(2,1)S(1)}, bf16[2,128,128]{2,1,0:T(8,128)(2,1)S(1)}, u32[]{:S(2)}, u32[]{:S(2)}) collective-permute-start(bf16[2,128,128]{2,1,0:T(8,128)(2,1)S(1)} %convert_element_type.4), channel_id=1, source_target_pairs={{24,3},{25,4},{26,5},{27,6},{28,7}} | collective-permute-start | bytes 196616 | tf_op jit(solution)/shard_map/ppermute | solution.py:218
  8.3 0.2 dynamic-slice_reduce_fusion
  8.5 0.1 compare_reduce_fusion
  8.6 0.1 broadcast_bitcast_fusion
  8.6 0.8 fusion.1.mask_ref
  9.4 0.6 collective-permute-done.2.edge_ref
  10.0 0.7 broadcast_in_dim.6.prev_ref
  10.7 10.8 %shard_map.82 = (f32[2,128,128]{2,1,0:T(8,128)}, bf16[2,128,128]{2,1,0:T(8,128)(2,1)}) custom-call(s32[1]{0:T(128)} %bitcast.3.keep_ref, f32[2,128,128]{2,1,0:T(8,128)} %broadcast_in_dim.6.prev_ref, f32[2,128,128]{2,1,0:T(8,128)} %own_ref.1, bf16[2,128,128]{2,1,0:T(8,128)(2,1)} %copy-done.4, bf16[2,128,128]{2,1,0:T(8,128)(2,1)} %copy-done.5, ...), custom_call_target="tpu_custom_call" | custom-call | flops 5033164800 | bytes 9633792 | tf_op jit(solution)/shard_map/pallas_call | solution.py:247
  21.5 0.7 collective-permute-start.3
  22.2 0.7 collective-permute-start.4
  22.9 0.7 collective-permute-start.5
  23.6 0.8 collective-permute-start.6
  24.5 0.5 copy-done.8
  25.1 10.8 %shard_map.83 = (f32[2,128,128]{2,1,0:T(8,128)}, bf16[2,128,128]{2,1,0:T(8,128)(2,1)}) custom-call(s32[1]{0:T(128)} %bitcast.2.keep_ref, f32[2,128,128]{2,1,0:T(8,128)} %get-tuple-element.12.prev_ref, f32[2,128,128]{2,1,0:T(8,128)} %copy-done.2, bf16[2,128,128]{2,1,0:T(8,128)(2,1)} %copy-done.8, bf16[2,128,128]{2,1,0:T(8,128)(2,1)} %copy-done.11, ...), custom_call_target="tpu_custom_call" | custom-call | flops 5033164800 | bytes 9633792 | tf_op jit(solution)/shard_map/pallas_call | solution.py:247
  36.0 0.7 collective-permute-start.7
  36.7 0.7 collective-permute-start.10
  37.3 0.7 collective-permute-start.8
  38.0 0.9 %collective-permute-start.9 = (bf16[2,128,128]{2,1,0:T(8,128)(2,1)}, bf16[2,128,128]{2,1,0:T(8,128)(2,1)S(1)}, u32[]{:S(2)}, u32[]{:S(2)}) collective-permute-start(bf16[2,128,128]{2,1,0:T(8,128)(2,1)} %get-tuple-element.15), channel_id=1, source_target_pairs={{10,23},{11,22},{12,21},{13,20},{14,19},{15,18}} | collective-permute-start | bytes 196616 | tf_op jit(solution)/shard_map/ppermute | solution.py:233
  39.0 0.6 copy-done.9
  39.6 0.0 copy-done.3
  39.6 10.8 %shard_map.84 = (f32[2,128,128]{2,1,0:T(8,128)}, bf16[2,128,128]{2,1,0:T(8,128)(2,1)}) custom-call(s32[1]{0:T(128)} %bitcast.1.keep_ref, f32[2,128,128]{2,1,0:T(8,128)} %get-tuple-element.14.prev_ref, f32[2,128,128]{2,1,0:T(8,128)} %copy-done.3, bf16[2,128,128]{2,1,0:T(8,128)(2,1)} %copy-done.12, bf16[2,128,128]{2,1,0:T(8,128)(2,1)} %copy-done.15, ...), custom_call_target="tpu_custom_call" | custom-call | flops 5033164800 | bytes 9633792 | tf_op jit(solution)/shard_map/pallas_call | solution.py:247
  50.5 1.3 %collective-permute-start.11 = (f32[2,128,128]{2,1,0:T(8,128)}, f32[2,128,128]{2,1,0:T(8,128)S(1)}, u32[]{:S(2)}, u32[]{:S(2)}) collective-permute-start(f32[2,128,128]{2,1,0:T(8,128)} %get-tuple-element.16.prev_ref), channel_id=1, source_target_pairs={{16,31},{17,30},{18,29},{19,28},{20,27},{21,26},{22,25},{23,24}} | collective-permute-start | bytes 393224 | tf_op jit(solution)/shard_map/ppermute | solution.py:233
  51.8 1.3 %collective-permute-start.12 = (bf16[2,128,128]{2,1,0:T(8,128)(2,1)}, bf16[2,128,128]{2,1,0:T(8,128)(2,1)S(1)}, u32[]{:S(2)}, u32[]{:S(2)}) collective-permute-start(bf16[2,128,128]{2,1,0:T(8,128)(2,1)} %get-tuple-element.17), channel_id=1, source_target_pairs={{17,31},{18,30},{19,29},{20,28},{21,27},{22,26},{23,25}} | collective-permute-start | bytes 196616 | tf_op jit(solution)/shard_map/ppermute | solution.py:233
  53.1 1.3 %collective-permute-start.13 = (bf16[2,128,128]{2,1,0:T(8,128)(2,1)}, bf16[2,128,128]{2,1,0:T(8,128)(2,1)S(1)}, u32[]{:S(2)}, u32[]{:S(2)}) collective-permute-start(bf16[2,128,128]{2,1,0:T(8,128)(2,1)} %get-tuple-element.17), channel_id=1, source_target_pairs={{18,31},{19,30},{20,29},{21,28},{22,27},{23,26}} | collective-permute-start | bytes 196616 | tf_op jit(solution)/shard_map/ppermute | solution.py:233
  54.4 1.6 %collective-permute-start.14 = (bf16[2,128,128]{2,1,0:T(8,128)(2,1)}, bf16[2,128,128]{2,1,0:T(8,128)(2,1)S(1)}, u32[]{:S(2)}, u32[]{:S(2)}) collective-permute-start(bf16[2,128,128]{2,1,0:T(8,128)(2,1)} %get-tuple-element.17), channel_id=1, source_target_pairs={{19,31},{20,30},{21,29},{22,28},{23,27}} | collective-permute-start | bytes 196616 | tf_op jit(solution)/shard_map/ppermute | solution.py:233
  56.0 17.5 %collective-permute-done.12.back1_ref = bf16[2,128,128]{2,1,0:T(8,128)(2,1)S(1)} collective-permute-done((bf16[2,128,128]{2,1,0:T(8,128)(2,1)}, bf16[2,128,128]{2,1,0:T(8,128)(2,1)S(1)}, u32[]{:S(2)}, u32[]{:S(2)}) %collective-permute-start.12) | collective-permute-done | bytes 65568 | tf_op jit(solution)/shard_map/ppermute | solution.py:233
  73.5 0.6 copy-done.7
  74.1 0.0 copy-done.1
  74.1 10.8 %shard_map.85 = (f32[2,128,128]{2,1,0:T(8,128)}, bf16[2,128,128]{2,1,0:T(8,128)(2,1)}) custom-call(s32[1]{0:T(128)} %bitcast.keep_ref, f32[2,128,128]{2,1,0:T(8,128)} %get-tuple-element.16.prev_ref, f32[2,128,128]{2,1,0:T(8,128)} %copy-done.1, bf16[2,128,128]{2,1,0:T(8,128)(2,1)} %copy-done.7, bf16[2,128,128]{2,1,0:T(8,128)(2,1)} %copy-done.10, ...), custom_call_target="tpu_custom_call" | custom-call | flops 5033164800 | bytes 9633792 | tf_op jit(solution)/shard_map/pallas_call | solution.py:247
  (43 shorter events, 0.3 us)
Async XLA Ops:
  0.0 8.3 %copy-start = (s32[8,4]{0,1:T(4,128)S(1)}, s32[8,4]{0,1:T(4,128)}, u32[]{:S(2)}) copy-start(s32[8,4]{0,1:T(4,128)} %param.9) | copy-start | bytes 388
  0.9 8.5 %collective-permute-start = (bf16[2,128,128]{2,1,0:T(8,128)(2,1)S(1)}, bf16[2,128,128]{2,1,0:T(8,128)(2,1)S(1)}, u32[]{:S(2)}, u32[]{:S(2)}) collective-permute-start(bf16[2,128,128]{2,1,0:T(8,128)(2,1)S(1)} %convert_element_type.4), channel_id=1, source_target_pairs={{24,1},{25,2},{26,3},{27,4},{28,5},{29,6},{30,7}} | collective-permute-start | bytes 196616 | tf_op jit(solution)/shard_map/ppermute | solution.py:218
  4.6 4.8 %collective-permute-start.1 = (bf16[2,128,128]{2,1,0:T(8,128)(2,1)S(1)}, bf16[2,128,128]{2,1,0:T(8,128)(2,1)S(1)}, u32[]{:S(2)}, u32[]{:S(2)}) collective-permute-start(bf16[2,128,128]{2,1,0:T(8,128)(2,1)S(1)} %convert_element_type.4), channel_id=1, source_target_pairs={{24,2},{25,3},{26,4},{27,5},{28,6},{29,7}} | collective-permute-start | bytes 196616 | tf_op jit(solution)/shard_map/ppermute | solution.py:218
  5.9 4.1 %collective-permute-start.2 = (bf16[2,128,128]{2,1,0:T(8,128)(2,1)S(1)}, bf16[2,128,128]{2,1,0:T(8,128)(2,1)S(1)}, u32[]{:S(2)}, u32[]{:S(2)}) collective-permute-start(bf16[2,128,128]{2,1,0:T(8,128)(2,1)S(1)} %convert_element_type.4), channel_id=1, source_target_pairs={{24,3},{25,4},{26,5},{27,6},{28,7}} | collective-permute-start | bytes 196616 | tf_op jit(solution)/shard_map/ppermute | solution.py:218
  9.4 1.3 %copy-start.4 = (bf16[2,128,128]{2,1,0:T(8,128)(2,1)}, bf16[2,128,128]{2,1,0:T(8,128)(2,1)S(1)}, u32[]{:S(2)}) copy-start(bf16[2,128,128]{2,1,0:T(8,128)(2,1)S(1)} %collective-permute-done.back1_ref) | copy-start | bytes 196612
  9.4 1.3 %copy-start.5 = (bf16[2,128,128]{2,1,0:T(8,128)(2,1)}, bf16[2,128,128]{2,1,0:T(8,128)(2,1)S(1)}, u32[]{:S(2)}) copy-start(bf16[2,128,128]{2,1,0:T(8,128)(2,1)S(1)} %collective-permute-done.1.back2_ref) | copy-start | bytes 196612
  10.0 0.7 copy-start.6
  21.5 2.9 %collective-permute-start.3 = (f32[2,128,128]{2,1,0:T(8,128)}, f32[2,128,128]{2,1,0:T(8,128)S(1)}, u32[]{:S(2)}, u32[]{:S(2)}) collective-permute-start(f32[2,128,128]{2,1,0:T(8,128)} %get-tuple-element.12.prev_ref), channel_id=1, source_target_pairs={{0,15},{1,14},{2,13},{3,12},{4,11},{5,10},{6,9},{7,8}} | collective-permute-start | bytes 393224 | tf_op jit(solution)/shard_map/ppermute | solution.py:233
  22.2 2.2 %collective-permute-start.4 = (bf16[2,128,128]{2,1,0:T(8,128)(2,1)}, bf16[2,128,128]{2,1,0:T(8,128)(2,1)S(1)}, u32[]{:S(2)}, u32[]{:S(2)}) collective-permute-start(bf16[2,128,128]{2,1,0:T(8,128)(2,1)} %get-tuple-element.13), channel_id=1, source_target_pairs={{1,15},{2,14},{3,13},{4,12},{5,11},{6,10},{7,9}} | collective-permute-start | bytes 196616 | tf_op jit(solution)/shard_map/ppermute | solution.py:233
  22.9 1.6 %collective-permute-start.5 = (bf16[2,128,128]{2,1,0:T(8,128)(2,1)}, bf16[2,128,128]{2,1,0:T(8,128)(2,1)S(1)}, u32[]{:S(2)}, u32[]{:S(2)}) collective-permute-start(bf16[2,128,128]{2,1,0:T(8,128)(2,1)} %get-tuple-element.13), channel_id=1, source_target_pairs={{2,15},{3,14},{4,13},{5,12},{6,11},{7,10}} | collective-permute-start | bytes 196616 | tf_op jit(solution)/shard_map/ppermute | solution.py:233
  23.6 0.9 %collective-permute-start.6 = (bf16[2,128,128]{2,1,0:T(8,128)(2,1)}, bf16[2,128,128]{2,1,0:T(8,128)(2,1)S(1)}, u32[]{:S(2)}, u32[]{:S(2)}) collective-permute-start(bf16[2,128,128]{2,1,0:T(8,128)(2,1)} %get-tuple-element.13), channel_id=1, source_target_pairs={{3,15},{4,14},{5,13},{6,12},{7,11}} | collective-permute-start | bytes 196616 | tf_op jit(solution)/shard_map/ppermute | solution.py:233
  24.4 0.6 copy-start.8
  24.4 0.6 copy-start.11
  24.5 0.6 copy-start.14
  24.5 0.7 copy-start.2
  36.0 3.0 %collective-permute-start.7 = (f32[2,128,128]{2,1,0:T(8,128)}, f32[2,128,128]{2,1,0:T(8,128)S(1)}, u32[]{:S(2)}, u32[]{:S(2)}) collective-permute-start(f32[2,128,128]{2,1,0:T(8,128)} %get-tuple-element.14.prev_ref), channel_id=1, source_target_pairs={{8,23},{9,22},{10,21},{11,20},{12,19},{13,18},{14,17},{15,16}} | collective-permute-start | bytes 393224 | tf_op jit(solution)/shard_map/ppermute | solution.py:233
  36.7 2.2 %collective-permute-start.10 = (bf16[2,128,128]{2,1,0:T(8,128)(2,1)}, bf16[2,128,128]{2,1,0:T(8,128)(2,1)S(1)}, u32[]{:S(2)}, u32[]{:S(2)}) collective-permute-start(bf16[2,128,128]{2,1,0:T(8,128)(2,1)} %get-tuple-element.15), channel_id=1, source_target_pairs={{11,23},{12,22},{13,21},{14,20},{15,19}} | collective-permute-start | bytes 196616 | tf_op jit(solution)/shard_map/ppermute | solution.py:233
  37.3 1.6 %collective-permute-start.8 = (bf16[2,128,128]{2,1,0:T(8,128)(2,1)}, bf16[2,128,128]{2,1,0:T(8,128)(2,1)S(1)}, u32[]{:S(2)}, u32[]{:S(2)}) collective-permute-start(bf16[2,128,128]{2,1,0:T(8,128)(2,1)} %get-tuple-element.15), channel_id=1, source_target_pairs={{9,23},{10,22},{11,21},{12,20},{13,19},{14,18},{15,17}} | collective-permute-start | bytes 196616 | tf_op jit(solution)/shard_map/ppermute | solution.py:233
  38.0 0.9 %collective-permute-start.9 = (bf16[2,128,128]{2,1,0:T(8,128)(2,1)}, bf16[2,128,128]{2,1,0:T(8,128)(2,1)S(1)}, u32[]{:S(2)}, u32[]{:S(2)}) collective-permute-start(bf16[2,128,128]{2,1,0:T(8,128)(2,1)} %get-tuple-element.15), channel_id=1, source_target_pairs={{10,23},{11,22},{12,21},{13,20},{14,19},{15,18}} | collective-permute-start | bytes 196616 | tf_op jit(solution)/shard_map/ppermute | solution.py:233
  38.9 0.6 copy-start.9
  39.0 0.6 copy-start.12
  39.0 0.6 copy-start.15
  39.0 0.7 copy-start.3
  50.5 23.0 %collective-permute-start.11 = (f32[2,128,128]{2,1,0:T(8,128)}, f32[2,128,128]{2,1,0:T(8,128)S(1)}, u32[]{:S(2)}, u32[]{:S(2)}) collective-permute-start(f32[2,128,128]{2,1,0:T(8,128)} %get-tuple-element.16.prev_ref), channel_id=1, source_target_pairs={{16,31},{17,30},{18,29},{19,28},{20,27},{21,26},{22,25},{23,24}} | collective-permute-start | bytes 393224 | tf_op jit(solution)/shard_map/ppermute | solution.py:233
  51.8 21.6 %collective-permute-start.12 = (bf16[2,128,128]{2,1,0:T(8,128)(2,1)}, bf16[2,128,128]{2,1,0:T(8,128)(2,1)S(1)}, u32[]{:S(2)}, u32[]{:S(2)}) collective-permute-start(bf16[2,128,128]{2,1,0:T(8,128)(2,1)} %get-tuple-element.17), channel_id=1, source_target_pairs={{17,31},{18,30},{19,29},{20,28},{21,27},{22,26},{23,25}} | collective-permute-start | bytes 196616 | tf_op jit(solution)/shard_map/ppermute | solution.py:233
  53.1 20.3 %collective-permute-start.13 = (bf16[2,128,128]{2,1,0:T(8,128)(2,1)}, bf16[2,128,128]{2,1,0:T(8,128)(2,1)S(1)}, u32[]{:S(2)}, u32[]{:S(2)}) collective-permute-start(bf16[2,128,128]{2,1,0:T(8,128)(2,1)} %get-tuple-element.17), channel_id=1, source_target_pairs={{18,31},{19,30},{20,29},{21,28},{22,27},{23,26}} | collective-permute-start | bytes 196616 | tf_op jit(solution)/shard_map/ppermute | solution.py:233
  54.4 19.0 %collective-permute-start.14 = (bf16[2,128,128]{2,1,0:T(8,128)(2,1)}, bf16[2,128,128]{2,1,0:T(8,128)(2,1)S(1)}, u32[]{:S(2)}, u32[]{:S(2)}) collective-permute-start(bf16[2,128,128]{2,1,0:T(8,128)(2,1)} %get-tuple-element.17), channel_id=1, source_target_pairs={{19,31},{20,30},{21,29},{22,28},{23,27}} | collective-permute-start | bytes 196616 | tf_op jit(solution)/shard_map/ppermute | solution.py:233
  73.4 0.6 copy-start.7
  73.4 0.7 copy-start.10
  73.4 0.7 copy-start.13
  73.4 0.7 copy-start.1

commit v13 on v12

--- a/solution.py
+++ b/solution.py
@@ -244,7 +244,12 @@
     for turn in range(n_seg):
         call = first_call if turn == 0 else later_call
         keep = (segment == turn).astype(jnp.int32).reshape(1)
-        out, result_low = call(keep, out, *inputs, mask, *weights)
+        out, result_low = lax.cond(
+            segment == turn,
+            lambda args, call=call: call(*args),
+            lambda args: (args[1], jnp.zeros(args[1].shape, jnp.bfloat16)),
+            (keep, out, *inputs, mask, *weights),
+        )
         if turn + 1 < n_seg:
             inputs = next_inputs(out, result_low, turn)
     return out[None]

time: 85.7 us -> 81.5 us (0.951)
  Pallas kernels: 43.3 us -> 10.6 us
  waiting for transfers between devices: 18.1 us -> 50 us
  local copies, waits for them, and re-layouts: 2.95 us -> 0.34 us
    pallas_call x4 -> x1, Pallas kernels: 43.3 us -> 10.6 us  [body(): call(*args)]
    ppermute x12, waiting for transfers between devices: 17.5 us -> 49.3 us  [send(): return lax.ppermute(block, axes, pairs)]
    unnamed x32 -> x5, local copies, waits for them, and re-layouts: 2.01 us -> 0.02 us
  transfers between devices with their start and end apart: 15 -> 15, of which waited for: 2 -> 4; matrix products, arithmetic and copies ran while one was open for 1% -> 1% of each run, Pallas kernels for 0% -> 0%
where the time goes in v13:
time: 81.5 us; the launch traced here: 80.8 us
  waiting for transfers between devices  50 us (61%)
  starting transfers between devices  17.8 us (22%)
  Pallas kernels  10.6 us (13%)
  other arithmetic  1.13 us (1%)
    ppermute x12, waiting for transfers between devices, send(): return lax.ppermute(block, axes, pairs)  49.3 us
    pallas_call x1, Pallas kernels, body(): call(*args)  10.6 us
    ppermute x12, starting transfers between devices, send(): return lax.ppermute(block, axes, pairs)  10.5 us
    ppermute x3, starting transfers between devices, behind(): return lax.ppermute(patches_low, axes, pairs)  7.28 us
  transfers between devices with their start and end apart: 15, of which 4 were waited for; matrix products, arithmetic and copies ran while one was open for 1% of the time, Pallas kernels for 0%

profile of v13, /device:TPU:15, one launch (start us, length us, event | category | flops | bytes accessed | tf_op | source)
XLA Modules:
  0.0 80.8 jit_solution(8058503785989192628)
XLA Ops:
  0.0 0.9 %convert_element_type.26 = bf16[2,128,128]{2,1,0:T(8,128)(2,1)S(1)} convert(f32[2,128,128]{2,1,0:T(8,128)} %param.16) | non-fusion elementwise | flops 32768 | bytes 196608 | tf_op jit(solution)/shard_map/convert_element_type | solution.py:220
  0.9 4.7 %collective-permute-start.2 = (bf16[2,128,128]{2,1,0:T(8,128)(2,1)S(1)}, bf16[2,128,128]{2,1,0:T(8,128)(2,1)S(1)}, u32[]{:S(2)}, u32[]{:S(2)}) collective-permute-start(bf16[2,128,128]{2,1,0:T(8,128)(2,1)S(1)} %convert_element_type.26), channel_id=1, source_target_pairs={{24,3},{25,4},{26,5},{27,6},{28,7}} | collective-permute-start | bytes 196616 | tf_op jit(solution)/shard_map/ppermute | solution.py:218
  5.6 1.3 %collective-permute-start.1 = (bf16[2,128,128]{2,1,0:T(8,128)(2,1)S(1)}, bf16[2,128,128]{2,1,0:T(8,128)(2,1)S(1)}, u32[]{:S(2)}, u32[]{:S(2)}) collective-permute-start(bf16[2,128,128]{2,1,0:T(8,128)(2,1)S(1)} %convert_element_type.26), channel_id=1, source_target_pairs={{24,2},{25,3},{26,4},{27,5},{28,6},{29,7}} | collective-permute-start | bytes 196616 | tf_op jit(solution)/shard_map/ppermute | solution.py:218
  6.9 1.3 %collective-permute-start = (bf16[2,128,128]{2,1,0:T(8,128)(2,1)S(1)}, bf16[2,128,128]{2,1,0:T(8,128)(2,1)S(1)}, u32[]{:S(2)}, u32[]{:S(2)}) collective-permute-start(bf16[2,128,128]{2,1,0:T(8,128)(2,1)S(1)} %convert_element_type.26), channel_id=1, source_target_pairs={{24,1},{25,2},{26,3},{27,4},{28,5},{29,6},{30,7}} | collective-permute-start | bytes 196616 | tf_op jit(solution)/shard_map/ppermute | solution.py:218
  8.3 0.2 dynamic-slice_reduce_fusion
  8.5 0.1 compare_reduce_fusion
  8.6 0.1 broadcast_bitcast_fusion
  8.6 0.1 fusion.1
  8.8 0.0 collective-permute-done.2
  8.8 0.8 collective-permute-done
  9.6 0.7 collective-permute-start.3
  10.3 0.7 collective-permute-start.6
  10.9 0.7 collective-permute-start.5
  11.6 0.7 collective-permute-start.4
  12.3 0.0 collective-permute-done.6
  12.3 0.0 collective-permute-done.4
  12.3 0.2 conditional.5
  12.6 0.7 collective-permute-start.7
  13.2 0.7 collective-permute-start.10
  13.9 0.7 collective-permute-start.9
  14.6 0.7 collective-permute-start.8
  15.3 0.3 conditional.6
  15.6 0.0 copy-start.1
  15.6 1.3 %collective-permute-start.11 = (f32[2,128,128]{2,1,0:T(8,128)S(1)}, f32[2,128,128]{2,1,0:T(8,128)S(1)}, u32[]{:S(2)}, u32[]{:S(2)}) collective-permute-start(f32[2,128,128]{2,1,0:T(8,128)S(1)} %get-tuple-element.188), channel_id=1, source_target_pairs={{16,31},{17,30},{18,29},{19,28},{20,27},{21,26},{22,25},{23,24}} | collective-permute-start | bytes 393224 | tf_op jit(solution)/shard_map/ppermute | solution.py:233
  16.9 1.3 %collective-permute-start.14 = (bf16[2,128,128]{2,1,0:T(8,128)(2,1)S(1)}, bf16[2,128,128]{2,1,0:T(8,128)(2,1)S(1)}, u32[]{:S(2)}, u32[]{:S(2)}) collective-permute-start(bf16[2,128,128]{2,1,0:T(8,128)(2,1)S(1)} %get-tuple-element.189), channel_id=1, source_target_pairs={{19,31},{20,30},{21,29},{22,28},{23,27}} | collective-permute-start | bytes 196616 | tf_op jit(solution)/shard_map/ppermute | solution.py:233
  18.2 1.3 %collective-permute-start.13 = (bf16[2,128,128]{2,1,0:T(8,128)(2,1)S(1)}, bf16[2,128,128]{2,1,0:T(8,128)(2,1)S(1)}, u32[]{:S(2)}, u32[]{:S(2)}) collective-permute-start(bf16[2,128,128]{2,1,0:T(8,128)(2,1)S(1)} %get-tuple-element.189), channel_id=1, source_target_pairs={{18,31},{19,30},{20,29},{21,28},{22,27},{23,26}} | collective-permute-start | bytes 196616 | tf_op jit(solution)/shard_map/ppermute | solution.py:233
  19.5 1.3 %collective-permute-start.12 = (bf16[2,128,128]{2,1,0:T(8,128)(2,1)S(1)}, bf16[2,128,128]{2,1,0:T(8,128)(2,1)S(1)}, u32[]{:S(2)}, u32[]{:S(2)}) collective-permute-start(bf16[2,128,128]{2,1,0:T(8,128)(2,1)S(1)} %get-tuple-element.189), channel_id=1, source_target_pairs={{17,31},{18,30},{19,29},{20,28},{21,27},{22,26},{23,25}} | collective-permute-start | bytes 196616 | tf_op jit(solution)/shard_map/ppermute | solution.py:233
  20.8 45.8 %collective-permute-done.14 = bf16[2,128,128]{2,1,0:T(8,128)(2,1)S(1)} collective-permute-done((bf16[2,128,128]{2,1,0:T(8,128)(2,1)S(1)}, bf16[2,128,128]{2,1,0:T(8,128)(2,1)S(1)}, u32[]{:S(2)}, u32[]{:S(2)}) %collective-permute-start.14) | collective-permute-done | bytes 65568 | tf_op jit(solution)/shard_map/ppermute | solution.py:233
  66.6 2.4 %collective-permute-done.13 = bf16[2,128,128]{2,1,0:T(8,128)(2,1)S(1)} collective-permute-done((bf16[2,128,128]{2,1,0:T(8,128)(2,1)S(1)}, bf16[2,128,128]{2,1,0:T(8,128)(2,1)S(1)}, u32[]{:S(2)}, u32[]{:S(2)}) %collective-permute-start.13) | collective-permute-done | bytes 65568 | tf_op jit(solution)/shard_map/ppermute | solution.py:233
  69.1 1.0 %collective-permute-done.12 = bf16[2,128,128]{2,1,0:T(8,128)(2,1)S(1)} collective-permute-done((bf16[2,128,128]{2,1,0:T(8,128)(2,1)S(1)}, bf16[2,128,128]{2,1,0:T(8,128)(2,1)S(1)}, u32[]{:S(2)}, u32[]{:S(2)}) %collective-permute-start.12) | collective-permute-done | bytes 65568 | tf_op jit(solution)/shard_map/ppermute | solution.py:233
  70.1 10.6 %conditional.7 = (f32[1,2,128,128]{3,2,1,0:T(8,128)}) conditional(s32[]{:T(128)} %convert_element_type.22, f32[2,128,128]{2,1,0:T(8,128)} %copy-done.1, (s32[]{:T(128)}, f32[2,128,128]{2,1,0:T(8,128)S(1)}, f32[2,128,128]{2,1,0:T(8,128)S(1)}, bf16[2,128,128]{2,1,0:T(8,128)(2,1)S(1)}, bf16[2,128,128]{2,1,0:T(8,128)(2,1)S(1)}, ...), branch_computations={%region_7.8_spmd, %region_8.9_spmd} | conditional | flops 5033164800 | bytes 9633800 | solution.py:247
  70.1 10.6 %branch_1_fun.6 = (f32[2,128,128]{2,1,0:T(8,128)}, bf16[2,128,128]{2,1,0:T(8,128)(2,1)}) custom-call(s32[1]{0:T(128)} %bitcast.3.keep_ref, f32[2,128,128]{2,1,0:T(8,128)S(1)} %get-tuple-element.163.prev_ref, f32[2,128,128]{2,1,0:T(8,128)S(1)} %get-tuple-element.164.own_ref, bf16[2,128,128]{2,1,0:T(8,128)(2,1)S(1)} %get-tuple-element.165.back1_ref, ...), custom_call_target="tpu_custom_call" | custom-call | flops 5033164800 | bytes 9633792 | tf_op jit(solution)/shard_map/cond/branch_1_fun/pallas_call | solution.py:249
  (21 shorter events, 0.1 us)
Async XLA Ops:
  0.0 8.3 %copy-start = (s32[8,4]{0,1:T(4,128)S(1)}, s32[8,4]{0,1:T(4,128)}, u32[]{:S(2)}) copy-start(s32[8,4]{0,1:T(4,128)} %param.17) | copy-start | bytes 388
  0.9 7.8 %collective-permute-start.2 = (bf16[2,128,128]{2,1,0:T(8,128)(2,1)S(1)}, bf16[2,128,128]{2,1,0:T(8,128)(2,1)S(1)}, u32[]{:S(2)}, u32[]{:S(2)}) collective-permute-start(bf16[2,128,128]{2,1,0:T(8,128)(2,1)S(1)} %convert_element_type.26), channel_id=1, source_target_pairs={{24,3},{25,4},{26,5},{27,6},{28,7}} | collective-permute-start | bytes 196616 | tf_op jit(solution)/shard_map/ppermute | solution.py:218
  5.6 3.1 %collective-permute-start.1 = (bf16[2,128,128]{2,1,0:T(8,128)(2,1)S(1)}, bf16[2,128,128]{2,1,0:T(8,128)(2,1)S(1)}, u32[]{:S(2)}, u32[]{:S(2)}) collective-permute-start(bf16[2,128,128]{2,1,0:T(8,128)(2,1)S(1)} %convert_element_type.26), channel_id=1, source_target_pairs={{24,2},{25,3},{26,4},{27,5},{28,6},{29,7}} | collective-permute-start | bytes 196616 | tf_op jit(solution)/shard_map/ppermute | solution.py:218
  6.9 2.6 %collective-permute-start = (bf16[2,128,128]{2,1,0:T(8,128)(2,1)S(1)}, bf16[2,128,128]{2,1,0:T(8,128)(2,1)S(1)}, u32[]{:S(2)}, u32[]{:S(2)}) collective-permute-start(bf16[2,128,128]{2,1,0:T(8,128)(2,1)S(1)} %convert_element_type.26), channel_id=1, source_target_pairs={{24,1},{25,2},{26,3},{27,4},{28,5},{29,6},{30,7}} | collective-permute-start | bytes 196616 | tf_op jit(solution)/shard_map/ppermute | solution.py:218
  9.6 2.7 %collective-permute-start.3 = (f32[2,128,128]{2,1,0:T(8,128)S(1)}, f32[2,128,128]{2,1,0:T(8,128)S(1)}, u32[]{:S(2)}, u32[]{:S(2)}) collective-permute-start(f32[2,128,128]{2,1,0:T(8,128)S(1)} %get-tuple-element.183), channel_id=1, source_target_pairs={{0,15},{1,14},{2,13},{3,12},{4,11},{5,10},{6,9},{7,8}} | collective-permute-start | bytes 393224 | tf_op jit(solution)/shard_map/ppermute | solution.py:233
  10.3 2.0 %collective-permute-start.6 = (bf16[2,128,128]{2,1,0:T(8,128)(2,1)S(1)}, bf16[2,128,128]{2,1,0:T(8,128)(2,1)S(1)}, u32[]{:S(2)}, u32[]{:S(2)}) collective-permute-start(bf16[2,128,128]{2,1,0:T(8,128)(2,1)S(1)} %get-tuple-element.185), channel_id=1, source_target_pairs={{3,15},{4,14},{5,13},{6,12},{7,11}} | collective-permute-start | bytes 196616 | tf_op jit(solution)/shard_map/ppermute | solution.py:233
  10.9 1.4 %collective-permute-start.5 = (bf16[2,128,128]{2,1,0:T(8,128)(2,1)S(1)}, bf16[2,128,128]{2,1,0:T(8,128)(2,1)S(1)}, u32[]{:S(2)}, u32[]{:S(2)}) collective-permute-start(bf16[2,128,128]{2,1,0:T(8,128)(2,1)S(1)} %get-tuple-element.185), channel_id=1, source_target_pairs={{2,15},{3,14},{4,13},{5,12},{6,11},{7,10}} | collective-permute-start | bytes 196616 | tf_op jit(solution)/shard_map/ppermute | solution.py:233
  11.6 0.7 collective-permute-start.4
  12.6 2.7 %collective-permute-start.7 = (f32[2,128,128]{2,1,0:T(8,128)S(1)}, f32[2,128,128]{2,1,0:T(8,128)S(1)}, u32[]{:S(2)}, u32[]{:S(2)}) collective-permute-start(f32[2,128,128]{2,1,0:T(8,128)S(1)} %get-tuple-element.186), channel_id=1, source_target_pairs={{8,23},{9,22},{10,21},{11,20},{12,19},{13,18},{14,17},{15,16}} | collective-permute-start | bytes 393224 | tf_op jit(solution)/shard_map/ppermute | solution.py:233
  13.2 2.0 %collective-permute-start.10 = (bf16[2,128,128]{2,1,0:T(8,128)(2,1)S(1)}, bf16[2,128,128]{2,1,0:T(8,128)(2,1)S(1)}, u32[]{:S(2)}, u32[]{:S(2)}) collective-permute-start(bf16[2,128,128]{2,1,0:T(8,128)(2,1)S(1)} %get-tuple-element.187), channel_id=1, source_target_pairs={{11,23},{12,22},{13,21},{14,20},{15,19}} | collective-permute-start | bytes 196616 | tf_op jit(solution)/shard_map/ppermute | solution.py:233
  13.9 1.4 %collective-permute-start.9 = (bf16[2,128,128]{2,1,0:T(8,128)(2,1)S(1)}, bf16[2,128,128]{2,1,0:T(8,128)(2,1)S(1)}, u32[]{:S(2)}, u32[]{:S(2)}) collective-permute-start(bf16[2,128,128]{2,1,0:T(8,128)(2,1)S(1)} %get-tuple-element.187), channel_id=1, source_target_pairs={{10,23},{11,22},{12,21},{13,20},{14,19},{15,18}} | collective-permute-start | bytes 196616 | tf_op jit(solution)/shard_map/ppermute | solution.py:233
  14.6 0.7 collective-permute-start.8
  15.6 54.5 %copy-start.1 = (f32[2,128,128]{2,1,0:T(8,128)}, f32[2,128,128]{2,1,0:T(8,128)S(1)}, u32[]{:S(2)}) copy-start(f32[2,128,128]{2,1,0:T(8,128)S(1)} %get-tuple-element.188) | copy-start | bytes 393220
  15.6 54.5 %collective-permute-start.11 = (f32[2,128,128]{2,1,0:T(8,128)S(1)}, f32[2,128,128]{2,1,0:T(8,128)S(1)}, u32[]{:S(2)}, u32[]{:S(2)}) collective-permute-start(f32[2,128,128]{2,1,0:T(8,128)S(1)} %get-tuple-element.188), channel_id=1, source_target_pairs={{16,31},{17,30},{18,29},{19,28},{20,27},{21,26},{22,25},{23,24}} | collective-permute-start | bytes 393224 | tf_op jit(solution)/shard_map/ppermute | solution.py:233
  16.9 49.8 %collective-permute-start.14 = (bf16[2,128,128]{2,1,0:T(8,128)(2,1)S(1)}, bf16[2,128,128]{2,1,0:T(8,128)(2,1)S(1)}, u32[]{:S(2)}, u32[]{:S(2)}) collective-permute-start(bf16[2,128,128]{2,1,0:T(8,128)(2,1)S(1)} %get-tuple-element.189), channel_id=1, source_target_pairs={{19,31},{20,30},{21,29},{22,28},{23,27}} | collective-permute-start | bytes 196616 | tf_op jit(solution)/shard_map/ppermute | solution.py:233
  18.2 50.9 %collective-permute-start.13 = (bf16[2,128,128]{2,1,0:T(8,128)(2,1)S(1)}, bf16[2,128,128]{2,1,0:T(8,128)(2,1)S(1)}, u32[]{:S(2)}, u32[]{:S(2)}) collective-permute-start(bf16[2,128,128]{2,1,0:T(8,128)(2,1)S(1)} %get-tuple-element.189), channel_id=1, source_target_pairs={{18,31},{19,30},{20,29},{21,28},{22,27},{23,26}} | collective-permute-start | bytes 196616 | tf_op jit(solution)/shard_map/ppermute | solution.py:233
  19.5 50.6 %collective-permute-start.12 = (bf16[2,128,128]{2,1,0:T(8,128)(2,1)S(1)}, bf16[2,128,128]{2,1,0:T(8,128)(2,1)S(1)}, u32[]{:S(2)}, u32[]{:S(2)}) collective-permute-start(bf16[2,128,128]{2,1,0:T(8,128)(2,1)S(1)} %get-tuple-element.189), channel_id=1, source_target_pairs={{17,31},{18,30},{19,29},{20,28},{21,27},{22,26},{23,25}} | collective-permute-start | bytes 196616 | tf_op jit(solution)/shard_map/ppermute | solution.py:233

commit v14 on v13

--- a/solution.py
+++ b/solution.py
@@ -20,7 +20,7 @@
     scale = HEAD_DIM ** (-0.5)
     heads = heads_all // HEAD_DIM
 
-    def kernel(keep_ref, prev_ref, own_ref, back1_ref, back2_ref, edge_ref, mask_ref, ga_ref, gb_ref,
+    def kernel(listed_ref, own_ref, back1_ref, back2_ref, edge_ref, ga_ref, gb_ref,
                embed_v, read_v, attn_hbm, mix_hbm,
                out_ref, outb_ref,
                attn_v, mix_v, sems,
@@ -80,6 +80,12 @@
 
         lax.fori_loop(0, heads_all // CHUNK, q_step, 0)
 
+        query = lax.broadcasted_iota(jnp.int32, (rows, span), 0)
+        key = lax.broadcasted_iota(jnp.int32, (rows, span), 1)
+        tile_ok = jnp.where(
+            key < rows, listed_ref[0], jnp.where(key < 2 * rows, listed_ref[1], listed_ref[2])
+        )
+        allowed = (tile_ok > 0) & (key <= query + own_at)
         for m in range(micro):
             q3 = jnp.stack([q_s[m * rows:(m + 1) * rows, h * HEAD_DIM:(h + 1) * HEAD_DIM] for h in range(heads)])
             k3 = jnp.stack([kv_s[m * span:(m + 1) * span, h * HEAD_DIM:(h + 1) * HEAD_DIM] for h in range(heads)])
@@ -88,7 +94,7 @@
                 for h in range(heads)
             ])
             scores = jnp.einsum("hqd,hkd->hqk", q3, k3, preferred_element_type=jnp.float32) * scale
-            scores = jnp.where(mask_ref[...][None] > 0.5, scores, -jnp.inf)
+            scores = jnp.where(allowed[None], scores, -jnp.inf)
             top = jnp.max(scores, axis=-1, keepdims=True)
             expo = jnp.exp(scores - top)
             total = jnp.sum(expo, axis=-1, keepdims=True)
@@ -124,7 +130,7 @@
                 own = (parts[0] + parts[1]) + parts[2]
             rows_m = slice(m * rows, (m + 1) * rows)
             result = (own - shift_mean[rows_m]) * jnp.exp(-log_scale[rows_m])
-            out_ref[m] = jnp.where(keep_ref[0] > 0, result, prev_ref[m])
+            out_ref[m] = result
             outb_ref[m] = result.astype(jnp.bfloat16)
 
     width = heads_all
@@ -138,7 +144,7 @@
             jax.ShapeDtypeStruct((micro, rows, width_in), jnp.float32),
             jax.ShapeDtypeStruct((micro, rows, width_in), jnp.bfloat16),
         ),
-        in_specs=[pl.BlockSpec(memory_space=pltpu.SMEM)] + [pl.BlockSpec(memory_space=vmem)] * 10
+        in_specs=[pl.BlockSpec(memory_space=pltpu.SMEM)] + [pl.BlockSpec(memory_space=vmem)] * 8
         + [pl.BlockSpec(memory_space=pl.ANY)] * 2,
         out_specs=(pl.BlockSpec(memory_space=vmem), pl.BlockSpec(memory_space=vmem)),
         scratch_shapes=[
@@ -192,14 +198,10 @@
     window_tiles = place - BACK + jnp.arange(BACK + 1, dtype=jnp.int32)
     my_list = lax.dynamic_index_in_dim(tile_list, place, 0, keepdims=False)
     listed = jnp.any(my_list[:, None] == window_tiles[None, :], axis=0) & (window_tiles >= 0)
-    listed = jnp.repeat(listed, rows)
-    query_pos = jnp.arange(rows, dtype=jnp.int32) + BACK * rows
-    key_pos = jnp.arange(span, dtype=jnp.int32)
-    allowed = listed[None, :] & (key_pos[None, :] <= query_pos[:, None])
+    listed = listed.astype(jnp.int32)
 
     first_call = make_block_call(micro, rows, width_in, heads_all, False, jnp.bfloat16)
     later_call = make_block_call(micro, rows, width_in, heads_all, True, jnp.bfloat16)
-    mask = allowed.astype(jnp.float32)
     weights = (
         norm_gain[0].reshape(1, -1),
         final_gain[0].reshape(1, -1),
@@ -243,12 +245,11 @@
     out = jnp.zeros((micro, rows, width_in), jnp.float32)
     for turn in range(n_seg):
         call = first_call if turn == 0 else later_call
-        keep = (segment == turn).astype(jnp.int32).reshape(1)
         out, result_low = lax.cond(
             segment == turn,
-            lambda args, call=call: call(*args),
-            lambda args: (args[1], jnp.zeros(args[1].shape, jnp.bfloat16)),
-            (keep, out, *inputs, mask, *weights),
+            lambda args, call=call: call(*args[1:]),
+            lambda args: (args[0], jnp.zeros(args[0].shape, jnp.bfloat16)),
+            (out, listed, *inputs, *weights),
         )
         if turn + 1 < n_seg:
             inputs = next_inputs(out, result_low, turn)

time: 81.5 us -> 79.1 us (0.971)
  waiting for transfers between devices: 50 us -> 48 us
    ppermute x12, waiting for transfers between devices: 49.3 us -> 46.6 us  [send(): return lax.ppermute(block, axes, pairs)]
  transfers between devices with their start and end apart: 15 -> 15, of which waited for: 4 -> 2; matrix products, arithmetic and copies ran while one was open for 1% -> 0% of each run, Pallas kernels for 0% -> 0%
where the time goes in v14:
time: 79.1 us; the launch traced here: 78.7 us
  waiting for transfers between devices  48 us (61%)
  starting transfers between devices  17.8 us (23%)
  Pallas kernels  10.5 us (13%)
  other arithmetic  1.03 us (1%)
    ppermute x12, waiting for transfers between devices, send(): return lax.ppermute(block, axes, pairs)  46.6 us
    ppermute x12, starting transfers between devices, send(): return lax.ppermute(block, axes, pairs)  10.5 us
    pallas_call x1, Pallas kernels, body(): call(*args[1:])  10.5 us
    ppermute x3, starting transfers between devices, behind(): return lax.ppermute(patches_low, axes, pairs)  7.28 us
  transfers between devices with their start and end apart: 15, of which 2 were waited for; matrix products, arithmetic and copies ran while one was open for 0% of the time, Pallas kernels for 0%

profile of v14, /device:TPU:15, one launch (start us, length us, event | category | flops | bytes accessed | tf_op | source)
XLA Modules:
  0.0 78.7 jit_solution(7129899840250248553)
XLA Ops:
  0.0 0.9 %convert_element_type.23 = bf16[2,128,128]{2,1,0:T(8,128)(2,1)S(1)} convert(f32[2,128,128]{2,1,0:T(8,128)} %param.16) | non-fusion elementwise | flops 32768 | bytes 196608 | tf_op jit(solution)/shard_map/convert_element_type | solution.py:222
  0.9 3.7 %collective-permute-start = (bf16[2,128,128]{2,1,0:T(8,128)(2,1)S(1)}, bf16[2,128,128]{2,1,0:T(8,128)(2,1)S(1)}, u32[]{:S(2)}, u32[]{:S(2)}) collective-permute-start(bf16[2,128,128]{2,1,0:T(8,128)(2,1)S(1)} %convert_element_type.23), channel_id=1, source_target_pairs={{24,1},{25,2},{26,3},{27,4},{28,5},{29,6},{30,7}} | collective-permute-start | bytes 196616 | tf_op jit(solution)/shard_map/ppermute | solution.py:220
  4.6 1.3 %collective-permute-start.1 = (bf16[2,128,128]{2,1,0:T(8,128)(2,1)S(1)}, bf16[2,128,128]{2,1,0:T(8,128)(2,1)S(1)}, u32[]{:S(2)}, u32[]{:S(2)}) collective-permute-start(bf16[2,128,128]{2,1,0:T(8,128)(2,1)S(1)} %convert_element_type.23), channel_id=1, source_target_pairs={{24,2},{25,3},{26,4},{27,5},{28,6},{29,7}} | collective-permute-start | bytes 196616 | tf_op jit(solution)/shard_map/ppermute | solution.py:220
  5.9 2.3 %collective-permute-start.2 = (bf16[2,128,128]{2,1,0:T(8,128)(2,1)S(1)}, bf16[2,128,128]{2,1,0:T(8,128)(2,1)S(1)}, u32[]{:S(2)}, u32[]{:S(2)}) collective-permute-start(bf16[2,128,128]{2,1,0:T(8,128)(2,1)S(1)} %convert_element_type.23), channel_id=1, source_target_pairs={{24,3},{25,4},{26,5},{27,6},{28,7}} | collective-permute-start | bytes 196616 | tf_op jit(solution)/shard_map/ppermute | solution.py:220
  8.3 0.2 dynamic-slice_reduce_fusion
  8.4 0.1 compare_reduce_fusion
  8.5 0.0 collective-permute-done
  8.6 0.0 collective-permute-done.1
  8.6 1.4 %collective-permute-done.2 = bf16[2,128,128]{2,1,0:T(8,128)(2,1)S(1)} collective-permute-done((bf16[2,128,128]{2,1,0:T(8,128)(2,1)S(1)}, bf16[2,128,128]{2,1,0:T(8,128)(2,1)S(1)}, u32[]{:S(2)}, u32[]{:S(2)}) %collective-permute-start.2) | collective-permute-done | bytes 65568 | tf_op jit(solution)/shard_map/ppermute | solution.py:220
  10.1 0.7 collective-permute-start.3
  10.7 0.7 collective-permute-start.4
  11.4 0.7 collective-permute-start.5
  12.1 0.7 collective-permute-start.6
  12.8 0.0 collective-permute-done.4
  12.8 0.0 collective-permute-done.5
  12.8 0.0 collective-permute-done.6
  12.8 0.2 conditional.5
  13.0 0.7 collective-permute-start.7
  13.7 0.7 collective-permute-start.10
  14.4 0.7 collective-permute-start.8
  15.0 0.7 collective-permute-start.9
  15.7 0.0 collective-permute-done.10
  15.7 0.0 collective-permute-done.8
  15.8 0.3 conditional.6
  16.0 0.0 copy-start.1
  16.0 1.3 %collective-permute-start.11 = (f32[2,128,128]{2,1,0:T(8,128)S(1)}, f32[2,128,128]{2,1,0:T(8,128)S(1)}, u32[]{:S(2)}, u32[]{:S(2)}) collective-permute-start(f32[2,128,128]{2,1,0:T(8,128)S(1)} %get-tuple-element.163), channel_id=1, source_target_pairs={{16,31},{17,30},{18,29},{19,28},{20,27},{21,26},{22,25},{23,24}} | collective-permute-start | bytes 393224 | tf_op jit(solution)/shard_map/ppermute | solution.py:235
  17.3 1.3 %collective-permute-start.12 = (bf16[2,128,128]{2,1,0:T(8,128)(2,1)S(1)}, bf16[2,128,128]{2,1,0:T(8,128)(2,1)S(1)}, u32[]{:S(2)}, u32[]{:S(2)}) collective-permute-start(bf16[2,128,128]{2,1,0:T(8,128)(2,1)S(1)} %get-tuple-element.164), channel_id=1, source_target_pairs={{17,31},{18,30},{19,29},{20,28},{21,27},{22,26},{23,25}} | collective-permute-start | bytes 196616 | tf_op jit(solution)/shard_map/ppermute | solution.py:235
  18.6 1.3 %collective-permute-start.13 = (bf16[2,128,128]{2,1,0:T(8,128)(2,1)S(1)}, bf16[2,128,128]{2,1,0:T(8,128)(2,1)S(1)}, u32[]{:S(2)}, u32[]{:S(2)}) collective-permute-start(bf16[2,128,128]{2,1,0:T(8,128)(2,1)S(1)} %get-tuple-element.164), channel_id=1, source_target_pairs={{18,31},{19,30},{20,29},{21,28},{22,27},{23,26}} | collective-permute-start | bytes 196616 | tf_op jit(solution)/shard_map/ppermute | solution.py:235
  19.9 1.3 %collective-permute-start.14 = (bf16[2,128,128]{2,1,0:T(8,128)(2,1)S(1)}, bf16[2,128,128]{2,1,0:T(8,128)(2,1)S(1)}, u32[]{:S(2)}, u32[]{:S(2)}) collective-permute-start(bf16[2,128,128]{2,1,0:T(8,128)(2,1)S(1)} %get-tuple-element.164), channel_id=1, source_target_pairs={{19,31},{20,30},{21,29},{22,28},{23,27}} | collective-permute-start | bytes 196616 | tf_op jit(solution)/shard_map/ppermute | solution.py:235
  21.2 46.5 %collective-permute-done.12 = bf16[2,128,128]{2,1,0:T(8,128)(2,1)S(1)} collective-permute-done((bf16[2,128,128]{2,1,0:T(8,128)(2,1)S(1)}, bf16[2,128,128]{2,1,0:T(8,128)(2,1)S(1)}, u32[]{:S(2)}, u32[]{:S(2)}) %collective-permute-start.12) | collective-permute-done | bytes 65568 | tf_op jit(solution)/shard_map/ppermute | solution.py:235
  67.8 10.8 %conditional.7 = (f32[1,2,128,128]{3,2,1,0:T(8,128)}) conditional(s32[]{:T(128)} %convert_element_type.18, f32[2,128,128]{2,1,0:T(8,128)} %copy-done.1, (s32[3]{0:T(128)S(1)}, f32[2,128,128]{2,1,0:T(8,128)S(1)}, bf16[2,128,128]{2,1,0:T(8,128)(2,1)S(1)}, bf16[2,128,128]{2,1,0:T(8,128)(2,1)S(1)}, bf16[2,128,128]{2,1,0:T(8,128)(2,1)S(1)}, ...), branch_computations={%region_7.8_spmd, %region_8.9_spmd} | conditional | flops 5033164800 | bytes 9633800 | solution.py:248
  68.1 10.5 %branch_1_fun.6 = (f32[2,128,128]{2,1,0:T(8,128)}, bf16[2,128,128]{2,1,0:T(8,128)(2,1)}) custom-call(s32[3]{0:T(128)S(1)} %get-tuple-element.139.listed_ref, f32[2,128,128]{2,1,0:T(8,128)S(1)} %get-tuple-element.140.own_ref, bf16[2,128,128]{2,1,0:T(8,128)(2,1)S(1)} %get-tuple-element.141.back1_ref, bf16[2,128,128]{2,1,0:T(8,128)(2,1)S(1)} %get-tuple-element.142.back2_ref, ...), custom_call_target="tpu_custom_call" | custom-call | flops 5033164800 | bytes 9633792 | tf_op jit(solution)/shard_map/cond/branch_1_fun/pallas_call | solution.py:250
  (16 shorter events, 0.1 us)
Async XLA Ops:
  0.0 8.3 %copy-start = (s32[8,4]{0,1:T(4,128)S(1)}, s32[8,4]{0,1:T(4,128)}, u32[]{:S(2)}) copy-start(s32[8,4]{0,1:T(4,128)} %param.17) | copy-start | bytes 388
  0.9 7.6 %collective-permute-start = (bf16[2,128,128]{2,1,0:T(8,128)(2,1)S(1)}, bf16[2,128,128]{2,1,0:T(8,128)(2,1)S(1)}, u32[]{:S(2)}, u32[]{:S(2)}) collective-permute-start(bf16[2,128,128]{2,1,0:T(8,128)(2,1)S(1)} %convert_element_type.23), channel_id=1, source_target_pairs={{24,1},{25,2},{26,3},{27,4},{28,5},{29,6},{30,7}} | collective-permute-start | bytes 196616 | tf_op jit(solution)/shard_map/ppermute | solution.py:220
  4.6 3.9 %collective-permute-start.1 = (bf16[2,128,128]{2,1,0:T(8,128)(2,1)S(1)}, bf16[2,128,128]{2,1,0:T(8,128)(2,1)S(1)}, u32[]{:S(2)}, u32[]{:S(2)}) collective-permute-start(bf16[2,128,128]{2,1,0:T(8,128)(2,1)S(1)} %convert_element_type.23), channel_id=1, source_target_pairs={{24,2},{25,3},{26,4},{27,5},{28,6},{29,7}} | collective-permute-start | bytes 196616 | tf_op jit(solution)/shard_map/ppermute | solution.py:220
  5.9 4.1 %collective-permute-start.2 = (bf16[2,128,128]{2,1,0:T(8,128)(2,1)S(1)}, bf16[2,128,128]{2,1,0:T(8,128)(2,1)S(1)}, u32[]{:S(2)}, u32[]{:S(2)}) collective-permute-start(bf16[2,128,128]{2,1,0:T(8,128)(2,1)S(1)} %convert_element_type.23), channel_id=1, source_target_pairs={{24,3},{25,4},{26,5},{27,6},{28,7}} | collective-permute-start | bytes 196616 | tf_op jit(solution)/shard_map/ppermute | solution.py:220
  10.1 2.7 %collective-permute-start.3 = (f32[2,128,128]{2,1,0:T(8,128)S(1)}, f32[2,128,128]{2,1,0:T(8,128)S(1)}, u32[]{:S(2)}, u32[]{:S(2)}) collective-permute-start(f32[2,128,128]{2,1,0:T(8,128)S(1)} %get-tuple-element.158), channel_id=1, source_target_pairs={{0,15},{1,14},{2,13},{3,12},{4,11},{5,10},{6,9},{7,8}} | collective-permute-start | bytes 393224 | tf_op jit(solution)/shard_map/ppermute | solution.py:235
  10.7 2.0 %collective-permute-start.4 = (bf16[2,128,128]{2,1,0:T(8,128)(2,1)S(1)}, bf16[2,128,128]{2,1,0:T(8,128)(2,1)S(1)}, u32[]{:S(2)}, u32[]{:S(2)}) collective-permute-start(bf16[2,128,128]{2,1,0:T(8,128)(2,1)S(1)} %get-tuple-element.160), channel_id=1, source_target_pairs={{1,15},{2,14},{3,13},{4,12},{5,11},{6,10},{7,9}} | collective-permute-start | bytes 196616 | tf_op jit(solution)/shard_map/ppermute | solution.py:235
  11.4 1.4 %collective-permute-start.5 = (bf16[2,128,128]{2,1,0:T(8,128)(2,1)S(1)}, bf16[2,128,128]{2,1,0:T(8,128)(2,1)S(1)}, u32[]{:S(2)}, u32[]{:S(2)}) collective-permute-start(bf16[2,128,128]{2,1,0:T(8,128)(2,1)S(1)} %get-tuple-element.160), channel_id=1, source_target_pairs={{2,15},{3,14},{4,13},{5,12},{6,11},{7,10}} | collective-permute-start | bytes 196616 | tf_op jit(solution)/shard_map/ppermute | solution.py:235
  12.1 0.7 collective-permute-start.6
  13.0 2.7 %collective-permute-start.7 = (f32[2,128,128]{2,1,0:T(8,128)S(1)}, f32[2,128,128]{2,1,0:T(8,128)S(1)}, u32[]{:S(2)}, u32[]{:S(2)}) collective-permute-start(f32[2,128,128]{2,1,0:T(8,128)S(1)} %get-tuple-element.161), channel_id=1, source_target_pairs={{8,23},{9,22},{10,21},{11,20},{12,19},{13,18},{14,17},{15,16}} | collective-permute-start | bytes 393224 | tf_op jit(solution)/shard_map/ppermute | solution.py:235
  13.7 2.0 %collective-permute-start.10 = (bf16[2,128,128]{2,1,0:T(8,128)(2,1)S(1)}, bf16[2,128,128]{2,1,0:T(8,128)(2,1)S(1)}, u32[]{:S(2)}, u32[]{:S(2)}) collective-permute-start(bf16[2,128,128]{2,1,0:T(8,128)(2,1)S(1)} %get-tuple-element.162), channel_id=1, source_target_pairs={{11,23},{12,22},{13,21},{14,20},{15,19}} | collective-permute-start | bytes 196616 | tf_op jit(solution)/shard_map/ppermute | solution.py:235
  14.4 1.4 %collective-permute-start.8 = (bf16[2,128,128]{2,1,0:T(8,128)(2,1)S(1)}, bf16[2,128,128]{2,1,0:T(8,128)(2,1)S(1)}, u32[]{:S(2)}, u32[]{:S(2)}) collective-permute-start(bf16[2,128,128]{2,1,0:T(8,128)(2,1)S(1)} %get-tuple-element.162), channel_id=1, source_target_pairs={{9,23},{10,22},{11,21},{12,20},{13,19},{14,18},{15,17}} | collective-permute-start | bytes 196616 | tf_op jit(solution)/shard_map/ppermute | solution.py:235
  15.0 0.7 collective-permute-start.9
  16.0 51.8 %copy-start.1 = (f32[2,128,128]{2,1,0:T(8,128)}, f32[2,128,128]{2,1,0:T(8,128)S(1)}, u32[]{:S(2)}) copy-start(f32[2,128,128]{2,1,0:T(8,128)S(1)} %get-tuple-element.163) | copy-start | bytes 393220
  16.0 51.7 %collective-permute-start.11 = (f32[2,128,128]{2,1,0:T(8,128)S(1)}, f32[2,128,128]{2,1,0:T(8,128)S(1)}, u32[]{:S(2)}, u32[]{:S(2)}) collective-permute-start(f32[2,128,128]{2,1,0:T(8,128)S(1)} %get-tuple-element.163), channel_id=1, source_target_pairs={{16,31},{17,30},{18,29},{19,28},{20,27},{21,26},{22,25},{23,24}} | collective-permute-start | bytes 393224 | tf_op jit(solution)/shard_map/ppermute | solution.py:235
  17.3 50.4 %collective-permute-start.12 = (bf16[2,128,128]{2,1,0:T(8,128)(2,1)S(1)}, bf16[2,128,128]{2,1,0:T(8,128)(2,1)S(1)}, u32[]{:S(2)}, u32[]{:S(2)}) collective-permute-start(bf16[2,128,128]{2,1,0:T(8,128)(2,1)S(1)} %get-tuple-element.164), channel_id=1, source_target_pairs={{17,31},{18,30},{19,29},{20,28},{21,27},{22,26},{23,25}} | collective-permute-start | bytes 196616 | tf_op jit(solution)/shard_map/ppermute | solution.py:235
  18.6 49.1 %collective-permute-start.13 = (bf16[2,128,128]{2,1,0:T(8,128)(2,1)S(1)}, bf16[2,128,128]{2,1,0:T(8,128)(2,1)S(1)}, u32[]{:S(2)}, u32[]{:S(2)}) collective-permute-start(bf16[2,128,128]{2,1,0:T(8,128)(2,1)S(1)} %get-tuple-element.164), channel_id=1, source_target_pairs={{18,31},{19,30},{20,29},{21,28},{22,27},{23,26}} | collective-permute-start | bytes 196616 | tf_op jit(solution)/shard_map/ppermute | solution.py:235
  19.9 47.8 %collective-permute-start.14 = (bf16[2,128,128]{2,1,0:T(8,128)(2,1)S(1)}, bf16[2,128,128]{2,1,0:T(8,128)(2,1)S(1)}, u32[]{:S(2)}, u32[]{:S(2)}) collective-permute-start(bf16[2,128,128]{2,1,0:T(8,128)(2,1)S(1)} %get-tuple-element.164), channel_id=1, source_target_pairs={{19,31},{20,30},{21,29},{22,28},{23,27}} | collective-permute-start | bytes 196616 | tf_op jit(solution)/shard_map/ppermute | solution.py:235

commit v15 on v14

--- a/solution.py
+++ b/solution.py
@@ -200,7 +200,7 @@
     listed = jnp.any(my_list[:, None] == window_tiles[None, :], axis=0) & (window_tiles >= 0)
     listed = listed.astype(jnp.int32)
 
-    first_call = make_block_call(micro, rows, width_in, heads_all, False, jnp.bfloat16)
+    first_call = make_block_call(micro, rows, width_in, heads_all, False, jnp.float32)
     later_call = make_block_call(micro, rows, width_in, heads_all, True, jnp.bfloat16)
     weights = (
         norm_gain[0].reshape(1, -1),
@@ -217,9 +217,8 @@
         def behind(distance):
             source = (n_seg - 1) * n_seq
             pairs = [(source + q, q + distance) for q in range(n_seq) if q + distance < n_seq]
-            return lax.ppermute(patches_low, axes, pairs)
-
-        patches_low = patches.astype(jnp.bfloat16)
+            return lax.ppermute(patches, axes, pairs)
+
         return patches, behind(1), behind(2), behind(BACK + 1)
 
     def next_inputs(result, result_low, turn):

time: 79.1 us -> 80 us (1.011)
  waiting for transfers between devices: 48 us -> 49.8 us
  other arithmetic: 1.03 us -> 0.1 us
    ppermute x3, waiting for transfers between devices: 1.45 us -> 3.17 us  [behind(): return lax.ppermute(patches, axes, pairs)]
    convert_element_type x1 -> x0, other arithmetic: 0.93 us -> none  [first_inputs(): patches_low = patches.astype(jnp.bfloat16)]
where the time goes in v15:
time: 80 us; the launch traced here: 79.7 us
  waiting for transfers between devices  49.8 us (62%)
  starting transfers between devices  17.9 us (22%)
  Pallas kernels  10.5 us (13%)
    ppermute x12, waiting for transfers between devices, send(): return lax.ppermute(block, axes, pairs)  46.6 us
    ppermute x12, starting transfers between devices, send(): return lax.ppermute(block, axes, pairs)  10.5 us
    pallas_call x1, Pallas kernels, body(): call(*args[1:])  10.5 us
    ppermute x3, starting transfers between devices, behind(): return lax.ppermute(patches, axes, pairs)  7.4 us
    ppermute x3, waiting for transfers between devices, behind(): return lax.ppermute(patches, axes, pairs)  3.17 us
  transfers between devices with their start and end apart: 15, of which 2 were waited for; matrix products, arithmetic and copies ran while one was open for 0% of the time, Pallas kernels for 0%

profile of v15, /device:TPU:15, one launch (start us, length us, event | category | flops | bytes accessed | tf_op | source)
XLA Modules:
  0.0 79.7 jit_solution(13560859273057898635)
XLA Ops:
  0.0 3.8 %collective-permute-start = (f32[2,128,128]{2,1,0:T(8,128)}, f32[2,128,128]{2,1,0:T(8,128)S(1)}, u32[]{:S(2)}, u32[]{:S(2)}) collective-permute-start(f32[2,128,128]{2,1,0:T(8,128)} %param.16), channel_id=1, source_target_pairs={{24,1},{25,2},{26,3},{27,4},{28,5},{29,6},{30,7}} | collective-permute-start | bytes 393224 | tf_op jit(solution)/shard_map/ppermute | solution.py:220
  3.8 1.3 %collective-permute-start.1 = (f32[2,128,128]{2,1,0:T(8,128)}, f32[2,128,128]{2,1,0:T(8,128)S(1)}, u32[]{:S(2)}, u32[]{:S(2)}) collective-permute-start(f32[2,128,128]{2,1,0:T(8,128)} %param.16), channel_id=1, source_target_pairs={{24,2},{25,3},{26,4},{27,5},{28,6},{29,7}} | collective-permute-start | bytes 393224 | tf_op jit(solution)/shard_map/ppermute | solution.py:220
  5.1 2.3 %collective-permute-start.2 = (f32[2,128,128]{2,1,0:T(8,128)}, f32[2,128,128]{2,1,0:T(8,128)S(1)}, u32[]{:S(2)}, u32[]{:S(2)}) collective-permute-start(f32[2,128,128]{2,1,0:T(8,128)} %param.16), channel_id=1, source_target_pairs={{24,3},{25,4},{26,5},{27,6},{28,7}} | collective-permute-start | bytes 393224 | tf_op jit(solution)/shard_map/ppermute | solution.py:220
  7.5 0.2 dynamic-slice_reduce_fusion
  7.6 0.1 compare_reduce_fusion
  7.7 0.0 collective-permute-done
  7.8 0.0 collective-permute-done.1
  7.8 3.2 %collective-permute-done.2 = f32[2,128,128]{2,1,0:T(8,128)S(1)} collective-permute-done((f32[2,128,128]{2,1,0:T(8,128)}, f32[2,128,128]{2,1,0:T(8,128)S(1)}, u32[]{:S(2)}, u32[]{:S(2)}) %collective-permute-start.2) | collective-permute-done | bytes 131104 | tf_op jit(solution)/shard_map/ppermute | solution.py:220
  11.0 0.7 collective-permute-start.3
  11.6 0.7 collective-permute-start.4
  12.3 0.7 collective-permute-start.5
  13.0 0.7 collective-permute-start.6
  13.7 0.0 collective-permute-done.4
  13.7 0.0 collective-permute-done.5
  13.7 0.0 collective-permute-done.3
  13.7 0.2 conditional.5
  13.9 0.7 collective-permute-start.7
  14.6 0.7 collective-permute-start.10
  15.3 0.7 collective-permute-start.8
  15.9 0.7 collective-permute-start.9
  16.6 0.0 collective-permute-done.9
  16.7 0.3 conditional.6
  16.9 0.0 copy-start.1
  16.9 1.3 %collective-permute-start.11 = (f32[2,128,128]{2,1,0:T(8,128)S(1)}, f32[2,128,128]{2,1,0:T(8,128)S(1)}, u32[]{:S(2)}, u32[]{:S(2)}) collective-permute-start(f32[2,128,128]{2,1,0:T(8,128)S(1)} %get-tuple-element.163), channel_id=1, source_target_pairs={{16,31},{17,30},{18,29},{19,28},{20,27},{21,26},{22,25},{23,24}} | collective-permute-start | bytes 393224 | tf_op jit(solution)/shard_map/ppermute | solution.py:234
  18.2 1.3 %collective-permute-start.12 = (bf16[2,128,128]{2,1,0:T(8,128)(2,1)S(1)}, bf16[2,128,128]{2,1,0:T(8,128)(2,1)S(1)}, u32[]{:S(2)}, u32[]{:S(2)}) collective-permute-start(bf16[2,128,128]{2,1,0:T(8,128)(2,1)S(1)} %get-tuple-element.164), channel_id=1, source_target_pairs={{17,31},{18,30},{19,29},{20,28},{21,27},{22,26},{23,25}} | collective-permute-start | bytes 196616 | tf_op jit(solution)/shard_map/ppermute | solution.py:234
  19.5 1.3 %collective-permute-start.13 = (bf16[2,128,128]{2,1,0:T(8,128)(2,1)S(1)}, bf16[2,128,128]{2,1,0:T(8,128)(2,1)S(1)}, u32[]{:S(2)}, u32[]{:S(2)}) collective-permute-start(bf16[2,128,128]{2,1,0:T(8,128)(2,1)S(1)} %get-tuple-element.164), channel_id=1, source_target_pairs={{18,31},{19,30},{20,29},{21,28},{22,27},{23,26}} | collective-permute-start | bytes 196616 | tf_op jit(solution)/shard_map/ppermute | solution.py:234
  20.8 1.3 %collective-permute-start.14 = (bf16[2,128,128]{2,1,0:T(8,128)(2,1)S(1)}, bf16[2,128,128]{2,1,0:T(8,128)(2,1)S(1)}, u32[]{:S(2)}, u32[]{:S(2)}) collective-permute-start(bf16[2,128,128]{2,1,0:T(8,128)(2,1)S(1)} %get-tuple-element.164), channel_id=1, source_target_pairs={{19,31},{20,30},{21,29},{22,28},{23,27}} | collective-permute-start | bytes 196616 | tf_op jit(solution)/shard_map/ppermute | solution.py:234
  22.1 46.6 %collective-permute-done.12 = bf16[2,128,128]{2,1,0:T(8,128)(2,1)S(1)} collective-permute-done((bf16[2,128,128]{2,1,0:T(8,128)(2,1)S(1)}, bf16[2,128,128]{2,1,0:T(8,128)(2,1)S(1)}, u32[]{:S(2)}, u32[]{:S(2)}) %collective-permute-start.12) | collective-permute-done | bytes 65568 | tf_op jit(solution)/shard_map/ppermute | solution.py:234
  68.7 0.0 collective-permute-done.13
  68.8 0.0 collective-permute-done.14
  68.8 10.8 %conditional.7 = (f32[1,2,128,128]{3,2,1,0:T(8,128)}) conditional(s32[]{:T(128)} %convert_element_type.15, f32[2,128,128]{2,1,0:T(8,128)} %copy-done.1, (s32[3]{0:T(128)S(1)}, f32[2,128,128]{2,1,0:T(8,128)S(1)}, bf16[2,128,128]{2,1,0:T(8,128)(2,1)S(1)}, bf16[2,128,128]{2,1,0:T(8,128)(2,1)S(1)}, bf16[2,128,128]{2,1,0:T(8,128)(2,1)S(1)}, ...), branch_computations={%region_7.8_spmd, %region_8.9_spmd} | conditional | flops 5033164800 | bytes 9633800 | solution.py:247
  69.0 10.5 %branch_1_fun.6 = (f32[2,128,128]{2,1,0:T(8,128)}, bf16[2,128,128]{2,1,0:T(8,128)(2,1)}) custom-call(s32[3]{0:T(128)S(1)} %get-tuple-element.139.listed_ref, f32[2,128,128]{2,1,0:T(8,128)S(1)} %get-tuple-element.140.own_ref, bf16[2,128,128]{2,1,0:T(8,128)(2,1)S(1)} %get-tuple-element.141.back1_ref, bf16[2,128,128]{2,1,0:T(8,128)(2,1)S(1)} %get-tuple-element.142.back2_ref, ...), custom_call_target="tpu_custom_call" | custom-call | flops 5033164800 | bytes 9633792 | tf_op jit(solution)/shard_map/cond/branch_1_fun/pallas_call | solution.py:249
  (15 shorter events, 0.1 us)
Async XLA Ops:
  0.0 7.5 %copy-start = (s32[8,4]{0,1:T(4,128)S(1)}, s32[8,4]{0,1:T(4,128)}, u32[]{:S(2)}) copy-start(s32[8,4]{0,1:T(4,128)} %param.17) | copy-start | bytes 388
  0.0 7.7 %collective-permute-start = (f32[2,128,128]{2,1,0:T(8,128)}, f32[2,128,128]{2,1,0:T(8,128)S(1)}, u32[]{:S(2)}, u32[]{:S(2)}) collective-permute-start(f32[2,128,128]{2,1,0:T(8,128)} %param.16), channel_id=1, source_target_pairs={{24,1},{25,2},{26,3},{27,4},{28,5},{29,6},{30,7}} | collective-permute-start | bytes 393224 | tf_op jit(solution)/shard_map/ppermute | solution.py:220
  3.8 3.9 %collective-permute-start.1 = (f32[2,128,128]{2,1,0:T(8,128)}, f32[2,128,128]{2,1,0:T(8,128)S(1)}, u32[]{:S(2)}, u32[]{:S(2)}) collective-permute-start(f32[2,128,128]{2,1,0:T(8,128)} %param.16), channel_id=1, source_target_pairs={{24,2},{25,3},{26,4},{27,5},{28,6},{29,7}} | collective-permute-start | bytes 393224 | tf_op jit(solution)/shard_map/ppermute | solution.py:220
  5.1 5.8 %collective-permute-start.2 = (f32[2,128,128]{2,1,0:T(8,128)}, f32[2,128,128]{2,1,0:T(8,128)S(1)}, u32[]{:S(2)}, u32[]{:S(2)}) collective-permute-start(f32[2,128,128]{2,1,0:T(8,128)} %param.16), channel_id=1, source_target_pairs={{24,3},{25,4},{26,5},{27,6},{28,7}} | collective-permute-start | bytes 393224 | tf_op jit(solution)/shard_map/ppermute | solution.py:220
  11.0 2.7 %collective-permute-start.3 = (f32[2,128,128]{2,1,0:T(8,128)S(1)}, f32[2,128,128]{2,1,0:T(8,128)S(1)}, u32[]{:S(2)}, u32[]{:S(2)}) collective-permute-start(f32[2,128,128]{2,1,0:T(8,128)S(1)} %get-tuple-element.158), channel_id=1, source_target_pairs={{0,15},{1,14},{2,13},{3,12},{4,11},{5,10},{6,9},{7,8}} | collective-permute-start | bytes 393224 | tf_op jit(solution)/shard_map/ppermute | solution.py:234
  11.6 2.0 %collective-permute-start.4 = (bf16[2,128,128]{2,1,0:T(8,128)(2,1)S(1)}, bf16[2,128,128]{2,1,0:T(8,128)(2,1)S(1)}, u32[]{:S(2)}, u32[]{:S(2)}) collective-permute-start(bf16[2,128,128]{2,1,0:T(8,128)(2,1)S(1)} %get-tuple-element.160), channel_id=1, source_target_pairs={{1,15},{2,14},{3,13},{4,12},{5,11},{6,10},{7,9}} | collective-permute-start | bytes 196616 | tf_op jit(solution)/shard_map/ppermute | solution.py:234
  12.3 1.4 %collective-permute-start.5 = (bf16[2,128,128]{2,1,0:T(8,128)(2,1)S(1)}, bf16[2,128,128]{2,1,0:T(8,128)(2,1)S(1)}, u32[]{:S(2)}, u32[]{:S(2)}) collective-permute-start(bf16[2,128,128]{2,1,0:T(8,128)(2,1)S(1)} %get-tuple-element.160), channel_id=1, source_target_pairs={{2,15},{3,14},{4,13},{5,12},{6,11},{7,10}} | collective-permute-start | bytes 196616 | tf_op jit(solution)/shard_map/ppermute | solution.py:234
  13.0 0.7 collective-permute-start.6
  13.9 2.7 %collective-permute-start.7 = (f32[2,128,128]{2,1,0:T(8,128)S(1)}, f32[2,128,128]{2,1,0:T(8,128)S(1)}, u32[]{:S(2)}, u32[]{:S(2)}) collective-permute-start(f32[2,128,128]{2,1,0:T(8,128)S(1)} %get-tuple-element.161), channel_id=1, source_target_pairs={{8,23},{9,22},{10,21},{11,20},{12,19},{13,18},{14,17},{15,16}} | collective-permute-start | bytes 393224 | tf_op jit(solution)/shard_map/ppermute | solution.py:234
  14.6 2.0 %collective-permute-start.10 = (bf16[2,128,128]{2,1,0:T(8,128)(2,1)S(1)}, bf16[2,128,128]{2,1,0:T(8,128)(2,1)S(1)}, u32[]{:S(2)}, u32[]{:S(2)}) collective-permute-start(bf16[2,128,128]{2,1,0:T(8,128)(2,1)S(1)} %get-tuple-element.162), channel_id=1, source_target_pairs={{11,23},{12,22},{13,21},{14,20},{15,19}} | collective-permute-start | bytes 196616 | tf_op jit(solution)/shard_map/ppermute | solution.py:234
  15.3 1.4 %collective-permute-start.8 = (bf16[2,128,128]{2,1,0:T(8,128)(2,1)S(1)}, bf16[2,128,128]{2,1,0:T(8,128)(2,1)S(1)}, u32[]{:S(2)}, u32[]{:S(2)}) collective-permute-start(bf16[2,128,128]{2,1,0:T(8,128)(2,1)S(1)} %get-tuple-element.162), channel_id=1, source_target_pairs={{9,23},{10,22},{11,21},{12,20},{13,19},{14,18},{15,17}} | collective-permute-start | bytes 196616 | tf_op jit(solution)/shard_map/ppermute | solution.py:234
  15.9 0.7 collective-permute-start.9
  16.9 51.8 %copy-start.1 = (f32[2,128,128]{2,1,0:T(8,128)}, f32[2,128,128]{2,1,0:T(8,128)S(1)}, u32[]{:S(2)}) copy-start(f32[2,128,128]{2,1,0:T(8,128)S(1)} %get-tuple-element.163) | copy-start | bytes 393220
  16.9 51.8 %collective-permute-start.11 = (f32[2,128,128]{2,1,0:T(8,128)S(1)}, f32[2,128,128]{2,1,0:T(8,128)S(1)}, u32[]{:S(2)}, u32[]{:S(2)}) collective-permute-start(f32[2,128,128]{2,1,0:T(8,128)S(1)} %get-tuple-element.163), channel_id=1, source_target_pairs={{16,31},{17,30},{18,29},{19,28},{20,27},{21,26},{22,25},{23,24}} | collective-permute-start | bytes 393224 | tf_op jit(solution)/shard_map/ppermute | solution.py:234
  18.2 50.5 %collective-permute-start.12 = (bf16[2,128,128]{2,1,0:T(8,128)(2,1)S(1)}, bf16[2,128,128]{2,1,0:T(8,128)(2,1)S(1)}, u32[]{:S(2)}, u32[]{:S(2)}) collective-permute-start(bf16[2,128,128]{2,1,0:T(8,128)(2,1)S(1)} %get-tuple-element.164), channel_id=1, source_target_pairs={{17,31},{18,30},{19,29},{20,28},{21,27},{22,26},{23,25}} | collective-permute-start | bytes 196616 | tf_op jit(solution)/shard_map/ppermute | solution.py:234
  19.5 49.2 %collective-permute-start.13 = (bf16[2,128,128]{2,1,0:T(8,128)(2,1)S(1)}, bf16[2,128,128]{2,1,0:T(8,128)(2,1)S(1)}, u32[]{:S(2)}, u32[]{:S(2)}) collective-permute-start(bf16[2,128,128]{2,1,0:T(8,128)(2,1)S(1)} %get-tuple-element.164), channel_id=1, source_target_pairs={{18,31},{19,30},{20,29},{21,28},{22,27},{23,26}} | collective-permute-start | bytes 196616 | tf_op jit(solution)/shard_map/ppermute | solution.py:234
  20.8 47.9 %collective-permute-start.14 = (bf16[2,128,128]{2,1,0:T(8,128)(2,1)S(1)}, bf16[2,128,128]{2,1,0:T(8,128)(2,1)S(1)}, u32[]{:S(2)}, u32[]{:S(2)}) collective-permute-start(bf16[2,128,128]{2,1,0:T(8,128)(2,1)S(1)} %get-tuple-element.164), channel_id=1, source_target_pairs={{19,31},{20,30},{21,29},{22,28},{23,27}} | collective-permute-start | bytes 196616 | tf_op jit(solution)/shard_map/ppermute | solution.py:234

commit v16 on v14

--- a/solution.py
+++ b/solution.py
@@ -215,7 +215,7 @@
 
     def first_inputs():
         def behind(distance):
-            source = (n_seg - 1) * n_seq
+            source = n_seq
             pairs = [(source + q, q + distance) for q in range(n_seq) if q + distance < n_seq]
             return lax.ppermute(patches_low, axes, pairs)
 

time: 79.1 us -> 78.2 us (0.989)
  starting transfers between devices: 17.8 us -> 12.5 us
  waiting for transfers between devices: 48 us -> 52.4 us
    ppermute x12, waiting for transfers between devices: 46.6 us -> 52.4 us  [send(): return lax.ppermute(block, axes, pairs)]
    ppermute x3, starting transfers between devices: 7.28 us -> 1.99 us  [behind(): return lax.ppermute(patches_low, axes, pairs)]
    ppermute x3, waiting for transfers between devices: 1.45 us -> 0.01 us  [behind(): return lax.ppermute(patches_low, axes, pairs)]
  transfers between devices with their start and end apart: 15 -> 15, of which waited for: 2 -> 1; matrix products, arithmetic and copies ran while one was open for 0% -> 0% of each run, Pallas kernels for 0% -> 0%
where the time goes in v16:
time: 78.2 us; the launch traced here: 77.9 us
  waiting for transfers between devices  52.4 us (67%)
  starting transfers between devices  12.5 us (16%)
  Pallas kernels  10.5 us (13%)
  other arithmetic  1.03 us (1%)
    ppermute x12, waiting for transfers between devices, send(): return lax.ppermute(block, axes, pairs)  52.4 us
    ppermute x12, starting transfers between devices, send(): return lax.ppermute(block, axes, pairs)  10.5 us
    pallas_call x1, Pallas kernels, body(): call(*args[1:])  10.5 us
    ppermute x3, starting transfers between devices, behind(): return lax.ppermute(patches_low, axes, pairs)  1.99 us
  transfers between devices with their start and end apart: 15, of which 1 were waited for; matrix products, arithmetic and copies ran while one was open for 0% of the time, Pallas kernels for 0%

profile of v16, /device:TPU:15, one launch (start us, length us, event | category | flops | bytes accessed | tf_op | source)
XLA Modules:
  0.0 77.9 jit_solution(2520449797023116035)
XLA Ops:
  0.0 0.9 %convert_element_type.23 = bf16[2,128,128]{2,1,0:T(8,128)(2,1)S(1)} convert(f32[2,128,128]{2,1,0:T(8,128)} %param.16) | non-fusion elementwise | flops 32768 | bytes 196608 | tf_op jit(solution)/shard_map/convert_element_type | solution.py:222
  0.9 0.7 collective-permute-start
  1.6 0.7 collective-permute-start.1
  2.3 0.7 collective-permute-start.2
  3.0 0.2 dynamic-slice_reduce_fusion
  3.2 0.1 compare_reduce_fusion
  3.3 0.0 collective-permute-done
  3.3 0.0 collective-permute-done.1
  3.4 0.7 collective-permute-start.3
  4.0 0.7 collective-permute-start.4
  4.7 0.7 collective-permute-start.5
  5.4 0.7 collective-permute-start.6
  6.1 0.0 collective-permute-done.4
  6.1 0.0 collective-permute-done.3
  6.1 0.2 conditional.5
  6.3 0.7 collective-permute-start.7
  7.0 0.7 collective-permute-start.10
  7.7 0.7 collective-permute-start.8
  8.3 0.7 collective-permute-start.9
  9.0 0.0 collective-permute-done.9
  9.0 0.0 collective-permute-done.7
  9.1 0.3 conditional.6
  9.3 0.0 copy-start.1
  9.3 1.3 %collective-permute-start.11 = (f32[2,128,128]{2,1,0:T(8,128)S(1)}, f32[2,128,128]{2,1,0:T(8,128)S(1)}, u32[]{:S(2)}, u32[]{:S(2)}) collective-permute-start(f32[2,128,128]{2,1,0:T(8,128)S(1)} %get-tuple-element.163), channel_id=1, source_target_pairs={{16,31},{17,30},{18,29},{19,28},{20,27},{21,26},{22,25},{23,24}} | collective-permute-start | bytes 393224 | tf_op jit(solution)/shard_map/ppermute | solution.py:235
  10.6 1.3 %collective-permute-start.12 = (bf16[2,128,128]{2,1,0:T(8,128)(2,1)S(1)}, bf16[2,128,128]{2,1,0:T(8,128)(2,1)S(1)}, u32[]{:S(2)}, u32[]{:S(2)}) collective-permute-start(bf16[2,128,128]{2,1,0:T(8,128)(2,1)S(1)} %get-tuple-element.164), channel_id=1, source_target_pairs={{17,31},{18,30},{19,29},{20,28},{21,27},{22,26},{23,25}} | collective-permute-start | bytes 196616 | tf_op jit(solution)/shard_map/ppermute | solution.py:235
  11.9 1.3 %collective-permute-start.13 = (bf16[2,128,128]{2,1,0:T(8,128)(2,1)S(1)}, bf16[2,128,128]{2,1,0:T(8,128)(2,1)S(1)}, u32[]{:S(2)}, u32[]{:S(2)}) collective-permute-start(bf16[2,128,128]{2,1,0:T(8,128)(2,1)S(1)} %get-tuple-element.164), channel_id=1, source_target_pairs={{18,31},{19,30},{20,29},{21,28},{22,27},{23,26}} | collective-permute-start | bytes 196616 | tf_op jit(solution)/shard_map/ppermute | solution.py:235
  13.2 1.3 %collective-permute-start.14 = (bf16[2,128,128]{2,1,0:T(8,128)(2,1)S(1)}, bf16[2,128,128]{2,1,0:T(8,128)(2,1)S(1)}, u32[]{:S(2)}, u32[]{:S(2)}) collective-permute-start(bf16[2,128,128]{2,1,0:T(8,128)(2,1)S(1)} %get-tuple-element.164), channel_id=1, source_target_pairs={{19,31},{20,30},{21,29},{22,28},{23,27}} | collective-permute-start | bytes 196616 | tf_op jit(solution)/shard_map/ppermute | solution.py:235
  14.5 52.4 %collective-permute-done.12 = bf16[2,128,128]{2,1,0:T(8,128)(2,1)S(1)} collective-permute-done((bf16[2,128,128]{2,1,0:T(8,128)(2,1)S(1)}, bf16[2,128,128]{2,1,0:T(8,128)(2,1)S(1)}, u32[]{:S(2)}, u32[]{:S(2)}) %collective-permute-start.12) | collective-permute-done | bytes 65568 | tf_op jit(solution)/shard_map/ppermute | solution.py:235
  66.9 0.0 collective-permute-done.13
  66.9 0.0 collective-permute-done.14
  66.9 10.8 %conditional.7 = (f32[1,2,128,128]{3,2,1,0:T(8,128)}) conditional(s32[]{:T(128)} %convert_element_type.18, f32[2,128,128]{2,1,0:T(8,128)} %copy-done.1, (s32[3]{0:T(128)S(1)}, f32[2,128,128]{2,1,0:T(8,128)S(1)}, bf16[2,128,128]{2,1,0:T(8,128)(2,1)S(1)}, bf16[2,128,128]{2,1,0:T(8,128)(2,1)S(1)}, bf16[2,128,128]{2,1,0:T(8,128)(2,1)S(1)}, ...), branch_computations={%region_7.8_spmd, %region_8.9_spmd} | conditional | flops 5033164800 | bytes 9633800 | solution.py:248
  67.2 10.5 %branch_1_fun.6 = (f32[2,128,128]{2,1,0:T(8,128)}, bf16[2,128,128]{2,1,0:T(8,128)(2,1)}) custom-call(s32[3]{0:T(128)S(1)} %get-tuple-element.139.listed_ref, f32[2,128,128]{2,1,0:T(8,128)S(1)} %get-tuple-element.140.own_ref, bf16[2,128,128]{2,1,0:T(8,128)(2,1)S(1)} %get-tuple-element.141.back1_ref, bf16[2,128,128]{2,1,0:T(8,128)(2,1)S(1)} %get-tuple-element.142.back2_ref, ...), custom_call_target="tpu_custom_call" | custom-call | flops 5033164800 | bytes 9633792 | tf_op jit(solution)/shard_map/cond/branch_1_fun/pallas_call | solution.py:250
  (16 shorter events, 0.1 us)
Async XLA Ops:
  0.0 3.0 %copy-start = (s32[8,4]{0,1:T(4,128)S(1)}, s32[8,4]{0,1:T(4,128)}, u32[]{:S(2)}) copy-start(s32[8,4]{0,1:T(4,128)} %param.17) | copy-start | bytes 388
  0.9 2.3 %collective-permute-start = (bf16[2,128,128]{2,1,0:T(8,128)(2,1)S(1)}, bf16[2,128,128]{2,1,0:T(8,128)(2,1)S(1)}, u32[]{:S(2)}, u32[]{:S(2)}) collective-permute-start(bf16[2,128,128]{2,1,0:T(8,128)(2,1)S(1)} %convert_element_type.23), channel_id=1, source_target_pairs={{8,1},{9,2},{10,3},{11,4},{12,5},{13,6},{14,7}} | collective-permute-start | bytes 196616 | tf_op jit(solution)/shard_map/ppermute | solution.py:220
  1.6 1.7 %collective-permute-start.1 = (bf16[2,128,128]{2,1,0:T(8,128)(2,1)S(1)}, bf16[2,128,128]{2,1,0:T(8,128)(2,1)S(1)}, u32[]{:S(2)}, u32[]{:S(2)}) collective-permute-start(bf16[2,128,128]{2,1,0:T(8,128)(2,1)S(1)} %convert_element_type.23), channel_id=1, source_target_pairs={{8,2},{9,3},{10,4},{11,5},{12,6},{13,7}} | collective-permute-start | bytes 196616 | tf_op jit(solution)/shard_map/ppermute | solution.py:220
  2.3 1.0 %collective-permute-start.2 = (bf16[2,128,128]{2,1,0:T(8,128)(2,1)S(1)}, bf16[2,128,128]{2,1,0:T(8,128)(2,1)S(1)}, u32[]{:S(2)}, u32[]{:S(2)}) collective-permute-start(bf16[2,128,128]{2,1,0:T(8,128)(2,1)S(1)} %convert_element_type.23), channel_id=1, source_target_pairs={{8,3},{9,4},{10,5},{11,6},{12,7}} | collective-permute-start | bytes 196616 | tf_op jit(solution)/shard_map/ppermute | solution.py:220
  3.4 2.7 %collective-permute-start.3 = (f32[2,128,128]{2,1,0:T(8,128)S(1)}, f32[2,128,128]{2,1,0:T(8,128)S(1)}, u32[]{:S(2)}, u32[]{:S(2)}) collective-permute-start(f32[2,128,128]{2,1,0:T(8,128)S(1)} %get-tuple-element.158), channel_id=1, source_target_pairs={{0,15},{1,14},{2,13},{3,12},{4,11},{5,10},{6,9},{7,8}} | collective-permute-start | bytes 393224 | tf_op jit(solution)/shard_map/ppermute | solution.py:235
  4.0 2.0 %collective-permute-start.4 = (bf16[2,128,128]{2,1,0:T(8,128)(2,1)S(1)}, bf16[2,128,128]{2,1,0:T(8,128)(2,1)S(1)}, u32[]{:S(2)}, u32[]{:S(2)}) collective-permute-start(bf16[2,128,128]{2,1,0:T(8,128)(2,1)S(1)} %get-tuple-element.160), channel_id=1, source_target_pairs={{1,15},{2,14},{3,13},{4,12},{5,11},{6,10},{7,9}} | collective-permute-start | bytes 196616 | tf_op jit(solution)/shard_map/ppermute | solution.py:235
  4.7 1.4 %collective-permute-start.5 = (bf16[2,128,128]{2,1,0:T(8,128)(2,1)S(1)}, bf16[2,128,128]{2,1,0:T(8,128)(2,1)S(1)}, u32[]{:S(2)}, u32[]{:S(2)}) collective-permute-start(bf16[2,128,128]{2,1,0:T(8,128)(2,1)S(1)} %get-tuple-element.160), channel_id=1, source_target_pairs={{2,15},{3,14},{4,13},{5,12},{6,11},{7,10}} | collective-permute-start | bytes 196616 | tf_op jit(solution)/shard_map/ppermute | solution.py:235
  5.4 0.7 collective-permute-start.6
  6.3 2.7 %collective-permute-start.7 = (f32[2,128,128]{2,1,0:T(8,128)S(1)}, f32[2,128,128]{2,1,0:T(8,128)S(1)}, u32[]{:S(2)}, u32[]{:S(2)}) collective-permute-start(f32[2,128,128]{2,1,0:T(8,128)S(1)} %get-tuple-element.161), channel_id=1, source_target_pairs={{8,23},{9,22},{10,21},{11,20},{12,19},{13,18},{14,17},{15,16}} | collective-permute-start | bytes 393224 | tf_op jit(solution)/shard_map/ppermute | solution.py:235
  7.0 2.0 %collective-permute-start.10 = (bf16[2,128,128]{2,1,0:T(8,128)(2,1)S(1)}, bf16[2,128,128]{2,1,0:T(8,128)(2,1)S(1)}, u32[]{:S(2)}, u32[]{:S(2)}) collective-permute-start(bf16[2,128,128]{2,1,0:T(8,128)(2,1)S(1)} %get-tuple-element.162), channel_id=1, source_target_pairs={{11,23},{12,22},{13,21},{14,20},{15,19}} | collective-permute-start | bytes 196616 | tf_op jit(solution)/shard_map/ppermute | solution.py:235
  7.7 1.4 %collective-permute-start.8 = (bf16[2,128,128]{2,1,0:T(8,128)(2,1)S(1)}, bf16[2,128,128]{2,1,0:T(8,128)(2,1)S(1)}, u32[]{:S(2)}, u32[]{:S(2)}) collective-permute-start(bf16[2,128,128]{2,1,0:T(8,128)(2,1)S(1)} %get-tuple-element.162), channel_id=1, source_target_pairs={{9,23},{10,22},{11,21},{12,20},{13,19},{14,18},{15,17}} | collective-permute-start | bytes 196616 | tf_op jit(solution)/shard_map/ppermute | solution.py:235
  8.3 0.7 collective-permute-start.9
  9.3 57.6 %copy-start.1 = (f32[2,128,128]{2,1,0:T(8,128)}, f32[2,128,128]{2,1,0:T(8,128)S(1)}, u32[]{:S(2)}) copy-start(f32[2,128,128]{2,1,0:T(8,128)S(1)} %get-tuple-element.163) | copy-start | bytes 393220
  9.3 57.6 %collective-permute-start.11 = (f32[2,128,128]{2,1,0:T(8,128)S(1)}, f32[2,128,128]{2,1,0:T(8,128)S(1)}, u32[]{:S(2)}, u32[]{:S(2)}) collective-permute-start(f32[2,128,128]{2,1,0:T(8,128)S(1)} %get-tuple-element.163), channel_id=1, source_target_pairs={{16,31},{17,30},{18,29},{19,28},{20,27},{21,26},{22,25},{23,24}} | collective-permute-start | bytes 393224 | tf_op jit(solution)/shard_map/ppermute | solution.py:235
  10.6 56.3 %collective-permute-start.12 = (bf16[2,128,128]{2,1,0:T(8,128)(2,1)S(1)}, bf16[2,128,128]{2,1,0:T(8,128)(2,1)S(1)}, u32[]{:S(2)}, u32[]{:S(2)}) collective-permute-start(bf16[2,128,128]{2,1,0:T(8,128)(2,1)S(1)} %get-tuple-element.164), channel_id=1, source_target_pairs={{17,31},{18,30},{19,29},{20,28},{21,27},{22,26},{23,25}} | collective-permute-start | bytes 196616 | tf_op jit(solution)/shard_map/ppermute | solution.py:235
  11.9 55.0 %collective-permute-start.13 = (bf16[2,128,128]{2,1,0:T(8,128)(2,1)S(1)}, bf16[2,128,128]{2,1,0:T(8,128)(2,1)S(1)}, u32[]{:S(2)}, u32[]{:S(2)}) collective-permute-start(bf16[2,128,128]{2,1,0:T(8,128)(2,1)S(1)} %get-tuple-element.164), channel_id=1, source_target_pairs={{18,31},{19,30},{20,29},{21,28},{22,27},{23,26}} | collective-permute-start | bytes 196616 | tf_op jit(solution)/shard_map/ppermute | solution.py:235
  13.2 53.7 %collective-permute-start.14 = (bf16[2,128,128]{2,1,0:T(8,128)(2,1)S(1)}, bf16[2,128,128]{2,1,0:T(8,128)(2,1)S(1)}, u32[]{:S(2)}, u32[]{:S(2)}) collective-permute-start(bf16[2,128,128]{2,1,0:T(8,128)(2,1)S(1)} %get-tuple-element.164), channel_id=1, source_target_pairs={{19,31},{20,30},{21,29},{22,28},{23,27}} | collective-permute-start | bytes 196616 | tf_op jit(solution)/shard_map/ppermute | solution.py:235

commit v17 on v15

--- a/solution.py
+++ b/solution.py
@@ -215,7 +215,7 @@
 
     def first_inputs():
         def behind(distance):
-            source = (n_seg - 1) * n_seq
+            source = n_seq
             pairs = [(source + q, q + distance) for q in range(n_seq) if q + distance < n_seq]
             return lax.ppermute(patches, axes, pairs)
 

time: 80 us -> 79.2 us (0.990)
  starting transfers between devices: 17.9 us -> 12.6 us
  waiting for transfers between devices: 49.8 us -> 54.1 us
    ppermute x12, waiting for transfers between devices: 46.6 us -> 54.1 us  [send(): return lax.ppermute(block, axes, pairs)]
    ppermute x3, starting transfers between devices: 7.4 us -> 2.13 us  [behind(): return lax.ppermute(patches, axes, pairs)]
    ppermute x3, waiting for transfers between devices: 3.17 us -> 0.01 us  [behind(): return lax.ppermute(patches, axes, pairs)]
  transfers between devices with their start and end apart: 15 -> 15, of which waited for: 2 -> 1; matrix products, arithmetic and copies ran while one was open for 0% -> 0% of each run, Pallas kernels for 0% -> 0%
where the time goes in v17:
time: 79.2 us; the launch traced here: 78.8 us
  waiting for transfers between devices  54.1 us (68%)
  starting transfers between devices  12.6 us (16%)
  Pallas kernels  10.5 us (13%)
    ppermute x12, waiting for transfers between devices, send(): return lax.ppermute(block, axes, pairs)  54.1 us
    ppermute x12, starting transfers between devices, send(): return lax.ppermute(block, axes, pairs)  10.5 us
    pallas_call x1, Pallas kernels, body(): call(*args[1:])  10.5 us
    ppermute x3, starting transfers between devices, behind(): return lax.ppermute(patches, axes, pairs)  2.13 us
  transfers between devices with their start and end apart: 15, of which 1 were waited for; matrix products, arithmetic and copies ran while one was open for 0% of the time, Pallas kernels for 0%

profile of v17, /device:TPU:15, one launch (start us, length us, event | category | flops | bytes accessed | tf_op | source)
XLA Modules:
  0.0 78.8 jit_solution(15387751968922908007)
XLA Ops:
  0.0 0.8 %collective-permute-start = (f32[2,128,128]{2,1,0:T(8,128)}, f32[2,128,128]{2,1,0:T(8,128)S(1)}, u32[]{:S(2)}, u32[]{:S(2)}) collective-permute-start(f32[2,128,128]{2,1,0:T(8,128)} %param.16), channel_id=1, source_target_pairs={{8,1},{9,2},{10,3},{11,4},{12,5},{13,6},{14,7}} | collective-permute-start | bytes 393224 | tf_op jit(solution)/shard_map/ppermute | solution.py:220
  0.8 0.7 collective-permute-start.1
  1.5 0.7 collective-permute-start.2
  2.2 0.2 dynamic-slice_reduce_fusion
  2.4 0.1 compare_reduce_fusion
  2.5 0.1 conditional.4
  2.6 0.7 collective-permute-start.3
  3.2 0.7 collective-permute-start.4
  3.9 0.7 collective-permute-start.5
  4.6 0.7 collective-permute-start.6
  5.3 0.0 collective-permute-done.4
  5.3 0.0 collective-permute-done.6
  5.3 0.0 collective-permute-done.3
  5.3 0.2 conditional.5
  5.5 0.7 collective-permute-start.7
  6.2 0.7 collective-permute-start.10
  6.9 0.7 collective-permute-start.8
  7.5 0.7 collective-permute-start.9
  8.2 0.0 collective-permute-done.8
  8.2 0.0 collective-permute-done.9
  8.3 0.3 conditional.6
  8.5 0.0 copy-start.1
  8.5 1.3 %collective-permute-start.11 = (f32[2,128,128]{2,1,0:T(8,128)S(1)}, f32[2,128,128]{2,1,0:T(8,128)S(1)}, u32[]{:S(2)}, u32[]{:S(2)}) collective-permute-start(f32[2,128,128]{2,1,0:T(8,128)S(1)} %get-tuple-element.163), channel_id=1, source_target_pairs={{16,31},{17,30},{18,29},{19,28},{20,27},{21,26},{22,25},{23,24}} | collective-permute-start | bytes 393224 | tf_op jit(solution)/shard_map/ppermute | solution.py:234
  9.8 1.3 %collective-permute-start.12 = (bf16[2,128,128]{2,1,0:T(8,128)(2,1)S(1)}, bf16[2,128,128]{2,1,0:T(8,128)(2,1)S(1)}, u32[]{:S(2)}, u32[]{:S(2)}) collective-permute-start(bf16[2,128,128]{2,1,0:T(8,128)(2,1)S(1)} %get-tuple-element.164), channel_id=1, source_target_pairs={{17,31},{18,30},{19,29},{20,28},{21,27},{22,26},{23,25}} | collective-permute-start | bytes 196616 | tf_op jit(solution)/shard_map/ppermute | solution.py:234
  11.1 1.3 %collective-permute-start.13 = (bf16[2,128,128]{2,1,0:T(8,128)(2,1)S(1)}, bf16[2,128,128]{2,1,0:T(8,128)(2,1)S(1)}, u32[]{:S(2)}, u32[]{:S(2)}) collective-permute-start(bf16[2,128,128]{2,1,0:T(8,128)(2,1)S(1)} %get-tuple-element.164), channel_id=1, source_target_pairs={{18,31},{19,30},{20,29},{21,28},{22,27},{23,26}} | collective-permute-start | bytes 196616 | tf_op jit(solution)/shard_map/ppermute | solution.py:234
  12.4 1.3 %collective-permute-start.14 = (bf16[2,128,128]{2,1,0:T(8,128)(2,1)S(1)}, bf16[2,128,128]{2,1,0:T(8,128)(2,1)S(1)}, u32[]{:S(2)}, u32[]{:S(2)}) collective-permute-start(bf16[2,128,128]{2,1,0:T(8,128)(2,1)S(1)} %get-tuple-element.164), channel_id=1, source_target_pairs={{19,31},{20,30},{21,29},{22,28},{23,27}} | collective-permute-start | bytes 196616 | tf_op jit(solution)/shard_map/ppermute | solution.py:234
  13.7 54.1 %collective-permute-done.12 = bf16[2,128,128]{2,1,0:T(8,128)(2,1)S(1)} collective-permute-done((bf16[2,128,128]{2,1,0:T(8,128)(2,1)S(1)}, bf16[2,128,128]{2,1,0:T(8,128)(2,1)S(1)}, u32[]{:S(2)}, u32[]{:S(2)}) %collective-permute-start.12) | collective-permute-done | bytes 65568 | tf_op jit(solution)/shard_map/ppermute | solution.py:234
  67.8 0.0 collective-permute-done.13
  67.9 0.0 collective-permute-done.14
  67.9 0.0 collective-permute-done.11
  67.9 10.8 %conditional.7 = (f32[1,2,128,128]{3,2,1,0:T(8,128)}) conditional(s32[]{:T(128)} %convert_element_type.15, f32[2,128,128]{2,1,0:T(8,128)} %copy-done.1, (s32[3]{0:T(128)S(1)}, f32[2,128,128]{2,1,0:T(8,128)S(1)}, bf16[2,128,128]{2,1,0:T(8,128)(2,1)S(1)}, bf16[2,128,128]{2,1,0:T(8,128)(2,1)S(1)}, bf16[2,128,128]{2,1,0:T(8,128)(2,1)S(1)}, ...), branch_computations={%region_7.8_spmd, %region_8.9_spmd} | conditional | flops 5033164800 | bytes 9633800 | solution.py:247
  68.1 10.5 %branch_1_fun.6 = (f32[2,128,128]{2,1,0:T(8,128)}, bf16[2,128,128]{2,1,0:T(8,128)(2,1)}) custom-call(s32[3]{0:T(128)S(1)} %get-tuple-element.139.listed_ref, f32[2,128,128]{2,1,0:T(8,128)S(1)} %get-tuple-element.140.own_ref, bf16[2,128,128]{2,1,0:T(8,128)(2,1)S(1)} %get-tuple-element.141.back1_ref, bf16[2,128,128]{2,1,0:T(8,128)(2,1)S(1)} %get-tuple-element.142.back2_ref, ...), custom_call_target="tpu_custom_call" | custom-call | flops 5033164800 | bytes 9633792 | tf_op jit(solution)/shard_map/cond/branch_1_fun/pallas_call | solution.py:249
  (15 shorter events, 0.1 us)
Async XLA Ops:
  0.0 2.2 %copy-start = (s32[8,4]{0,1:T(4,128)S(1)}, s32[8,4]{0,1:T(4,128)}, u32[]{:S(2)}) copy-start(s32[8,4]{0,1:T(4,128)} %param.17) | copy-start | bytes 388
  0.0 2.5 %collective-permute-start = (f32[2,128,128]{2,1,0:T(8,128)}, f32[2,128,128]{2,1,0:T(8,128)S(1)}, u32[]{:S(2)}, u32[]{:S(2)}) collective-permute-start(f32[2,128,128]{2,1,0:T(8,128)} %param.16), channel_id=1, source_target_pairs={{8,1},{9,2},{10,3},{11,4},{12,5},{13,6},{14,7}} | collective-permute-start | bytes 393224 | tf_op jit(solution)/shard_map/ppermute | solution.py:220
  0.8 1.7 %collective-permute-start.1 = (f32[2,128,128]{2,1,0:T(8,128)}, f32[2,128,128]{2,1,0:T(8,128)S(1)}, u32[]{:S(2)}, u32[]{:S(2)}) collective-permute-start(f32[2,128,128]{2,1,0:T(8,128)} %param.16), channel_id=1, source_target_pairs={{8,2},{9,3},{10,4},{11,5},{12,6},{13,7}} | collective-permute-start | bytes 393224 | tf_op jit(solution)/shard_map/ppermute | solution.py:220
  1.5 1.0 %collective-permute-start.2 = (f32[2,128,128]{2,1,0:T(8,128)}, f32[2,128,128]{2,1,0:T(8,128)S(1)}, u32[]{:S(2)}, u32[]{:S(2)}) collective-permute-start(f32[2,128,128]{2,1,0:T(8,128)} %param.16), channel_id=1, source_target_pairs={{8,3},{9,4},{10,5},{11,6},{12,7}} | collective-permute-start | bytes 393224 | tf_op jit(solution)/shard_map/ppermute | solution.py:220
  2.6 2.7 %collective-permute-start.3 = (f32[2,128,128]{2,1,0:T(8,128)S(1)}, f32[2,128,128]{2,1,0:T(8,128)S(1)}, u32[]{:S(2)}, u32[]{:S(2)}) collective-permute-start(f32[2,128,128]{2,1,0:T(8,128)S(1)} %get-tuple-element.158), channel_id=1, source_target_pairs={{0,15},{1,14},{2,13},{3,12},{4,11},{5,10},{6,9},{7,8}} | collective-permute-start | bytes 393224 | tf_op jit(solution)/shard_map/ppermute | solution.py:234
  3.2 2.0 %collective-permute-start.4 = (bf16[2,128,128]{2,1,0:T(8,128)(2,1)S(1)}, bf16[2,128,128]{2,1,0:T(8,128)(2,1)S(1)}, u32[]{:S(2)}, u32[]{:S(2)}) collective-permute-start(bf16[2,128,128]{2,1,0:T(8,128)(2,1)S(1)} %get-tuple-element.160), channel_id=1, source_target_pairs={{1,15},{2,14},{3,13},{4,12},{5,11},{6,10},{7,9}} | collective-permute-start | bytes 196616 | tf_op jit(solution)/shard_map/ppermute | solution.py:234
  3.9 1.4 %collective-permute-start.5 = (bf16[2,128,128]{2,1,0:T(8,128)(2,1)S(1)}, bf16[2,128,128]{2,1,0:T(8,128)(2,1)S(1)}, u32[]{:S(2)}, u32[]{:S(2)}) collective-permute-start(bf16[2,128,128]{2,1,0:T(8,128)(2,1)S(1)} %get-tuple-element.160), channel_id=1, source_target_pairs={{2,15},{3,14},{4,13},{5,12},{6,11},{7,10}} | collective-permute-start | bytes 196616 | tf_op jit(solution)/shard_map/ppermute | solution.py:234
  4.6 0.7 collective-permute-start.6
  5.5 2.7 %collective-permute-start.7 = (f32[2,128,128]{2,1,0:T(8,128)S(1)}, f32[2,128,128]{2,1,0:T(8,128)S(1)}, u32[]{:S(2)}, u32[]{:S(2)}) collective-permute-start(f32[2,128,128]{2,1,0:T(8,128)S(1)} %get-tuple-element.161), channel_id=1, source_target_pairs={{8,23},{9,22},{10,21},{11,20},{12,19},{13,18},{14,17},{15,16}} | collective-permute-start | bytes 393224 | tf_op jit(solution)/shard_map/ppermute | solution.py:234
  6.2 2.0 %collective-permute-start.10 = (bf16[2,128,128]{2,1,0:T(8,128)(2,1)S(1)}, bf16[2,128,128]{2,1,0:T(8,128)(2,1)S(1)}, u32[]{:S(2)}, u32[]{:S(2)}) collective-permute-start(bf16[2,128,128]{2,1,0:T(8,128)(2,1)S(1)} %get-tuple-element.162), channel_id=1, source_target_pairs={{11,23},{12,22},{13,21},{14,20},{15,19}} | collective-permute-start | bytes 196616 | tf_op jit(solution)/shard_map/ppermute | solution.py:234
  6.9 1.4 %collective-permute-start.8 = (bf16[2,128,128]{2,1,0:T(8,128)(2,1)S(1)}, bf16[2,128,128]{2,1,0:T(8,128)(2,1)S(1)}, u32[]{:S(2)}, u32[]{:S(2)}) collective-permute-start(bf16[2,128,128]{2,1,0:T(8,128)(2,1)S(1)} %get-tuple-element.162), channel_id=1, source_target_pairs={{9,23},{10,22},{11,21},{12,20},{13,19},{14,18},{15,17}} | collective-permute-start | bytes 196616 | tf_op jit(solution)/shard_map/ppermute | solution.py:234
  7.5 0.7 collective-permute-start.9
  8.5 59.3 %copy-start.1 = (f32[2,128,128]{2,1,0:T(8,128)}, f32[2,128,128]{2,1,0:T(8,128)S(1)}, u32[]{:S(2)}) copy-start(f32[2,128,128]{2,1,0:T(8,128)S(1)} %get-tuple-element.163) | copy-start | bytes 393220
  8.5 59.3 %collective-permute-start.11 = (f32[2,128,128]{2,1,0:T(8,128)S(1)}, f32[2,128,128]{2,1,0:T(8,128)S(1)}, u32[]{:S(2)}, u32[]{:S(2)}) collective-permute-start(f32[2,128,128]{2,1,0:T(8,128)S(1)} %get-tuple-element.163), channel_id=1, source_target_pairs={{16,31},{17,30},{18,29},{19,28},{20,27},{21,26},{22,25},{23,24}} | collective-permute-start | bytes 393224 | tf_op jit(solution)/shard_map/ppermute | solution.py:234
  9.8 58.0 %collective-permute-start.12 = (bf16[2,128,128]{2,1,0:T(8,128)(2,1)S(1)}, bf16[2,128,128]{2,1,0:T(8,128)(2,1)S(1)}, u32[]{:S(2)}, u32[]{:S(2)}) collective-permute-start(bf16[2,128,128]{2,1,0:T(8,128)(2,1)S(1)} %get-tuple-element.164), channel_id=1, source_target_pairs={{17,31},{18,30},{19,29},{20,28},{21,27},{22,26},{23,25}} | collective-permute-start | bytes 196616 | tf_op jit(solution)/shard_map/ppermute | solution.py:234
  11.1 56.7 %collective-permute-start.13 = (bf16[2,128,128]{2,1,0:T(8,128)(2,1)S(1)}, bf16[2,128,128]{2,1,0:T(8,128)(2,1)S(1)}, u32[]{:S(2)}, u32[]{:S(2)}) collective-permute-start(bf16[2,128,128]{2,1,0:T(8,128)(2,1)S(1)} %get-tuple-element.164), channel_id=1, source_target_pairs={{18,31},{19,30},{20,29},{21,28},{22,27},{23,26}} | collective-permute-start | bytes 196616 | tf_op jit(solution)/shard_map/ppermute | solution.py:234
  12.4 55.4 %collective-permute-start.14 = (bf16[2,128,128]{2,1,0:T(8,128)(2,1)S(1)}, bf16[2,128,128]{2,1,0:T(8,128)(2,1)S(1)}, u32[]{:S(2)}, u32[]{:S(2)}) collective-permute-start(bf16[2,128,128]{2,1,0:T(8,128)(2,1)S(1)} %get-tuple-element.164), channel_id=1, source_target_pairs={{19,31},{20,30},{21,29},{22,28},{23,27}} | collective-permute-start | bytes 196616 | tf_op jit(solution)/shard_map/ppermute | solution.py:234
